TPU v7x, 512 devices: a whole 4x8x8 slice. The times are simulated.
512 devices in a mesh: dp: 32 (over y, x), section: 4 (over z_hi), space: 4 (over z_lo, core).
Axes of the slice: x: 4, y: 8, z: 8 (z_hi: 4, z_lo: 2; z = z_hi * 2 + z_lo), core: 2. Of those that a mesh axis runs over, the one named last changes fastest.
Arguments:
- images: bfloat16 [64, 4, 64, 256], P('dp', 'space'), may hold values from -6 to 6
- steps: int32 [64], P('dp'), may hold values from 0 to 999
- out_grad: bfloat16 [64, 4, 64, 256], P('dp', 'space'), may hold values from -0.125 to 0.125
- conv_weight: bfloat16 [4, 3, 3, 256, 256], P('section'), may hold values from -0.125 to 0.125
- gn_gain: float32 [4, 256], P('section'), may hold values from 0.5 to 2
- emb_weight: bfloat16 [4, 256, 512], P('section'), may hold values from -0.375 to 0.375
Outputs:
- grad_conv: float32 [4, 3, 3, 256, 256], P('section')
- grad_gain: float32 [4, 256], P('section')
- grad_emb: float32 [4, 256, 512], P('section')
All inputs are finite; a program needn't handle non-finite values.
Results may differ from a plain program's by a relative error of at most 0.0064.
Values may be sent and summed in bfloat16 or wider, within the bound.
No kernel may reach another device: no remote copies, remote signals or barrier semaphores. Data moves between devices by JAX's collectives and lax.ppermute only.
A program may use at most 64 MiB of HBM per device.

v0:
```python
import math

import jax
import jax.numpy as jnp
from jax import lax
from jax.sharding import PartitionSpec as P

G = 32
FREQ = 256
MICRO = 2


EPS = 1e-05


def from_behind(value, axis, steps):
    count = lax.axis_size(axis)
    initial, last = (max(0, -steps), min(count, count - steps))
    return lax.ppermute(value, axis, [(source, source + steps) for source in range(initial, last)])


def extended(shard, sides, width):
    for axis, dim in sides:
        size, length = (lax.axis_size(axis), shard.shape[dim])
        up = [(i, (i + 1) % size) for i in range(size - 1)]
        down = [(j, i) for i, j in up]
        last = lax.slice_in_dim(shard, length - width, length, axis=dim)
        initial = lax.slice_in_dim(shard, 0, width, axis=dim)
        before = lax.ppermute(last, axis, up)
        after = lax.ppermute(initial, axis, down)
        shard = jnp.concatenate([before, shard, after], axis=dim)
    return shard


def sinusoid(timesteps, feature_n):
    half_n = feature_n // 2
    freqs = jnp.exp(-math.log(10000.0) * jnp.arange(half_n, dtype=jnp.float32) / half_n)
    angles = timesteps.astype(jnp.float32)[:, None] * freqs[None, :]
    return jnp.concatenate([jnp.cos(angles), jnp.sin(angles)], axis=1)


def group_sums(tensor, groups):
    batch_n, height_n, width_n, channels = tensor.shape
    split = tensor.reshape(batch_n, height_n, width_n, groups, channels // groups)
    return (jnp.sum(split, axis=(1, 2, 4)), jnp.sum(split * split, axis=(1, 2, 4)))


def spread(values, channels):
    return jnp.repeat(values, channels // values.shape[1], axis=1)[:, None, None, :]


def normalize(tensor, first_sum, square_sum, gains, scales, shifts, cell_count):
    channels = tensor.shape[3]
    average = first_sum / cell_count
    inverse = lax.rsqrt(square_sum / cell_count - average * average + EPS)
    normed = (tensor - spread(average, channels)) * spread(inverse, channels) * gains
    return normed * (1.0 + scales[:, None, None, :]) + shifts[:, None, None, :]


def patches(padded, height_n, width_n):
    return jnp.concatenate(
        [
            padded[:, vertical : vertical + height_n, lateral : lateral + width_n, :]
            for vertical in range(3)
            for lateral in range(3)
        ],
        axis=3,
    )


def convolve(padded, matrix):
    batch_n, height_p, width_p, channels = padded.shape
    flat = patches(padded, height_p - 2, width_p - 2).reshape(-1, 9 * channels)
    return jnp.dot(flat, matrix, preferred_element_type=jnp.float32).reshape(
        batch_n, height_p - 2, width_p - 2, matrix.shape[1]
    )


def flip_weight(weight):
    channels = weight.shape[2]
    return jnp.transpose(weight[::-1, ::-1], (0, 1, 3, 2)).reshape(9 * channels, channels)


def silu_slope(pre_act):
    sigmoid_v = jax.nn.sigmoid(pre_act)
    return sigmoid_v * (1.0 + pre_act * (1.0 - sigmoid_v))


def pad_columns(tensor):
    return jnp.pad(tensor, ((0, 0), (0, 0), (1, 1), (0, 0)))


def pick(stacked, index):
    return lax.dynamic_index_in_dim(stacked, index, 0, keepdims=False)


def norm_backward(tensor, first_sum, square_sum, gains, scales, shifts, cell_count, d_pre):

    def mapping(tensor_v, first_v, square_v, gains_v, scales_v, shifts_v):
        return normalize(tensor_v, first_v, square_v, gains_v, scales_v, shifts_v, cell_count)

    _, pull_back = jax.vjp(mapping, tensor, first_sum, square_sum, gains, scales, shifts)
    return pull_back(d_pre)


def per_device(images, steps, out_grad, conv_weight, gn_gain, emb_weight):
    section_count = lax.axis_size("section")
    tick_count = MICRO + section_count - 1
    section_no = lax.axis_index("section")
    local_n = images.shape[0] // MICRO
    row_count = images.shape[1]
    col_count = images.shape[2]
    channels = images.shape[3]
    cell_count = row_count * lax.axis_size("space") * col_count * (channels // G)
    weight = conv_weight[0]
    flat_weight = weight.reshape(9 * channels, channels)
    flipped = flip_weight(weight)
    gains = gn_gain[0]
    all_features = sinusoid(steps, FREQ)
    features = all_features.reshape(MICRO, local_n, FREQ)
    embedded = jnp.dot(
        all_features, emb_weight[0].astype(jnp.float32), precision=lax.Precision.HIGHEST
    ).reshape(MICRO, local_n, 2 * channels)
    batches = images.reshape(MICRO, local_n, row_count, col_count, channels)
    cotangents = out_grad.reshape(MICRO, local_n, row_count, col_count, channels)
    blank = jnp.zeros((local_n, row_count, col_count, channels), jnp.bfloat16)
    carried = blank
    skips = []
    kept_in = []
    kept_first = []
    kept_square = []
    kept_pad = []
    for moment in range(tick_count):
        arrived = blank
        if moment > 0:
            arrived = from_behind(carried, "section", 1)
        inputs = jnp.where(section_no == 0, batches[min(moment, MICRO - 1)], arrived)
        late = moment - (section_count - 1)
        if 0 <= late < MICRO:
            joined = (arrived.astype(jnp.float32) + skips[late].astype(jnp.float32)).astype(
                jnp.bfloat16
            )
            inputs = jnp.where(section_no == section_count - 1, joined, inputs)
        which = jnp.clip(moment - section_no, 0, MICRO - 1)
        chosen = pick(embedded, which)
        tensor = inputs.astype(jnp.float32)
        first_sum, square_sum = group_sums(tensor, G)
        first_sum, square_sum = lax.psum((first_sum, square_sum), "space")
        pre_act = normalize(
            tensor,
            first_sum,
            square_sum,
            gains,
            chosen[:, :channels],
            chosen[:, channels:],
            cell_count,
        )
        activation = jax.nn.silu(pre_act).astype(jnp.bfloat16)
        padded = pad_columns(extended(activation, (("space", 1),), 1))
        conv_out = convolve(padded, flat_weight)
        output = (tensor + conv_out).astype(jnp.bfloat16)
        if moment < MICRO:
            skips.append(from_behind(output, "section", section_count - 1))
        kept_in.append(inputs)
        kept_first.append(first_sum)
        kept_square.append(square_sum)
        kept_pad.append(padded)
        carried = output
    stack_in = jnp.stack(kept_in)
    stack_first = jnp.stack(kept_first)
    stack_square = jnp.stack(kept_square)
    stack_pad = jnp.stack(kept_pad)
    weight_grad = jnp.zeros((9 * channels, channels), jnp.float32)
    gain_grad = jnp.zeros((channels,), jnp.float32)
    emb_grad = jnp.zeros((FREQ, 2 * channels), jnp.float32)
    carried = blank
    skip_grads = []
    for moment in range(tick_count):
        arrived = blank
        if moment > 0:
            arrived = from_behind(carried, "section", -1)
        top_grad = cotangents[moment] if moment < MICRO else blank
        upstream = jnp.where(section_no == section_count - 1, top_grad, arrived)
        early = moment - (section_count - 1)
        if 0 <= early < MICRO:
            joined = (arrived.astype(jnp.float32) + skip_grads[early].astype(jnp.float32)).astype(
                jnp.bfloat16
            )
            upstream = jnp.where(section_no == 0, joined, upstream)
        which_raw = moment - (section_count - 1) + section_no
        valid = (which_raw >= 0) & (which_raw < MICRO)
        upstream = jnp.where(valid, upstream, blank)
        which = jnp.clip(which_raw, 0, MICRO - 1)
        forward_at = jnp.clip(which_raw + section_no, 0, tick_count - 1)
        tensor = pick(stack_in, forward_at).astype(jnp.float32)
        first_sum = pick(stack_first, forward_at)
        square_sum = pick(stack_square, forward_at)
        chosen = pick(embedded, which)
        scales = chosen[:, :channels]
        shifts = chosen[:, channels:]
        pre_act = normalize(tensor, first_sum, square_sum, gains, scales, shifts, cell_count)
        padded = pick(stack_pad, forward_at)
        flat_patch = patches(padded, row_count, col_count).reshape(-1, 9 * channels)
        weight_grad = weight_grad + jnp.dot(
            flat_patch.T, upstream.reshape(-1, channels), preferred_element_type=jnp.float32
        )
        up_pad = pad_columns(extended(upstream, (("space", 1),), 1))
        d_act = convolve(up_pad, flipped)
        d_pre = d_act * silu_slope(pre_act)
        d_tensor, d_first, d_square, d_gains, d_scales, d_shifts = norm_backward(
            tensor, first_sum, square_sum, gains, scales, shifts, cell_count, d_pre
        )
        d_first, d_square = lax.psum((d_first, d_square), "space")
        d_tensor = d_tensor + spread(d_first, channels) + 2.0 * tensor * spread(d_square, channels)
        d_input = (upstream.astype(jnp.float32) + d_tensor).astype(jnp.bfloat16)
        gain_grad = gain_grad + d_gains
        emb_grad = emb_grad + jnp.dot(
            pick(features, which).T,
            jnp.concatenate([d_scales, d_shifts], axis=1),
            precision=lax.Precision.HIGHEST,
        )
        if moment < MICRO:
            skip_grads.append(from_behind(d_input, "section", -(section_count - 1)))
        carried = d_input
    grads = (weight_grad.reshape(1, 3, 3, channels, channels), gain_grad[None], emb_grad[None])
    totals = lax.psum((grads[0], grads[1], grads[2]), ("dp", "space"))
    return (totals[0], totals[1], totals[2])


def solution(mesh):
    in_specs = (
        P("dp", "space", None, None),
        P("dp"),
        P("dp", "space", None, None),
        P("section", None, None, None, None),
        P("section", None),
        P("section", None, None),
    )
    out_specs = (P("section", None, None, None, None), P("section", None), P("section", None, None))
    return jax.shard_map(
        per_device, mesh=mesh, in_specs=in_specs, out_specs=out_specs, check_vma=False
    )
```

profile of v0, /device:TPU:1, one launch (start us, length us, event | category | flops | bytes accessed | tf_op | source)
XLA Modules:
  0.0 1326.0 jit_solution(16995887459301476496)
XLA Ops:
  8.0 8.8 collective-permute-start.17
  20.7 5.5 all-reduce.19
  31.0 3.2 collective-permute-start
  39.9 6.3 collective-permute-start.9
  54.2 5.1 all-reduce.18
  59.7 3.0 collective-permute-start.4
  62.7 3.2 collective-permute-start.3
  72.0 7.0 all-reduce.17
  81.5 3.7 collective-permute-start.6
  86.8 4.8 collective-permute-start.8
  93.7 7.0 all-reduce.16
  103.7 3.7 collective-permute-start.10
  109.8 5.5 collective-permute-start.12
  117.3 7.0 all-reduce.15
  127.8 5.8 all-reduce.14
  135.3 5.9 collective-permute-done.18
  141.3 4.8 collective-permute-start.20
  150.8 5.4 all-reduce.13
  157.9 6.2 collective-permute-done.21
  164.2 3.0 collective-permute-start.23
  167.2 3.7 collective-permute-start.22
  175.2 5.1 all-reduce.12
  182.0 5.1 collective-permute-done.24
  187.1 4.2 collective-permute-start.27
  191.3 2.8 collective-permute-start.26
  196.2 6.1 all-reduce.11
  204.9 3.7 collective-permute-start.14
  209.9 5.7 collective-permute-done.28
  217.5 3.8 collective-permute-start.30
  228.0 275.3 %psum.178 = f32[1,256]{1,0:T(1,128)} all-reduce(f32[1,256]{1,0:T(1,128)S(1)} %bitcast.511), channel_id=1, replica_groups=mesh['dp'=32,'section'=4,'space'=4] {'dp','space'}, use_global_device_ids=true, to_apply=%region_60.61 | all-reduce | flops 256 | bytes 2048 | tf_op jit(solution)/shard_map/psum | solution.py:226
  503.4 811.7 %all-reduce.22.cloned.1.call-done = (f32[1,3,3,256,256]{4,3,2,1,0:T(8,128)}, f32[1,256,512]{2,1,0:T(8,128)}) async-done(((f32[1,3,3,256,256]{4,3,2,1,0:T(8,128)}, f32[1,256,512]{2,1,0:T(8,128)}), (f32[1,3,3,256,256]{4,3,2,1,0:T(8,128)}, f32[1,256,512]{2,1,0:T(8,128)})) %all-reduce.22.cloned.1.call-update) | async-done | bytes 2883600 | tf_op jit(solution)/shard_map/psum | solution.py:226
  1315.1 3.3 copy.140
  (416 shorter events, 74.5 us)
Async XLA Ops:
  7.2 1307.9 %all-reduce.22.cloned.1.call-start = ((), (), s32[]{:S(2)}) async-start(), calls=%async_computation | async-start | bytes 5767168 | tf_op jit(solution)/shard_map/psum | solution.py:226
  8.0 39.4 %collective-permute-start.17 = (bf16[1,1,64,256]{3,2,1,0:T(8,128)(2,1)S(1)}, bf16[1,1,64,256]{3,2,1,0:T(8,128)(2,1)S(1)}, u32[]{:S(2)}, u32[]{:S(2)}) collective-permute-start(bf16[1,1,64,256]{3,2,1,0:T(8,128)(2,1)S(1)} %select_select_fusion.2), channel_id=1, source_target_pairs={{1,0},{2,1},{3,2},{5,4},{6,5},{7,6},{9,8},{10,9},{11,10},{13,12},{... | collective-permute-start | bytes 98312 | tf_op jit(solution)/shard_map/ppermute | solution.py:30
  16.8 30.6 %collective-permute-start.16 = (bf16[1,1,64,256]{3,2,1,0:T(8,128)(2,1)S(1)}, bf16[1,1,64,256]{3,2,1,0:T(8,128)(2,1)S(1)}, u32[]{:S(2)}, u32[]{:S(2)}) collective-permute-start(bf16[1,1,64,256]{3,2,1,0:T(8,128)(2,1)S(1)} %select_select_fusion.2), channel_id=1, source_target_pairs={{0,1},{1,2},{2,3},{4,5},{5,6},{6,7},{8,9},{9,10},{10,11},{12,13},{... | collective-permute-start | bytes 98312 | tf_op jit(solution)/shard_map/ppermute | solution.py:29
  28.4 10.5 collective-permute-start.1
  31.0 7.9 collective-permute-start
  39.9 51.8 %collective-permute-start.9 = (bf16[1,1,64,256]{3,2,1,0:T(8,128)(2,1)S(1)}, bf16[1,1,64,256]{3,2,1,0:T(8,128)(2,1)S(1)}, u32[]{:S(2)}, u32[]{:S(2)}) collective-permute-start(bf16[1,1,64,256]{3,2,1,0:T(8,128)(2,1)S(1)} %fusion.8), channel_id=1, source_target_pairs={{0,12},{1,13},{2,14},{3,15},{16,28},{17,29},{18,30},{19,31},{32,44... | collective-permute-start | bytes 98312 | tf_op jit(solution)/shard_map/ppermute | solution.py:19
  46.1 7.0 collective-permute-start.2
  59.7 6.1 collective-permute-start.4
  62.7 4.2 collective-permute-start.3
  67.4 48.4 %collective-permute-start.13 = (bf16[1,1,64,256]{3,2,1,0:T(8,128)(2,1)S(1)}, bf16[1,1,64,256]{3,2,1,0:T(8,128)(2,1)S(1)}, u32[]{:S(2)}, u32[]{:S(2)}) collective-permute-start(bf16[1,1,64,256]{3,2,1,0:T(8,128)(2,1)S(1)} %fusion.6), channel_id=1, source_target_pairs={{0,12},{1,13},{2,14},{3,15},{16,28},{17,29},{18,30},{19,31},{32,44... | collective-permute-start | bytes 98312 | tf_op jit(solution)/shard_map/ppermute | solution.py:19
  79.4 5.9 collective-permute-start.7
  81.5 4.7 collective-permute-start.6
  86.8 5.9 collective-permute-start.8
  101.6 5.8 collective-permute-start.11
  103.7 4.7 collective-permute-start.10
  109.8 6.5 collective-permute-start.12
  134.0 7.3 collective-permute-start.18
  141.3 8.4 collective-permute-start.20
  146.1 3.7 collective-permute-start.19
  148.1 33.9 %collective-permute-start.25 = (bf16[1,1,64,256]{3,2,1,0:T(8,128)(2,1)S(1)}, bf16[1,1,64,256]{3,2,1,0:T(8,128)(2,1)S(1)}, u32[]{:S(2)}, u32[]{:S(2)}) collective-permute-start(bf16[1,1,64,256]{3,2,1,0:T(8,128)(2,1)S(1)} %fusion.123), channel_id=1, source_target_pairs={{12,0},{13,1},{14,2},{15,3},{28,16},{29,17},{30,18},{31,19},{44,32... | collective-permute-start | bytes 98312 | tf_op jit(solution)/shard_map/ppermute | solution.py:19
  156.6 7.6 collective-permute-start.21
  164.2 9.9 collective-permute-start.23
  167.2 6.9 collective-permute-start.22
  172.8 37.1 %collective-permute-start.29 = (bf16[1,1,64,256]{3,2,1,0:T(8,128)(2,1)S(1)}, bf16[1,1,64,256]{3,2,1,0:T(8,128)(2,1)S(1)}, u32[]{:S(2)}, u32[]{:S(2)}) collective-permute-start(bf16[1,1,64,256]{3,2,1,0:T(8,128)(2,1)S(1)} %fusion.75), channel_id=1, source_target_pairs={{12,0},{13,1},{14,2},{15,3},{28,16},{29,17},{30,18},{31,19},{44,32... | collective-permute-start | bytes 98312 | tf_op jit(solution)/shard_map/ppermute | solution.py:19
  180.7 6.4 collective-permute-start.24
  187.1 7.0 collective-permute-start.27
  191.3 3.8 collective-permute-start.26
  202.7 18.7 %collective-permute-start.15 = (bf16[1,1,64,256]{3,2,1,0:T(8,128)(2,1)S(1)}, bf16[1,1,64,256]{3,2,1,0:T(8,128)(2,1)S(1)}, u32[]{:S(2)}, u32[]{:S(2)}) collective-permute-start(bf16[1,1,64,256]{3,2,1,0:T(8,128)(2,1)S(1)} %get-tuple-element.118), channel_id=1, source_target_pairs={{1,0},{2,1},{3,2},{5,4},{6,5},{7,6},{9,8},{10,9},{11,10},{13,12},{... | collective-permute-start | bytes 98312 | tf_op jit(solution)/shard_map/ppermute | solution.py:30
  204.9 16.5 %collective-permute-start.14 = (bf16[1,1,64,256]{3,2,1,0:T(8,128)(2,1)S(1)}, bf16[1,1,64,256]{3,2,1,0:T(8,128)(2,1)S(1)}, u32[]{:S(2)}, u32[]{:S(2)}) collective-permute-start(bf16[1,1,64,256]{3,2,1,0:T(8,128)(2,1)S(1)} %get-tuple-element.118), channel_id=1, source_target_pairs={{0,1},{1,2},{2,3},{4,5},{5,6},{6,7},{8,9},{9,10},{10,11},{12,13},{... | collective-permute-start | bytes 98312 | tf_op jit(solution)/shard_map/ppermute | solution.py:29
  208.5 7.0 collective-permute-start.28
  215.6 10.7 collective-permute-start.31
  217.5 8.8 collective-permute-start.30
  (29 other events, 276.0 us)
Sparse Core Ops, SparseCore 0:
  228.2 1086.9 all-reduce.21
where the time goes:
time: 1330 us
  waiting for transfers between devices  841 us (63%)
  blocking collectives  329 us (25%)
  starting transfers between devices  94.5 us (7%)
  local copies, waits for them, and re-layouts  20.9 us (2%)
  between operations  16.3 us (1%)
  other arithmetic  15.7 us (1%)
    psum x1, waiting for transfers between devices, per_device(): totals = lax.psum((grads[0], grads[1], grads[2]), ('dp', 'space'))  812 us
    psum x1, blocking collectives, per_device(): totals = lax.psum((grads[0], grads[1], grads[2]), ('dp', 'space'))  275 us
    ppermute x10, starting transfers between devices, extended(): after = lax.ppermute(initial, axis, down)  34.5 us
    ppermute x10, starting transfers between devices, extended(): before = lax.ppermute(last, axis, up)  31.7 us
    psum x5, blocking collectives, per_device(): first_sum, square_sum = lax.psum((first_sum, square_sum), 'space')  31.5 us
    ppermute x12, starting transfers between devices, from_behind(): lax.ppermute(value, axis, [(source, source + steps) for source in range(i...  28.2 us
  transfers between devices with their start and end apart: 33, of which 12 were waited for; matrix products, arithmetic and copies ran while one was open for 2% of the time, Pallas kernels for 0%

commit v1 on v0

v1 whole, which is shorter than its diff:
```python
import math

import jax
import jax.numpy as jnp
from jax import lax
from jax.sharding import Mesh, PartitionSpec as P

G = 32
FREQ = 256
MICRO = 2


EPS = 1e-05


def from_behind(value, axis, steps):
    count = lax.axis_size(axis)
    initial, last = (max(0, -steps), min(count, count - steps))
    return lax.ppermute(value, axis, [(source, source + steps) for source in range(initial, last)])


def extended(shard, sides, width):
    for axis, dim in sides:
        size, length = (lax.axis_size(axis), shard.shape[dim])
        up = [(i, (i + 1) % size) for i in range(size - 1)]
        down = [(j, i) for i, j in up]
        last = lax.slice_in_dim(shard, length - width, length, axis=dim)
        initial = lax.slice_in_dim(shard, 0, width, axis=dim)
        before = lax.ppermute(last, axis, up)
        after = lax.ppermute(initial, axis, down)
        shard = jnp.concatenate([before, shard, after], axis=dim)
    return shard


def sinusoid(timesteps, feature_n):
    half_n = feature_n // 2
    freqs = jnp.exp(-math.log(10000.0) * jnp.arange(half_n, dtype=jnp.float32) / half_n)
    angles = timesteps.astype(jnp.float32)[:, None] * freqs[None, :]
    return jnp.concatenate([jnp.cos(angles), jnp.sin(angles)], axis=1)


def group_sums(tensor, groups):
    batch_n, height_n, width_n, channels = tensor.shape
    split = tensor.reshape(batch_n, height_n, width_n, groups, channels // groups)
    return (jnp.sum(split, axis=(1, 2, 4)), jnp.sum(split * split, axis=(1, 2, 4)))


def spread(values, channels):
    return jnp.repeat(values, channels // values.shape[1], axis=1)[:, None, None, :]


def normalize(tensor, first_sum, square_sum, gains, scales, shifts, cell_count):
    channels = tensor.shape[3]
    average = first_sum / cell_count
    inverse = lax.rsqrt(square_sum / cell_count - average * average + EPS)
    normed = (tensor - spread(average, channels)) * spread(inverse, channels) * gains
    return normed * (1.0 + scales[:, None, None, :]) + shifts[:, None, None, :]


def patches(padded, height_n, width_n):
    return jnp.concatenate(
        [
            padded[:, vertical : vertical + height_n, lateral : lateral + width_n, :]
            for vertical in range(3)
            for lateral in range(3)
        ],
        axis=3,
    )


def convolve(padded, matrix):
    batch_n, height_p, width_p, channels = padded.shape
    flat = patches(padded, height_p - 2, width_p - 2).reshape(-1, 9 * channels)
    return jnp.dot(flat, matrix, preferred_element_type=jnp.float32).reshape(
        batch_n, height_p - 2, width_p - 2, matrix.shape[1]
    )


def flip_weight(weight):
    channels = weight.shape[2]
    return jnp.transpose(weight[::-1, ::-1], (0, 1, 3, 2)).reshape(9 * channels, channels)


def silu_slope(pre_act):
    sigmoid_v = jax.nn.sigmoid(pre_act)
    return sigmoid_v * (1.0 + pre_act * (1.0 - sigmoid_v))


def pad_columns(tensor):
    return jnp.pad(tensor, ((0, 0), (0, 0), (1, 1), (0, 0)))


def pick(stacked, index):
    return lax.dynamic_index_in_dim(stacked, index, 0, keepdims=False)


def norm_backward(tensor, first_sum, square_sum, gains, scales, shifts, cell_count, d_pre):

    def mapping(tensor_v, first_v, square_v, gains_v, scales_v, shifts_v):
        return normalize(tensor_v, first_v, square_v, gains_v, scales_v, shifts_v, cell_count)

    _, pull_back = jax.vjp(mapping, tensor, first_sum, square_sum, gains, scales, shifts)
    return pull_back(d_pre)


def pad_both(tensor):
    return jnp.pad(tensor, ((0, 0), (1, 1), (1, 1), (0, 0)))


def block_forward(inputs, flat_weight, gains, scales, shifts, cell_count):
    tensor = inputs.astype(jnp.float32)
    first_sum, square_sum = group_sums(tensor, G)
    pre_act = normalize(tensor, first_sum, square_sum, gains, scales, shifts, cell_count)
    activation = jax.nn.silu(pre_act).astype(jnp.bfloat16)
    padded = pad_both(activation)
    output = (tensor + convolve(padded, flat_weight)).astype(jnp.bfloat16)
    return output, (first_sum, square_sum, padded)


def block_backward(upstream, inputs, saved, flipped, gains, scales, shifts, cell_count):
    first_sum, square_sum, _ = saved
    channels = inputs.shape[3]
    tensor = inputs.astype(jnp.float32)
    pre_act = normalize(tensor, first_sum, square_sum, gains, scales, shifts, cell_count)
    d_act = convolve(pad_both(upstream), flipped)
    d_pre = d_act * silu_slope(pre_act)
    d_tensor, d_first, d_square, d_gains, d_scales, d_shifts = norm_backward(
        tensor, first_sum, square_sum, gains, scales, shifts, cell_count, d_pre
    )
    d_tensor = d_tensor + spread(d_first, channels) + 2.0 * tensor * spread(d_square, channels)
    d_input = (upstream.astype(jnp.float32) + d_tensor).astype(jnp.bfloat16)
    return d_input, (d_gains, d_scales, d_shifts)


def keep(flag, new, old):
    return jax.tree.map(lambda a, b: jnp.where(flag, a, b), new, old)


def per_device(images, steps, out_grad, conv_weight, gn_gain, emb_weight):
    section_count = lax.axis_size("section")
    section_no = lax.axis_index("section")
    images = lax.all_gather(images, "space", axis=1, tiled=True)
    out_grad = lax.all_gather(out_grad, "space", axis=1, tiled=True)
    row_count = images.shape[1]
    col_count = images.shape[2]
    channels = images.shape[3]
    cell_count = row_count * col_count * (channels // G)
    weight = conv_weight[0]
    flat_weight = weight.reshape(9 * channels, channels)
    flipped = flip_weight(weight)
    gains = gn_gain[0]
    features = sinusoid(steps, FREQ)
    embedded = jnp.dot(features, emb_weight[0].astype(jnp.float32), precision=lax.Precision.HIGHEST)
    scales = embedded[:, :channels]
    shifts = embedded[:, channels:]
    last = section_count - 1
    carried = images
    kept = None
    for moment in range(section_count):
        inputs = images
        if moment > 0:
            inputs = lax.ppermute(carried, "section", [(moment - 1, moment)])
        if moment == last:
            inputs = (inputs.astype(jnp.float32) + skip.astype(jnp.float32)).astype(jnp.bfloat16)
        output, saved = block_forward(inputs, flat_weight, gains, scales, shifts, cell_count)
        if moment == 0:
            skip = lax.ppermute(output, "section", [(0, last)])
        state = (inputs, saved)
        kept = state if kept is None else keep(section_no == moment, state, kept)
        carried = output
    kept_in, kept_saved = kept
    carried = out_grad
    kept = None
    for moment in range(section_count):
        active = last - moment
        upstream = out_grad
        if moment > 0:
            upstream = lax.ppermute(carried, "section", [(active + 1, active)])
        if active == 0:
            upstream = (upstream.astype(jnp.float32) + skip_grad.astype(jnp.float32)).astype(
                jnp.bfloat16
            )
        d_input, pieces = block_backward(
            upstream, kept_in, kept_saved, flipped, gains, scales, shifts, cell_count
        )
        if moment == 0:
            skip_grad = lax.ppermute(d_input, "section", [(last, 0)])
        state = (upstream, pieces)
        kept = state if kept is None else keep(section_no == active, state, kept)
        carried = d_input
    kept_up, (d_gains, d_scales, d_shifts) = kept
    space_count = lax.axis_size("space")
    space_no = lax.axis_index("space")
    patch_rows = 9 * channels // space_count
    flat_patch = patches(kept_saved[2], row_count, col_count).reshape(-1, 9 * channels)
    own_patch = lax.dynamic_slice_in_dim(flat_patch, space_no * patch_rows, patch_rows, axis=1)
    weight_grad = jnp.dot(
        own_patch.T, kept_up.reshape(-1, channels), preferred_element_type=jnp.float32
    )
    emb_rows = FREQ // space_count
    own_features = lax.dynamic_slice_in_dim(features, space_no * emb_rows, emb_rows, axis=1)
    emb_grad = jnp.dot(
        own_features.T,
        jnp.concatenate([d_scales, d_shifts], axis=1),
        precision=lax.Precision.HIGHEST,
    )
    return reduce_grads(weight_grad, d_gains, emb_grad)


def reduce_grads(weight_grad, gain_grad, emb_grad):
    channels = gain_grad.shape[0]
    parts = [weight_grad, emb_grad.reshape(-1, channels), gain_grad[None]]
    rows = sum(part.shape[0] for part in parts)
    devices = lax.axis_size("dx") * lax.axis_size("dy")
    padded_rows = -(-rows // (8 * devices)) * 8 * devices
    parts.append(jnp.zeros((padded_rows - rows, channels), jnp.float32))
    flat = jnp.concatenate(parts, axis=0)
    for axis in ("dx", "dy"):
        flat = lax.psum_scatter(flat, axis, scatter_dimension=0, tiled=True)
    for axis in ("dy", "dx"):
        flat = lax.all_gather(flat, axis, axis=0, tiled=True)
    flat = lax.all_gather(flat, "space", axis=0)
    space_count = flat.shape[0]
    weight_rows = weight_grad.shape[0]
    emb_rows = emb_grad.size // channels
    conv = flat[:, :weight_rows].reshape(1, 3, 3, channels, channels)
    emb = flat[:, weight_rows : weight_rows + emb_rows].reshape(1, emb_grad.shape[0] * space_count, -1)
    gain = flat[0, weight_rows + emb_rows][None]
    return (conv, gain, emb)


def solution(mesh):
    dp_n = mesh.shape["dp"]
    dx_n = 4 if dp_n % 4 == 0 else 1
    mesh = Mesh(
        mesh.devices.reshape(dp_n // dx_n, dx_n, *mesh.devices.shape[1:]),
        ("dy", "dx", "section", "space"),
    )
    data = ("dy", "dx")
    in_specs = (
        P(data, "space", None, None),
        P(data),
        P(data, "space", None, None),
        P("section", None, None, None, None),
        P("section", None),
        P("section", None, None),
    )
    out_specs = (P("section", None, None, None, None), P("section", None), P("section", None, None))
    return jax.shard_map(
        per_device, mesh=mesh, in_specs=in_specs, out_specs=out_specs, check_vma=False
    )
```

time: 1330 us -> 302 us (0.23)
  waiting for transfers between devices: 841 us -> 144 us
  blocking collectives: 329 us -> 54.2 us
  starting transfers between devices: 94.5 us -> 12.2 us
  local copies, waits for them, and re-layouts: 20.9 us -> 43.6 us
    psum x1 -> x0, waiting for transfers between devices: 812 us -> none  [per_device(): totals = lax.psum((grads[0], grads[1], grads[2]), ('dp', 'space'))]
    psum x10 -> x0, blocking collectives: 329 us -> none  [the longest x1 275 us: per_device(): totals = lax.psum((grads[0], grads[1], grads[2]), ('dp', 'space'))]
    ppermute x32 -> x8, starting transfers between devices: 94.4 us -> 12.1 us  [the longest x1 4.67 us: per_device(): skip = lax.ppermute(output, 'section', [(0, last)])]
    reduce_scatter x0 -> x2, waiting for transfers between devices: none -> 73.4 us  [reduce_grads(): flat = lax.psum_scatter(flat, axis, scatter_dimension=0, tiled=True)]
    all_gather x0 -> x1, waiting for transfers between devices: none -> 56.3 us  [reduce_grads(): flat = lax.all_gather(flat, 'space', axis=0)]
    all_gather x0 -> x4, blocking collectives: none -> 54.2 us  [the longest x2 30.7 us: reduce_grads(): flat = lax.all_gather(flat, axis, axis=0, tiled=True)]
    ppermute x32 -> x8, waiting for transfers between devices: 29.3 us -> 13.9 us  [the longest x3 13.3 us: per_device(): upstream = lax.ppermute(carried, 'section', [(active + 1, active)])]
  transfers between devices with their start and end apart: 33 -> 11, of which waited for: 12 -> 5; matrix products, arithmetic and copies ran while one was open for 2% -> 9% of each run, Pallas kernels for 0% -> 0%
where the time goes in v1:
time: 302 us; the launch traced here: 301 us
  waiting for transfers between devices  144 us (48%)
  blocking collectives  54.2 us (18%)
  local copies, waits for them, and re-layouts  43.6 us (14%)
  other arithmetic  17.7 us (6%)
  between operations  15 us (5%)
  matrix products  14.7 us (5%)
  starting transfers between devices  12.2 us (4%)
    reduce_scatter x2, waiting for transfers between devices, reduce_grads(): flat = lax.psum_scatter(flat, axis, scatter_dimension=0, tiled=True)  73.4 us
    all_gather x1, waiting for transfers between devices, reduce_grads(): flat = lax.all_gather(flat, 'space', axis=0)  56.3 us
    all_gather x2, blocking collectives, reduce_grads(): flat = lax.all_gather(flat, axis, axis=0, tiled=True)  30.7 us
    unnamed x144, local copies, waits for them, and re-layouts  14.3 us
    ppermute x3, waiting for transfers between devices, per_device(): upstream = lax.ppermute(carried, 'section', [(active + 1, active)])  13.3 us
    all_gather x1, blocking collectives, per_device(): images = lax.all_gather(images, 'space', axis=1, tiled=True)  12.7 us
    dot_general x7, matrix products, convolve(): jnp.dot(flat, matrix, preferred_element_type=jnp.float32)  12.3 us
    all_gather x1, blocking collectives, per_device(): out_grad = lax.all_gather(out_grad, 'space', axis=1, tiled=True)  10.7 us
  transfers between devices with their start and end apart: 11, of which 5 were waited for; matrix products, arithmetic and copies ran while one was open for 9% of the time, Pallas kernels for 0%

profile of v1, /device:TPU:1, one launch (start us, length us, event | category | flops | bytes accessed | tf_op | source)
XLA Modules:
  0.0 301.1 jit_solution(14954645292781372341)
XLA Ops:
  8.3 12.7 %all_gather.18 = bf16[2,4,64,256]{3,2,1,0:T(8,128)(2,1)S(1)} all-gather(bf16[2,1,64,256]{3,2,1,0:T(8,128)(2,1)} %param.6), channel_id=1, replica_groups=mesh['dy'=8,'dx'=4,'section'=4,'space'=4] {'space'}, dimensions={1}, use_global_device_ids=true | all-gather | bytes 327680 | tf_op jit(solution)/shard_map/all_gather | solution.py:142
  24.6 1.5 fusion
  27.4 4.7 %collective-permute-start.3 = (bf16[2,4,64,256]{3,2,1,0:T(8,128)(2,1)}, bf16[2,4,64,256]{3,2,1,0:T(8,128)(2,1)S(1)}, u32[]{:S(2)}, u32[]{:S(2)}) collective-permute-start(bf16[2,4,64,256]{3,2,1,0:T(8,128)(2,1)} %fusion), channel_id=1, source_target_pairs={{0,12},{1,13},{2,14},{3,15},{16,28},{17,29},{18,30},{19,31},{32,44... | collective-permute-start | bytes 786440 | tf_op jit(solution)/shard_map/ppermute | solution.py:167
  32.1 10.7 %all_gather.19 = bf16[2,4,64,256]{3,2,1,0:T(8,128)(2,1)S(1)} all-gather(bf16[2,1,64,256]{3,2,1,0:T(8,128)(2,1)S(1)} %copy-done.7), channel_id=1, replica_groups=mesh['dy'=8,'dx'=4,'section'=4,'space'=4] {'space'}, dimensions={1}, use_global_device_ids=true | all-gather | bytes 327680 | tf_op jit(solution)/shard_map/all_gather | solution.py:143
  54.2 1.5 fusion.2
  55.6 1.3 collective-permute-start.2
  57.7 1.6 copy.9
  61.9 2.3 fusion.28
  68.2 3.3 %fusion.23 = (f32[2,256]{1,0:T(2,128)}, f32[256]{0:T(256)}, f32[2,256]{1,0:T(2,128)S(1)}, f32[2,256]{1,0:T(2,128)S(1)}, f32[2,256]{1,0:T(2,128)}, /*index=5*/f32[2,4,64,256]{3,2,1,0:T(8,128)S(1)}) fusion(bf16[2,4,64,256]{3,2,1,0:T(8,128)(2,1)S(1)} %select_select_fusion.1, f32[2,256]{1,0:T(2,128)S(1)} %mul.236, f32[2,256]{1,0:T(2,128)} %sub.58, ...), kind=kOutput, calls=%fused_computation.105 | convolution fusion | flops 607254272 | bytes 4343808 | tf_op jit(solution)/shard_map/dot_general | solution.py:74
  74.2 1.7 fusion.22
  75.9 1.4 reduce_sum.452
  77.2 1.4 reduce_sum.453
  78.7 1.4 reshape.213
  80.0 1.4 reduce_sum.455
  83.4 1.4 add.223
  84.8 1.4 broadcast_in_dim.47
  86.2 1.4 mul.509
  89.2 1.5 collective-permute-start.7
  91.2 2.4 fusion.21
  98.7 1.4 broadcast_in_dim.41
  100.0 1.4 mul.228
  101.5 1.4 broadcast_in_dim.40
  102.8 1.4 sub.54
  104.9 13.3 %collective-permute-done.6 = bf16[2,4,64,256]{3,2,1,0:T(8,128)(2,1)} collective-permute-done((bf16[2,4,64,256]{3,2,1,0:T(8,128)(2,1)S(1)}, bf16[2,4,64,256]{3,2,1,0:T(8,128)(2,1)}, u32[]{:S(2)}, u32[]{:S(2)}) %collective-permute-start.6) | collective-permute-done | bytes 262176 | tf_op jit(solution)/shard_map/ppermute | solution.py:178
  122.8 1.3 copy-done.4
  124.5 1.8 fusion.17
  127.5 36.3 %reduce-scatter.3.cloned.1.call-done = f32[192,256]{1,0:T(8,128)} async-done(((f32[768,256]{1,0:T(8,128)}), f32[192,256]{1,0:T(8,128)}) %reduce-scatter.3.cloned.1.call-update) | async-done | bytes 196624 | tf_op jit(solution)/shard_map/reduce_scatter | solution.py:219
  163.9 37.1 %reduce-scatter.5.cloned.1.call-done = f32[24,256]{1,0:T(8,128)} async-done(((f32[192,256]{1,0:T(8,128)}), f32[24,256]{1,0:T(8,128)}) %reduce-scatter.5.cloned.1.call-update) | async-done | bytes 24592 | tf_op jit(solution)/shard_map/reduce_scatter | solution.py:219
  201.0 19.2 %all_gather.20 = f32[192,256]{1,0:T(8,128)S(1)} all-gather(f32[24,256]{1,0:T(8,128)} %reduce-scatter.5.cloned.1.call-done), channel_id=1, replica_groups=mesh['dy'=8,'dx'=4,'section'=4,'space'=4] {'dy'}, dimensions={0}, use_global_device_ids=true | all-gather | bytes 221184 | tf_op jit(solution)/shard_map/all_gather | solution.py:221
  220.2 11.6 %all_gather.21 = f32[768,256]{1,0:T(8,128)} all-gather(f32[192,256]{1,0:T(8,128)S(1)} %all_gather.20), channel_id=1, replica_groups=mesh['dy'=8,'dx'=4,'section'=4,'space'=4] {'dx'}, dimensions={0}, use_global_device_ids=true | all-gather | bytes 983040 | tf_op jit(solution)/shard_map/all_gather | solution.py:221
  231.7 56.3 %all-gather.3.cloned.1.call-done = f32[3072,256]{1,0:T(8,128)} async-done(((f32[768,256]{1,0:T(8,128)}), f32[3072,256]{1,0:T(8,128)}) %all-gather.3.cloned.1.call-update) | async-done | bytes 3145744 | tf_op jit(solution)/shard_map/all_gather | solution.py:222
  288.1 3.2 %slice.298 = f32[4,576,256]{2,1,0:T(8,128)} slice(f32[4,768,256]{2,1,0:T(8,128)} %bitcast.40), slice={[0:4], [0:576], [0:256]} | slice | bytes 4718592 | tf_op jit(solution)/shard_map/slice | solution.py:226
  (258 shorter events, 45.4 us)
Async XLA Ops:
  7.2 16.4 %copy-start.6 = (f32[1,256]{1,0:T(1,128)S(1)}, f32[1,256]{1,0:T(1,128)}, u32[]{:S(2)}) copy-start(f32[1,256]{1,0:T(1,128)} %param.10) | copy-start | bytes 3076
  7.2 156.6 %reduce-scatter.3.cloned.1.call-start = ((), (), s32[]{:S(2)}) async-start(), calls=%async_computation.2 | async-start | bytes 983040 | tf_op jit(solution)/shard_map/reduce_scatter | solution.py:219
  8.0 13.1 %copy-start.15 = (f32[2,128]{1,0:T(2,128)}, f32[2,128]{1,0:T(2,128)S(1)}, u32[]{:S(2)}) copy-start(f32[2,128]{1,0:T(2,128)S(1)} %get-tuple-element.52) | copy-start | bytes 3076
  8.0 13.1 %copy-start.17 = (f32[2,128]{1,0:T(2,128)}, f32[2,128]{1,0:T(2,128)S(1)}, u32[]{:S(2)}) copy-start(f32[2,128]{1,0:T(2,128)S(1)} %get-tuple-element.53) | copy-start | bytes 3076
  21.4 2.5 copy-start.19
  23.3 1.3 copy-start.1
  24.0 8.1 %copy-start.7 = (bf16[2,1,64,256]{3,2,1,0:T(8,128)(2,1)S(1)}, bf16[2,1,64,256]{3,2,1,0:T(8,128)(2,1)}, u32[]{:S(2)}) copy-start(bf16[2,1,64,256]{3,2,1,0:T(8,128)(2,1)} %param.8) | copy-start | bytes 196612
  26.1 19.0 %collective-permute-start = (bf16[2,4,64,256]{3,2,1,0:T(8,128)(2,1)}, bf16[2,4,64,256]{3,2,1,0:T(8,128)(2,1)S(1)}, u32[]{:S(2)}, u32[]{:S(2)}) collective-permute-start(bf16[2,4,64,256]{3,2,1,0:T(8,128)(2,1)} %fusion), channel_id=1, source_target_pairs={{0,4},{1,5},{2,6},{3,7},{16,20},{17,21},{18,22},{19,23},{32,36},{3... | collective-permute-start | bytes 786440 | tf_op jit(solution)/shard_map/ppermute | solution.py:162
  27.4 34.5 %collective-permute-start.3 = (bf16[2,4,64,256]{3,2,1,0:T(8,128)(2,1)}, bf16[2,4,64,256]{3,2,1,0:T(8,128)(2,1)S(1)}, u32[]{:S(2)}, u32[]{:S(2)}) collective-permute-start(bf16[2,4,64,256]{3,2,1,0:T(8,128)(2,1)} %fusion), channel_id=1, source_target_pairs={{0,12},{1,13},{2,14},{3,15},{16,28},{17,29},{18,30},{19,31},{32,44... | collective-permute-start | bytes 786440 | tf_op jit(solution)/shard_map/ppermute | solution.py:167
  47.9 2.9 collective-permute-start.1
  52.5 1.2 copy-start.11
  55.6 6.3 %collective-permute-start.2 = (bf16[2,4,64,256]{3,2,1,0:T(8,128)(2,1)}, bf16[2,4,64,256]{3,2,1,0:T(8,128)(2,1)}, u32[]{:S(2)}, u32[]{:S(2)}) collective-permute-start(bf16[2,4,64,256]{3,2,1,0:T(8,128)(2,1)} %fusion.2), channel_id=1, source_target_pairs={{8,12},{9,13},{10,14},{11,15},{24,28},{25,29},{26,30},{27,31},{40,... | collective-permute-start | bytes 786440 | tf_op jit(solution)/shard_map/ppermute | solution.py:162
  59.3 6.6 %copy-start.20 = (f32[2,32]{1,0:T(2,128)S(1)}, f32[2,32]{1,0:T(2,128)}, u32[]{:S(2)}) copy-start(f32[2,32]{1,0:T(2,128)} %copy-done.19) | copy-start | bytes 772
  60.4 7.8 %copy-start.2 = (bf16[3,3,256,256]{2,3,1,0:T(8,128)(2,1)S(1)}, bf16[3,3,256,256]{2,3,1,0:T(8,128)(2,1)}, u32[]{:S(2)}) copy-start(bf16[3,3,256,256]{2,3,1,0:T(8,128)(2,1)} %rev.3) | copy-start | bytes 3538948
  68.2 3.7 %copy-start.9 = (f32[2,32]{1,0:T(2,128)S(1)}, f32[2,32]{1,0:T(2,128)}, u32[]{:S(2)}) copy-start(f32[2,32]{1,0:T(2,128)} %copy-done.8) | copy-start | bytes 772
  68.2 3.7 %copy-start.26 = (f32[2,32]{1,0:T(2,128)S(1)}, f32[2,32]{1,0:T(2,128)}, u32[]{:S(2)}) copy-start(f32[2,32]{1,0:T(2,128)} %get-tuple-element.34) | copy-start | bytes 772
  73.0 0.7 collective-permute-start.4
  88.5 2.6 copy-start.28
  88.5 2.2 collective-permute-start.5
  89.2 15.7 %collective-permute-start.7 = (bf16[2,4,64,256]{3,2,1,0:T(8,128)(2,1)}, bf16[2,4,64,256]{3,2,1,0:T(8,128)(2,1)}, u32[]{:S(2)}, u32[]{:S(2)}) collective-permute-start(bf16[2,4,64,256]{3,2,1,0:T(8,128)(2,1)} %copy-done.5), channel_id=1, source_target_pairs={{12,0},{13,1},{14,2},{15,3},{28,16},{29,17},{30,18},{31,19},{44,32... | collective-permute-start | bytes 786440 | tf_op jit(solution)/shard_map/ppermute | solution.py:187
  91.1 2.8 copy-start.10
  91.1 2.8 copy-start.14
  96.7 21.4 %collective-permute-start.6 = (bf16[2,4,64,256]{3,2,1,0:T(8,128)(2,1)S(1)}, bf16[2,4,64,256]{3,2,1,0:T(8,128)(2,1)}, u32[]{:S(2)}, u32[]{:S(2)}) collective-permute-start(bf16[2,4,64,256]{3,2,1,0:T(8,128)(2,1)S(1)} %fusion.59), channel_id=1, source_target_pairs={{4,0},{5,1},{6,2},{7,3},{20,16},{21,17},{22,18},{23,19},{36,32},{3... | collective-permute-start | bytes 786440 | tf_op jit(solution)/shard_map/ppermute | solution.py:178
  122.1 2.0 copy-start.16
  122.1 2.0 copy-start.18
  122.3 4.0 %copy-start.38 = (f32[256]{0:T(256)S(1)}, f32[256]{0:T(256)}, u32[]{:S(2)}) copy-start(f32[256]{0:T(256)} %get-tuple-element.4) | copy-start | bytes 3076
  122.3 4.0 %copy-start.39 = (f32[256]{0:T(256)S(1)}, f32[256]{0:T(256)}, u32[]{:S(2)}) copy-start(f32[256]{0:T(256)} %get-tuple-element.7) | copy-start | bytes 3076
  122.3 4.0 %copy-start.40 = (f32[256]{0:T(256)S(1)}, f32[256]{0:T(256)}, u32[]{:S(2)}) copy-start(f32[256]{0:T(256)} %get-tuple-element.10) | copy-start | bytes 3076
  122.3 4.0 %copy-start.12 = (f32[768]{0:T(1024)S(1)}, f32[768]{0:T(1024)}, u32[]{:S(2)}) copy-start(f32[768]{0:T(1024)} %pad.36.clone) | copy-start | bytes 9220
  122.7 1.4 copy-start.4
  127.4 73.5 %reduce-scatter.5.cloned.1.call-start = ((), (), s32[]{:S(2)}) async-start(), calls=%async_computation.3 | async-start | bytes 221184 | tf_op jit(solution)/shard_map/reduce_scatter | solution.py:219
  163.8 124.2 %all-gather.3.cloned.1.call-start = ((), (), s32[]{:S(2)}) async-start(), calls=%async_computation.4 | async-start | bytes 3932160 | tf_op jit(solution)/shard_map/all_gather | solution.py:222
  (20 other events, 15.4 us)
Sparse Core Ops, SparseCore 0:
  127.6 36.1 reduce-scatter.2
  166.6 34.3 reduce-scatter.4
  231.9 56.1 all-gather.2

commit v2 on v1

--- a/solution.py
+++ b/solution.py
@@ -190,7 +190,7 @@
         carried = d_input
     kept_up, (d_gains, d_scales, d_shifts) = kept
     space_count = lax.axis_size("space")
-    space_no = lax.axis_index("space")
+    space_no = quarter_of(lax.axis_index("space"), space_count)
     patch_rows = 9 * channels // space_count
     flat_patch = patches(kept_saved[2], row_count, col_count).reshape(-1, 9 * channels)
     own_patch = lax.dynamic_slice_in_dim(flat_patch, space_no * patch_rows, patch_rows, axis=1)
@@ -205,6 +205,43 @@
         precision=lax.Precision.HIGHEST,
     )
     return reduce_grads(weight_grad, d_gains, emb_grad)
+
+
+def butterfly_scatter(flat, axis):
+    count = lax.axis_size(axis)
+    index = lax.axis_index(axis)
+    step = 1
+    while step < count:
+        bit = (index // step) % 2
+        half = flat.shape[0] // 2
+        kept = lax.dynamic_slice_in_dim(flat, bit * half, half, 0)
+        sent = lax.dynamic_slice_in_dim(flat, (1 - bit) * half, half, 0)
+        flat = kept + lax.ppermute(sent, axis, [(j, j ^ step) for j in range(count)])
+        step *= 2
+    return flat
+
+
+def butterfly_gather(flat, axis, steps):
+    count = lax.axis_size(axis)
+    index = lax.axis_index(axis)
+    for step in steps:
+        bit = (index // step) % 2
+        got = lax.ppermute(flat, axis, [(j, j ^ step) for j in range(count)])
+        flat = jnp.where(bit == 1, jnp.concatenate([got, flat]), jnp.concatenate([flat, got]))
+    return flat
+
+
+def descending(count):
+    steps = []
+    step = count // 2
+    while step >= 1:
+        steps.append(step)
+        step //= 2
+    return steps
+
+
+def quarter_of(space_no, space_count):
+    return (space_no % 2) * (space_count // 2) + space_no // 2
 
 
 def reduce_grads(weight_grad, gain_grad, emb_grad):
@@ -216,11 +253,12 @@
     parts.append(jnp.zeros((padded_rows - rows, channels), jnp.float32))
     flat = jnp.concatenate(parts, axis=0)
     for axis in ("dx", "dy"):
-        flat = lax.psum_scatter(flat, axis, scatter_dimension=0, tiled=True)
+        flat = butterfly_scatter(flat, axis)
     for axis in ("dy", "dx"):
-        flat = lax.all_gather(flat, axis, axis=0, tiled=True)
-    flat = lax.all_gather(flat, "space", axis=0)
-    space_count = flat.shape[0]
+        flat = butterfly_gather(flat, axis, descending(lax.axis_size(axis)))
+    space_count = lax.axis_size("space")
+    flat = butterfly_gather(flat, "space", descending(space_count))
+    flat = flat.reshape(space_count, padded_rows, channels)
     weight_rows = weight_grad.shape[0]
     emb_rows = emb_grad.size // channels
     conv = flat[:, :weight_rows].reshape(1, 3, 3, channels, channels)

time: 302 us -> 238 us (0.79)
  waiting for transfers between devices: 144 us -> 54.3 us
  starting transfers between devices: 12.2 us -> 86.9 us
  blocking collectives: 54.2 us -> 23.5 us
  between operations: 15 us -> 2.32 us
  local copies, waits for them, and re-layouts: 43.6 us -> 36.5 us
    ppermute x0 -> x12, starting transfers between devices: none -> 74.7 us  [the longest x7 51.8 us: butterfly_gather(): got = lax.ppermute(flat, axis, [(j, j ^ step) for j in range(count)])]
    reduce_scatter x2 -> x0, waiting for transfers between devices: 73.4 us -> none  [reduce_grads(): flat = lax.psum_scatter(flat, axis, scatter_dimension=0, tiled=True)]
    all_gather x1 -> x0, waiting for transfers between devices: 56.3 us -> none  [reduce_grads(): flat = lax.all_gather(flat, 'space', axis=0)]
    ppermute x0 -> x12, waiting for transfers between devices: none -> 40.3 us  [the longest x7 26.3 us: butterfly_gather(): got = lax.ppermute(flat, axis, [(j, j ^ step) for j in range(count)])]
    all_gather x2 -> x0, blocking collectives: 30.7 us -> none  [reduce_grads(): flat = lax.all_gather(flat, axis, axis=0, tiled=True)]
    unnamed x144 -> x142, local copies, waits for them, and re-layouts: 14.3 us -> 13.6 us
  transfers between devices with their start and end apart: 11 -> 20, of which waited for: 5 -> 13; matrix products, arithmetic and copies ran while one was open for 9% -> 16% of each run, Pallas kernels for 0% -> 0%
where the time goes in v2:
time: 238 us; the launch traced here: 236 us
  starting transfers between devices  86.9 us (37%)
  waiting for transfers between devices  54.3 us (23%)
  local copies, waits for them, and re-layouts  36.5 us (15%)
  blocking collectives  23.5 us (10%)
  other arithmetic  18.2 us (8%)
  matrix products  14.7 us (6%)
    ppermute x7, starting transfers between devices, butterfly_gather(): got = lax.ppermute(flat, axis, [(j, j ^ step) for j in range(count)])  51.8 us
    ppermute x7, waiting for transfers between devices, butterfly_gather(): got = lax.ppermute(flat, axis, [(j, j ^ step) for j in range(count)])  26.3 us
    ppermute x5, starting transfers between devices, butterfly_scatter(): lax.ppermute(sent, axis, [(j, j ^ step) for j in range(count)])  22.9 us
    ppermute x5, waiting for transfers between devices, butterfly_scatter(): lax.ppermute(sent, axis, [(j, j ^ step) for j in range(count)])  14 us
    ppermute x3, waiting for transfers between devices, per_device(): upstream = lax.ppermute(carried, 'section', [(active + 1, active)])  14 us
    unnamed x142, local copies, waits for them, and re-layouts  13.6 us
    dot_general x7, matrix products, convolve(): jnp.dot(flat, matrix, preferred_element_type=jnp.float32)  13.4 us
    all_gather x1, blocking collectives, per_device(): images = lax.all_gather(images, 'space', axis=1, tiled=True)  12.7 us
  transfers between devices with their start and end apart: 20, of which 13 were waited for; matrix products, arithmetic and copies ran while one was open for 16% of the time, Pallas kernels for 0%

profile of v2, /device:TPU:1, one launch (start us, length us, event | category | flops | bytes accessed | tf_op | source)
XLA Modules:
  0.0 236.3 jit_solution(9168739043917346120)
XLA Ops:
  1.8 12.7 %all_gather.6 = bf16[2,4,64,256]{3,2,1,0:T(8,128)(2,1)S(1)} all-gather(bf16[2,1,64,256]{3,2,1,0:T(8,128)(2,1)} %param.6), channel_id=1, replica_groups=mesh['dy'=8,'dx'=4,'section'=4,'space'=4] {'space'}, dimensions={1}, use_global_device_ids=true | all-gather | bytes 327680 | tf_op jit(solution)/shard_map/all_gather | solution.py:142
  20.9 4.7 %collective-permute-start.3 = (bf16[2,4,64,256]{3,2,1,0:T(8,128)(2,1)}, bf16[2,4,64,256]{3,2,1,0:T(8,128)(2,1)S(1)}, u32[]{:S(2)}, u32[]{:S(2)}) collective-permute-start(bf16[2,4,64,256]{3,2,1,0:T(8,128)(2,1)} %fusion), channel_id=1, source_target_pairs={{0,12},{1,13},{2,14},{3,15},{16,28},{17,29},{18,30},{19,31},{32,44... | collective-permute-start | bytes 786440 | tf_op jit(solution)/shard_map/ppermute | solution.py:167
  25.6 10.7 %all_gather.7 = bf16[2,4,64,256]{3,2,1,0:T(8,128)(2,1)S(1)} all-gather(bf16[2,1,64,256]{3,2,1,0:T(8,128)(2,1)S(1)} %copy-done.7), channel_id=1, replica_groups=mesh['dy'=8,'dx'=4,'section'=4,'space'=4] {'space'}, dimensions={1}, use_global_device_ids=true | all-gather | bytes 327680 | tf_op jit(solution)/shard_map/all_gather | solution.py:143
  51.2 1.6 copy.9
  59.3 3.6 %fusion.23 = (f32[2,256]{1,0:T(2,128)}, f32[256]{0:T(256)}, f32[2,256]{1,0:T(2,128)S(1)}, f32[2,256]{1,0:T(2,128)S(1)}, f32[2,256]{1,0:T(2,128)}, /*index=5*/f32[2,4,64,256]{3,2,1,0:T(8,128)S(1)}) fusion(bf16[2,4,64,256]{3,2,1,0:T(8,128)(2,1)S(1)} %select_select_fusion.1, f32[2,256]{1,0:T(2,128)S(1)} %mul.515, f32[2,256]{1,0:T(2,128)S(1)} %sub.163, ...), kind=kOutput, calls=%fused_computation.108 | convolution fusion | flops 607254272 | bytes 4343808 | tf_op jit(solution)/shard_map/dot_general | solution.py:74
  65.9 2.4 %fusion.22 = (f32[2,256]{1,0:T(2,128)}, f32[256]{0:T(256)}, f32[2,256]{1,0:T(2,128)S(1)}, f32[2,256]{1,0:T(2,128)S(1)}, f32[2,256]{1,0:T(2,128)}, /*index=5*/f32[2,4,64,256]{3,2,1,0:T(8,128)}) fusion(bf16[2,4,64,256]{3,2,1,0:T(8,128)(2,1)S(1)} %select_select_fusion.1, f32[2,256]{1,0:T(2,128)S(1)} %mul.515, f32[2,256]{1,0:T(2,128)S(1)} %copy-done.26, ...), kind=kOutput, calls=%fused_computation.107 | convolution fusion | flops 607254272 | bytes 4343808 | tf_op jit(solution)/shard_map/dot_general | solution.py:74
  72.9 2.4 %fusion.21 = (f32[2,256]{1,0:T(2,128)}, f32[256]{0:T(256)}, f32[2,256]{1,0:T(2,128)}, f32[2,256]{1,0:T(2,128)}, f32[2,256]{1,0:T(2,128)}, /*index=5*/f32[2,4,64,256]{3,2,1,0:T(8,128)}) fusion(bf16[2,4,64,256]{3,2,1,0:T(8,128)(2,1)S(1)} %select_select_fusion.1, f32[2,256]{1,0:T(2,128)S(1)} %mul.515, f32[2,256]{1,0:T(2,128)S(1)} %copy-done.27, ...), kind=kOutput, calls=%fused_computation.106 | convolution fusion | flops 607254272 | bytes 4343808 | tf_op jit(solution)/shard_map/dot_general | solution.py:74
  87.0 1.9 fusion.59
  96.6 14.0 %collective-permute-done.6 = bf16[2,4,64,256]{3,2,1,0:T(8,128)(2,1)} collective-permute-done((bf16[2,4,64,256]{3,2,1,0:T(8,128)(2,1)}, bf16[2,4,64,256]{3,2,1,0:T(8,128)(2,1)}, u32[]{:S(2)}, u32[]{:S(2)}) %collective-permute-start.6) | collective-permute-done | bytes 262176 | tf_op jit(solution)/shard_map/ppermute | solution.py:178
  110.6 1.9 select_select_fusion
  117.0 3.1 %collective-permute-start.8 = (f32[384,256]{1,0:T(8,128)S(1)}, f32[384,256]{1,0:T(8,128)S(1)}, u32[]{:S(2)}, u32[]{:S(2)}) collective-permute-start(f32[384,256]{1,0:T(8,128)S(1)} %constant_dynamic-slice_fusion.5), channel_id=1, source_target_pairs={{0,16},{16,0},{32,48},{48,32},{1,17},{17,1},{33,49},{49,33},{2,18}... | collective-permute-start | bytes 1179656 | tf_op jit(solution)/shard_map/ppermute | solution.py:219
  120.2 5.8 %collective-permute-done.8 = f32[384,256]{1,0:T(8,128)S(1)} collective-permute-done((f32[384,256]{1,0:T(8,128)S(1)}, f32[384,256]{1,0:T(8,128)S(1)}, u32[]{:S(2)}, u32[]{:S(2)}) %collective-permute-start.8) | collective-permute-done | bytes 393248 | tf_op jit(solution)/shard_map/ppermute | solution.py:219
  126.1 4.6 %collective-permute-start.9 = (f32[192,256]{1,0:T(8,128)S(1)}, f32[192,256]{1,0:T(8,128)S(1)}, u32[]{:S(2)}, u32[]{:S(2)}) collective-permute-start(f32[192,256]{1,0:T(8,128)S(1)} %constant_dynamic-slice_fusion.4), channel_id=1, source_target_pairs={{0,32},{16,48},{32,0},{48,16},{1,33},{17,49},{33,1},{49,17},{2,34}... | collective-permute-start | bytes 589832 | tf_op jit(solution)/shard_map/ppermute | solution.py:219
  130.8 3.3 %collective-permute-done.9 = f32[192,256]{1,0:T(8,128)S(1)} collective-permute-done((f32[192,256]{1,0:T(8,128)S(1)}, f32[192,256]{1,0:T(8,128)S(1)}, u32[]{:S(2)}, u32[]{:S(2)}) %collective-permute-start.9) | collective-permute-done | bytes 196640 | tf_op jit(solution)/shard_map/ppermute | solution.py:219
  134.1 3.2 %collective-permute-start.10 = (f32[96,256]{1,0:T(8,128)S(1)}, f32[96,256]{1,0:T(8,128)S(1)}, u32[]{:S(2)}, u32[]{:S(2)}) collective-permute-start(f32[96,256]{1,0:T(8,128)S(1)} %constant_dynamic-slice_fusion.3), channel_id=1, source_target_pairs={{0,64},{64,0},{128,192},{192,128},{256,320},{320,256},{384,448},{4... | collective-permute-start | bytes 294920 | tf_op jit(solution)/shard_map/ppermute | solution.py:219
  137.4 2.1 collective-permute-done.10
  139.5 4.2 %collective-permute-start.11 = (f32[48,256]{1,0:T(8,128)S(1)}, f32[48,256]{1,0:T(8,128)S(1)}, u32[]{:S(2)}, u32[]{:S(2)}) collective-permute-start(f32[48,256]{1,0:T(8,128)S(1)} %constant_dynamic-slice_fusion.2), channel_id=1, source_target_pairs={{0,128},{64,192},{128,0},{192,64},{256,384},{320,448},{384,256},{4... | collective-permute-start | bytes 147464 | tf_op jit(solution)/shard_map/ppermute | solution.py:219
  143.8 1.6 collective-permute-done.11
  145.4 7.7 %collective-permute-start.12 = (f32[24,256]{1,0:T(8,128)S(1)}, f32[24,256]{1,0:T(8,128)S(1)}, u32[]{:S(2)}, u32[]{:S(2)}) collective-permute-start(f32[24,256]{1,0:T(8,128)S(1)} %constant_dynamic-slice_fusion.1), channel_id=1, source_target_pairs={{0,256},{64,320},{128,384},{192,448},{256,0},{320,64},{384,128},{4... | collective-permute-start | bytes 73736 | tf_op jit(solution)/shard_map/ppermute | solution.py:219
  154.4 7.5 %collective-permute-start.13 = (f32[24,256]{1,0:T(8,128)S(1)}, f32[24,256]{1,0:T(8,128)S(1)}, u32[]{:S(2)}, u32[]{:S(2)}) collective-permute-start(f32[24,256]{1,0:T(8,128)S(1)} %dynamic-slice_add_fusion.4), channel_id=1, source_target_pairs={{0,256},{64,320},{128,384},{192,448},{256,0},{320,64},{384,128},{4... | collective-permute-start | bytes 73736 | tf_op jit(solution)/shard_map/ppermute | solution.py:229
  163.1 4.3 %collective-permute-start.14 = (f32[48,256]{1,0:T(8,128)S(1)}, f32[48,256]{1,0:T(8,128)S(1)}, u32[]{:S(2)}, u32[]{:S(2)}) collective-permute-start(f32[48,256]{1,0:T(8,128)S(1)} %maximum_select_fusion.6), channel_id=1, source_target_pairs={{0,128},{64,192},{128,0},{192,64},{256,384},{320,448},{384,256},{4... | collective-permute-start | bytes 147464 | tf_op jit(solution)/shard_map/ppermute | solution.py:229
  168.9 3.0 %collective-permute-start.15 = (f32[96,256]{1,0:T(8,128)S(1)}, f32[96,256]{1,0:T(8,128)S(1)}, u32[]{:S(2)}, u32[]{:S(2)}) collective-permute-start(f32[96,256]{1,0:T(8,128)S(1)} %maximum_select_fusion.5), channel_id=1, source_target_pairs={{0,64},{64,0},{128,192},{192,128},{256,320},{320,256},{384,448},{4... | collective-permute-start | bytes 294920 | tf_op jit(solution)/shard_map/ppermute | solution.py:229
  171.9 2.6 %collective-permute-done.15 = f32[96,256]{1,0:T(8,128)S(1)} collective-permute-done((f32[96,256]{1,0:T(8,128)S(1)}, f32[96,256]{1,0:T(8,128)S(1)}, u32[]{:S(2)}, u32[]{:S(2)}) %collective-permute-start.15) | collective-permute-done | bytes 98336 | tf_op jit(solution)/shard_map/ppermute | solution.py:229
  174.6 4.6 %collective-permute-start.16 = (f32[192,256]{1,0:T(8,128)S(1)}, f32[192,256]{1,0:T(8,128)S(1)}, u32[]{:S(2)}, u32[]{:S(2)}) collective-permute-start(f32[192,256]{1,0:T(8,128)S(1)} %maximum_select_fusion.4), channel_id=1, source_target_pairs={{0,32},{16,48},{32,0},{48,16},{1,33},{17,49},{33,1},{49,17},{2,34}... | collective-permute-start | bytes 589832 | tf_op jit(solution)/shard_map/ppermute | solution.py:229
  179.2 3.3 %collective-permute-done.16 = f32[192,256]{1,0:T(8,128)S(1)} collective-permute-done((f32[192,256]{1,0:T(8,128)S(1)}, f32[192,256]{1,0:T(8,128)S(1)}, u32[]{:S(2)}, u32[]{:S(2)}) %collective-permute-start.16) | collective-permute-done | bytes 196640 | tf_op jit(solution)/shard_map/ppermute | solution.py:229
  182.5 3.1 %collective-permute-start.17 = (f32[384,256]{1,0:T(8,128)S(1)}, f32[384,256]{1,0:T(8,128)S(1)}, u32[]{:S(2)}, u32[]{:S(2)}) collective-permute-start(f32[384,256]{1,0:T(8,128)S(1)} %maximum_select_fusion.3), channel_id=1, source_target_pairs={{0,16},{16,0},{32,48},{48,32},{1,17},{17,1},{33,49},{49,33},{2,18}... | collective-permute-start | bytes 1179656 | tf_op jit(solution)/shard_map/ppermute | solution.py:229
  185.6 5.4 %collective-permute-done.17 = f32[384,256]{1,0:T(8,128)S(1)} collective-permute-done((f32[384,256]{1,0:T(8,128)S(1)}, f32[384,256]{1,0:T(8,128)S(1)}, u32[]{:S(2)}, u32[]{:S(2)}) %collective-permute-start.17) | collective-permute-done | bytes 393248 | tf_op jit(solution)/shard_map/ppermute | solution.py:229
  191.1 11.7 %collective-permute-start.18 = (f32[768,256]{1,0:T(8,128)S(1)}, f32[768,256]{1,0:T(8,128)S(1)}, u32[]{:S(2)}, u32[]{:S(2)}) collective-permute-start(f32[768,256]{1,0:T(8,128)S(1)} %maximum_select_fusion.2), channel_id=1, source_target_pairs={{0,2},{1,3},{2,0},{3,1},{4,6},{5,7},{6,4},{7,5},{8,10},{9,11},{10,... | collective-permute-start | bytes 2359304 | tf_op jit(solution)/shard_map/ppermute | solution.py:229
  202.8 9.3 %collective-permute-done.18 = f32[768,256]{1,0:T(8,128)S(1)} collective-permute-done((f32[768,256]{1,0:T(8,128)S(1)}, f32[768,256]{1,0:T(8,128)S(1)}, u32[]{:S(2)}, u32[]{:S(2)}) %collective-permute-start.18) | collective-permute-done | bytes 786464 | tf_op jit(solution)/shard_map/ppermute | solution.py:229
  212.3 17.5 %collective-permute-start.19 = (f32[1536,256]{1,0:T(8,128)S(1)}, f32[1536,256]{1,0:T(8,128)S(1)}, u32[]{:S(2)}, u32[]{:S(2)}) collective-permute-start(f32[1536,256]{1,0:T(8,128)S(1)} %maximum_select_fusion.1), channel_id=1, source_target_pairs={{0,1},{1,0},{2,3},{3,2},{4,5},{5,4},{6,7},{7,6},{8,9},{9,8},{10,11... | collective-permute-start | bytes 4718600 | tf_op jit(solution)/shard_map/ppermute | solution.py:229
  229.8 3.0 %collective-permute-done.19 = f32[1536,256]{1,0:T(8,128)S(1)} collective-permute-done((f32[1536,256]{1,0:T(8,128)S(1)}, f32[1536,256]{1,0:T(8,128)S(1)}, u32[]{:S(2)}, u32[]{:S(2)}) %collective-permute-start.19) | collective-permute-done | bytes 1572896 | tf_op jit(solution)/shard_map/ppermute | solution.py:229
  233.2 1.6 slice.298
  (286 shorter events, 65.4 us)
Async XLA Ops:
  0.6 16.4 %copy-start.6 = (f32[1,256]{1,0:T(1,128)S(1)}, f32[1,256]{1,0:T(1,128)}, u32[]{:S(2)}) copy-start(f32[1,256]{1,0:T(1,128)} %param.10) | copy-start | bytes 3076
  1.5 13.1 %copy-start.14 = (f32[2,128]{1,0:T(2,128)}, f32[2,128]{1,0:T(2,128)S(1)}, u32[]{:S(2)}) copy-start(f32[2,128]{1,0:T(2,128)S(1)} %get-tuple-element.52) | copy-start | bytes 3076
  1.5 13.1 %copy-start.16 = (f32[2,128]{1,0:T(2,128)}, f32[2,128]{1,0:T(2,128)S(1)}, u32[]{:S(2)}) copy-start(f32[2,128]{1,0:T(2,128)S(1)} %get-tuple-element.53) | copy-start | bytes 3076
  14.9 2.5 %copy-start.18 = (f32[2,32]{1,0:T(2,128)}, f32[2,32]{1,0:T(2,128)S(1)}, u32[]{:S(2)}) copy-start(f32[2,32]{1,0:T(2,128)S(1)} %reduce_sum.424) | copy-start | bytes 772
  17.5 8.1 %copy-start.7 = (bf16[2,1,64,256]{3,2,1,0:T(8,128)(2,1)S(1)}, bf16[2,1,64,256]{3,2,1,0:T(8,128)(2,1)}, u32[]{:S(2)}) copy-start(bf16[2,1,64,256]{3,2,1,0:T(8,128)(2,1)} %param.8) | copy-start | bytes 196612
  19.6 19.0 %collective-permute-start = (bf16[2,4,64,256]{3,2,1,0:T(8,128)(2,1)}, bf16[2,4,64,256]{3,2,1,0:T(8,128)(2,1)S(1)}, u32[]{:S(2)}, u32[]{:S(2)}) collective-permute-start(bf16[2,4,64,256]{3,2,1,0:T(8,128)(2,1)} %fusion), channel_id=1, source_target_pairs={{0,4},{1,5},{2,6},{3,7},{16,20},{17,21},{18,22},{19,23},{32,36},{3... | collective-permute-start | bytes 786440 | tf_op jit(solution)/shard_map/ppermute | solution.py:162
  20.9 34.5 %collective-permute-start.3 = (bf16[2,4,64,256]{3,2,1,0:T(8,128)(2,1)}, bf16[2,4,64,256]{3,2,1,0:T(8,128)(2,1)S(1)}, u32[]{:S(2)}, u32[]{:S(2)}) collective-permute-start(bf16[2,4,64,256]{3,2,1,0:T(8,128)(2,1)} %fusion), channel_id=1, source_target_pairs={{0,12},{1,13},{2,14},{3,15},{16,28},{17,29},{18,30},{19,31},{32,44... | collective-permute-start | bytes 786440 | tf_op jit(solution)/shard_map/ppermute | solution.py:167
  41.4 2.9 %collective-permute-start.1 = (bf16[2,4,64,256]{3,2,1,0:T(8,128)(2,1)S(1)}, bf16[2,4,64,256]{3,2,1,0:T(8,128)(2,1)S(1)}, u32[]{:S(2)}, u32[]{:S(2)}) collective-permute-start(bf16[2,4,64,256]{3,2,1,0:T(8,128)(2,1)S(1)} %fusion.1), channel_id=1, source_target_pairs={{4,8},{5,9},{6,10},{7,11},{20,24},{21,25},{22,26},{23,27},{36,40},... | collective-permute-start | bytes 786440 | tf_op jit(solution)/shard_map/ppermute | solution.py:162
  49.1 7.0 %collective-permute-start.2 = (bf16[2,4,64,256]{3,2,1,0:T(8,128)(2,1)}, bf16[2,4,64,256]{3,2,1,0:T(8,128)(2,1)}, u32[]{:S(2)}, u32[]{:S(2)}) collective-permute-start(bf16[2,4,64,256]{3,2,1,0:T(8,128)(2,1)} %fusion.2), channel_id=1, source_target_pairs={{8,12},{9,13},{10,14},{11,15},{24,28},{25,29},{26,30},{27,31},{40,... | collective-permute-start | bytes 786440 | tf_op jit(solution)/shard_map/ppermute | solution.py:162
  52.8 4.8 %copy-start.19 = (f32[2,32]{1,0:T(2,128)S(1)}, f32[2,32]{1,0:T(2,128)}, u32[]{:S(2)}) copy-start(f32[2,32]{1,0:T(2,128)} %copy-done.18) | copy-start | bytes 772
  58.9 4.4 %copy-start.8 = (f32[2,32]{1,0:T(2,128)}, f32[2,32]{1,0:T(2,128)S(1)}, u32[]{:S(2)}) copy-start(f32[2,32]{1,0:T(2,128)S(1)} %get-tuple-element.35) | copy-start | bytes 772
  59.3 3.7 %copy-start.25 = (f32[2,256]{1,0:T(2,128)}, f32[2,256]{1,0:T(2,128)S(1)}, u32[]{:S(2)}) copy-start(f32[2,256]{1,0:T(2,128)S(1)} %sub.163) | copy-start | bytes 6148
  64.5 0.8 collective-permute-start.4
  65.9 2.8 %copy-start.9 = (f32[2,32]{1,0:T(2,128)S(1)}, f32[2,32]{1,0:T(2,128)}, u32[]{:S(2)}) copy-start(f32[2,32]{1,0:T(2,128)} %copy-done.8) | copy-start | bytes 772
  65.9 2.8 %copy-start.13 = (f32[2,32]{1,0:T(2,128)S(1)}, f32[2,32]{1,0:T(2,128)}, u32[]{:S(2)}) copy-start(f32[2,32]{1,0:T(2,128)} %copy-done.12) | copy-start | bytes 772
  70.2 2.6 %copy-start.27 = (f32[2,256]{1,0:T(2,128)S(1)}, f32[2,256]{1,0:T(2,128)}, u32[]{:S(2)}) copy-start(f32[2,256]{1,0:T(2,128)} %copy-done.25) | copy-start | bytes 6148
  70.2 2.2 collective-permute-start.5
  70.9 25.6 %collective-permute-start.7 = (bf16[2,4,64,256]{3,2,1,0:T(8,128)(2,1)}, bf16[2,4,64,256]{3,2,1,0:T(8,128)(2,1)}, u32[]{:S(2)}, u32[]{:S(2)}) collective-permute-start(bf16[2,4,64,256]{3,2,1,0:T(8,128)(2,1)} %copy-done.5), channel_id=1, source_target_pairs={{12,0},{13,1},{14,2},{15,3},{28,16},{29,17},{30,18},{31,19},{44,32... | collective-permute-start | bytes 786440 | tf_op jit(solution)/shard_map/ppermute | solution.py:187
  88.9 21.6 %collective-permute-start.6 = (bf16[2,4,64,256]{3,2,1,0:T(8,128)(2,1)}, bf16[2,4,64,256]{3,2,1,0:T(8,128)(2,1)}, u32[]{:S(2)}, u32[]{:S(2)}) collective-permute-start(bf16[2,4,64,256]{3,2,1,0:T(8,128)(2,1)} %fusion.59), channel_id=1, source_target_pairs={{4,0},{5,1},{6,2},{7,3},{20,16},{21,17},{22,18},{23,19},{36,32},{3... | collective-permute-start | bytes 786440 | tf_op jit(solution)/shard_map/ppermute | solution.py:178
  115.2 1.6 copy-start.11
  117.0 9.0 %collective-permute-start.8 = (f32[384,256]{1,0:T(8,128)S(1)}, f32[384,256]{1,0:T(8,128)S(1)}, u32[]{:S(2)}, u32[]{:S(2)}) collective-permute-start(f32[384,256]{1,0:T(8,128)S(1)} %constant_dynamic-slice_fusion.5), channel_id=1, source_target_pairs={{0,16},{16,0},{32,48},{48,32},{1,17},{17,1},{33,49},{49,33},{2,18}... | collective-permute-start | bytes 1179656 | tf_op jit(solution)/shard_map/ppermute | solution.py:219
  126.1 7.9 %collective-permute-start.9 = (f32[192,256]{1,0:T(8,128)S(1)}, f32[192,256]{1,0:T(8,128)S(1)}, u32[]{:S(2)}, u32[]{:S(2)}) collective-permute-start(f32[192,256]{1,0:T(8,128)S(1)} %constant_dynamic-slice_fusion.4), channel_id=1, source_target_pairs={{0,32},{16,48},{32,0},{48,16},{1,33},{17,49},{33,1},{49,17},{2,34}... | collective-permute-start | bytes 589832 | tf_op jit(solution)/shard_map/ppermute | solution.py:219
  134.1 5.4 %collective-permute-start.10 = (f32[96,256]{1,0:T(8,128)S(1)}, f32[96,256]{1,0:T(8,128)S(1)}, u32[]{:S(2)}, u32[]{:S(2)}) collective-permute-start(f32[96,256]{1,0:T(8,128)S(1)} %constant_dynamic-slice_fusion.3), channel_id=1, source_target_pairs={{0,64},{64,0},{128,192},{192,128},{256,320},{320,256},{384,448},{4... | collective-permute-start | bytes 294920 | tf_op jit(solution)/shard_map/ppermute | solution.py:219
  139.5 5.8 %collective-permute-start.11 = (f32[48,256]{1,0:T(8,128)S(1)}, f32[48,256]{1,0:T(8,128)S(1)}, u32[]{:S(2)}, u32[]{:S(2)}) collective-permute-start(f32[48,256]{1,0:T(8,128)S(1)} %constant_dynamic-slice_fusion.2), channel_id=1, source_target_pairs={{0,128},{64,192},{128,0},{192,64},{256,384},{320,448},{384,256},{4... | collective-permute-start | bytes 147464 | tf_op jit(solution)/shard_map/ppermute | solution.py:219
  145.4 9.0 %collective-permute-start.12 = (f32[24,256]{1,0:T(8,128)S(1)}, f32[24,256]{1,0:T(8,128)S(1)}, u32[]{:S(2)}, u32[]{:S(2)}) collective-permute-start(f32[24,256]{1,0:T(8,128)S(1)} %constant_dynamic-slice_fusion.1), channel_id=1, source_target_pairs={{0,256},{64,320},{128,384},{192,448},{256,0},{320,64},{384,128},{4... | collective-permute-start | bytes 73736 | tf_op jit(solution)/shard_map/ppermute | solution.py:219
  154.4 8.7 %collective-permute-start.13 = (f32[24,256]{1,0:T(8,128)S(1)}, f32[24,256]{1,0:T(8,128)S(1)}, u32[]{:S(2)}, u32[]{:S(2)}) collective-permute-start(f32[24,256]{1,0:T(8,128)S(1)} %dynamic-slice_add_fusion.4), channel_id=1, source_target_pairs={{0,256},{64,320},{128,384},{192,448},{256,0},{320,64},{384,128},{4... | collective-permute-start | bytes 73736 | tf_op jit(solution)/shard_map/ppermute | solution.py:229
  163.1 5.8 %collective-permute-start.14 = (f32[48,256]{1,0:T(8,128)S(1)}, f32[48,256]{1,0:T(8,128)S(1)}, u32[]{:S(2)}, u32[]{:S(2)}) collective-permute-start(f32[48,256]{1,0:T(8,128)S(1)} %maximum_select_fusion.6), channel_id=1, source_target_pairs={{0,128},{64,192},{128,0},{192,64},{256,384},{320,448},{384,256},{4... | collective-permute-start | bytes 147464 | tf_op jit(solution)/shard_map/ppermute | solution.py:229
  168.9 5.6 %collective-permute-start.15 = (f32[96,256]{1,0:T(8,128)S(1)}, f32[96,256]{1,0:T(8,128)S(1)}, u32[]{:S(2)}, u32[]{:S(2)}) collective-permute-start(f32[96,256]{1,0:T(8,128)S(1)} %maximum_select_fusion.5), channel_id=1, source_target_pairs={{0,64},{64,0},{128,192},{192,128},{256,320},{320,256},{384,448},{4... | collective-permute-start | bytes 294920 | tf_op jit(solution)/shard_map/ppermute | solution.py:229
  174.6 7.9 %collective-permute-start.16 = (f32[192,256]{1,0:T(8,128)S(1)}, f32[192,256]{1,0:T(8,128)S(1)}, u32[]{:S(2)}, u32[]{:S(2)}) collective-permute-start(f32[192,256]{1,0:T(8,128)S(1)} %maximum_select_fusion.4), channel_id=1, source_target_pairs={{0,32},{16,48},{32,0},{48,16},{1,33},{17,49},{33,1},{49,17},{2,34}... | collective-permute-start | bytes 589832 | tf_op jit(solution)/shard_map/ppermute | solution.py:229
  182.5 8.5 %collective-permute-start.17 = (f32[384,256]{1,0:T(8,128)S(1)}, f32[384,256]{1,0:T(8,128)S(1)}, u32[]{:S(2)}, u32[]{:S(2)}) collective-permute-start(f32[384,256]{1,0:T(8,128)S(1)} %maximum_select_fusion.3), channel_id=1, source_target_pairs={{0,16},{16,0},{32,48},{48,32},{1,17},{17,1},{33,49},{49,33},{2,18}... | collective-permute-start | bytes 1179656 | tf_op jit(solution)/shard_map/ppermute | solution.py:229
  191.1 21.1 %collective-permute-start.18 = (f32[768,256]{1,0:T(8,128)S(1)}, f32[768,256]{1,0:T(8,128)S(1)}, u32[]{:S(2)}, u32[]{:S(2)}) collective-permute-start(f32[768,256]{1,0:T(8,128)S(1)} %maximum_select_fusion.2), channel_id=1, source_target_pairs={{0,2},{1,3},{2,0},{3,1},{4,6},{5,7},{6,4},{7,5},{8,10},{9,11},{10,... | collective-permute-start | bytes 2359304 | tf_op jit(solution)/shard_map/ppermute | solution.py:229
  212.3 20.5 %collective-permute-start.19 = (f32[1536,256]{1,0:T(8,128)S(1)}, f32[1536,256]{1,0:T(8,128)S(1)}, u32[]{:S(2)}, u32[]{:S(2)}) collective-permute-start(f32[1536,256]{1,0:T(8,128)S(1)} %maximum_select_fusion.1), channel_id=1, source_target_pairs={{0,1},{1,0},{2,3},{3,2},{4,5},{5,4},{6,7},{7,6},{8,9},{9,8},{10,11... | collective-permute-start | bytes 4718600 | tf_op jit(solution)/shard_map/ppermute | solution.py:229
  (28 other events, 24.4 us)

commit v3 on v2

--- a/solution.py
+++ b/solution.py
@@ -139,8 +139,9 @@
 def per_device(images, steps, out_grad, conv_weight, gn_gain, emb_weight):
     section_count = lax.axis_size("section")
     section_no = lax.axis_index("section")
-    images = lax.all_gather(images, "space", axis=1, tiled=True)
-    out_grad = lax.all_gather(out_grad, "space", axis=1, tiled=True)
+    space_steps = ascending(lax.axis_size("space"))
+    images = butterfly_gather(images, "space", space_steps, dim=1)
+    out_grad = butterfly_gather(out_grad, "space", space_steps, dim=1)
     row_count = images.shape[1]
     col_count = images.shape[2]
     channels = images.shape[3]
@@ -221,14 +222,20 @@
     return flat
 
 
-def butterfly_gather(flat, axis, steps):
+def butterfly_gather(flat, axis, steps, dim=0):
     count = lax.axis_size(axis)
     index = lax.axis_index(axis)
     for step in steps:
         bit = (index // step) % 2
         got = lax.ppermute(flat, axis, [(j, j ^ step) for j in range(count)])
-        flat = jnp.where(bit == 1, jnp.concatenate([got, flat]), jnp.concatenate([flat, got]))
+        flat = jnp.where(
+            bit == 1, jnp.concatenate([got, flat], axis=dim), jnp.concatenate([flat, got], axis=dim)
+        )
     return flat
+
+
+def ascending(count):
+    return descending(count)[::-1]
 
 
 def descending(count):

time: 238 us -> 243 us (1.021)
  blocking collectives: 23.5 us -> 0 us
  waiting for transfers between devices: 54.3 us -> 69.4 us
  starting transfers between devices: 86.9 us -> 98.3 us
  local copies, waits for them, and re-layouts: 36.5 us -> 41.1 us
    all_gather x2 -> x0, blocking collectives: 23.5 us -> none  [the longest x1 12.7 us: per_device(): images = lax.all_gather(images, 'space', axis=1, tiled=True)]
    ppermute x1, waiting for transfers between devices: 0.01 us -> 12.8 us  [per_device(): skip_grad = lax.ppermute(d_input, 'section', [(last, 0)])]
    ppermute x7 -> x11, starting transfers between devices: 51.8 us -> 64.3 us  [butterfly_gather(): got = lax.ppermute(flat, axis, [(j, j ^ step) for j in range(count)])]
    ppermute x7 -> x11, waiting for transfers between devices: 26.3 us -> 27.4 us  [butterfly_gather(): got = lax.ppermute(flat, axis, [(j, j ^ step) for j in range(count)])]
  transfers between devices with their start and end apart: 20 -> 24, of which waited for: 13 -> 15; matrix products, arithmetic and copies ran while one was open for 16% -> 13% of each run, Pallas kernels for 0% -> 0%
where the time goes in v3:
time: 243 us; the launch traced here: 242 us
  starting transfers between devices  98.3 us (40%)
  waiting for transfers between devices  69.4 us (29%)
  local copies, waits for them, and re-layouts  41.1 us (17%)
  other arithmetic  16.3 us (7%)
  matrix products  14 us (6%)
  between operations  2.43 us (1%)
    ppermute x11, starting transfers between devices, butterfly_gather(): got = lax.ppermute(flat, axis, [(j, j ^ step) for j in range(count)])  64.3 us
    ppermute x11, waiting for transfers between devices, butterfly_gather(): got = lax.ppermute(flat, axis, [(j, j ^ step) for j in range(count)])  27.4 us
    ppermute x5, starting transfers between devices, butterfly_scatter(): lax.ppermute(sent, axis, [(j, j ^ step) for j in range(count)])  21.8 us
    unnamed x142, local copies, waits for them, and re-layouts  15.6 us
    ppermute x5, waiting for transfers between devices, butterfly_scatter(): lax.ppermute(sent, axis, [(j, j ^ step) for j in range(count)])  15.5 us
    ppermute x3, waiting for transfers between devices, per_device(): upstream = lax.ppermute(carried, 'section', [(active + 1, active)])  13.8 us
    ppermute x1, waiting for transfers between devices, per_device(): skip_grad = lax.ppermute(d_input, 'section', [(last, 0)])  12.8 us
    dot_general x7, matrix products, convolve(): jnp.dot(flat, matrix, preferred_element_type=jnp.float32)  11.6 us
  transfers between devices with their start and end apart: 24, of which 15 were waited for; matrix products, arithmetic and copies ran while one was open for 13% of the time, Pallas kernels for 0%

profile of v3, /device:TPU:1, one launch (start us, length us, event | category | flops | bytes accessed | tf_op | source)
XLA Modules:
  0.0 241.6 jit_solution(13663667966273614365)
XLA Ops:
  0.6 8.9 %collective-permute-start = (bf16[2,1,64,256]{3,2,1,0:T(8,128)(2,1)}, bf16[2,1,64,256]{3,2,1,0:T(8,128)(2,1)S(1)}, u32[]{:S(2)}, u32[]{:S(2)}) collective-permute-start(bf16[2,1,64,256]{3,2,1,0:T(8,128)(2,1)} %param.6), channel_id=1, source_target_pairs={{0,1},{1,0},{2,3},{3,2},{4,5},{5,4},{6,7},{7,6},{8,9},{9,8},{10,11... | collective-permute-start | bytes 196616 | tf_op jit(solution)/shard_map/ppermute | solution.py:230
  9.6 1.9 collective-permute-start.6
  16.3 1.9 collective-permute-start.1
  18.3 3.4 %collective-permute-start.7 = (bf16[2,2,64,256]{3,2,1,0:T(8,128)(2,1)S(1)}, bf16[2,2,64,256]{3,2,1,0:T(8,128)(2,1)S(1)}, u32[]{:S(2)}, u32[]{:S(2)}) collective-permute-start(bf16[2,2,64,256]{3,2,1,0:T(8,128)(2,1)S(1)} %maximum_select_fusion.10), channel_id=1, source_target_pairs={{0,2},{1,3},{2,0},{3,1},{4,6},{5,7},{6,4},{7,5},{8,10},{9,11},{10,... | collective-permute-start | bytes 393224 | tf_op jit(solution)/shard_map/ppermute | solution.py:230
  28.8 5.2 %collective-permute-start.5 = (bf16[2,4,64,256]{3,2,1,0:T(8,128)(2,1)}, bf16[2,4,64,256]{3,2,1,0:T(8,128)(2,1)}, u32[]{:S(2)}, u32[]{:S(2)}) collective-permute-start(bf16[2,4,64,256]{3,2,1,0:T(8,128)(2,1)} %fusion), channel_id=1, source_target_pairs={{0,12},{1,13},{2,14},{3,15},{16,28},{17,29},{18,30},{19,31},{32,44... | collective-permute-start | bytes 786440 | tf_op jit(solution)/shard_map/ppermute | solution.py:168
  48.1 2.3 fusion.33
  54.4 3.3 %fusion.28 = (f32[2,256]{1,0:T(2,128)}, f32[256]{0:T(256)}, f32[2,256]{1,0:T(2,128)S(1)}, f32[2,256]{1,0:T(2,128)S(1)}, f32[2,256]{1,0:T(2,128)}, /*index=5*/f32[2,4,64,256]{3,2,1,0:T(8,128)S(1)}) fusion(bf16[2,4,64,256]{3,2,1,0:T(8,128)(2,1)S(1)} %select_select_fusion.1, f32[2,256]{1,0:T(2,128)S(1)} %mul.514, f32[2,256]{1,0:T(2,128)} %sub.167, ...), kind=kOutput, calls=%fused_computation.113 | convolution fusion | flops 607254272 | bytes 4343808 | tf_op jit(solution)/shard_map/dot_general | solution.py:74
  77.3 2.4 %fusion.26 = (f32[2,256]{1,0:T(2,128)}, f32[256]{0:T(256)}, f32[2,256]{1,0:T(2,128)S(1)}, f32[2,256]{1,0:T(2,128)S(1)}, f32[2,256]{1,0:T(2,128)}, /*index=5*/f32[2,4,64,256]{3,2,1,0:T(8,128)}) fusion(bf16[2,4,64,256]{3,2,1,0:T(8,128)(2,1)S(1)} %select_select_fusion.1, f32[2,256]{1,0:T(2,128)S(1)} %mul.514, f32[2,256]{1,0:T(2,128)S(1)} %copy-done.26, ...), kind=kOutput, calls=%fused_computation.111 | convolution fusion | flops 607254272 | bytes 4343808 | tf_op jit(solution)/shard_map/dot_general | solution.py:74
  90.4 12.8 %collective-permute-done.11 = bf16[2,4,64,256]{3,2,1,0:T(8,128)(2,1)} collective-permute-done((bf16[2,4,64,256]{3,2,1,0:T(8,128)(2,1)}, bf16[2,4,64,256]{3,2,1,0:T(8,128)(2,1)}, u32[]{:S(2)}, u32[]{:S(2)}) %collective-permute-start.11) | collective-permute-done | bytes 262176 | tf_op jit(solution)/shard_map/ppermute | solution.py:188
  103.2 13.7 %collective-permute-done.10 = bf16[2,4,64,256]{3,2,1,0:T(8,128)(2,1)} collective-permute-done((bf16[2,4,64,256]{3,2,1,0:T(8,128)(2,1)S(1)}, bf16[2,4,64,256]{3,2,1,0:T(8,128)(2,1)}, u32[]{:S(2)}, u32[]{:S(2)}) %collective-permute-start.10) | collective-permute-done | bytes 262176 | tf_op jit(solution)/shard_map/ppermute | solution.py:179
  123.3 1.8 fusion.18
  125.4 2.9 %collective-permute-start.12 = (f32[384,256]{1,0:T(8,128)S(1)}, f32[384,256]{1,0:T(8,128)S(1)}, u32[]{:S(2)}, u32[]{:S(2)}) collective-permute-start(f32[384,256]{1,0:T(8,128)S(1)} %constant_dynamic-slice_fusion.5), channel_id=1, source_target_pairs={{0,16},{16,0},{32,48},{48,32},{1,17},{17,1},{33,49},{49,33},{2,18}... | collective-permute-start | bytes 1179656 | tf_op jit(solution)/shard_map/ppermute | solution.py:220
  128.4 6.5 %collective-permute-done.12 = f32[384,256]{1,0:T(8,128)S(1)} collective-permute-done((f32[384,256]{1,0:T(8,128)S(1)}, f32[384,256]{1,0:T(8,128)S(1)}, u32[]{:S(2)}, u32[]{:S(2)}) %collective-permute-start.12) | collective-permute-done | bytes 393248 | tf_op jit(solution)/shard_map/ppermute | solution.py:220
  135.0 4.4 %collective-permute-start.13 = (f32[192,256]{1,0:T(8,128)S(1)}, f32[192,256]{1,0:T(8,128)S(1)}, u32[]{:S(2)}, u32[]{:S(2)}) collective-permute-start(f32[192,256]{1,0:T(8,128)S(1)} %constant_dynamic-slice_fusion.4), channel_id=1, source_target_pairs={{0,32},{16,48},{32,0},{48,16},{1,33},{17,49},{33,1},{49,17},{2,34}... | collective-permute-start | bytes 589832 | tf_op jit(solution)/shard_map/ppermute | solution.py:220
  139.4 3.5 %collective-permute-done.13 = f32[192,256]{1,0:T(8,128)S(1)} collective-permute-done((f32[192,256]{1,0:T(8,128)S(1)}, f32[192,256]{1,0:T(8,128)S(1)}, u32[]{:S(2)}, u32[]{:S(2)}) %collective-permute-start.13) | collective-permute-done | bytes 196640 | tf_op jit(solution)/shard_map/ppermute | solution.py:220
  143.0 3.0 %collective-permute-start.14 = (f32[96,256]{1,0:T(8,128)S(1)}, f32[96,256]{1,0:T(8,128)S(1)}, u32[]{:S(2)}, u32[]{:S(2)}) collective-permute-start(f32[96,256]{1,0:T(8,128)S(1)} %constant_dynamic-slice_fusion.3), channel_id=1, source_target_pairs={{0,64},{64,0},{128,192},{192,128},{256,320},{320,256},{384,448},{4... | collective-permute-start | bytes 294920 | tf_op jit(solution)/shard_map/ppermute | solution.py:220
  146.0 2.3 collective-permute-done.14
  148.4 4.0 %collective-permute-start.15 = (f32[48,256]{1,0:T(8,128)S(1)}, f32[48,256]{1,0:T(8,128)S(1)}, u32[]{:S(2)}, u32[]{:S(2)}) collective-permute-start(f32[48,256]{1,0:T(8,128)S(1)} %constant_dynamic-slice_fusion.2), channel_id=1, source_target_pairs={{0,128},{64,192},{128,0},{192,64},{256,384},{320,448},{384,256},{4... | collective-permute-start | bytes 147464 | tf_op jit(solution)/shard_map/ppermute | solution.py:220
  152.4 1.8 collective-permute-done.15
  154.2 7.6 %collective-permute-start.16 = (f32[24,256]{1,0:T(8,128)S(1)}, f32[24,256]{1,0:T(8,128)S(1)}, u32[]{:S(2)}, u32[]{:S(2)}) collective-permute-start(f32[24,256]{1,0:T(8,128)S(1)} %constant_dynamic-slice_fusion.1), channel_id=1, source_target_pairs={{0,256},{64,320},{128,384},{192,448},{256,0},{320,64},{384,128},{4... | collective-permute-start | bytes 73736 | tf_op jit(solution)/shard_map/ppermute | solution.py:220
  163.1 7.2 %collective-permute-start.17 = (f32[24,256]{1,0:T(8,128)S(1)}, f32[24,256]{1,0:T(8,128)S(1)}, u32[]{:S(2)}, u32[]{:S(2)}) collective-permute-start(f32[24,256]{1,0:T(8,128)S(1)} %dynamic-slice_add_fusion.4), channel_id=1, source_target_pairs={{0,256},{64,320},{128,384},{192,448},{256,0},{320,64},{384,128},{4... | collective-permute-start | bytes 73736 | tf_op jit(solution)/shard_map/ppermute | solution.py:230
  171.6 4.3 %collective-permute-start.18 = (f32[48,256]{1,0:T(8,128)S(1)}, f32[48,256]{1,0:T(8,128)S(1)}, u32[]{:S(2)}, u32[]{:S(2)}) collective-permute-start(f32[48,256]{1,0:T(8,128)S(1)} %maximum_select_fusion.12), channel_id=1, source_target_pairs={{0,128},{64,192},{128,0},{192,64},{256,384},{320,448},{384,256},{4... | collective-permute-start | bytes 147464 | tf_op jit(solution)/shard_map/ppermute | solution.py:230
  177.4 2.8 %collective-permute-start.19 = (f32[96,256]{1,0:T(8,128)S(1)}, f32[96,256]{1,0:T(8,128)S(1)}, u32[]{:S(2)}, u32[]{:S(2)}) collective-permute-start(f32[96,256]{1,0:T(8,128)S(1)} %maximum_select_fusion.11), channel_id=1, source_target_pairs={{0,64},{64,0},{128,192},{192,128},{256,320},{320,256},{384,448},{4... | collective-permute-start | bytes 294920 | tf_op jit(solution)/shard_map/ppermute | solution.py:230
  180.2 2.7 %collective-permute-done.19 = f32[96,256]{1,0:T(8,128)S(1)} collective-permute-done((f32[96,256]{1,0:T(8,128)S(1)}, f32[96,256]{1,0:T(8,128)S(1)}, u32[]{:S(2)}, u32[]{:S(2)}) %collective-permute-start.19) | collective-permute-done | bytes 98336 | tf_op jit(solution)/shard_map/ppermute | solution.py:230
  183.0 4.6 %collective-permute-start.20 = (f32[192,256]{1,0:T(8,128)S(1)}, f32[192,256]{1,0:T(8,128)S(1)}, u32[]{:S(2)}, u32[]{:S(2)}) collective-permute-start(f32[192,256]{1,0:T(8,128)S(1)} %maximum_select_fusion.8), channel_id=1, source_target_pairs={{0,32},{16,48},{32,0},{48,16},{1,33},{17,49},{33,1},{49,17},{2,34}... | collective-permute-start | bytes 589832 | tf_op jit(solution)/shard_map/ppermute | solution.py:230
  187.6 3.3 %collective-permute-done.20 = f32[192,256]{1,0:T(8,128)S(1)} collective-permute-done((f32[192,256]{1,0:T(8,128)S(1)}, f32[192,256]{1,0:T(8,128)S(1)}, u32[]{:S(2)}, u32[]{:S(2)}) %collective-permute-start.20) | collective-permute-done | bytes 196640 | tf_op jit(solution)/shard_map/ppermute | solution.py:230
  190.9 3.1 %collective-permute-start.21 = (f32[384,256]{1,0:T(8,128)S(1)}, f32[384,256]{1,0:T(8,128)S(1)}, u32[]{:S(2)}, u32[]{:S(2)}) collective-permute-start(f32[384,256]{1,0:T(8,128)S(1)} %maximum_select_fusion.4), channel_id=1, source_target_pairs={{0,16},{16,0},{32,48},{48,32},{1,17},{17,1},{33,49},{49,33},{2,18}... | collective-permute-start | bytes 1179656 | tf_op jit(solution)/shard_map/ppermute | solution.py:230
  194.0 5.4 %collective-permute-done.21 = f32[384,256]{1,0:T(8,128)S(1)} collective-permute-done((f32[384,256]{1,0:T(8,128)S(1)}, f32[384,256]{1,0:T(8,128)S(1)}, u32[]{:S(2)}, u32[]{:S(2)}) %collective-permute-start.21) | collective-permute-done | bytes 393248 | tf_op jit(solution)/shard_map/ppermute | solution.py:230
  199.5 8.4 %collective-permute-start.22 = (f32[768,256]{1,0:T(8,128)S(1)}, f32[768,256]{1,0:T(8,128)S(1)}, u32[]{:S(2)}, u32[]{:S(2)}) collective-permute-start(f32[768,256]{1,0:T(8,128)S(1)} %maximum_select_fusion.2), channel_id=1, source_target_pairs={{0,2},{1,3},{2,0},{3,1},{4,6},{5,7},{6,4},{7,5},{8,10},{9,11},{10,... | collective-permute-start | bytes 2359304 | tf_op jit(solution)/shard_map/ppermute | solution.py:230
  207.9 9.4 %collective-permute-done.22 = f32[768,256]{1,0:T(8,128)S(1)} collective-permute-done((f32[768,256]{1,0:T(8,128)S(1)}, f32[768,256]{1,0:T(8,128)S(1)}, u32[]{:S(2)}, u32[]{:S(2)}) %collective-permute-start.22) | collective-permute-done | bytes 786464 | tf_op jit(solution)/shard_map/ppermute | solution.py:230
  217.4 17.7 %collective-permute-start.23 = (f32[1536,256]{1,0:T(8,128)S(1)}, f32[1536,256]{1,0:T(8,128)S(1)}, u32[]{:S(2)}, u32[]{:S(2)}) collective-permute-start(f32[1536,256]{1,0:T(8,128)S(1)} %maximum_select_fusion.1), channel_id=1, source_target_pairs={{0,1},{1,0},{2,3},{3,2},{4,5},{5,4},{6,7},{7,6},{8,9},{9,8},{10,11... | collective-permute-start | bytes 4718600 | tf_op jit(solution)/shard_map/ppermute | solution.py:230
  235.1 3.0 %collective-permute-done.23 = f32[1536,256]{1,0:T(8,128)S(1)} collective-permute-done((f32[1536,256]{1,0:T(8,128)S(1)}, f32[1536,256]{1,0:T(8,128)S(1)}, u32[]{:S(2)}, u32[]{:S(2)}) %collective-permute-start.23) | collective-permute-done | bytes 1572896 | tf_op jit(solution)/shard_map/ppermute | solution.py:230
  (293 shorter events, 73.5 us)
Async XLA Ops:
  0.6 11.7 %copy-start = (bf16[1,256,512]{2,1,0:T(8,128)(2,1)S(1)}, bf16[1,256,512]{2,1,0:T(8,128)(2,1)}, u32[]{:S(2)}) copy-start(bf16[1,256,512]{2,1,0:T(8,128)(2,1)} %param.11) | copy-start | bytes 786436
  0.6 15.7 %collective-permute-start = (bf16[2,1,64,256]{3,2,1,0:T(8,128)(2,1)}, bf16[2,1,64,256]{3,2,1,0:T(8,128)(2,1)S(1)}, u32[]{:S(2)}, u32[]{:S(2)}) collective-permute-start(bf16[2,1,64,256]{3,2,1,0:T(8,128)(2,1)} %param.6), channel_id=1, source_target_pairs={{0,1},{1,0},{2,3},{3,2},{4,5},{5,4},{6,7},{7,6},{8,9},{9,8},{10,11... | collective-permute-start | bytes 196616 | tf_op jit(solution)/shard_map/ppermute | solution.py:230
  9.6 8.7 %collective-permute-start.6 = (bf16[2,1,64,256]{3,2,1,0:T(8,128)(2,1)}, bf16[2,1,64,256]{3,2,1,0:T(8,128)(2,1)S(1)}, u32[]{:S(2)}, u32[]{:S(2)}) collective-permute-start(bf16[2,1,64,256]{3,2,1,0:T(8,128)(2,1)} %param.8), channel_id=1, source_target_pairs={{0,1},{1,0},{2,3},{3,2},{4,5},{5,4},{6,7},{7,6},{8,9},{9,8},{10,11... | collective-permute-start | bytes 196616 | tf_op jit(solution)/shard_map/ppermute | solution.py:230
  13.6 4.7 %copy-start.7 = (bf16[2,1,64,256]{3,2,1,0:T(8,128)(2,1)S(1)}, bf16[2,1,64,256]{3,2,1,0:T(8,128)(2,1)}, u32[]{:S(2)}) copy-start(bf16[2,1,64,256]{3,2,1,0:T(8,128)(2,1)} %param.8) | copy-start | bytes 196612
  15.2 9.2 %copy-start.8 = (f32[1,256]{1,0:T(1,128)S(1)}, f32[1,256]{1,0:T(1,128)}, u32[]{:S(2)}) copy-start(f32[1,256]{1,0:T(1,128)} %param.10) | copy-start | bytes 3076
  16.3 6.5 %collective-permute-start.1 = (bf16[2,2,64,256]{3,2,1,0:T(8,128)(2,1)S(1)}, bf16[2,2,64,256]{3,2,1,0:T(8,128)(2,1)S(1)}, u32[]{:S(2)}, u32[]{:S(2)}) collective-permute-start(bf16[2,2,64,256]{3,2,1,0:T(8,128)(2,1)S(1)} %maximum_select_fusion.9), channel_id=1, source_target_pairs={{0,2},{1,3},{2,0},{3,1},{4,6},{5,7},{6,4},{7,5},{8,10},{9,11},{10,... | collective-permute-start | bytes 393224 | tf_op jit(solution)/shard_map/ppermute | solution.py:230
  18.3 15.7 %collective-permute-start.7 = (bf16[2,2,64,256]{3,2,1,0:T(8,128)(2,1)S(1)}, bf16[2,2,64,256]{3,2,1,0:T(8,128)(2,1)S(1)}, u32[]{:S(2)}, u32[]{:S(2)}) collective-permute-start(bf16[2,2,64,256]{3,2,1,0:T(8,128)(2,1)S(1)} %maximum_select_fusion.10), channel_id=1, source_target_pairs={{0,2},{1,3},{2,0},{3,1},{4,6},{5,7},{6,4},{7,5},{8,10},{9,11},{10,... | collective-permute-start | bytes 393224 | tf_op jit(solution)/shard_map/ppermute | solution.py:230
  27.4 8.9 %collective-permute-start.2 = (bf16[2,4,64,256]{3,2,1,0:T(8,128)(2,1)}, bf16[2,4,64,256]{3,2,1,0:T(8,128)(2,1)S(1)}, u32[]{:S(2)}, u32[]{:S(2)}) collective-permute-start(bf16[2,4,64,256]{3,2,1,0:T(8,128)(2,1)} %fusion), channel_id=1, source_target_pairs={{0,4},{1,5},{2,6},{3,7},{16,20},{17,21},{18,22},{19,23},{32,36},{3... | collective-permute-start | bytes 786440 | tf_op jit(solution)/shard_map/ppermute | solution.py:163
  28.8 19.3 %collective-permute-start.5 = (bf16[2,4,64,256]{3,2,1,0:T(8,128)(2,1)}, bf16[2,4,64,256]{3,2,1,0:T(8,128)(2,1)}, u32[]{:S(2)}, u32[]{:S(2)}) collective-permute-start(bf16[2,4,64,256]{3,2,1,0:T(8,128)(2,1)} %fusion), channel_id=1, source_target_pairs={{0,12},{1,13},{2,14},{3,15},{16,28},{17,29},{18,30},{19,31},{32,44... | collective-permute-start | bytes 786440 | tf_op jit(solution)/shard_map/ppermute | solution.py:168
  39.3 2.9 %collective-permute-start.3 = (bf16[2,4,64,256]{3,2,1,0:T(8,128)(2,1)S(1)}, bf16[2,4,64,256]{3,2,1,0:T(8,128)(2,1)S(1)}, u32[]{:S(2)}, u32[]{:S(2)}) collective-permute-start(bf16[2,4,64,256]{3,2,1,0:T(8,128)(2,1)S(1)} %fusion.1), channel_id=1, source_target_pairs={{4,8},{5,9},{6,10},{7,11},{20,24},{21,25},{22,26},{23,27},{36,40},... | collective-permute-start | bytes 786440 | tf_op jit(solution)/shard_map/ppermute | solution.py:163
  45.0 9.4 %copy-start.2 = (bf16[3,3,256,256]{2,3,1,0:T(8,128)(2,1)S(1)}, bf16[3,3,256,256]{2,3,1,0:T(8,128)(2,1)}, u32[]{:S(2)}) copy-start(bf16[3,3,256,256]{2,3,1,0:T(8,128)(2,1)} %rev.3) | copy-start | bytes 3538948
  45.0 3.0 %collective-permute-start.4 = (bf16[2,4,64,256]{3,2,1,0:T(8,128)(2,1)S(1)}, bf16[2,4,64,256]{3,2,1,0:T(8,128)(2,1)S(1)}, u32[]{:S(2)}, u32[]{:S(2)}) collective-permute-start(bf16[2,4,64,256]{3,2,1,0:T(8,128)(2,1)S(1)} %fusion.2), channel_id=1, source_target_pairs={{8,12},{9,13},{10,14},{11,15},{24,28},{25,29},{26,30},{27,31},{40,... | collective-permute-start | bytes 786440 | tf_op jit(solution)/shard_map/ppermute | solution.py:163
  59.2 0.7 collective-permute-start.8
  74.7 2.2 collective-permute-start.9
  75.4 27.8 %collective-permute-start.11 = (bf16[2,4,64,256]{3,2,1,0:T(8,128)(2,1)}, bf16[2,4,64,256]{3,2,1,0:T(8,128)(2,1)}, u32[]{:S(2)}, u32[]{:S(2)}) collective-permute-start(bf16[2,4,64,256]{3,2,1,0:T(8,128)(2,1)} %copy-done.6), channel_id=1, source_target_pairs={{12,0},{13,1},{14,2},{15,3},{28,16},{29,17},{30,18},{31,19},{44,32... | collective-permute-start | bytes 786440 | tf_op jit(solution)/shard_map/ppermute | solution.py:188
  82.9 34.1 %collective-permute-start.10 = (bf16[2,4,64,256]{3,2,1,0:T(8,128)(2,1)S(1)}, bf16[2,4,64,256]{3,2,1,0:T(8,128)(2,1)}, u32[]{:S(2)}, u32[]{:S(2)}) collective-permute-start(bf16[2,4,64,256]{3,2,1,0:T(8,128)(2,1)S(1)} %fusion.59), channel_id=1, source_target_pairs={{4,0},{5,1},{6,2},{7,3},{20,16},{21,17},{22,18},{23,19},{36,32},{3... | collective-permute-start | bytes 786440 | tf_op jit(solution)/shard_map/ppermute | solution.py:179
  121.1 4.0 %copy-start.36 = (f32[256]{0:T(256)S(1)}, f32[256]{0:T(256)}, u32[]{:S(2)}) copy-start(f32[256]{0:T(256)} %get-tuple-element.4) | copy-start | bytes 3076
  121.1 4.0 %copy-start.37 = (f32[256]{0:T(256)S(1)}, f32[256]{0:T(256)}, u32[]{:S(2)}) copy-start(f32[256]{0:T(256)} %get-tuple-element.7) | copy-start | bytes 3076
  121.1 4.0 %copy-start.38 = (f32[256]{0:T(256)S(1)}, f32[256]{0:T(256)}, u32[]{:S(2)}) copy-start(f32[256]{0:T(256)} %get-tuple-element.10) | copy-start | bytes 3076
  121.2 4.0 %copy-start.12 = (f32[768]{0:T(1024)S(1)}, f32[768]{0:T(1024)}, u32[]{:S(2)}) copy-start(f32[768]{0:T(1024)} %pad.64.clone) | copy-start | bytes 9220
  125.4 9.5 %collective-permute-start.12 = (f32[384,256]{1,0:T(8,128)S(1)}, f32[384,256]{1,0:T(8,128)S(1)}, u32[]{:S(2)}, u32[]{:S(2)}) collective-permute-start(f32[384,256]{1,0:T(8,128)S(1)} %constant_dynamic-slice_fusion.5), channel_id=1, source_target_pairs={{0,16},{16,0},{32,48},{48,32},{1,17},{17,1},{33,49},{49,33},{2,18}... | collective-permute-start | bytes 1179656 | tf_op jit(solution)/shard_map/ppermute | solution.py:220
  135.0 7.9 %collective-permute-start.13 = (f32[192,256]{1,0:T(8,128)S(1)}, f32[192,256]{1,0:T(8,128)S(1)}, u32[]{:S(2)}, u32[]{:S(2)}) collective-permute-start(f32[192,256]{1,0:T(8,128)S(1)} %constant_dynamic-slice_fusion.4), channel_id=1, source_target_pairs={{0,32},{16,48},{32,0},{48,16},{1,33},{17,49},{33,1},{49,17},{2,34}... | collective-permute-start | bytes 589832 | tf_op jit(solution)/shard_map/ppermute | solution.py:220
  143.0 5.4 %collective-permute-start.14 = (f32[96,256]{1,0:T(8,128)S(1)}, f32[96,256]{1,0:T(8,128)S(1)}, u32[]{:S(2)}, u32[]{:S(2)}) collective-permute-start(f32[96,256]{1,0:T(8,128)S(1)} %constant_dynamic-slice_fusion.3), channel_id=1, source_target_pairs={{0,64},{64,0},{128,192},{192,128},{256,320},{320,256},{384,448},{4... | collective-permute-start | bytes 294920 | tf_op jit(solution)/shard_map/ppermute | solution.py:220
  148.4 5.8 %collective-permute-start.15 = (f32[48,256]{1,0:T(8,128)S(1)}, f32[48,256]{1,0:T(8,128)S(1)}, u32[]{:S(2)}, u32[]{:S(2)}) collective-permute-start(f32[48,256]{1,0:T(8,128)S(1)} %constant_dynamic-slice_fusion.2), channel_id=1, source_target_pairs={{0,128},{64,192},{128,0},{192,64},{256,384},{320,448},{384,256},{4... | collective-permute-start | bytes 147464 | tf_op jit(solution)/shard_map/ppermute | solution.py:220
  154.2 8.9 %collective-permute-start.16 = (f32[24,256]{1,0:T(8,128)S(1)}, f32[24,256]{1,0:T(8,128)S(1)}, u32[]{:S(2)}, u32[]{:S(2)}) collective-permute-start(f32[24,256]{1,0:T(8,128)S(1)} %constant_dynamic-slice_fusion.1), channel_id=1, source_target_pairs={{0,256},{64,320},{128,384},{192,448},{256,0},{320,64},{384,128},{4... | collective-permute-start | bytes 73736 | tf_op jit(solution)/shard_map/ppermute | solution.py:220
  163.1 8.5 %collective-permute-start.17 = (f32[24,256]{1,0:T(8,128)S(1)}, f32[24,256]{1,0:T(8,128)S(1)}, u32[]{:S(2)}, u32[]{:S(2)}) collective-permute-start(f32[24,256]{1,0:T(8,128)S(1)} %dynamic-slice_add_fusion.4), channel_id=1, source_target_pairs={{0,256},{64,320},{128,384},{192,448},{256,0},{320,64},{384,128},{4... | collective-permute-start | bytes 73736 | tf_op jit(solution)/shard_map/ppermute | solution.py:230
  171.6 5.8 %collective-permute-start.18 = (f32[48,256]{1,0:T(8,128)S(1)}, f32[48,256]{1,0:T(8,128)S(1)}, u32[]{:S(2)}, u32[]{:S(2)}) collective-permute-start(f32[48,256]{1,0:T(8,128)S(1)} %maximum_select_fusion.12), channel_id=1, source_target_pairs={{0,128},{64,192},{128,0},{192,64},{256,384},{320,448},{384,256},{4... | collective-permute-start | bytes 147464 | tf_op jit(solution)/shard_map/ppermute | solution.py:230
  177.4 5.5 %collective-permute-start.19 = (f32[96,256]{1,0:T(8,128)S(1)}, f32[96,256]{1,0:T(8,128)S(1)}, u32[]{:S(2)}, u32[]{:S(2)}) collective-permute-start(f32[96,256]{1,0:T(8,128)S(1)} %maximum_select_fusion.11), channel_id=1, source_target_pairs={{0,64},{64,0},{128,192},{192,128},{256,320},{320,256},{384,448},{4... | collective-permute-start | bytes 294920 | tf_op jit(solution)/shard_map/ppermute | solution.py:230
  183.0 7.9 %collective-permute-start.20 = (f32[192,256]{1,0:T(8,128)S(1)}, f32[192,256]{1,0:T(8,128)S(1)}, u32[]{:S(2)}, u32[]{:S(2)}) collective-permute-start(f32[192,256]{1,0:T(8,128)S(1)} %maximum_select_fusion.8), channel_id=1, source_target_pairs={{0,32},{16,48},{32,0},{48,16},{1,33},{17,49},{33,1},{49,17},{2,34}... | collective-permute-start | bytes 589832 | tf_op jit(solution)/shard_map/ppermute | solution.py:230
  190.9 8.5 %collective-permute-start.21 = (f32[384,256]{1,0:T(8,128)S(1)}, f32[384,256]{1,0:T(8,128)S(1)}, u32[]{:S(2)}, u32[]{:S(2)}) collective-permute-start(f32[384,256]{1,0:T(8,128)S(1)} %maximum_select_fusion.4), channel_id=1, source_target_pairs={{0,16},{16,0},{32,48},{48,32},{1,17},{17,1},{33,49},{49,33},{2,18}... | collective-permute-start | bytes 1179656 | tf_op jit(solution)/shard_map/ppermute | solution.py:230
  199.5 17.7 %collective-permute-start.22 = (f32[768,256]{1,0:T(8,128)S(1)}, f32[768,256]{1,0:T(8,128)S(1)}, u32[]{:S(2)}, u32[]{:S(2)}) collective-permute-start(f32[768,256]{1,0:T(8,128)S(1)} %maximum_select_fusion.2), channel_id=1, source_target_pairs={{0,2},{1,3},{2,0},{3,1},{4,6},{5,7},{6,4},{7,5},{8,10},{9,11},{10,... | collective-permute-start | bytes 2359304 | tf_op jit(solution)/shard_map/ppermute | solution.py:230
  217.4 20.7 %collective-permute-start.23 = (f32[1536,256]{1,0:T(8,128)S(1)}, f32[1536,256]{1,0:T(8,128)S(1)}, u32[]{:S(2)}, u32[]{:S(2)}) collective-permute-start(f32[1536,256]{1,0:T(8,128)S(1)} %maximum_select_fusion.1), channel_id=1, source_target_pairs={{0,1},{1,0},{2,3},{3,2},{4,5},{5,4},{6,7},{7,6},{8,9},{9,8},{10,11... | collective-permute-start | bytes 4718600 | tf_op jit(solution)/shard_map/ppermute | solution.py:230
  (31 other events, 43.2 us)

commit v4 on v2

--- a/solution.py
+++ b/solution.py
@@ -107,27 +107,50 @@
     return jnp.pad(tensor, ((0, 0), (1, 1), (1, 1), (0, 0)))
 
 
+def group_blocks(channels):
+    group = jnp.arange(channels) // (channels // G)
+    return (group[:, None] == group[None, :]).astype(jnp.float32)
+
+
+def over_groups(values, blocks):
+    return jnp.dot(values, blocks, precision=lax.Precision.HIGHEST)
+
+
+def normalize_spread(tensor, first_c, square_c, gains, scales, shifts, cell_count):
+    average = first_c / cell_count
+    inverse = lax.rsqrt(square_c / cell_count - average * average + EPS)
+    normed = (tensor - average[:, None, None, :]) * inverse[:, None, None, :] * gains
+    return normed * (1.0 + scales[:, None, None, :]) + shifts[:, None, None, :]
+
+
 def block_forward(inputs, flat_weight, gains, scales, shifts, cell_count):
     tensor = inputs.astype(jnp.float32)
-    first_sum, square_sum = group_sums(tensor, G)
-    pre_act = normalize(tensor, first_sum, square_sum, gains, scales, shifts, cell_count)
+    blocks = group_blocks(tensor.shape[3])
+    first_c = over_groups(jnp.sum(tensor, axis=(1, 2)), blocks)
+    square_c = over_groups(jnp.sum(tensor * tensor, axis=(1, 2)), blocks)
+    pre_act = normalize_spread(tensor, first_c, square_c, gains, scales, shifts, cell_count)
     activation = jax.nn.silu(pre_act).astype(jnp.bfloat16)
     padded = pad_both(activation)
     output = (tensor + convolve(padded, flat_weight)).astype(jnp.bfloat16)
-    return output, (first_sum, square_sum, padded)
+    return output, (first_c, square_c, padded)
 
 
 def block_backward(upstream, inputs, saved, flipped, gains, scales, shifts, cell_count):
-    first_sum, square_sum, _ = saved
-    channels = inputs.shape[3]
+    first_c, square_c, _ = saved
     tensor = inputs.astype(jnp.float32)
-    pre_act = normalize(tensor, first_sum, square_sum, gains, scales, shifts, cell_count)
+    blocks = group_blocks(tensor.shape[3])
+    pre_act = normalize_spread(tensor, first_c, square_c, gains, scales, shifts, cell_count)
     d_act = convolve(pad_both(upstream), flipped)
     d_pre = d_act * silu_slope(pre_act)
-    d_tensor, d_first, d_square, d_gains, d_scales, d_shifts = norm_backward(
-        tensor, first_sum, square_sum, gains, scales, shifts, cell_count, d_pre
-    )
-    d_tensor = d_tensor + spread(d_first, channels) + 2.0 * tensor * spread(d_square, channels)
+
+    def mapping(tensor_v, first_v, square_v, gains_v, scales_v, shifts_v):
+        return normalize_spread(tensor_v, first_v, square_v, gains_v, scales_v, shifts_v, cell_count)
+
+    _, pull_back = jax.vjp(mapping, tensor, first_c, square_c, gains, scales, shifts)
+    d_tensor, d_first, d_square, d_gains, d_scales, d_shifts = pull_back(d_pre)
+    d_first = over_groups(d_first, blocks)[:, None, None, :]
+    d_square = over_groups(d_square, blocks)[:, None, None, :]
+    d_tensor = d_tensor + d_first + 2.0 * tensor * d_square
     d_input = (upstream.astype(jnp.float32) + d_tensor).astype(jnp.bfloat16)
     return d_input, (d_gains, d_scales, d_shifts)
 

time: 238 us -> 213 us (0.89)
  local copies, waits for them, and re-layouts: 36.5 us -> 16.8 us
  other arithmetic: 18.2 us -> 6.47 us
  waiting for transfers between devices: 54.3 us -> 62.8 us
  matrix products: 14.7 us -> 17.8 us
  starting transfers between devices: 86.9 us -> 84.3 us
    ppermute x1, waiting for transfers between devices: 0.01 us -> 10.9 us  [per_device(): skip_grad = lax.ppermute(d_input, 'section', [(last, 0)])]
    dot_general x0 -> x14, matrix products: none -> 6.79 us  [over_groups(): return jnp.dot(values, blocks, precision=lax.Precision.HIGHEST)]
    broadcast_in_dim x16 -> x0, local copies, waits for them, and re-layouts: 5.6 us -> none  [spread(): jnp.repeat(values, channels // values.shape[1], axis=1)[:, None, None, :]]
    ppermute x3, waiting for transfers between devices: 14 us -> 9.67 us  [per_device(): upstream = lax.ppermute(carried, 'section', [(active + 1, active)])]
    reduce_sum x18 -> x4, other arithmetic: 5.29 us -> 1.34 us  [the longest x1 1.08 us: block_forward(): square_c = over_groups(jnp.sum(tensor * tensor, axis=(1, 2)), blocks)]
    dot_general x7, matrix products: 13.4 us -> 9.75 us  [convolve(): jnp.dot(flat, matrix, preferred_element_type=jnp.float32)]
    mul x8 -> x0, local copies, waits for them, and re-layouts: 3.43 us -> none  [the longest x5 1.81 us: normalize(): (tensor - spread(average, channels)) * spread(inverse, channels) * gains]
    ppermute x7, starting transfers between devices: 51.8 us -> 48.6 us  [butterfly_gather(): got = lax.ppermute(flat, axis, [(j, j ^ step) for j in range(count)])]
  transfers between devices with their start and end apart: 20 -> 20, of which waited for: 13 -> 14; matrix products, arithmetic and copies ran while one was open for 16% -> 8% of each run, Pallas kernels for 0% -> 0%
where the time goes in v4:
time: 213 us; the launch traced here: 212 us
  starting transfers between devices  84.3 us (40%)
  waiting for transfers between devices  62.8 us (29%)
  blocking collectives  22.3 us (10%)
  matrix products  17.8 us (8%)
  local copies, waits for them, and re-layouts  16.8 us (8%)
  other arithmetic  6.47 us (3%)
    ppermute x7, starting transfers between devices, butterfly_gather(): got = lax.ppermute(flat, axis, [(j, j ^ step) for j in range(count)])  48.6 us
    ppermute x7, waiting for transfers between devices, butterfly_gather(): got = lax.ppermute(flat, axis, [(j, j ^ step) for j in range(count)])  27.7 us
    ppermute x5, starting transfers between devices, butterfly_scatter(): lax.ppermute(sent, axis, [(j, j ^ step) for j in range(count)])  23 us
    ppermute x5, waiting for transfers between devices, butterfly_scatter(): lax.ppermute(sent, axis, [(j, j ^ step) for j in range(count)])  14.6 us
    all_gather x1, blocking collectives, per_device(): images = lax.all_gather(images, 'space', axis=1, tiled=True)  12.8 us
    unnamed x88, local copies, waits for them, and re-layouts  11.3 us
    ppermute x1, waiting for transfers between devices, per_device(): skip_grad = lax.ppermute(d_input, 'section', [(last, 0)])  10.9 us
    dot_general x7, matrix products, convolve(): jnp.dot(flat, matrix, preferred_element_type=jnp.float32)  9.75 us
  transfers between devices with their start and end apart: 20, of which 14 were waited for; matrix products, arithmetic and copies ran while one was open for 8% of the time, Pallas kernels for 0%

profile of v4, /device:TPU:1, one launch (start us, length us, event | category | flops | bytes accessed | tf_op | source)
XLA Modules:
  0.0 212.4 jit_solution(3520016265494975689)
XLA Ops:
  0.7 12.8 %all_gather.6 = bf16[2,4,64,256]{3,2,1,0:T(8,128)(2,1)S(1)} all-gather(bf16[2,1,64,256]{3,2,1,0:T(8,128)(2,1)} %param.6), channel_id=1, replica_groups=mesh['dy'=8,'dx'=4,'section'=4,'space'=4] {'space'}, dimensions={1}, use_global_device_ids=true | all-gather | bytes 327680 | tf_op jit(solution)/shard_map/all_gather | solution.py:165
  17.9 1.5 fusion
  19.4 5.3 %collective-permute-start.3 = (bf16[2,4,64,256]{3,2,1,0:T(8,128)(2,1)}, bf16[2,4,64,256]{3,2,1,0:T(8,128)(2,1)S(1)}, u32[]{:S(2)}, u32[]{:S(2)}) collective-permute-start(bf16[2,4,64,256]{3,2,1,0:T(8,128)(2,1)} %fusion), channel_id=1, source_target_pairs={{0,12},{1,13},{2,14},{3,15},{16,28},{17,29},{18,30},{19,31},{32,44... | collective-permute-start | bytes 786440 | tf_op jit(solution)/shard_map/ppermute | solution.py:190
  26.0 9.4 %all_gather.7 = bf16[2,4,64,256]{3,2,1,0:T(8,128)(2,1)S(1)} all-gather(bf16[2,1,64,256]{3,2,1,0:T(8,128)(2,1)S(1)} %copy-done.5), channel_id=1, replica_groups=mesh['dy'=8,'dx'=4,'section'=4,'space'=4] {'space'}, dimensions={1}, use_global_device_ids=true | all-gather | bytes 327680 | tf_op jit(solution)/shard_map/all_gather | solution.py:166
  45.5 1.5 fusion.2
  49.1 1.6 copy.9
  56.5 2.7 %fusion.60 = (f32[2,256]{1,0:T(2,128)S(1)}, f32[256]{0:T(256)S(1)}, f32[2,256]{1,0:T(2,128)S(1)}, f32[2,256]{1,0:T(2,128)S(1)}, f32[2,256]{1,0:T(2,128)S(1)}, /*index=5*/f32[2,4,64,256]{3,2,1,0:T(8,128)S(1)}) fusion(bf16[2,4,64,256]{3,2,1,0:T(8,128)(2,1)S(1)} %select_select_fusion.1, f32[2,256]{1,0:T(2,128)S(1)} %rsqrt.26, ...), kind=kOutput, calls=%fused_computation.139 | convolution fusion | flops 607254272 | bytes 4343808 | tf_op jit(solution)/shard_map/dot_general | solution.py:74
  63.5 1.5 collective-permute-start.7
  68.7 10.9 %collective-permute-done.7 = bf16[2,4,64,256]{3,2,1,0:T(8,128)(2,1)S(1)} collective-permute-done((bf16[2,4,64,256]{3,2,1,0:T(8,128)(2,1)S(1)}, bf16[2,4,64,256]{3,2,1,0:T(8,128)(2,1)S(1)}, u32[]{:S(2)}, u32[]{:S(2)}) %collective-permute-start.7) | collective-permute-done | bytes 262176 | tf_op jit(solution)/shard_map/ppermute | solution.py:210
  79.5 9.7 %collective-permute-done.6 = bf16[2,4,64,256]{3,2,1,0:T(8,128)(2,1)S(1)} collective-permute-done((bf16[2,4,64,256]{3,2,1,0:T(8,128)(2,1)S(1)}, bf16[2,4,64,256]{3,2,1,0:T(8,128)(2,1)S(1)}, u32[]{:S(2)}, u32[]{:S(2)}) %collective-permute-start.6) | collective-permute-done | bytes 262176 | tf_op jit(solution)/shard_map/ppermute | solution.py:201
  94.3 3.1 %collective-permute-start.8 = (f32[384,256]{1,0:T(8,128)S(1)}, f32[384,256]{1,0:T(8,128)S(1)}, u32[]{:S(2)}, u32[]{:S(2)}) collective-permute-start(f32[384,256]{1,0:T(8,128)S(1)} %constant_dynamic-slice_fusion.5), channel_id=1, source_target_pairs={{0,16},{16,0},{32,48},{48,32},{1,17},{17,1},{33,49},{49,33},{2,18}... | collective-permute-start | bytes 1179656 | tf_op jit(solution)/shard_map/ppermute | solution.py:242
  97.5 5.3 %collective-permute-done.8 = f32[384,256]{1,0:T(8,128)S(1)} collective-permute-done((f32[384,256]{1,0:T(8,128)S(1)}, f32[384,256]{1,0:T(8,128)S(1)}, u32[]{:S(2)}, u32[]{:S(2)}) %collective-permute-start.8) | collective-permute-done | bytes 393248 | tf_op jit(solution)/shard_map/ppermute | solution.py:242
  102.9 4.7 %collective-permute-start.9 = (f32[192,256]{1,0:T(8,128)S(1)}, f32[192,256]{1,0:T(8,128)S(1)}, u32[]{:S(2)}, u32[]{:S(2)}) collective-permute-start(f32[192,256]{1,0:T(8,128)S(1)} %constant_dynamic-slice_fusion.4), channel_id=1, source_target_pairs={{0,32},{16,48},{32,0},{48,16},{1,33},{17,49},{33,1},{49,17},{2,34}... | collective-permute-start | bytes 589832 | tf_op jit(solution)/shard_map/ppermute | solution.py:242
  107.6 4.4 %collective-permute-done.9 = f32[192,256]{1,0:T(8,128)S(1)} collective-permute-done((f32[192,256]{1,0:T(8,128)S(1)}, f32[192,256]{1,0:T(8,128)S(1)}, u32[]{:S(2)}, u32[]{:S(2)}) %collective-permute-start.9) | collective-permute-done | bytes 196640 | tf_op jit(solution)/shard_map/ppermute | solution.py:242
  112.0 3.2 %collective-permute-start.10 = (f32[96,256]{1,0:T(8,128)S(1)}, f32[96,256]{1,0:T(8,128)S(1)}, u32[]{:S(2)}, u32[]{:S(2)}) collective-permute-start(f32[96,256]{1,0:T(8,128)S(1)} %constant_dynamic-slice_fusion.3), channel_id=1, source_target_pairs={{0,64},{64,0},{128,192},{192,128},{256,320},{320,256},{384,448},{4... | collective-permute-start | bytes 294920 | tf_op jit(solution)/shard_map/ppermute | solution.py:242
  115.2 2.1 collective-permute-done.10
  117.4 4.2 %collective-permute-start.11 = (f32[48,256]{1,0:T(8,128)S(1)}, f32[48,256]{1,0:T(8,128)S(1)}, u32[]{:S(2)}, u32[]{:S(2)}) collective-permute-start(f32[48,256]{1,0:T(8,128)S(1)} %constant_dynamic-slice_fusion.2), channel_id=1, source_target_pairs={{0,128},{64,192},{128,0},{192,64},{256,384},{320,448},{384,256},{4... | collective-permute-start | bytes 147464 | tf_op jit(solution)/shard_map/ppermute | solution.py:242
  121.7 1.6 collective-permute-done.11
  123.3 7.8 %collective-permute-start.12 = (f32[24,256]{1,0:T(8,128)S(1)}, f32[24,256]{1,0:T(8,128)S(1)}, u32[]{:S(2)}, u32[]{:S(2)}) collective-permute-start(f32[24,256]{1,0:T(8,128)S(1)} %constant_dynamic-slice_fusion.1), channel_id=1, source_target_pairs={{0,256},{64,320},{128,384},{192,448},{256,0},{320,64},{384,128},{4... | collective-permute-start | bytes 73736 | tf_op jit(solution)/shard_map/ppermute | solution.py:242
  132.2 7.5 %collective-permute-start.13 = (f32[24,256]{1,0:T(8,128)S(1)}, f32[24,256]{1,0:T(8,128)S(1)}, u32[]{:S(2)}, u32[]{:S(2)}) collective-permute-start(f32[24,256]{1,0:T(8,128)S(1)} %dynamic-slice_add_fusion.4), channel_id=1, source_target_pairs={{0,256},{64,320},{128,384},{192,448},{256,0},{320,64},{384,128},{4... | collective-permute-start | bytes 73736 | tf_op jit(solution)/shard_map/ppermute | solution.py:252
  141.0 4.3 %collective-permute-start.14 = (f32[48,256]{1,0:T(8,128)S(1)}, f32[48,256]{1,0:T(8,128)S(1)}, u32[]{:S(2)}, u32[]{:S(2)}) collective-permute-start(f32[48,256]{1,0:T(8,128)S(1)} %maximum_select_fusion.6), channel_id=1, source_target_pairs={{0,128},{64,192},{128,0},{192,64},{256,384},{320,448},{384,256},{4... | collective-permute-start | bytes 147464 | tf_op jit(solution)/shard_map/ppermute | solution.py:252
  146.8 3.0 %collective-permute-start.15 = (f32[96,256]{1,0:T(8,128)S(1)}, f32[96,256]{1,0:T(8,128)S(1)}, u32[]{:S(2)}, u32[]{:S(2)}) collective-permute-start(f32[96,256]{1,0:T(8,128)S(1)} %maximum_select_fusion.5), channel_id=1, source_target_pairs={{0,64},{64,0},{128,192},{192,128},{256,320},{320,256},{384,448},{4... | collective-permute-start | bytes 294920 | tf_op jit(solution)/shard_map/ppermute | solution.py:252
  149.8 2.6 %collective-permute-done.15 = f32[96,256]{1,0:T(8,128)S(1)} collective-permute-done((f32[96,256]{1,0:T(8,128)S(1)}, f32[96,256]{1,0:T(8,128)S(1)}, u32[]{:S(2)}, u32[]{:S(2)}) %collective-permute-start.15) | collective-permute-done | bytes 98336 | tf_op jit(solution)/shard_map/ppermute | solution.py:252
  152.4 4.0 %collective-permute-start.16 = (f32[192,256]{1,0:T(8,128)S(1)}, f32[192,256]{1,0:T(8,128)S(1)}, u32[]{:S(2)}, u32[]{:S(2)}) collective-permute-start(f32[192,256]{1,0:T(8,128)S(1)} %maximum_select_fusion.4), channel_id=1, source_target_pairs={{0,32},{16,48},{32,0},{48,16},{1,33},{17,49},{33,1},{49,17},{2,34}... | collective-permute-start | bytes 589832 | tf_op jit(solution)/shard_map/ppermute | solution.py:252
  156.4 3.9 %collective-permute-done.16 = f32[192,256]{1,0:T(8,128)S(1)} collective-permute-done((f32[192,256]{1,0:T(8,128)S(1)}, f32[192,256]{1,0:T(8,128)S(1)}, u32[]{:S(2)}, u32[]{:S(2)}) %collective-permute-start.16) | collective-permute-done | bytes 196640 | tf_op jit(solution)/shard_map/ppermute | solution.py:252
  160.4 2.4 %collective-permute-start.17 = (f32[384,256]{1,0:T(8,128)S(1)}, f32[384,256]{1,0:T(8,128)S(1)}, u32[]{:S(2)}, u32[]{:S(2)}) collective-permute-start(f32[384,256]{1,0:T(8,128)S(1)} %maximum_select_fusion.3), channel_id=1, source_target_pairs={{0,16},{16,0},{32,48},{48,32},{1,17},{17,1},{33,49},{49,33},{2,18}... | collective-permute-start | bytes 1179656 | tf_op jit(solution)/shard_map/ppermute | solution.py:252
  162.8 6.1 %collective-permute-done.17 = f32[384,256]{1,0:T(8,128)S(1)} collective-permute-done((f32[384,256]{1,0:T(8,128)S(1)}, f32[384,256]{1,0:T(8,128)S(1)}, u32[]{:S(2)}, u32[]{:S(2)}) %collective-permute-start.17) | collective-permute-done | bytes 393248 | tf_op jit(solution)/shard_map/ppermute | solution.py:252
  169.0 9.9 %collective-permute-start.18 = (f32[768,256]{1,0:T(8,128)S(1)}, f32[768,256]{1,0:T(8,128)S(1)}, u32[]{:S(2)}, u32[]{:S(2)}) collective-permute-start(f32[768,256]{1,0:T(8,128)S(1)} %maximum_select_fusion.2), channel_id=1, source_target_pairs={{0,2},{1,3},{2,0},{3,1},{4,6},{5,7},{6,4},{7,5},{8,10},{9,11},{10,... | collective-permute-start | bytes 2359304 | tf_op jit(solution)/shard_map/ppermute | solution.py:252
  178.9 9.3 %collective-permute-done.18 = f32[768,256]{1,0:T(8,128)S(1)} collective-permute-done((f32[768,256]{1,0:T(8,128)S(1)}, f32[768,256]{1,0:T(8,128)S(1)}, u32[]{:S(2)}, u32[]{:S(2)}) %collective-permute-start.18) | collective-permute-done | bytes 786464 | tf_op jit(solution)/shard_map/ppermute | solution.py:252
  188.4 17.5 %collective-permute-start.19 = (f32[1536,256]{1,0:T(8,128)S(1)}, f32[1536,256]{1,0:T(8,128)S(1)}, u32[]{:S(2)}, u32[]{:S(2)}) collective-permute-start(f32[1536,256]{1,0:T(8,128)S(1)} %maximum_select_fusion.1), channel_id=1, source_target_pairs={{0,1},{1,0},{2,3},{3,2},{4,5},{5,4},{6,7},{7,6},{8,9},{9,8},{10,11... | collective-permute-start | bytes 4718600 | tf_op jit(solution)/shard_map/ppermute | solution.py:252
  205.9 3.0 %collective-permute-done.19 = f32[1536,256]{1,0:T(8,128)S(1)} collective-permute-done((f32[1536,256]{1,0:T(8,128)S(1)}, f32[1536,256]{1,0:T(8,128)S(1)}, u32[]{:S(2)}, u32[]{:S(2)}) %collective-permute-start.19) | collective-permute-done | bytes 1572896 | tf_op jit(solution)/shard_map/ppermute | solution.py:252
  209.3 1.6 slice.298
  (180 shorter events, 42.1 us)
Async XLA Ops:
  0.6 13.7 %copy-start = (bf16[1,256,512]{2,1,0:T(8,128)(2,1)S(1)}, bf16[1,256,512]{2,1,0:T(8,128)(2,1)}, u32[]{:S(2)}) copy-start(bf16[1,256,512]{2,1,0:T(8,128)(2,1)} %param.11) | copy-start | bytes 786436
  0.6 16.2 %copy-start.4 = (f32[1,256]{1,0:T(1,128)S(1)}, f32[1,256]{1,0:T(1,128)}, u32[]{:S(2)}) copy-start(f32[1,256]{1,0:T(1,128)} %param.10) | copy-start | bytes 3076
  0.7 43.1 %copy-start.8 = (s32[256]{0:T(256)}, s32[256]{0:T(256)S(1)}, u32[]{:S(2)}) copy-start(s32[256]{0:T(256)S(1)} %and_select_fusion) | copy-start | bytes 3076
  14.3 2.9 %copy-start.6 = (f32[2,128]{1,0:T(2,128)}, f32[2,128]{1,0:T(2,128)S(1)}, u32[]{:S(2)}) copy-start(f32[2,128]{1,0:T(2,128)S(1)} %get-tuple-element.47) | copy-start | bytes 3076
  14.9 9.8 %copy-start.10 = (f32[2,256]{1,0:T(2,128)}, f32[2,256]{1,0:T(2,128)S(1)}, u32[]{:S(2)}) copy-start(f32[2,256]{1,0:T(2,128)S(1)} %fusion.27) | copy-start | bytes 6148
  16.6 1.3 copy-start.1
  17.3 8.7 %copy-start.5 = (bf16[2,1,64,256]{3,2,1,0:T(8,128)(2,1)S(1)}, bf16[2,1,64,256]{3,2,1,0:T(8,128)(2,1)}, u32[]{:S(2)}) copy-start(bf16[2,1,64,256]{3,2,1,0:T(8,128)(2,1)} %param.8) | copy-start | bytes 196612
  19.4 33.8 %collective-permute-start.3 = (bf16[2,4,64,256]{3,2,1,0:T(8,128)(2,1)}, bf16[2,4,64,256]{3,2,1,0:T(8,128)(2,1)S(1)}, u32[]{:S(2)}, u32[]{:S(2)}) collective-permute-start(bf16[2,4,64,256]{3,2,1,0:T(8,128)(2,1)} %fusion), channel_id=1, source_target_pairs={{0,12},{1,13},{2,14},{3,15},{16,28},{17,29},{18,30},{19,31},{32,44... | collective-permute-start | bytes 786440 | tf_op jit(solution)/shard_map/ppermute | solution.py:190
  24.7 13.0 %collective-permute-start = (bf16[2,4,64,256]{3,2,1,0:T(8,128)(2,1)}, bf16[2,4,64,256]{3,2,1,0:T(8,128)(2,1)S(1)}, u32[]{:S(2)}, u32[]{:S(2)}) collective-permute-start(bf16[2,4,64,256]{3,2,1,0:T(8,128)(2,1)} %fusion), channel_id=1, source_target_pairs={{0,4},{1,5},{2,6},{3,7},{16,20},{17,21},{18,22},{19,23},{32,36},{3... | collective-permute-start | bytes 786440 | tf_op jit(solution)/shard_map/ppermute | solution.py:185
  38.0 1.7 copy-start.11
  40.5 2.9 %collective-permute-start.1 = (bf16[2,4,64,256]{3,2,1,0:T(8,128)(2,1)S(1)}, bf16[2,4,64,256]{3,2,1,0:T(8,128)(2,1)S(1)}, u32[]{:S(2)}, u32[]{:S(2)}) collective-permute-start(bf16[2,4,64,256]{3,2,1,0:T(8,128)(2,1)S(1)} %fusion.1), channel_id=1, source_target_pairs={{4,8},{5,9},{6,10},{7,11},{20,24},{21,25},{22,26},{23,27},{36,40},... | collective-permute-start | bytes 786440 | tf_op jit(solution)/shard_map/ppermute | solution.py:185
  47.0 6.3 %collective-permute-start.2 = (bf16[2,4,64,256]{3,2,1,0:T(8,128)(2,1)}, bf16[2,4,64,256]{3,2,1,0:T(8,128)(2,1)}, u32[]{:S(2)}, u32[]{:S(2)}) collective-permute-start(bf16[2,4,64,256]{3,2,1,0:T(8,128)(2,1)} %fusion.2), channel_id=1, source_target_pairs={{8,12},{9,13},{10,14},{11,15},{24,28},{25,29},{26,30},{27,31},{40,... | collective-permute-start | bytes 786440 | tf_op jit(solution)/shard_map/ppermute | solution.py:185
  51.8 4.7 %copy-start.2 = (bf16[3,3,256,256]{2,3,1,0:T(8,128)(2,1)S(1)}, bf16[3,3,256,256]{2,3,1,0:T(8,128)(2,1)}, u32[]{:S(2)}) copy-start(bf16[3,3,256,256]{2,3,1,0:T(8,128)(2,1)} %rev.3) | copy-start | bytes 3538948
  56.5 2.8 %copy-start.9 = (s32[256]{0:T(256)S(1)}, s32[256]{0:T(256)}, u32[]{:S(2)}) copy-start(s32[256]{0:T(256)} %copy-done.8) | copy-start | bytes 3076
  59.9 0.7 collective-permute-start.4
  62.8 2.2 %collective-permute-start.5 = (bf16[2,4,64,256]{3,2,1,0:T(8,128)(2,1)S(1)}, bf16[2,4,64,256]{3,2,1,0:T(8,128)(2,1)S(1)}, u32[]{:S(2)}, u32[]{:S(2)}) collective-permute-start(bf16[2,4,64,256]{3,2,1,0:T(8,128)(2,1)S(1)} %fusion.93), channel_id=1, source_target_pairs={{8,4},{9,5},{10,6},{11,7},{24,20},{25,21},{26,22},{27,23},{40,36},... | collective-permute-start | bytes 786440 | tf_op jit(solution)/shard_map/ppermute | solution.py:201
  63.5 16.0 %collective-permute-start.7 = (bf16[2,4,64,256]{3,2,1,0:T(8,128)(2,1)S(1)}, bf16[2,4,64,256]{3,2,1,0:T(8,128)(2,1)S(1)}, u32[]{:S(2)}, u32[]{:S(2)}) collective-permute-start(bf16[2,4,64,256]{3,2,1,0:T(8,128)(2,1)S(1)} %fusion.90), channel_id=1, source_target_pairs={{12,0},{13,1},{14,2},{15,3},{28,16},{29,17},{30,18},{31,19},{44,32... | collective-permute-start | bytes 786440 | tf_op jit(solution)/shard_map/ppermute | solution.py:210
  67.2 22.0 %collective-permute-start.6 = (bf16[2,4,64,256]{3,2,1,0:T(8,128)(2,1)S(1)}, bf16[2,4,64,256]{3,2,1,0:T(8,128)(2,1)S(1)}, u32[]{:S(2)}, u32[]{:S(2)}) collective-permute-start(bf16[2,4,64,256]{3,2,1,0:T(8,128)(2,1)S(1)} %fusion.96), channel_id=1, source_target_pairs={{4,0},{5,1},{6,2},{7,3},{20,16},{21,17},{22,18},{23,19},{36,32},{3... | collective-permute-start | bytes 786440 | tf_op jit(solution)/shard_map/ppermute | solution.py:201
  89.4 1.3 copy-start.3
  90.7 1.2 copy-start.7
  94.3 8.5 %collective-permute-start.8 = (f32[384,256]{1,0:T(8,128)S(1)}, f32[384,256]{1,0:T(8,128)S(1)}, u32[]{:S(2)}, u32[]{:S(2)}) collective-permute-start(f32[384,256]{1,0:T(8,128)S(1)} %constant_dynamic-slice_fusion.5), channel_id=1, source_target_pairs={{0,16},{16,0},{32,48},{48,32},{1,17},{17,1},{33,49},{49,33},{2,18}... | collective-permute-start | bytes 1179656 | tf_op jit(solution)/shard_map/ppermute | solution.py:242
  102.9 9.1 %collective-permute-start.9 = (f32[192,256]{1,0:T(8,128)S(1)}, f32[192,256]{1,0:T(8,128)S(1)}, u32[]{:S(2)}, u32[]{:S(2)}) collective-permute-start(f32[192,256]{1,0:T(8,128)S(1)} %constant_dynamic-slice_fusion.4), channel_id=1, source_target_pairs={{0,32},{16,48},{32,0},{48,16},{1,33},{17,49},{33,1},{49,17},{2,34}... | collective-permute-start | bytes 589832 | tf_op jit(solution)/shard_map/ppermute | solution.py:242
  112.0 5.4 %collective-permute-start.10 = (f32[96,256]{1,0:T(8,128)S(1)}, f32[96,256]{1,0:T(8,128)S(1)}, u32[]{:S(2)}, u32[]{:S(2)}) collective-permute-start(f32[96,256]{1,0:T(8,128)S(1)} %constant_dynamic-slice_fusion.3), channel_id=1, source_target_pairs={{0,64},{64,0},{128,192},{192,128},{256,320},{320,256},{384,448},{4... | collective-permute-start | bytes 294920 | tf_op jit(solution)/shard_map/ppermute | solution.py:242
  117.4 5.8 %collective-permute-start.11 = (f32[48,256]{1,0:T(8,128)S(1)}, f32[48,256]{1,0:T(8,128)S(1)}, u32[]{:S(2)}, u32[]{:S(2)}) collective-permute-start(f32[48,256]{1,0:T(8,128)S(1)} %constant_dynamic-slice_fusion.2), channel_id=1, source_target_pairs={{0,128},{64,192},{128,0},{192,64},{256,384},{320,448},{384,256},{4... | collective-permute-start | bytes 147464 | tf_op jit(solution)/shard_map/ppermute | solution.py:242
  123.3 9.0 %collective-permute-start.12 = (f32[24,256]{1,0:T(8,128)S(1)}, f32[24,256]{1,0:T(8,128)S(1)}, u32[]{:S(2)}, u32[]{:S(2)}) collective-permute-start(f32[24,256]{1,0:T(8,128)S(1)} %constant_dynamic-slice_fusion.1), channel_id=1, source_target_pairs={{0,256},{64,320},{128,384},{192,448},{256,0},{320,64},{384,128},{4... | collective-permute-start | bytes 73736 | tf_op jit(solution)/shard_map/ppermute | solution.py:242
  132.2 8.7 %collective-permute-start.13 = (f32[24,256]{1,0:T(8,128)S(1)}, f32[24,256]{1,0:T(8,128)S(1)}, u32[]{:S(2)}, u32[]{:S(2)}) collective-permute-start(f32[24,256]{1,0:T(8,128)S(1)} %dynamic-slice_add_fusion.4), channel_id=1, source_target_pairs={{0,256},{64,320},{128,384},{192,448},{256,0},{320,64},{384,128},{4... | collective-permute-start | bytes 73736 | tf_op jit(solution)/shard_map/ppermute | solution.py:252
  141.0 5.8 %collective-permute-start.14 = (f32[48,256]{1,0:T(8,128)S(1)}, f32[48,256]{1,0:T(8,128)S(1)}, u32[]{:S(2)}, u32[]{:S(2)}) collective-permute-start(f32[48,256]{1,0:T(8,128)S(1)} %maximum_select_fusion.6), channel_id=1, source_target_pairs={{0,128},{64,192},{128,0},{192,64},{256,384},{320,448},{384,256},{4... | collective-permute-start | bytes 147464 | tf_op jit(solution)/shard_map/ppermute | solution.py:252
  146.8 5.6 %collective-permute-start.15 = (f32[96,256]{1,0:T(8,128)S(1)}, f32[96,256]{1,0:T(8,128)S(1)}, u32[]{:S(2)}, u32[]{:S(2)}) collective-permute-start(f32[96,256]{1,0:T(8,128)S(1)} %maximum_select_fusion.5), channel_id=1, source_target_pairs={{0,64},{64,0},{128,192},{192,128},{256,320},{320,256},{384,448},{4... | collective-permute-start | bytes 294920 | tf_op jit(solution)/shard_map/ppermute | solution.py:252
  152.4 7.9 %collective-permute-start.16 = (f32[192,256]{1,0:T(8,128)S(1)}, f32[192,256]{1,0:T(8,128)S(1)}, u32[]{:S(2)}, u32[]{:S(2)}) collective-permute-start(f32[192,256]{1,0:T(8,128)S(1)} %maximum_select_fusion.4), channel_id=1, source_target_pairs={{0,32},{16,48},{32,0},{48,16},{1,33},{17,49},{33,1},{49,17},{2,34}... | collective-permute-start | bytes 589832 | tf_op jit(solution)/shard_map/ppermute | solution.py:252
  160.4 8.5 %collective-permute-start.17 = (f32[384,256]{1,0:T(8,128)S(1)}, f32[384,256]{1,0:T(8,128)S(1)}, u32[]{:S(2)}, u32[]{:S(2)}) collective-permute-start(f32[384,256]{1,0:T(8,128)S(1)} %maximum_select_fusion.3), channel_id=1, source_target_pairs={{0,16},{16,0},{32,48},{48,32},{1,17},{17,1},{33,49},{49,33},{2,18}... | collective-permute-start | bytes 1179656 | tf_op jit(solution)/shard_map/ppermute | solution.py:252
  169.0 19.3 %collective-permute-start.18 = (f32[768,256]{1,0:T(8,128)S(1)}, f32[768,256]{1,0:T(8,128)S(1)}, u32[]{:S(2)}, u32[]{:S(2)}) collective-permute-start(f32[768,256]{1,0:T(8,128)S(1)} %maximum_select_fusion.2), channel_id=1, source_target_pairs={{0,2},{1,3},{2,0},{3,1},{4,6},{5,7},{6,4},{7,5},{8,10},{9,11},{10,... | collective-permute-start | bytes 2359304 | tf_op jit(solution)/shard_map/ppermute | solution.py:252
  188.4 20.5 %collective-permute-start.19 = (f32[1536,256]{1,0:T(8,128)S(1)}, f32[1536,256]{1,0:T(8,128)S(1)}, u32[]{:S(2)}, u32[]{:S(2)}) collective-permute-start(f32[1536,256]{1,0:T(8,128)S(1)} %maximum_select_fusion.1), channel_id=1, source_target_pairs={{0,1},{1,0},{2,3},{3,2},{4,5},{5,4},{6,7},{7,6},{8,9},{9,8},{10,11... | collective-permute-start | bytes 4718600 | tf_op jit(solution)/shard_map/ppermute | solution.py:252
  (1 other events, 0.9 us)

commit v5 on v4

--- a/solution.py
+++ b/solution.py
@@ -162,8 +162,9 @@
 def per_device(images, steps, out_grad, conv_weight, gn_gain, emb_weight):
     section_count = lax.axis_size("section")
     section_no = lax.axis_index("section")
-    images = lax.all_gather(images, "space", axis=1, tiled=True)
-    out_grad = lax.all_gather(out_grad, "space", axis=1, tiled=True)
+    both = lax.all_gather(jnp.stack([images, out_grad]), "space", axis=2, tiled=True)
+    images = both[0]
+    out_grad = both[1]
     row_count = images.shape[1]
     col_count = images.shape[2]
     channels = images.shape[3]

time: 213 us -> 221 us (1.038)
  blocking collectives: 22.3 us -> 13.2 us
  waiting for transfers between devices: 62.8 us -> 70.1 us
  local copies, waits for them, and re-layouts: 16.8 us -> 22.5 us
  other arithmetic: 6.47 us -> 9.26 us
    all_gather x2 -> x1, blocking collectives: 22.3 us -> 13.2 us  [per_device(): lax.all_gather(jnp.stack([images, out_grad]), 'space', axis=2, tiled=True)]
    ppermute x1, waiting for transfers between devices: 10.9 us -> 18.5 us  [per_device(): skip_grad = lax.ppermute(d_input, 'section', [(last, 0)])]
    unnamed x88 -> x97, local copies, waits for them, and re-layouts: 11.3 us -> 16.2 us
  transfers between devices with their start and end apart: 20 -> 20, of which waited for: 14 -> 15; matrix products, arithmetic and copies ran while one was open for 8% -> 6% of each run, Pallas kernels for 0% -> 0%
where the time goes in v5:
time: 221 us; the launch traced here: 220 us
  starting transfers between devices  85.3 us (39%)
  waiting for transfers between devices  70.1 us (32%)
  local copies, waits for them, and re-layouts  22.5 us (10%)
  matrix products  17.4 us (8%)
  blocking collectives  13.2 us (6%)
  other arithmetic  9.26 us (4%)
    ppermute x7, starting transfers between devices, butterfly_gather(): got = lax.ppermute(flat, axis, [(j, j ^ step) for j in range(count)])  48.9 us
    ppermute x7, waiting for transfers between devices, butterfly_gather(): got = lax.ppermute(flat, axis, [(j, j ^ step) for j in range(count)])  27.1 us
    ppermute x5, starting transfers between devices, butterfly_scatter(): lax.ppermute(sent, axis, [(j, j ^ step) for j in range(count)])  23 us
    ppermute x1, waiting for transfers between devices, per_device(): skip_grad = lax.ppermute(d_input, 'section', [(last, 0)])  18.5 us
    unnamed x97, local copies, waits for them, and re-layouts  16.2 us
    ppermute x5, waiting for transfers between devices, butterfly_scatter(): lax.ppermute(sent, axis, [(j, j ^ step) for j in range(count)])  14.2 us
    all_gather x1, blocking collectives, per_device(): lax.all_gather(jnp.stack([images, out_grad]), 'space', axis=2, tiled=True)  13.2 us
    ppermute x3, waiting for transfers between devices, per_device(): upstream = lax.ppermute(carried, 'section', [(active + 1, active)])  9.78 us
  transfers between devices with their start and end apart: 20, of which 15 were waited for; matrix products, arithmetic and copies ran while one was open for 6% of the time, Pallas kernels for 0%

profile of v5, /device:TPU:1, one launch (start us, length us, event | category | flops | bytes accessed | tf_op | source)
XLA Modules:
  0.0 219.7 jit_solution(16012981139288783623)
XLA Ops:
  1.6 13.2 %all_gather.3 = bf16[2,2,4,64,256]{4,3,2,1,0:T(8,128)(2,1)S(1)} all-gather(bf16[2,2,1,64,256]{4,3,2,1,0:T(8,128)(2,1)S(1)} %pad_maximum_fusion), channel_id=1, replica_groups=mesh['dy'=8,'dx'=4,'section'=4,'space'=4] {'space'}, dimensions={2}, use_global_device_ids=true | all-gather | bytes 655360 | tf_op jit(solution)/shard_map/all_gather | solution.py:165
  19.2 1.5 fusion
  20.7 2.0 collective-permute-start
  22.7 5.3 %collective-permute-start.3 = (bf16[2,4,64,256]{3,2,1,0:T(8,128)(2,1)}, bf16[2,4,64,256]{3,2,1,0:T(8,128)(2,1)}, u32[]{:S(2)}, u32[]{:S(2)}) collective-permute-start(bf16[2,4,64,256]{3,2,1,0:T(8,128)(2,1)} %fusion), channel_id=1, source_target_pairs={{0,12},{1,13},{2,14},{3,15},{16,28},{17,29},{18,30},{19,31},{32,44... | collective-permute-start | bytes 786440 | tf_op jit(solution)/shard_map/ppermute | solution.py:191
  38.5 1.6 copy.9
  48.4 2.7 %fusion.60 = (f32[2,256]{1,0:T(2,128)S(1)}, f32[256]{0:T(256)S(1)}, f32[2,256]{1,0:T(2,128)S(1)}, f32[2,256]{1,0:T(2,128)S(1)}, f32[2,256]{1,0:T(2,128)S(1)}, /*index=5*/f32[2,4,64,256]{3,2,1,0:T(8,128)S(1)}) fusion(bf16[2,4,64,256]{3,2,1,0:T(8,128)(2,1)S(1)} %get-tuple-element.36, f32[2,256]{1,0:T(2,128)S(1)} %rsqrt.26, ...), kind=kOutput, calls=%fused_computation.139 | convolution fusion | flops 607254272 | bytes 4343808 | tf_op jit(solution)/shard_map/dot_general | solution.py:74
  55.4 1.5 collective-permute-start.7
  60.6 18.5 %collective-permute-done.7 = bf16[2,4,64,256]{3,2,1,0:T(8,128)(2,1)S(1)} collective-permute-done((bf16[2,4,64,256]{3,2,1,0:T(8,128)(2,1)S(1)}, bf16[2,4,64,256]{3,2,1,0:T(8,128)(2,1)S(1)}, u32[]{:S(2)}, u32[]{:S(2)}) %collective-permute-start.7) | collective-permute-done | bytes 262176 | tf_op jit(solution)/shard_map/ppermute | solution.py:211
  79.1 9.8 %collective-permute-done.6 = bf16[2,4,64,256]{3,2,1,0:T(8,128)(2,1)} collective-permute-done((bf16[2,4,64,256]{3,2,1,0:T(8,128)(2,1)S(1)}, bf16[2,4,64,256]{3,2,1,0:T(8,128)(2,1)}, u32[]{:S(2)}, u32[]{:S(2)}) %collective-permute-start.6) | collective-permute-done | bytes 262176 | tf_op jit(solution)/shard_map/ppermute | solution.py:202
  100.2 1.8 fusion.54
  102.3 3.1 %collective-permute-start.8 = (f32[384,256]{1,0:T(8,128)S(1)}, f32[384,256]{1,0:T(8,128)S(1)}, u32[]{:S(2)}, u32[]{:S(2)}) collective-permute-start(f32[384,256]{1,0:T(8,128)S(1)} %constant_dynamic-slice_fusion.5), channel_id=1, source_target_pairs={{0,16},{16,0},{32,48},{48,32},{1,17},{17,1},{33,49},{49,33},{2,18}... | collective-permute-start | bytes 1179656 | tf_op jit(solution)/shard_map/ppermute | solution.py:243
  105.4 5.4 %collective-permute-done.8 = f32[384,256]{1,0:T(8,128)S(1)} collective-permute-done((f32[384,256]{1,0:T(8,128)S(1)}, f32[384,256]{1,0:T(8,128)S(1)}, u32[]{:S(2)}, u32[]{:S(2)}) %collective-permute-start.8) | collective-permute-done | bytes 393248 | tf_op jit(solution)/shard_map/ppermute | solution.py:243
  110.9 4.7 %collective-permute-start.9 = (f32[192,256]{1,0:T(8,128)S(1)}, f32[192,256]{1,0:T(8,128)S(1)}, u32[]{:S(2)}, u32[]{:S(2)}) collective-permute-start(f32[192,256]{1,0:T(8,128)S(1)} %constant_dynamic-slice_fusion.4), channel_id=1, source_target_pairs={{0,32},{16,48},{32,0},{48,16},{1,33},{17,49},{33,1},{49,17},{2,34}... | collective-permute-start | bytes 589832 | tf_op jit(solution)/shard_map/ppermute | solution.py:243
  115.5 3.9 %collective-permute-done.9 = f32[192,256]{1,0:T(8,128)S(1)} collective-permute-done((f32[192,256]{1,0:T(8,128)S(1)}, f32[192,256]{1,0:T(8,128)S(1)}, u32[]{:S(2)}, u32[]{:S(2)}) %collective-permute-start.9) | collective-permute-done | bytes 196640 | tf_op jit(solution)/shard_map/ppermute | solution.py:243
  119.5 3.2 %collective-permute-start.10 = (f32[96,256]{1,0:T(8,128)S(1)}, f32[96,256]{1,0:T(8,128)S(1)}, u32[]{:S(2)}, u32[]{:S(2)}) collective-permute-start(f32[96,256]{1,0:T(8,128)S(1)} %constant_dynamic-slice_fusion.3), channel_id=1, source_target_pairs={{0,64},{64,0},{128,192},{192,128},{256,320},{320,256},{384,448},{4... | collective-permute-start | bytes 294920 | tf_op jit(solution)/shard_map/ppermute | solution.py:243
  122.8 2.1 collective-permute-done.10
  124.9 4.2 %collective-permute-start.11 = (f32[48,256]{1,0:T(8,128)S(1)}, f32[48,256]{1,0:T(8,128)S(1)}, u32[]{:S(2)}, u32[]{:S(2)}) collective-permute-start(f32[48,256]{1,0:T(8,128)S(1)} %constant_dynamic-slice_fusion.2), channel_id=1, source_target_pairs={{0,128},{64,192},{128,0},{192,64},{256,384},{320,448},{384,256},{4... | collective-permute-start | bytes 147464 | tf_op jit(solution)/shard_map/ppermute | solution.py:243
  129.2 1.6 collective-permute-done.11
  130.8 7.8 %collective-permute-start.12 = (f32[24,256]{1,0:T(8,128)S(1)}, f32[24,256]{1,0:T(8,128)S(1)}, u32[]{:S(2)}, u32[]{:S(2)}) collective-permute-start(f32[24,256]{1,0:T(8,128)S(1)} %constant_dynamic-slice_fusion.1), channel_id=1, source_target_pairs={{0,256},{64,320},{128,384},{192,448},{256,0},{320,64},{384,128},{4... | collective-permute-start | bytes 73736 | tf_op jit(solution)/shard_map/ppermute | solution.py:243
  139.8 7.5 %collective-permute-start.13 = (f32[24,256]{1,0:T(8,128)S(1)}, f32[24,256]{1,0:T(8,128)S(1)}, u32[]{:S(2)}, u32[]{:S(2)}) collective-permute-start(f32[24,256]{1,0:T(8,128)S(1)} %dynamic-slice_add_fusion.4), channel_id=1, source_target_pairs={{0,256},{64,320},{128,384},{192,448},{256,0},{320,64},{384,128},{4... | collective-permute-start | bytes 73736 | tf_op jit(solution)/shard_map/ppermute | solution.py:253
  148.5 4.3 %collective-permute-start.14 = (f32[48,256]{1,0:T(8,128)S(1)}, f32[48,256]{1,0:T(8,128)S(1)}, u32[]{:S(2)}, u32[]{:S(2)}) collective-permute-start(f32[48,256]{1,0:T(8,128)S(1)} %maximum_select_fusion.6), channel_id=1, source_target_pairs={{0,128},{64,192},{128,0},{192,64},{256,384},{320,448},{384,256},{4... | collective-permute-start | bytes 147464 | tf_op jit(solution)/shard_map/ppermute | solution.py:253
  154.3 3.0 %collective-permute-start.15 = (f32[96,256]{1,0:T(8,128)S(1)}, f32[96,256]{1,0:T(8,128)S(1)}, u32[]{:S(2)}, u32[]{:S(2)}) collective-permute-start(f32[96,256]{1,0:T(8,128)S(1)} %maximum_select_fusion.5), channel_id=1, source_target_pairs={{0,64},{64,0},{128,192},{192,128},{256,320},{320,256},{384,448},{4... | collective-permute-start | bytes 294920 | tf_op jit(solution)/shard_map/ppermute | solution.py:253
  157.4 2.6 %collective-permute-done.15 = f32[96,256]{1,0:T(8,128)S(1)} collective-permute-done((f32[96,256]{1,0:T(8,128)S(1)}, f32[96,256]{1,0:T(8,128)S(1)}, u32[]{:S(2)}, u32[]{:S(2)}) %collective-permute-start.15) | collective-permute-done | bytes 98336 | tf_op jit(solution)/shard_map/ppermute | solution.py:253
  160.0 4.2 %collective-permute-start.16 = (f32[192,256]{1,0:T(8,128)S(1)}, f32[192,256]{1,0:T(8,128)S(1)}, u32[]{:S(2)}, u32[]{:S(2)}) collective-permute-start(f32[192,256]{1,0:T(8,128)S(1)} %maximum_select_fusion.4), channel_id=1, source_target_pairs={{0,32},{16,48},{32,0},{48,16},{1,33},{17,49},{33,1},{49,17},{2,34}... | collective-permute-start | bytes 589832 | tf_op jit(solution)/shard_map/ppermute | solution.py:253
  164.2 3.7 %collective-permute-done.16 = f32[192,256]{1,0:T(8,128)S(1)} collective-permute-done((f32[192,256]{1,0:T(8,128)S(1)}, f32[192,256]{1,0:T(8,128)S(1)}, u32[]{:S(2)}, u32[]{:S(2)}) %collective-permute-start.16) | collective-permute-done | bytes 196640 | tf_op jit(solution)/shard_map/ppermute | solution.py:253
  167.9 2.7 %collective-permute-start.17 = (f32[384,256]{1,0:T(8,128)S(1)}, f32[384,256]{1,0:T(8,128)S(1)}, u32[]{:S(2)}, u32[]{:S(2)}) collective-permute-start(f32[384,256]{1,0:T(8,128)S(1)} %maximum_select_fusion.3), channel_id=1, source_target_pairs={{0,16},{16,0},{32,48},{48,32},{1,17},{17,1},{33,49},{49,33},{2,18}... | collective-permute-start | bytes 1179656 | tf_op jit(solution)/shard_map/ppermute | solution.py:253
  170.7 5.8 %collective-permute-done.17 = f32[384,256]{1,0:T(8,128)S(1)} collective-permute-done((f32[384,256]{1,0:T(8,128)S(1)}, f32[384,256]{1,0:T(8,128)S(1)}, u32[]{:S(2)}, u32[]{:S(2)}) %collective-permute-start.17) | collective-permute-done | bytes 393248 | tf_op jit(solution)/shard_map/ppermute | solution.py:253
  176.5 9.7 %collective-permute-start.18 = (f32[768,256]{1,0:T(8,128)S(1)}, f32[768,256]{1,0:T(8,128)S(1)}, u32[]{:S(2)}, u32[]{:S(2)}) collective-permute-start(f32[768,256]{1,0:T(8,128)S(1)} %maximum_select_fusion.2), channel_id=1, source_target_pairs={{0,2},{1,3},{2,0},{3,1},{4,6},{5,7},{6,4},{7,5},{8,10},{9,11},{10,... | collective-permute-start | bytes 2359304 | tf_op jit(solution)/shard_map/ppermute | solution.py:253
  186.3 9.3 %collective-permute-done.18 = f32[768,256]{1,0:T(8,128)S(1)} collective-permute-done((f32[768,256]{1,0:T(8,128)S(1)}, f32[768,256]{1,0:T(8,128)S(1)}, u32[]{:S(2)}, u32[]{:S(2)}) %collective-permute-start.18) | collective-permute-done | bytes 786464 | tf_op jit(solution)/shard_map/ppermute | solution.py:253
  195.8 17.4 %collective-permute-start.19 = (f32[1536,256]{1,0:T(8,128)S(1)}, f32[1536,256]{1,0:T(8,128)S(1)}, u32[]{:S(2)}, u32[]{:S(2)}) collective-permute-start(f32[1536,256]{1,0:T(8,128)S(1)} %maximum_select_fusion.1), channel_id=1, source_target_pairs={{0,1},{1,0},{2,3},{3,2},{4,5},{5,4},{6,7},{7,6},{8,9},{9,8},{10,11... | collective-permute-start | bytes 4718600 | tf_op jit(solution)/shard_map/ppermute | solution.py:253
  213.2 3.0 %collective-permute-done.19 = f32[1536,256]{1,0:T(8,128)S(1)} collective-permute-done((f32[1536,256]{1,0:T(8,128)S(1)}, f32[1536,256]{1,0:T(8,128)S(1)}, u32[]{:S(2)}, u32[]{:S(2)}) %collective-permute-start.19) | collective-permute-done | bytes 1572896 | tf_op jit(solution)/shard_map/ppermute | solution.py:253
  216.6 1.6 slice.308
  (190 shorter events, 49.1 us)
Async XLA Ops:
  0.6 15.1 %copy-start = (bf16[1,256,512]{2,1,0:T(8,128)(2,1)S(1)}, bf16[1,256,512]{2,1,0:T(8,128)(2,1)}, u32[]{:S(2)}) copy-start(bf16[1,256,512]{2,1,0:T(8,128)(2,1)} %param.11) | copy-start | bytes 786436
  0.6 17.5 %copy-start.4 = (f32[1,256]{1,0:T(1,128)S(1)}, f32[1,256]{1,0:T(1,128)}, u32[]{:S(2)}) copy-start(f32[1,256]{1,0:T(1,128)} %param.10) | copy-start | bytes 3076
  0.7 32.5 %copy-start.7 = (s32[256]{0:T(256)}, s32[256]{0:T(256)S(1)}, u32[]{:S(2)}) copy-start(s32[256]{0:T(256)S(1)} %and_select_fusion) | copy-start | bytes 3076
  20.7 7.9 %collective-permute-start = (bf16[2,4,64,256]{3,2,1,0:T(8,128)(2,1)}, bf16[2,4,64,256]{3,2,1,0:T(8,128)(2,1)S(1)}, u32[]{:S(2)}, u32[]{:S(2)}) collective-permute-start(bf16[2,4,64,256]{3,2,1,0:T(8,128)(2,1)} %fusion), channel_id=1, source_target_pairs={{0,4},{1,5},{2,6},{3,7},{16,20},{17,21},{18,22},{19,23},{32,36},{3... | collective-permute-start | bytes 786440 | tf_op jit(solution)/shard_map/ppermute | solution.py:186
  22.7 20.0 %collective-permute-start.3 = (bf16[2,4,64,256]{3,2,1,0:T(8,128)(2,1)}, bf16[2,4,64,256]{3,2,1,0:T(8,128)(2,1)}, u32[]{:S(2)}, u32[]{:S(2)}) collective-permute-start(bf16[2,4,64,256]{3,2,1,0:T(8,128)(2,1)} %fusion), channel_id=1, source_target_pairs={{0,12},{1,13},{2,14},{3,15},{16,28},{17,29},{18,30},{19,31},{32,44... | collective-permute-start | bytes 786440 | tf_op jit(solution)/shard_map/ppermute | solution.py:191
  31.4 1.5 collective-permute-start.1
  36.4 6.3 %collective-permute-start.2 = (bf16[2,4,64,256]{3,2,1,0:T(8,128)(2,1)}, bf16[2,4,64,256]{3,2,1,0:T(8,128)(2,1)}, u32[]{:S(2)}, u32[]{:S(2)}) collective-permute-start(bf16[2,4,64,256]{3,2,1,0:T(8,128)(2,1)} %fusion.2), channel_id=1, source_target_pairs={{8,12},{9,13},{10,14},{11,15},{24,28},{25,29},{26,30},{27,31},{40,... | collective-permute-start | bytes 786440 | tf_op jit(solution)/shard_map/ppermute | solution.py:186
  42.7 5.1 %copy-start.8 = (s32[256]{0:T(256)S(1)}, s32[256]{0:T(256)}, u32[]{:S(2)}) copy-start(s32[256]{0:T(256)} %copy-done.7) | copy-start | bytes 3076
  42.7 5.3 %copy-start.10 = (f32[2,256]{1,0:T(2,128)S(1)}, f32[2,256]{1,0:T(2,128)}, u32[]{:S(2)}) copy-start(f32[2,256]{1,0:T(2,128)} %copy-done.9) | copy-start | bytes 6148
  42.7 5.4 %copy-start.12 = (f32[2,256]{1,0:T(2,128)S(1)}, f32[2,256]{1,0:T(2,128)}, u32[]{:S(2)}) copy-start(f32[2,256]{1,0:T(2,128)} %copy-done.11) | copy-start | bytes 6148
  42.7 5.4 %copy-start.14 = (f32[2,256]{1,0:T(2,128)S(1)}, f32[2,256]{1,0:T(2,128)}, u32[]{:S(2)}) copy-start(f32[2,256]{1,0:T(2,128)} %copy-done.13) | copy-start | bytes 6148
  42.7 5.4 %copy-start.15 = (f32[2,256]{1,0:T(2,128)S(1)}, f32[2,256]{1,0:T(2,128)}, u32[]{:S(2)}) copy-start(f32[2,256]{1,0:T(2,128)} %get-tuple-element.50) | copy-start | bytes 6148
  42.7 5.4 %copy-start.16 = (f32[2,256]{1,0:T(2,128)S(1)}, f32[2,256]{1,0:T(2,128)}, u32[]{:S(2)}) copy-start(f32[2,256]{1,0:T(2,128)} %get-tuple-element.51) | copy-start | bytes 6148
  42.7 5.4 %copy-start.17 = (f32[2,256]{1,0:T(2,128)S(1)}, f32[2,256]{1,0:T(2,128)}, u32[]{:S(2)}) copy-start(f32[2,256]{1,0:T(2,128)} %get-tuple-element.52) | copy-start | bytes 6148
  42.7 5.7 %copy-start.2 = (bf16[3,3,256,256]{2,3,1,0:T(8,128)(2,1)S(1)}, bf16[3,3,256,256]{2,3,1,0:T(8,128)(2,1)}, u32[]{:S(2)}) copy-start(bf16[3,3,256,256]{2,3,1,0:T(8,128)(2,1)} %rev.3) | copy-start | bytes 3538948
  51.8 0.7 collective-permute-start.4
  54.8 2.2 collective-permute-start.5
  55.4 23.6 %collective-permute-start.7 = (bf16[2,4,64,256]{3,2,1,0:T(8,128)(2,1)S(1)}, bf16[2,4,64,256]{3,2,1,0:T(8,128)(2,1)S(1)}, u32[]{:S(2)}, u32[]{:S(2)}) collective-permute-start(bf16[2,4,64,256]{3,2,1,0:T(8,128)(2,1)S(1)} %fusion.90), channel_id=1, source_target_pairs={{12,0},{13,1},{14,2},{15,3},{28,16},{29,17},{30,18},{31,19},{44,32... | collective-permute-start | bytes 786440 | tf_op jit(solution)/shard_map/ppermute | solution.py:211
  59.2 29.7 %collective-permute-start.6 = (bf16[2,4,64,256]{3,2,1,0:T(8,128)(2,1)S(1)}, bf16[2,4,64,256]{3,2,1,0:T(8,128)(2,1)}, u32[]{:S(2)}, u32[]{:S(2)}) collective-permute-start(bf16[2,4,64,256]{3,2,1,0:T(8,128)(2,1)S(1)} %fusion.96), channel_id=1, source_target_pairs={{4,0},{5,1},{6,2},{7,3},{20,16},{21,17},{22,18},{23,19},{36,32},{3... | collective-permute-start | bytes 786440 | tf_op jit(solution)/shard_map/ppermute | solution.py:202
  93.0 6.8 %copy-start.6 = (f32[2,128]{1,0:T(2,128)S(1)}, f32[2,128]{1,0:T(2,128)}, u32[]{:S(2)}) copy-start(f32[2,128]{1,0:T(2,128)} %copy-done.5) | copy-start | bytes 3076
  102.3 8.5 %collective-permute-start.8 = (f32[384,256]{1,0:T(8,128)S(1)}, f32[384,256]{1,0:T(8,128)S(1)}, u32[]{:S(2)}, u32[]{:S(2)}) collective-permute-start(f32[384,256]{1,0:T(8,128)S(1)} %constant_dynamic-slice_fusion.5), channel_id=1, source_target_pairs={{0,16},{16,0},{32,48},{48,32},{1,17},{17,1},{33,49},{49,33},{2,18}... | collective-permute-start | bytes 1179656 | tf_op jit(solution)/shard_map/ppermute | solution.py:243
  110.9 8.6 %collective-permute-start.9 = (f32[192,256]{1,0:T(8,128)S(1)}, f32[192,256]{1,0:T(8,128)S(1)}, u32[]{:S(2)}, u32[]{:S(2)}) collective-permute-start(f32[192,256]{1,0:T(8,128)S(1)} %constant_dynamic-slice_fusion.4), channel_id=1, source_target_pairs={{0,32},{16,48},{32,0},{48,16},{1,33},{17,49},{33,1},{49,17},{2,34}... | collective-permute-start | bytes 589832 | tf_op jit(solution)/shard_map/ppermute | solution.py:243
  119.5 5.4 %collective-permute-start.10 = (f32[96,256]{1,0:T(8,128)S(1)}, f32[96,256]{1,0:T(8,128)S(1)}, u32[]{:S(2)}, u32[]{:S(2)}) collective-permute-start(f32[96,256]{1,0:T(8,128)S(1)} %constant_dynamic-slice_fusion.3), channel_id=1, source_target_pairs={{0,64},{64,0},{128,192},{192,128},{256,320},{320,256},{384,448},{4... | collective-permute-start | bytes 294920 | tf_op jit(solution)/shard_map/ppermute | solution.py:243
  124.9 5.8 %collective-permute-start.11 = (f32[48,256]{1,0:T(8,128)S(1)}, f32[48,256]{1,0:T(8,128)S(1)}, u32[]{:S(2)}, u32[]{:S(2)}) collective-permute-start(f32[48,256]{1,0:T(8,128)S(1)} %constant_dynamic-slice_fusion.2), channel_id=1, source_target_pairs={{0,128},{64,192},{128,0},{192,64},{256,384},{320,448},{384,256},{4... | collective-permute-start | bytes 147464 | tf_op jit(solution)/shard_map/ppermute | solution.py:243
  130.8 9.0 %collective-permute-start.12 = (f32[24,256]{1,0:T(8,128)S(1)}, f32[24,256]{1,0:T(8,128)S(1)}, u32[]{:S(2)}, u32[]{:S(2)}) collective-permute-start(f32[24,256]{1,0:T(8,128)S(1)} %constant_dynamic-slice_fusion.1), channel_id=1, source_target_pairs={{0,256},{64,320},{128,384},{192,448},{256,0},{320,64},{384,128},{4... | collective-permute-start | bytes 73736 | tf_op jit(solution)/shard_map/ppermute | solution.py:243
  139.8 8.7 %collective-permute-start.13 = (f32[24,256]{1,0:T(8,128)S(1)}, f32[24,256]{1,0:T(8,128)S(1)}, u32[]{:S(2)}, u32[]{:S(2)}) collective-permute-start(f32[24,256]{1,0:T(8,128)S(1)} %dynamic-slice_add_fusion.4), channel_id=1, source_target_pairs={{0,256},{64,320},{128,384},{192,448},{256,0},{320,64},{384,128},{4... | collective-permute-start | bytes 73736 | tf_op jit(solution)/shard_map/ppermute | solution.py:253
  148.5 5.8 %collective-permute-start.14 = (f32[48,256]{1,0:T(8,128)S(1)}, f32[48,256]{1,0:T(8,128)S(1)}, u32[]{:S(2)}, u32[]{:S(2)}) collective-permute-start(f32[48,256]{1,0:T(8,128)S(1)} %maximum_select_fusion.6), channel_id=1, source_target_pairs={{0,128},{64,192},{128,0},{192,64},{256,384},{320,448},{384,256},{4... | collective-permute-start | bytes 147464 | tf_op jit(solution)/shard_map/ppermute | solution.py:253
  154.3 5.6 %collective-permute-start.15 = (f32[96,256]{1,0:T(8,128)S(1)}, f32[96,256]{1,0:T(8,128)S(1)}, u32[]{:S(2)}, u32[]{:S(2)}) collective-permute-start(f32[96,256]{1,0:T(8,128)S(1)} %maximum_select_fusion.5), channel_id=1, source_target_pairs={{0,64},{64,0},{128,192},{192,128},{256,320},{320,256},{384,448},{4... | collective-permute-start | bytes 294920 | tf_op jit(solution)/shard_map/ppermute | solution.py:253
  160.0 7.9 %collective-permute-start.16 = (f32[192,256]{1,0:T(8,128)S(1)}, f32[192,256]{1,0:T(8,128)S(1)}, u32[]{:S(2)}, u32[]{:S(2)}) collective-permute-start(f32[192,256]{1,0:T(8,128)S(1)} %maximum_select_fusion.4), channel_id=1, source_target_pairs={{0,32},{16,48},{32,0},{48,16},{1,33},{17,49},{33,1},{49,17},{2,34}... | collective-permute-start | bytes 589832 | tf_op jit(solution)/shard_map/ppermute | solution.py:253
  167.9 8.5 %collective-permute-start.17 = (f32[384,256]{1,0:T(8,128)S(1)}, f32[384,256]{1,0:T(8,128)S(1)}, u32[]{:S(2)}, u32[]{:S(2)}) collective-permute-start(f32[384,256]{1,0:T(8,128)S(1)} %maximum_select_fusion.3), channel_id=1, source_target_pairs={{0,16},{16,0},{32,48},{48,32},{1,17},{17,1},{33,49},{49,33},{2,18}... | collective-permute-start | bytes 1179656 | tf_op jit(solution)/shard_map/ppermute | solution.py:253
  176.5 19.1 %collective-permute-start.18 = (f32[768,256]{1,0:T(8,128)S(1)}, f32[768,256]{1,0:T(8,128)S(1)}, u32[]{:S(2)}, u32[]{:S(2)}) collective-permute-start(f32[768,256]{1,0:T(8,128)S(1)} %maximum_select_fusion.2), channel_id=1, source_target_pairs={{0,2},{1,3},{2,0},{3,1},{4,6},{5,7},{6,4},{7,5},{8,10},{9,11},{10,... | collective-permute-start | bytes 2359304 | tf_op jit(solution)/shard_map/ppermute | solution.py:253
  195.8 20.4 %collective-permute-start.19 = (f32[1536,256]{1,0:T(8,128)S(1)}, f32[1536,256]{1,0:T(8,128)S(1)}, u32[]{:S(2)}, u32[]{:S(2)}) collective-permute-start(f32[1536,256]{1,0:T(8,128)S(1)} %maximum_select_fusion.1), channel_id=1, source_target_pairs={{0,1},{1,0},{2,3},{3,2},{4,5},{5,4},{6,7},{7,6},{8,9},{9,8},{10,11... | collective-permute-start | bytes 4718600 | tf_op jit(solution)/shard_map/ppermute | solution.py:253
  (6 other events, 10.4 us)

commit v6 on v4

--- a/solution.py
+++ b/solution.py
@@ -277,11 +277,12 @@
     flat = jnp.concatenate(parts, axis=0)
     for axis in ("dx", "dy"):
         flat = butterfly_scatter(flat, axis)
+    flat = flat.astype(jnp.bfloat16)
     for axis in ("dy", "dx"):
         flat = butterfly_gather(flat, axis, descending(lax.axis_size(axis)))
     space_count = lax.axis_size("space")
     flat = butterfly_gather(flat, "space", descending(space_count))
-    flat = flat.reshape(space_count, padded_rows, channels)
+    flat = flat.reshape(space_count, padded_rows, channels).astype(jnp.float32)
     weight_rows = weight_grad.shape[0]
     emb_rows = emb_grad.size // channels
     conv = flat[:, :weight_rows].reshape(1, 3, 3, channels, channels)

time: 213 us -> 210 us (0.986)
  waiting for transfers between devices: 62.8 us -> 57 us
  local copies, waits for them, and re-layouts: 16.8 us -> 13.7 us
  matrix products: 17.8 us -> 20.2 us
  other arithmetic: 6.47 us -> 8.79 us
    ppermute x7, waiting for transfers between devices: 27.7 us -> 18 us  [butterfly_gather(): got = lax.ppermute(flat, axis, [(j, j ^ step) for j in range(count)])]
    unnamed x88 -> x124, local copies, waits for them, and re-layouts: 11.3 us -> 7.55 us
    ppermute x1, waiting for transfers between devices: 10.9 us -> 14.4 us  [per_device(): skip_grad = lax.ppermute(d_input, 'section', [(last, 0)])]
  transfers between devices with their start and end apart: 20 -> 20, of which waited for: 14 -> 14; matrix products, arithmetic and copies ran while one was open for 8% -> 7% of each run, Pallas kernels for 0% -> 0%
where the time goes in v6:
time: 210 us; the launch traced here: 209 us
  starting transfers between devices  84.6 us (40%)
  waiting for transfers between devices  57 us (27%)
  blocking collectives  22.3 us (11%)
  matrix products  20.2 us (10%)
  local copies, waits for them, and re-layouts  13.7 us (7%)
  other arithmetic  8.79 us (4%)
  between operations  2.21 us (1%)
    ppermute x7, starting transfers between devices, butterfly_gather(): got = lax.ppermute(flat, axis, [(j, j ^ step) for j in range(count)])  49 us
    ppermute x5, starting transfers between devices, butterfly_scatter(): lax.ppermute(sent, axis, [(j, j ^ step) for j in range(count)])  22.9 us
    ppermute x7, waiting for transfers between devices, butterfly_gather(): got = lax.ppermute(flat, axis, [(j, j ^ step) for j in range(count)])  18 us
    ppermute x5, waiting for transfers between devices, butterfly_scatter(): lax.ppermute(sent, axis, [(j, j ^ step) for j in range(count)])  14.6 us
    ppermute x1, waiting for transfers between devices, per_device(): skip_grad = lax.ppermute(d_input, 'section', [(last, 0)])  14.4 us
    all_gather x1, blocking collectives, per_device(): images = lax.all_gather(images, 'space', axis=1, tiled=True)  12.8 us
    dot_general x7, matrix products, convolve(): jnp.dot(flat, matrix, preferred_element_type=jnp.float32)  11.6 us
    ppermute x3, waiting for transfers between devices, per_device(): upstream = lax.ppermute(carried, 'section', [(active + 1, active)])  9.97 us
  transfers between devices with their start and end apart: 20, of which 14 were waited for; matrix products, arithmetic and copies ran while one was open for 7% of the time, Pallas kernels for 0%

profile of v6, /device:TPU:1, one launch (start us, length us, event | category | flops | bytes accessed | tf_op | source)
XLA Modules:
  0.0 208.8 jit_solution(10930628819896615592)
XLA Ops:
  0.7 12.8 %all_gather.6 = bf16[2,4,64,256]{3,2,1,0:T(8,128)(2,1)S(1)} all-gather(bf16[2,1,64,256]{3,2,1,0:T(8,128)(2,1)} %param.6), channel_id=1, replica_groups=mesh['dy'=8,'dx'=4,'section'=4,'space'=4] {'space'}, dimensions={1}, use_global_device_ids=true | all-gather | bytes 327680 | tf_op jit(solution)/shard_map/all_gather | solution.py:165
  19.4 5.3 %collective-permute-start.3 = (bf16[2,4,64,256]{3,2,1,0:T(8,128)(2,1)}, bf16[2,4,64,256]{3,2,1,0:T(8,128)(2,1)S(1)}, u32[]{:S(2)}, u32[]{:S(2)}) collective-permute-start(bf16[2,4,64,256]{3,2,1,0:T(8,128)(2,1)} %fusion), channel_id=1, source_target_pairs={{0,12},{1,13},{2,14},{3,15},{16,28},{17,29},{18,30},{19,31},{32,44... | collective-permute-start | bytes 786440 | tf_op jit(solution)/shard_map/ppermute | solution.py:190
  26.0 9.4 %all_gather.7 = bf16[2,4,64,256]{3,2,1,0:T(8,128)(2,1)S(1)} all-gather(bf16[2,1,64,256]{3,2,1,0:T(8,128)(2,1)S(1)} %copy-done.6), channel_id=1, replica_groups=mesh['dy'=8,'dx'=4,'section'=4,'space'=4] {'space'}, dimensions={1}, use_global_device_ids=true | all-gather | bytes 327680 | tf_op jit(solution)/shard_map/all_gather | solution.py:166
  45.7 1.6 copy.9
  51.9 1.7 divide_multiply_fusion
  53.7 3.3 %fusion.60 = (f32[2,256]{1,0:T(2,128)}, f32[256]{0:T(256)}, f32[2,256]{1,0:T(2,128)S(1)}, f32[2,256]{1,0:T(2,128)S(1)}, f32[2,256]{1,0:T(2,128)}, /*index=5*/f32[2,4,64,256]{3,2,1,0:T(8,128)S(1)}) fusion(bf16[2,4,64,256]{3,2,1,0:T(8,128)(2,1)S(1)} %select_select_fusion.1, f32[2,256]{1,0:T(2,128)S(1)} %rsqrt.26, f32[2,256]{1,0:T(2,128)S(1)} %get-tuple-element.33, ...), kind=kOutput, calls=%fused_computation.138 | convolution fusion | flops 607254272 | bytes 4343808 | tf_op jit(solution)/shard_map/dot_general | solution.py:74
  59.6 1.7 fusion.59
  64.6 1.7 fusion.58
  69.0 14.4 %collective-permute-done.7 = bf16[2,4,64,256]{3,2,1,0:T(8,128)(2,1)} collective-permute-done((bf16[2,4,64,256]{3,2,1,0:T(8,128)(2,1)}, bf16[2,4,64,256]{3,2,1,0:T(8,128)(2,1)}, u32[]{:S(2)}, u32[]{:S(2)}) %collective-permute-start.7) | collective-permute-done | bytes 262176 | tf_op jit(solution)/shard_map/ppermute | solution.py:210
  83.4 10.0 %collective-permute-done.6 = bf16[2,4,64,256]{3,2,1,0:T(8,128)(2,1)} collective-permute-done((bf16[2,4,64,256]{3,2,1,0:T(8,128)(2,1)S(1)}, bf16[2,4,64,256]{3,2,1,0:T(8,128)(2,1)}, u32[]{:S(2)}, u32[]{:S(2)}) %collective-permute-start.6) | collective-permute-done | bytes 262176 | tf_op jit(solution)/shard_map/ppermute | solution.py:201
  99.4 3.1 %collective-permute-start.8 = (f32[384,256]{1,0:T(8,128)S(1)}, f32[384,256]{1,0:T(8,128)S(1)}, u32[]{:S(2)}, u32[]{:S(2)}) collective-permute-start(f32[384,256]{1,0:T(8,128)S(1)} %constant_dynamic-slice_fusion.5), channel_id=1, source_target_pairs={{0,16},{16,0},{32,48},{48,32},{1,17},{17,1},{33,49},{49,33},{2,18}... | collective-permute-start | bytes 1179656 | tf_op jit(solution)/shard_map/ppermute | solution.py:242
  102.6 5.4 %collective-permute-done.8 = f32[384,256]{1,0:T(8,128)S(1)} collective-permute-done((f32[384,256]{1,0:T(8,128)S(1)}, f32[384,256]{1,0:T(8,128)S(1)}, u32[]{:S(2)}, u32[]{:S(2)}) %collective-permute-start.8) | collective-permute-done | bytes 393248 | tf_op jit(solution)/shard_map/ppermute | solution.py:242
  108.0 4.6 %collective-permute-start.9 = (f32[192,256]{1,0:T(8,128)S(1)}, f32[192,256]{1,0:T(8,128)S(1)}, u32[]{:S(2)}, u32[]{:S(2)}) collective-permute-start(f32[192,256]{1,0:T(8,128)S(1)} %constant_dynamic-slice_fusion.4), channel_id=1, source_target_pairs={{0,32},{16,48},{32,0},{48,16},{1,33},{17,49},{33,1},{49,17},{2,34}... | collective-permute-start | bytes 589832 | tf_op jit(solution)/shard_map/ppermute | solution.py:242
  112.7 4.4 %collective-permute-done.9 = f32[192,256]{1,0:T(8,128)S(1)} collective-permute-done((f32[192,256]{1,0:T(8,128)S(1)}, f32[192,256]{1,0:T(8,128)S(1)}, u32[]{:S(2)}, u32[]{:S(2)}) %collective-permute-start.9) | collective-permute-done | bytes 196640 | tf_op jit(solution)/shard_map/ppermute | solution.py:242
  117.1 3.2 %collective-permute-start.10 = (f32[96,256]{1,0:T(8,128)S(1)}, f32[96,256]{1,0:T(8,128)S(1)}, u32[]{:S(2)}, u32[]{:S(2)}) collective-permute-start(f32[96,256]{1,0:T(8,128)S(1)} %constant_dynamic-slice_fusion.3), channel_id=1, source_target_pairs={{0,64},{64,0},{128,192},{192,128},{256,320},{320,256},{384,448},{4... | collective-permute-start | bytes 294920 | tf_op jit(solution)/shard_map/ppermute | solution.py:242
  120.4 2.1 %collective-permute-done.10 = f32[96,256]{1,0:T(8,128)S(1)} collective-permute-done((f32[96,256]{1,0:T(8,128)S(1)}, f32[96,256]{1,0:T(8,128)S(1)}, u32[]{:S(2)}, u32[]{:S(2)}) %collective-permute-start.10) | collective-permute-done | bytes 98336 | tf_op jit(solution)/shard_map/ppermute | solution.py:242
  122.5 4.2 %collective-permute-start.11 = (f32[48,256]{1,0:T(8,128)S(1)}, f32[48,256]{1,0:T(8,128)S(1)}, u32[]{:S(2)}, u32[]{:S(2)}) collective-permute-start(f32[48,256]{1,0:T(8,128)S(1)} %constant_dynamic-slice_fusion.2), channel_id=1, source_target_pairs={{0,128},{64,192},{128,0},{192,64},{256,384},{320,448},{384,256},{4... | collective-permute-start | bytes 147464 | tf_op jit(solution)/shard_map/ppermute | solution.py:242
  126.8 1.6 collective-permute-done.11
  128.4 7.8 %collective-permute-start.12 = (f32[24,256]{1,0:T(8,128)S(1)}, f32[24,256]{1,0:T(8,128)S(1)}, u32[]{:S(2)}, u32[]{:S(2)}) collective-permute-start(f32[24,256]{1,0:T(8,128)S(1)} %constant_dynamic-slice_fusion.1), channel_id=1, source_target_pairs={{0,256},{64,320},{128,384},{192,448},{256,0},{320,64},{384,128},{4... | collective-permute-start | bytes 73736 | tf_op jit(solution)/shard_map/ppermute | solution.py:242
  137.4 7.5 %collective-permute-start.13 = (bf16[24,256]{1,0:T(8,128)(2,1)S(1)}, bf16[24,256]{1,0:T(8,128)(2,1)S(1)}, u32[]{:S(2)}, u32[]{:S(2)}) collective-permute-start(bf16[24,256]{1,0:T(8,128)(2,1)S(1)} %add_convert_fusion.2), channel_id=1, source_target_pairs={{0,256},{64,320},{128,384},{192,448},{256,0},{320,64},{384,128},{4... | collective-permute-start | bytes 36872 | tf_op jit(solution)/shard_map/ppermute | solution.py:252
  146.0 4.1 %collective-permute-start.14 = (bf16[48,256]{1,0:T(8,128)(2,1)S(1)}, bf16[48,256]{1,0:T(8,128)(2,1)S(1)}, u32[]{:S(2)}, u32[]{:S(2)}) collective-permute-start(bf16[48,256]{1,0:T(8,128)(2,1)S(1)} %maximum_select_fusion.6), channel_id=1, source_target_pairs={{0,128},{64,192},{128,0},{192,64},{256,384},{320,448},{384,256},{4... | collective-permute-start | bytes 73736 | tf_op jit(solution)/shard_map/ppermute | solution.py:252
  151.5 3.1 %collective-permute-start.15 = (bf16[96,256]{1,0:T(8,128)(2,1)S(1)}, bf16[96,256]{1,0:T(8,128)(2,1)S(1)}, u32[]{:S(2)}, u32[]{:S(2)}) collective-permute-start(bf16[96,256]{1,0:T(8,128)(2,1)S(1)} %maximum_select_fusion.5), channel_id=1, source_target_pairs={{0,64},{64,0},{128,192},{192,128},{256,320},{320,256},{384,448},{4... | collective-permute-start | bytes 147464 | tf_op jit(solution)/shard_map/ppermute | solution.py:252
  154.6 1.7 collective-permute-done.15
  156.4 4.0 %collective-permute-start.16 = (bf16[192,256]{1,0:T(8,128)(2,1)S(1)}, bf16[192,256]{1,0:T(8,128)(2,1)S(1)}, u32[]{:S(2)}, u32[]{:S(2)}) collective-permute-start(bf16[192,256]{1,0:T(8,128)(2,1)S(1)} %maximum_select_fusion.4), channel_id=1, source_target_pairs={{0,32},{16,48},{32,0},{48,16},{1,33},{17,49},{33,1},{49,17},{2,34}... | collective-permute-start | bytes 294920 | tf_op jit(solution)/shard_map/ppermute | solution.py:252
  160.4 2.8 %collective-permute-done.16 = bf16[192,256]{1,0:T(8,128)(2,1)S(1)} collective-permute-done((bf16[192,256]{1,0:T(8,128)(2,1)S(1)}, bf16[192,256]{1,0:T(8,128)(2,1)S(1)}, u32[]{:S(2)}, u32[]{:S(2)}) %collective-permute-start.16) | collective-permute-done | bytes 98336 | tf_op jit(solution)/shard_map/ppermute | solution.py:252
  163.3 2.5 %collective-permute-start.17 = (bf16[384,256]{1,0:T(8,128)(2,1)S(1)}, bf16[384,256]{1,0:T(8,128)(2,1)S(1)}, u32[]{:S(2)}, u32[]{:S(2)}) collective-permute-start(bf16[384,256]{1,0:T(8,128)(2,1)S(1)} %maximum_select_fusion.3), channel_id=1, source_target_pairs={{0,16},{16,0},{32,48},{48,32},{1,17},{17,1},{33,49},{49,33},{2,18}... | collective-permute-start | bytes 589832 | tf_op jit(solution)/shard_map/ppermute | solution.py:252
  165.8 3.9 %collective-permute-done.17 = bf16[384,256]{1,0:T(8,128)(2,1)S(1)} collective-permute-done((bf16[384,256]{1,0:T(8,128)(2,1)S(1)}, bf16[384,256]{1,0:T(8,128)(2,1)S(1)}, u32[]{:S(2)}, u32[]{:S(2)}) %collective-permute-start.17) | collective-permute-done | bytes 196640 | tf_op jit(solution)/shard_map/ppermute | solution.py:252
  169.9 10.3 %collective-permute-start.18 = (bf16[768,256]{1,0:T(8,128)(2,1)S(1)}, bf16[768,256]{1,0:T(8,128)(2,1)S(1)}, u32[]{:S(2)}, u32[]{:S(2)}) collective-permute-start(bf16[768,256]{1,0:T(8,128)(2,1)S(1)} %maximum_select_fusion.2), channel_id=1, source_target_pairs={{0,2},{1,3},{2,0},{3,1},{4,6},{5,7},{6,4},{7,5},{8,10},{9,11},{10,... | collective-permute-start | bytes 1179656 | tf_op jit(solution)/shard_map/ppermute | solution.py:252
  180.2 5.1 %collective-permute-done.18 = bf16[768,256]{1,0:T(8,128)(2,1)S(1)} collective-permute-done((bf16[768,256]{1,0:T(8,128)(2,1)S(1)}, bf16[768,256]{1,0:T(8,128)(2,1)S(1)}, u32[]{:S(2)}, u32[]{:S(2)}) %collective-permute-start.18) | collective-permute-done | bytes 393248 | tf_op jit(solution)/shard_map/ppermute | solution.py:252
  185.6 17.5 %collective-permute-start.19 = (bf16[1536,256]{1,0:T(8,128)(2,1)S(1)}, bf16[1536,256]{1,0:T(8,128)(2,1)S(1)}, u32[]{:S(2)}, u32[]{:S(2)}) collective-permute-start(bf16[1536,256]{1,0:T(8,128)(2,1)S(1)} %maximum_select_fusion.1), channel_id=1, source_target_pairs={{0,1},{1,0},{2,3},{3,2},{4,5},{5,4},{6,7},{7,6},{8,9},{9,8},{10,11... | collective-permute-start | bytes 2359304 | tf_op jit(solution)/shard_map/ppermute | solution.py:252
  203.1 1.9 collective-permute-done.19
  205.4 1.6 slice.298
  (217 shorter events, 42.4 us)
Async XLA Ops:
  0.6 13.7 %copy-start = (bf16[1,256,512]{2,1,0:T(8,128)(2,1)S(1)}, bf16[1,256,512]{2,1,0:T(8,128)(2,1)}, u32[]{:S(2)}) copy-start(bf16[1,256,512]{2,1,0:T(8,128)(2,1)} %param.11) | copy-start | bytes 786436
  0.6 16.2 %copy-start.5 = (f32[1,256]{1,0:T(1,128)S(1)}, f32[1,256]{1,0:T(1,128)}, u32[]{:S(2)}) copy-start(f32[1,256]{1,0:T(1,128)} %param.10) | copy-start | bytes 3076
  0.7 38.9 %copy-start.22 = (s32[256]{0:T(256)}, s32[256]{0:T(256)S(1)}, u32[]{:S(2)}) copy-start(s32[256]{0:T(256)S(1)} %and_select_fusion) | copy-start | bytes 3076
  14.3 1.4 copy-start.9
  14.3 1.4 copy-start.11
  17.3 8.7 %copy-start.6 = (bf16[2,1,64,256]{3,2,1,0:T(8,128)(2,1)S(1)}, bf16[2,1,64,256]{3,2,1,0:T(8,128)(2,1)}, u32[]{:S(2)}) copy-start(bf16[2,1,64,256]{3,2,1,0:T(8,128)(2,1)} %param.8) | copy-start | bytes 196612
  19.4 30.4 %collective-permute-start.3 = (bf16[2,4,64,256]{3,2,1,0:T(8,128)(2,1)}, bf16[2,4,64,256]{3,2,1,0:T(8,128)(2,1)S(1)}, u32[]{:S(2)}, u32[]{:S(2)}) collective-permute-start(bf16[2,4,64,256]{3,2,1,0:T(8,128)(2,1)} %fusion), channel_id=1, source_target_pairs={{0,12},{1,13},{2,14},{3,15},{16,28},{17,29},{18,30},{19,31},{32,44... | collective-permute-start | bytes 786440 | tf_op jit(solution)/shard_map/ppermute | solution.py:190
  24.7 10.9 %collective-permute-start = (bf16[2,4,64,256]{3,2,1,0:T(8,128)(2,1)}, bf16[2,4,64,256]{3,2,1,0:T(8,128)(2,1)S(1)}, u32[]{:S(2)}, u32[]{:S(2)}) collective-permute-start(bf16[2,4,64,256]{3,2,1,0:T(8,128)(2,1)} %fusion), channel_id=1, source_target_pairs={{0,4},{1,5},{2,6},{3,7},{16,20},{17,21},{18,22},{19,23},{32,36},{3... | collective-permute-start | bytes 786440 | tf_op jit(solution)/shard_map/ppermute | solution.py:185
  35.9 1.7 copy-start.25
  38.5 0.9 collective-permute-start.1
  42.9 7.0 %collective-permute-start.2 = (bf16[2,4,64,256]{3,2,1,0:T(8,128)(2,1)}, bf16[2,4,64,256]{3,2,1,0:T(8,128)(2,1)}, u32[]{:S(2)}, u32[]{:S(2)}) collective-permute-start(bf16[2,4,64,256]{3,2,1,0:T(8,128)(2,1)} %fusion.2), channel_id=1, source_target_pairs={{8,12},{9,13},{10,14},{11,15},{24,28},{25,29},{26,30},{27,31},{40,... | collective-permute-start | bytes 786440 | tf_op jit(solution)/shard_map/ppermute | solution.py:185
  44.3 1.4 copy-start.7
  48.4 5.3 %copy-start.2 = (bf16[3,3,256,256]{2,3,1,0:T(8,128)(2,1)S(1)}, bf16[3,3,256,256]{2,3,1,0:T(8,128)(2,1)}, u32[]{:S(2)}) copy-start(bf16[3,3,256,256]{2,3,1,0:T(8,128)(2,1)} %rev.3) | copy-start | bytes 3538948
  50.9 2.7 %copy-start.3 = (bf16[2,4,64,256]{3,2,1,0:T(8,128)(2,1)}, bf16[2,4,64,256]{3,2,1,0:T(8,128)(2,1)S(1)}, u32[]{:S(2)}) copy-start(bf16[2,4,64,256]{3,2,1,0:T(8,128)(2,1)S(1)} %get-tuple-element.34) | copy-start | bytes 786436
  53.6 12.9 %copy-start.27 = (f32[2,256]{1,0:T(2,128)}, f32[2,256]{1,0:T(2,128)S(1)}, u32[]{:S(2)}) copy-start(f32[2,256]{1,0:T(2,128)S(1)} %get-tuple-element.33) | copy-start | bytes 6148
  53.7 3.3 %copy-start.23 = (s32[256]{0:T(256)S(1)}, s32[256]{0:T(256)}, u32[]{:S(2)}) copy-start(s32[256]{0:T(256)} %copy-done.22) | copy-start | bytes 3076
  58.4 0.7 collective-permute-start.4
  62.0 2.2 %collective-permute-start.5 = (bf16[2,4,64,256]{3,2,1,0:T(8,128)(2,1)S(1)}, bf16[2,4,64,256]{3,2,1,0:T(8,128)(2,1)S(1)}, u32[]{:S(2)}, u32[]{:S(2)}) collective-permute-start(bf16[2,4,64,256]{3,2,1,0:T(8,128)(2,1)S(1)} %fusion.93), channel_id=1, source_target_pairs={{8,4},{9,5},{10,6},{11,7},{24,20},{25,21},{26,22},{27,23},{40,36},... | collective-permute-start | bytes 786440 | tf_op jit(solution)/shard_map/ppermute | solution.py:201
  62.7 20.8 %collective-permute-start.7 = (bf16[2,4,64,256]{3,2,1,0:T(8,128)(2,1)}, bf16[2,4,64,256]{3,2,1,0:T(8,128)(2,1)}, u32[]{:S(2)}, u32[]{:S(2)}) collective-permute-start(bf16[2,4,64,256]{3,2,1,0:T(8,128)(2,1)} %fusion.90), channel_id=1, source_target_pairs={{12,0},{13,1},{14,2},{15,3},{28,16},{29,17},{30,18},{31,19},{44,32... | collective-permute-start | bytes 786440 | tf_op jit(solution)/shard_map/ppermute | solution.py:210
  67.0 26.4 %collective-permute-start.6 = (bf16[2,4,64,256]{3,2,1,0:T(8,128)(2,1)S(1)}, bf16[2,4,64,256]{3,2,1,0:T(8,128)(2,1)}, u32[]{:S(2)}, u32[]{:S(2)}) collective-permute-start(bf16[2,4,64,256]{3,2,1,0:T(8,128)(2,1)S(1)} %fusion.96), channel_id=1, source_target_pairs={{4,0},{5,1},{6,2},{7,3},{20,16},{21,17},{22,18},{23,19},{36,32},{3... | collective-permute-start | bytes 786440 | tf_op jit(solution)/shard_map/ppermute | solution.py:201
  99.4 8.5 %collective-permute-start.8 = (f32[384,256]{1,0:T(8,128)S(1)}, f32[384,256]{1,0:T(8,128)S(1)}, u32[]{:S(2)}, u32[]{:S(2)}) collective-permute-start(f32[384,256]{1,0:T(8,128)S(1)} %constant_dynamic-slice_fusion.5), channel_id=1, source_target_pairs={{0,16},{16,0},{32,48},{48,32},{1,17},{17,1},{33,49},{49,33},{2,18}... | collective-permute-start | bytes 1179656 | tf_op jit(solution)/shard_map/ppermute | solution.py:242
  108.0 9.1 %collective-permute-start.9 = (f32[192,256]{1,0:T(8,128)S(1)}, f32[192,256]{1,0:T(8,128)S(1)}, u32[]{:S(2)}, u32[]{:S(2)}) collective-permute-start(f32[192,256]{1,0:T(8,128)S(1)} %constant_dynamic-slice_fusion.4), channel_id=1, source_target_pairs={{0,32},{16,48},{32,0},{48,16},{1,33},{17,49},{33,1},{49,17},{2,34}... | collective-permute-start | bytes 589832 | tf_op jit(solution)/shard_map/ppermute | solution.py:242
  117.1 5.4 %collective-permute-start.10 = (f32[96,256]{1,0:T(8,128)S(1)}, f32[96,256]{1,0:T(8,128)S(1)}, u32[]{:S(2)}, u32[]{:S(2)}) collective-permute-start(f32[96,256]{1,0:T(8,128)S(1)} %constant_dynamic-slice_fusion.3), channel_id=1, source_target_pairs={{0,64},{64,0},{128,192},{192,128},{256,320},{320,256},{384,448},{4... | collective-permute-start | bytes 294920 | tf_op jit(solution)/shard_map/ppermute | solution.py:242
  122.5 5.8 %collective-permute-start.11 = (f32[48,256]{1,0:T(8,128)S(1)}, f32[48,256]{1,0:T(8,128)S(1)}, u32[]{:S(2)}, u32[]{:S(2)}) collective-permute-start(f32[48,256]{1,0:T(8,128)S(1)} %constant_dynamic-slice_fusion.2), channel_id=1, source_target_pairs={{0,128},{64,192},{128,0},{192,64},{256,384},{320,448},{384,256},{4... | collective-permute-start | bytes 147464 | tf_op jit(solution)/shard_map/ppermute | solution.py:242
  128.4 9.0 %collective-permute-start.12 = (f32[24,256]{1,0:T(8,128)S(1)}, f32[24,256]{1,0:T(8,128)S(1)}, u32[]{:S(2)}, u32[]{:S(2)}) collective-permute-start(f32[24,256]{1,0:T(8,128)S(1)} %constant_dynamic-slice_fusion.1), channel_id=1, source_target_pairs={{0,256},{64,320},{128,384},{192,448},{256,0},{320,64},{384,128},{4... | collective-permute-start | bytes 73736 | tf_op jit(solution)/shard_map/ppermute | solution.py:242
  137.4 8.6 %collective-permute-start.13 = (bf16[24,256]{1,0:T(8,128)(2,1)S(1)}, bf16[24,256]{1,0:T(8,128)(2,1)S(1)}, u32[]{:S(2)}, u32[]{:S(2)}) collective-permute-start(bf16[24,256]{1,0:T(8,128)(2,1)S(1)} %add_convert_fusion.2), channel_id=1, source_target_pairs={{0,256},{64,320},{128,384},{192,448},{256,0},{320,64},{384,128},{4... | collective-permute-start | bytes 36872 | tf_op jit(solution)/shard_map/ppermute | solution.py:252
  146.0 5.5 %collective-permute-start.14 = (bf16[48,256]{1,0:T(8,128)(2,1)S(1)}, bf16[48,256]{1,0:T(8,128)(2,1)S(1)}, u32[]{:S(2)}, u32[]{:S(2)}) collective-permute-start(bf16[48,256]{1,0:T(8,128)(2,1)S(1)} %maximum_select_fusion.6), channel_id=1, source_target_pairs={{0,128},{64,192},{128,0},{192,64},{256,384},{320,448},{384,256},{4... | collective-permute-start | bytes 73736 | tf_op jit(solution)/shard_map/ppermute | solution.py:252
  151.5 4.8 %collective-permute-start.15 = (bf16[96,256]{1,0:T(8,128)(2,1)S(1)}, bf16[96,256]{1,0:T(8,128)(2,1)S(1)}, u32[]{:S(2)}, u32[]{:S(2)}) collective-permute-start(bf16[96,256]{1,0:T(8,128)(2,1)S(1)} %maximum_select_fusion.5), channel_id=1, source_target_pairs={{0,64},{64,0},{128,192},{192,128},{256,320},{320,256},{384,448},{4... | collective-permute-start | bytes 147464 | tf_op jit(solution)/shard_map/ppermute | solution.py:252
  156.4 6.9 %collective-permute-start.16 = (bf16[192,256]{1,0:T(8,128)(2,1)S(1)}, bf16[192,256]{1,0:T(8,128)(2,1)S(1)}, u32[]{:S(2)}, u32[]{:S(2)}) collective-permute-start(bf16[192,256]{1,0:T(8,128)(2,1)S(1)} %maximum_select_fusion.4), channel_id=1, source_target_pairs={{0,32},{16,48},{32,0},{48,16},{1,33},{17,49},{33,1},{49,17},{2,34}... | collective-permute-start | bytes 294920 | tf_op jit(solution)/shard_map/ppermute | solution.py:252
  163.3 6.4 %collective-permute-start.17 = (bf16[384,256]{1,0:T(8,128)(2,1)S(1)}, bf16[384,256]{1,0:T(8,128)(2,1)S(1)}, u32[]{:S(2)}, u32[]{:S(2)}) collective-permute-start(bf16[384,256]{1,0:T(8,128)(2,1)S(1)} %maximum_select_fusion.3), channel_id=1, source_target_pairs={{0,16},{16,0},{32,48},{48,32},{1,17},{17,1},{33,49},{49,33},{2,18}... | collective-permute-start | bytes 589832 | tf_op jit(solution)/shard_map/ppermute | solution.py:252
  169.9 15.4 %collective-permute-start.18 = (bf16[768,256]{1,0:T(8,128)(2,1)S(1)}, bf16[768,256]{1,0:T(8,128)(2,1)S(1)}, u32[]{:S(2)}, u32[]{:S(2)}) collective-permute-start(bf16[768,256]{1,0:T(8,128)(2,1)S(1)} %maximum_select_fusion.2), channel_id=1, source_target_pairs={{0,2},{1,3},{2,0},{3,1},{4,6},{5,7},{6,4},{7,5},{8,10},{9,11},{10,... | collective-permute-start | bytes 1179656 | tf_op jit(solution)/shard_map/ppermute | solution.py:252
  185.6 19.4 %collective-permute-start.19 = (bf16[1536,256]{1,0:T(8,128)(2,1)S(1)}, bf16[1536,256]{1,0:T(8,128)(2,1)S(1)}, u32[]{:S(2)}, u32[]{:S(2)}) collective-permute-start(bf16[1536,256]{1,0:T(8,128)(2,1)S(1)} %maximum_select_fusion.1), channel_id=1, source_target_pairs={{0,1},{1,0},{2,3},{3,2},{4,5},{5,4},{6,7},{7,6},{8,9},{9,8},{10,11... | collective-permute-start | bytes 2359304 | tf_op jit(solution)/shard_map/ppermute | solution.py:252
  (19 other events, 21.1 us)

commit v7 on v6

--- a/solution.py
+++ b/solution.py
@@ -244,6 +244,15 @@
     return flat
 
 
+def butterfly_sum(flat, axis):
+    count = lax.axis_size(axis)
+    step = 1
+    while step < count:
+        flat = flat + lax.ppermute(flat, axis, [(j, j ^ step) for j in range(count)])
+        step *= 2
+    return flat
+
+
 def butterfly_gather(flat, axis, steps):
     count = lax.axis_size(axis)
     index = lax.axis_index(axis)
@@ -271,15 +280,13 @@
     channels = gain_grad.shape[0]
     parts = [weight_grad, emb_grad.reshape(-1, channels), gain_grad[None]]
     rows = sum(part.shape[0] for part in parts)
-    devices = lax.axis_size("dx") * lax.axis_size("dy")
+    devices = lax.axis_size("dx")
     padded_rows = -(-rows // (8 * devices)) * 8 * devices
     parts.append(jnp.zeros((padded_rows - rows, channels), jnp.float32))
     flat = jnp.concatenate(parts, axis=0)
-    for axis in ("dx", "dy"):
-        flat = butterfly_scatter(flat, axis)
-    flat = flat.astype(jnp.bfloat16)
-    for axis in ("dy", "dx"):
-        flat = butterfly_gather(flat, axis, descending(lax.axis_size(axis)))
+    flat = butterfly_scatter(flat, "dx")
+    flat = butterfly_sum(flat, "dy")
+    flat = butterfly_gather(flat.astype(jnp.bfloat16), "dx", descending(lax.axis_size("dx")))
     space_count = lax.axis_size("space")
     flat = butterfly_gather(flat, "space", descending(space_count))
     flat = flat.reshape(space_count, padded_rows, channels).astype(jnp.float32)

time: 210 us -> 199 us (0.948)
  starting transfers between devices: 84.6 us -> 68.7 us
  waiting for transfers between devices: 57 us -> 63.2 us
    ppermute x7 -> x4, starting transfers between devices: 49 us -> 32.4 us  [butterfly_gather(): got = lax.ppermute(flat, axis, [(j, j ^ step) for j in range(count)])]
    ppermute x0 -> x3, starting transfers between devices: none -> 15.8 us  [butterfly_sum(): lax.ppermute(flat, axis, [(j, j ^ step) for j in range(count)])]
    ppermute x5 -> x2, starting transfers between devices: 22.9 us -> 7.78 us  [butterfly_scatter(): lax.ppermute(sent, axis, [(j, j ^ step) for j in range(count)])]
    ppermute x0 -> x3, waiting for transfers between devices: none -> 13.2 us  [butterfly_sum(): lax.ppermute(flat, axis, [(j, j ^ step) for j in range(count)])]
    ppermute x5 -> x2, waiting for transfers between devices: 14.6 us -> 9.45 us  [butterfly_scatter(): lax.ppermute(sent, axis, [(j, j ^ step) for j in range(count)])]
    ppermute x7 -> x4, waiting for transfers between devices: 18 us -> 16.1 us  [butterfly_gather(): got = lax.ppermute(flat, axis, [(j, j ^ step) for j in range(count)])]
  transfers between devices with their start and end apart: 20 -> 17, of which waited for: 14 -> 11; matrix products, arithmetic and copies ran while one was open for 7% -> 7% of each run, Pallas kernels for 0% -> 0%
where the time goes in v7:
time: 199 us
  starting transfers between devices  68.7 us (35%)
  waiting for transfers between devices  63.2 us (32%)
  blocking collectives  22.3 us (11%)
  matrix products  20.2 us (10%)
  local copies, waits for them, and re-layouts  13.6 us (7%)
  other arithmetic  8.74 us (4%)
  between operations  2.04 us (1%)
    ppermute x4, starting transfers between devices, butterfly_gather(): got = lax.ppermute(flat, axis, [(j, j ^ step) for j in range(count)])  32.4 us
    ppermute x4, waiting for transfers between devices, butterfly_gather(): got = lax.ppermute(flat, axis, [(j, j ^ step) for j in range(count)])  16.1 us
    ppermute x3, starting transfers between devices, butterfly_sum(): lax.ppermute(flat, axis, [(j, j ^ step) for j in range(count)])  15.8 us
    ppermute x1, waiting for transfers between devices, per_device(): skip_grad = lax.ppermute(d_input, 'section', [(last, 0)])  14.4 us
    ppermute x3, waiting for transfers between devices, butterfly_sum(): lax.ppermute(flat, axis, [(j, j ^ step) for j in range(count)])  13.2 us
    all_gather x1, blocking collectives, per_device(): images = lax.all_gather(images, 'space', axis=1, tiled=True)  12.8 us
    dot_general x7, matrix products, convolve(): jnp.dot(flat, matrix, preferred_element_type=jnp.float32)  11.6 us
    ppermute x3, waiting for transfers between devices, per_device(): upstream = lax.ppermute(carried, 'section', [(active + 1, active)])  9.95 us
  transfers between devices with their start and end apart: 17, of which 11 were waited for; matrix products, arithmetic and copies ran while one was open for 7% of the time, Pallas kernels for 0%

profile of v7, /device:TPU:1, one launch (start us, length us, event | category | flops | bytes accessed | tf_op | source)
XLA Modules:
  0.0 198.8 jit_solution(13434507881862276885)
XLA Ops:
  0.7 12.8 %all_gather.6 = bf16[2,4,64,256]{3,2,1,0:T(8,128)(2,1)S(1)} all-gather(bf16[2,1,64,256]{3,2,1,0:T(8,128)(2,1)} %param.6), channel_id=1, replica_groups=mesh['dy'=8,'dx'=4,'section'=4,'space'=4] {'space'}, dimensions={1}, use_global_device_ids=true | all-gather | bytes 327680 | tf_op jit(solution)/shard_map/all_gather | solution.py:165
  17.9 1.5 fusion
  19.4 5.3 %collective-permute-start.3 = (bf16[2,4,64,256]{3,2,1,0:T(8,128)(2,1)}, bf16[2,4,64,256]{3,2,1,0:T(8,128)(2,1)S(1)}, u32[]{:S(2)}, u32[]{:S(2)}) collective-permute-start(bf16[2,4,64,256]{3,2,1,0:T(8,128)(2,1)} %fusion), channel_id=1, source_target_pairs={{0,12},{1,13},{2,14},{3,15},{16,28},{17,29},{18,30},{19,31},{32,44... | collective-permute-start | bytes 786440 | tf_op jit(solution)/shard_map/ppermute | solution.py:190
  26.0 9.4 %all_gather.7 = bf16[2,4,64,256]{3,2,1,0:T(8,128)(2,1)S(1)} all-gather(bf16[2,1,64,256]{3,2,1,0:T(8,128)(2,1)S(1)} %copy-done.6), channel_id=1, replica_groups=mesh['dy'=8,'dx'=4,'section'=4,'space'=4] {'space'}, dimensions={1}, use_global_device_ids=true | all-gather | bytes 327680 | tf_op jit(solution)/shard_map/all_gather | solution.py:166
  41.4 1.5 fusion.2
  45.7 1.6 copy.9
  51.9 1.7 divide_multiply_fusion
  53.7 3.3 %fusion.60 = (f32[2,256]{1,0:T(2,128)}, f32[256]{0:T(256)}, f32[2,256]{1,0:T(2,128)S(1)}, f32[2,256]{1,0:T(2,128)S(1)}, f32[2,256]{1,0:T(2,128)}, /*index=5*/f32[2,4,64,256]{3,2,1,0:T(8,128)S(1)}) fusion(bf16[2,4,64,256]{3,2,1,0:T(8,128)(2,1)S(1)} %select_select_fusion.1, f32[2,256]{1,0:T(2,128)S(1)} %rsqrt.26, f32[2,256]{1,0:T(2,128)S(1)} %get-tuple-element.33, ...), kind=kOutput, calls=%fused_computation.138 | convolution fusion | flops 607254272 | bytes 4343808 | tf_op jit(solution)/shard_map/dot_general | solution.py:74
  59.5 1.7 fusion.59
  62.6 1.5 collective-permute-start.7
  64.5 1.7 fusion.58
  68.9 14.4 %collective-permute-done.7 = bf16[2,4,64,256]{3,2,1,0:T(8,128)(2,1)} collective-permute-done((bf16[2,4,64,256]{3,2,1,0:T(8,128)(2,1)}, bf16[2,4,64,256]{3,2,1,0:T(8,128)(2,1)}, u32[]{:S(2)}, u32[]{:S(2)}) %collective-permute-start.7) | collective-permute-done | bytes 262176 | tf_op jit(solution)/shard_map/ppermute | solution.py:210
  83.4 9.9 %collective-permute-done.6 = bf16[2,4,64,256]{3,2,1,0:T(8,128)(2,1)} collective-permute-done((bf16[2,4,64,256]{3,2,1,0:T(8,128)(2,1)S(1)}, bf16[2,4,64,256]{3,2,1,0:T(8,128)(2,1)}, u32[]{:S(2)}, u32[]{:S(2)}) %collective-permute-start.6) | collective-permute-done | bytes 262176 | tf_op jit(solution)/shard_map/ppermute | solution.py:201
  99.3 3.1 %collective-permute-start.8 = (f32[368,256]{1,0:T(8,128)S(1)}, f32[368,256]{1,0:T(8,128)S(1)}, u32[]{:S(2)}, u32[]{:S(2)}) collective-permute-start(f32[368,256]{1,0:T(8,128)S(1)} %constant_dynamic-slice_fusion.1), channel_id=1, source_target_pairs={{0,16},{16,0},{32,48},{48,32},{1,17},{17,1},{33,49},{49,33},{2,18}... | collective-permute-start | bytes 1130504 | tf_op jit(solution)/shard_map/ppermute | solution.py:242
  102.5 5.2 %collective-permute-done.8 = f32[368,256]{1,0:T(8,128)S(1)} collective-permute-done((f32[368,256]{1,0:T(8,128)S(1)}, f32[368,256]{1,0:T(8,128)S(1)}, u32[]{:S(2)}, u32[]{:S(2)}) %collective-permute-start.8) | collective-permute-done | bytes 376864 | tf_op jit(solution)/shard_map/ppermute | solution.py:242
  107.8 4.7 %collective-permute-start.9 = (f32[184,256]{1,0:T(8,128)S(1)}, f32[184,256]{1,0:T(8,128)S(1)}, u32[]{:S(2)}, u32[]{:S(2)}) collective-permute-start(f32[184,256]{1,0:T(8,128)S(1)} %constant_dynamic-slice_fusion), channel_id=1, source_target_pairs={{0,32},{16,48},{32,0},{48,16},{1,33},{17,49},{33,1},{49,17},{2,34}... | collective-permute-start | bytes 565256 | tf_op jit(solution)/shard_map/ppermute | solution.py:242
  112.4 4.3 %collective-permute-done.9 = f32[184,256]{1,0:T(8,128)S(1)} collective-permute-done((f32[184,256]{1,0:T(8,128)S(1)}, f32[184,256]{1,0:T(8,128)S(1)}, u32[]{:S(2)}, u32[]{:S(2)}) %collective-permute-start.9) | collective-permute-done | bytes 188448 | tf_op jit(solution)/shard_map/ppermute | solution.py:242
  116.7 3.2 %collective-permute-start.10 = (f32[184,256]{1,0:T(8,128)S(1)}, f32[184,256]{1,0:T(8,128)S(1)}, u32[]{:S(2)}, u32[]{:S(2)}) collective-permute-start(f32[184,256]{1,0:T(8,128)S(1)} %dynamic-slice_add_fusion.1), channel_id=1, source_target_pairs={{0,64},{64,0},{128,192},{192,128},{256,320},{320,256},{384,448},{4... | collective-permute-start | bytes 565256 | tf_op jit(solution)/shard_map/ppermute | solution.py:251
  120.0 3.1 %collective-permute-done.10 = f32[184,256]{1,0:T(8,128)S(1)} collective-permute-done((f32[184,256]{1,0:T(8,128)S(1)}, f32[184,256]{1,0:T(8,128)S(1)}, u32[]{:S(2)}, u32[]{:S(2)}) %collective-permute-start.10) | collective-permute-done | bytes 188448 | tf_op jit(solution)/shard_map/ppermute | solution.py:251
  123.1 4.2 %collective-permute-start.11 = (f32[184,256]{1,0:T(8,128)S(1)}, f32[184,256]{1,0:T(8,128)S(1)}, u32[]{:S(2)}, u32[]{:S(2)}) collective-permute-start(f32[184,256]{1,0:T(8,128)S(1)} %add.292), channel_id=1, source_target_pairs={{0,128},{64,192},{128,0},{192,64},{256,384},{320,448},{384,256},{4... | collective-permute-start | bytes 565256 | tf_op jit(solution)/shard_map/ppermute | solution.py:251
  127.3 4.1 %collective-permute-done.11 = f32[184,256]{1,0:T(8,128)S(1)} collective-permute-done((f32[184,256]{1,0:T(8,128)S(1)}, f32[184,256]{1,0:T(8,128)S(1)}, u32[]{:S(2)}, u32[]{:S(2)}) %collective-permute-start.11) | collective-permute-done | bytes 188448 | tf_op jit(solution)/shard_map/ppermute | solution.py:251
  131.4 8.4 %collective-permute-start.12 = (f32[184,256]{1,0:T(8,128)S(1)}, f32[184,256]{1,0:T(8,128)S(1)}, u32[]{:S(2)}, u32[]{:S(2)}) collective-permute-start(f32[184,256]{1,0:T(8,128)S(1)} %add.293), channel_id=1, source_target_pairs={{0,256},{64,320},{128,384},{192,448},{256,0},{320,64},{384,128},{4... | collective-permute-start | bytes 565256 | tf_op jit(solution)/shard_map/ppermute | solution.py:251
  139.8 6.0 %collective-permute-done.12 = f32[184,256]{1,0:T(8,128)S(1)} collective-permute-done((f32[184,256]{1,0:T(8,128)S(1)}, f32[184,256]{1,0:T(8,128)S(1)}, u32[]{:S(2)}, u32[]{:S(2)}) %collective-permute-start.12) | collective-permute-done | bytes 188448 | tf_op jit(solution)/shard_map/ppermute | solution.py:251
  145.9 1.9 collective-permute-start.13
  147.8 4.9 %collective-permute-done.13 = bf16[184,256]{1,0:T(8,128)(2,1)S(1)} collective-permute-done((bf16[184,256]{1,0:T(8,128)(2,1)S(1)}, bf16[184,256]{1,0:T(8,128)(2,1)S(1)}, u32[]{:S(2)}, u32[]{:S(2)}) %collective-permute-start.13) | collective-permute-done | bytes 94240 | tf_op jit(solution)/shard_map/ppermute | solution.py:261
  152.8 1.9 collective-permute-start.14
  154.7 4.4 %collective-permute-done.14 = bf16[368,256]{1,0:T(8,128)(2,1)S(1)} collective-permute-done((bf16[368,256]{1,0:T(8,128)(2,1)S(1)}, bf16[368,256]{1,0:T(8,128)(2,1)S(1)}, u32[]{:S(2)}, u32[]{:S(2)}) %collective-permute-start.14) | collective-permute-done | bytes 188448 | tf_op jit(solution)/shard_map/ppermute | solution.py:261
  159.3 10.1 %collective-permute-start.15 = (bf16[736,256]{1,0:T(8,128)(2,1)S(1)}, bf16[736,256]{1,0:T(8,128)(2,1)S(1)}, u32[]{:S(2)}, u32[]{:S(2)}) collective-permute-start(bf16[736,256]{1,0:T(8,128)(2,1)S(1)} %maximum_select_fusion.2), channel_id=1, source_target_pairs={{0,2},{1,3},{2,0},{3,1},{4,6},{5,7},{6,4},{7,5},{8,10},{9,11},{10,... | collective-permute-start | bytes 1130504 | tf_op jit(solution)/shard_map/ppermute | solution.py:261
  169.4 5.0 %collective-permute-done.15 = bf16[736,256]{1,0:T(8,128)(2,1)S(1)} collective-permute-done((bf16[736,256]{1,0:T(8,128)(2,1)S(1)}, bf16[736,256]{1,0:T(8,128)(2,1)S(1)}, u32[]{:S(2)}, u32[]{:S(2)}) %collective-permute-start.15) | collective-permute-done | bytes 376864 | tf_op jit(solution)/shard_map/ppermute | solution.py:261
  174.7 18.4 %collective-permute-start.16 = (bf16[1472,256]{1,0:T(8,128)(2,1)S(1)}, bf16[1472,256]{1,0:T(8,128)(2,1)S(1)}, u32[]{:S(2)}, u32[]{:S(2)}) collective-permute-start(bf16[1472,256]{1,0:T(8,128)(2,1)S(1)} %maximum_select_fusion.1), channel_id=1, source_target_pairs={{0,1},{1,0},{2,3},{3,2},{4,5},{5,4},{6,7},{7,6},{8,9},{9,8},{10,11... | collective-permute-start | bytes 2261000 | tf_op jit(solution)/shard_map/ppermute | solution.py:261
  193.1 1.8 collective-permute-done.16
  195.4 1.6 slice.298
  (205 shorter events, 34.1 us)
Async XLA Ops:
  0.6 13.7 %copy-start = (bf16[1,256,512]{2,1,0:T(8,128)(2,1)S(1)}, bf16[1,256,512]{2,1,0:T(8,128)(2,1)}, u32[]{:S(2)}) copy-start(bf16[1,256,512]{2,1,0:T(8,128)(2,1)} %param.11) | copy-start | bytes 786436
  0.6 16.2 %copy-start.5 = (f32[1,256]{1,0:T(1,128)S(1)}, f32[1,256]{1,0:T(1,128)}, u32[]{:S(2)}) copy-start(f32[1,256]{1,0:T(1,128)} %param.10) | copy-start | bytes 3076
  0.7 38.9 %copy-start.22 = (s32[256]{0:T(256)}, s32[256]{0:T(256)S(1)}, u32[]{:S(2)}) copy-start(s32[256]{0:T(256)S(1)} %and_select_fusion) | copy-start | bytes 3076
  14.3 1.4 copy-start.9
  14.3 1.4 copy-start.11
  16.7 1.3 copy-start.1
  17.3 8.7 %copy-start.6 = (bf16[2,1,64,256]{3,2,1,0:T(8,128)(2,1)S(1)}, bf16[2,1,64,256]{3,2,1,0:T(8,128)(2,1)}, u32[]{:S(2)}) copy-start(bf16[2,1,64,256]{3,2,1,0:T(8,128)(2,1)} %param.8) | copy-start | bytes 196612
  19.4 30.4 %collective-permute-start.3 = (bf16[2,4,64,256]{3,2,1,0:T(8,128)(2,1)}, bf16[2,4,64,256]{3,2,1,0:T(8,128)(2,1)S(1)}, u32[]{:S(2)}, u32[]{:S(2)}) collective-permute-start(bf16[2,4,64,256]{3,2,1,0:T(8,128)(2,1)} %fusion), channel_id=1, source_target_pairs={{0,12},{1,13},{2,14},{3,15},{16,28},{17,29},{18,30},{19,31},{32,44... | collective-permute-start | bytes 786440 | tf_op jit(solution)/shard_map/ppermute | solution.py:190
  24.7 10.9 %collective-permute-start = (bf16[2,4,64,256]{3,2,1,0:T(8,128)(2,1)}, bf16[2,4,64,256]{3,2,1,0:T(8,128)(2,1)S(1)}, u32[]{:S(2)}, u32[]{:S(2)}) collective-permute-start(bf16[2,4,64,256]{3,2,1,0:T(8,128)(2,1)} %fusion), channel_id=1, source_target_pairs={{0,4},{1,5},{2,6},{3,7},{16,20},{17,21},{18,22},{19,23},{32,36},{3... | collective-permute-start | bytes 786440 | tf_op jit(solution)/shard_map/ppermute | solution.py:185
  35.9 1.7 copy-start.25
  38.4 0.9 collective-permute-start.1
  42.9 7.0 %collective-permute-start.2 = (bf16[2,4,64,256]{3,2,1,0:T(8,128)(2,1)}, bf16[2,4,64,256]{3,2,1,0:T(8,128)(2,1)}, u32[]{:S(2)}, u32[]{:S(2)}) collective-permute-start(bf16[2,4,64,256]{3,2,1,0:T(8,128)(2,1)} %fusion.2), channel_id=1, source_target_pairs={{8,12},{9,13},{10,14},{11,15},{24,28},{25,29},{26,30},{27,31},{40,... | collective-permute-start | bytes 786440 | tf_op jit(solution)/shard_map/ppermute | solution.py:185
  44.3 1.4 copy-start.7
  48.3 5.3 %copy-start.2 = (bf16[3,3,256,256]{2,3,1,0:T(8,128)(2,1)S(1)}, bf16[3,3,256,256]{2,3,1,0:T(8,128)(2,1)}, u32[]{:S(2)}) copy-start(bf16[3,3,256,256]{2,3,1,0:T(8,128)(2,1)} %rev.3) | copy-start | bytes 3538948
  50.9 2.7 %copy-start.3 = (bf16[2,4,64,256]{3,2,1,0:T(8,128)(2,1)}, bf16[2,4,64,256]{3,2,1,0:T(8,128)(2,1)S(1)}, u32[]{:S(2)}) copy-start(bf16[2,4,64,256]{3,2,1,0:T(8,128)(2,1)S(1)} %get-tuple-element.34) | copy-start | bytes 786436
  53.6 12.8 %copy-start.27 = (f32[2,256]{1,0:T(2,128)}, f32[2,256]{1,0:T(2,128)S(1)}, u32[]{:S(2)}) copy-start(f32[2,256]{1,0:T(2,128)S(1)} %get-tuple-element.33) | copy-start | bytes 6148
  53.6 3.3 %copy-start.23 = (s32[256]{0:T(256)S(1)}, s32[256]{0:T(256)}, u32[]{:S(2)}) copy-start(s32[256]{0:T(256)} %copy-done.22) | copy-start | bytes 3076
  58.4 0.7 collective-permute-start.4
  61.9 2.2 %collective-permute-start.5 = (bf16[2,4,64,256]{3,2,1,0:T(8,128)(2,1)S(1)}, bf16[2,4,64,256]{3,2,1,0:T(8,128)(2,1)S(1)}, u32[]{:S(2)}, u32[]{:S(2)}) collective-permute-start(bf16[2,4,64,256]{3,2,1,0:T(8,128)(2,1)S(1)} %fusion.93), channel_id=1, source_target_pairs={{8,4},{9,5},{10,6},{11,7},{24,20},{25,21},{26,22},{27,23},{40,36},... | collective-permute-start | bytes 786440 | tf_op jit(solution)/shard_map/ppermute | solution.py:201
  62.6 20.8 %collective-permute-start.7 = (bf16[2,4,64,256]{3,2,1,0:T(8,128)(2,1)}, bf16[2,4,64,256]{3,2,1,0:T(8,128)(2,1)}, u32[]{:S(2)}, u32[]{:S(2)}) collective-permute-start(bf16[2,4,64,256]{3,2,1,0:T(8,128)(2,1)} %fusion.90), channel_id=1, source_target_pairs={{12,0},{13,1},{14,2},{15,3},{28,16},{29,17},{30,18},{31,19},{44,32... | collective-permute-start | bytes 786440 | tf_op jit(solution)/shard_map/ppermute | solution.py:210
  66.9 26.4 %collective-permute-start.6 = (bf16[2,4,64,256]{3,2,1,0:T(8,128)(2,1)S(1)}, bf16[2,4,64,256]{3,2,1,0:T(8,128)(2,1)}, u32[]{:S(2)}, u32[]{:S(2)}) collective-permute-start(bf16[2,4,64,256]{3,2,1,0:T(8,128)(2,1)S(1)} %fusion.96), channel_id=1, source_target_pairs={{4,0},{5,1},{6,2},{7,3},{20,16},{21,17},{22,18},{23,19},{36,32},{3... | collective-permute-start | bytes 786440 | tf_op jit(solution)/shard_map/ppermute | solution.py:201
  95.6 1.3 copy-start.10
  95.6 1.3 copy-start.12
  99.3 8.3 %collective-permute-start.8 = (f32[368,256]{1,0:T(8,128)S(1)}, f32[368,256]{1,0:T(8,128)S(1)}, u32[]{:S(2)}, u32[]{:S(2)}) collective-permute-start(f32[368,256]{1,0:T(8,128)S(1)} %constant_dynamic-slice_fusion.1), channel_id=1, source_target_pairs={{0,16},{16,0},{32,48},{48,32},{1,17},{17,1},{33,49},{49,33},{2,18}... | collective-permute-start | bytes 1130504 | tf_op jit(solution)/shard_map/ppermute | solution.py:242
  107.8 9.0 %collective-permute-start.9 = (f32[184,256]{1,0:T(8,128)S(1)}, f32[184,256]{1,0:T(8,128)S(1)}, u32[]{:S(2)}, u32[]{:S(2)}) collective-permute-start(f32[184,256]{1,0:T(8,128)S(1)} %constant_dynamic-slice_fusion), channel_id=1, source_target_pairs={{0,32},{16,48},{32,0},{48,16},{1,33},{17,49},{33,1},{49,17},{2,34}... | collective-permute-start | bytes 565256 | tf_op jit(solution)/shard_map/ppermute | solution.py:242
  116.7 6.3 %collective-permute-start.10 = (f32[184,256]{1,0:T(8,128)S(1)}, f32[184,256]{1,0:T(8,128)S(1)}, u32[]{:S(2)}, u32[]{:S(2)}) collective-permute-start(f32[184,256]{1,0:T(8,128)S(1)} %dynamic-slice_add_fusion.1), channel_id=1, source_target_pairs={{0,64},{64,0},{128,192},{192,128},{256,320},{320,256},{384,448},{4... | collective-permute-start | bytes 565256 | tf_op jit(solution)/shard_map/ppermute | solution.py:251
  123.1 8.3 %collective-permute-start.11 = (f32[184,256]{1,0:T(8,128)S(1)}, f32[184,256]{1,0:T(8,128)S(1)}, u32[]{:S(2)}, u32[]{:S(2)}) collective-permute-start(f32[184,256]{1,0:T(8,128)S(1)} %add.292), channel_id=1, source_target_pairs={{0,128},{64,192},{128,0},{192,64},{256,384},{320,448},{384,256},{4... | collective-permute-start | bytes 565256 | tf_op jit(solution)/shard_map/ppermute | solution.py:251
  131.4 14.4 %collective-permute-start.12 = (f32[184,256]{1,0:T(8,128)S(1)}, f32[184,256]{1,0:T(8,128)S(1)}, u32[]{:S(2)}, u32[]{:S(2)}) collective-permute-start(f32[184,256]{1,0:T(8,128)S(1)} %add.293), channel_id=1, source_target_pairs={{0,256},{64,320},{128,384},{192,448},{256,0},{320,64},{384,128},{4... | collective-permute-start | bytes 565256 | tf_op jit(solution)/shard_map/ppermute | solution.py:251
  145.9 6.8 %collective-permute-start.13 = (bf16[184,256]{1,0:T(8,128)(2,1)S(1)}, bf16[184,256]{1,0:T(8,128)(2,1)S(1)}, u32[]{:S(2)}, u32[]{:S(2)}) collective-permute-start(bf16[184,256]{1,0:T(8,128)(2,1)S(1)} %add_convert_fusion.2), channel_id=1, source_target_pairs={{0,32},{16,48},{32,0},{48,16},{1,33},{17,49},{33,1},{49,17},{2,34}... | collective-permute-start | bytes 282632 | tf_op jit(solution)/shard_map/ppermute | solution.py:261
  152.8 6.3 %collective-permute-start.14 = (bf16[368,256]{1,0:T(8,128)(2,1)S(1)}, bf16[368,256]{1,0:T(8,128)(2,1)S(1)}, u32[]{:S(2)}, u32[]{:S(2)}) collective-permute-start(bf16[368,256]{1,0:T(8,128)(2,1)S(1)} %maximum_select_fusion.3), channel_id=1, source_target_pairs={{0,16},{16,0},{32,48},{48,32},{1,17},{17,1},{33,49},{49,33},{2,18}... | collective-permute-start | bytes 565256 | tf_op jit(solution)/shard_map/ppermute | solution.py:261
  159.3 15.1 %collective-permute-start.15 = (bf16[736,256]{1,0:T(8,128)(2,1)S(1)}, bf16[736,256]{1,0:T(8,128)(2,1)S(1)}, u32[]{:S(2)}, u32[]{:S(2)}) collective-permute-start(bf16[736,256]{1,0:T(8,128)(2,1)S(1)} %maximum_select_fusion.2), channel_id=1, source_target_pairs={{0,2},{1,3},{2,0},{3,1},{4,6},{5,7},{6,4},{7,5},{8,10},{9,11},{10,... | collective-permute-start | bytes 1130504 | tf_op jit(solution)/shard_map/ppermute | solution.py:261
  174.7 20.3 %collective-permute-start.16 = (bf16[1472,256]{1,0:T(8,128)(2,1)S(1)}, bf16[1472,256]{1,0:T(8,128)(2,1)S(1)}, u32[]{:S(2)}, u32[]{:S(2)}) collective-permute-start(bf16[1472,256]{1,0:T(8,128)(2,1)S(1)} %maximum_select_fusion.1), channel_id=1, source_target_pairs={{0,1},{1,0},{2,3},{3,2},{4,5},{5,4},{6,7},{7,6},{8,9},{9,8},{10,11... | collective-permute-start | bytes 2261000 | tf_op jit(solution)/shard_map/ppermute | solution.py:261
  (16 other events, 17.4 us)

commit v8 on v7

--- a/solution.py
+++ b/solution.py
@@ -162,8 +162,9 @@
 def per_device(images, steps, out_grad, conv_weight, gn_gain, emb_weight):
     section_count = lax.axis_size("section")
     section_no = lax.axis_index("section")
-    images = lax.all_gather(images, "space", axis=1, tiled=True)
-    out_grad = lax.all_gather(out_grad, "space", axis=1, tiled=True)
+    both = lax.all_gather(jnp.stack([images, out_grad]), "space", axis=2, tiled=True)
+    images = both[0]
+    out_grad = both[1]
     row_count = images.shape[1]
     col_count = images.shape[2]
     channels = images.shape[3]

time: 199 us -> 201 us (1.010)
  blocking collectives: 22.3 us -> 13.2 us
  local copies, waits for them, and re-layouts: 13.6 us -> 22.5 us
  waiting for transfers between devices: 63.2 us -> 66.2 us
  matrix products: 20.2 us -> 17.4 us
    all_gather x2 -> x1, blocking collectives: 22.3 us -> 13.2 us  [per_device(): lax.all_gather(jnp.stack([images, out_grad]), 'space', axis=2, tiled=True)]
    unnamed x124 -> x97, local copies, waits for them, and re-layouts: 7.55 us -> 16.2 us
    ppermute x1, waiting for transfers between devices: 14.4 us -> 18.5 us  [per_device(): skip_grad = lax.ppermute(d_input, 'section', [(last, 0)])]
    dot_general x14, matrix products: 7.37 us -> 5.24 us  [over_groups(): return jnp.dot(values, blocks, precision=lax.Precision.HIGHEST)]
  transfers between devices with their start and end apart: 17 -> 17, of which waited for: 11 -> 12; matrix products, arithmetic and copies ran while one was open for 7% -> 7% of each run, Pallas kernels for 0% -> 0%
where the time goes in v8:
time: 201 us
  starting transfers between devices  69.9 us (35%)
  waiting for transfers between devices  66.2 us (33%)
  local copies, waits for them, and re-layouts  22.5 us (11%)
  matrix products  17.4 us (9%)
  blocking collectives  13.2 us (7%)
  other arithmetic  9.73 us (5%)
    ppermute x4, starting transfers between devices, butterfly_gather(): got = lax.ppermute(flat, axis, [(j, j ^ step) for j in range(count)])  32.9 us
    ppermute x1, waiting for transfers between devices, per_device(): skip_grad = lax.ppermute(d_input, 'section', [(last, 0)])  18.5 us
    unnamed x97, local copies, waits for them, and re-layouts  16.2 us
    ppermute x3, starting transfers between devices, butterfly_sum(): lax.ppermute(flat, axis, [(j, j ^ step) for j in range(count)])  15.8 us
    ppermute x4, waiting for transfers between devices, butterfly_gather(): got = lax.ppermute(flat, axis, [(j, j ^ step) for j in range(count)])  15 us
    ppermute x3, waiting for transfers between devices, butterfly_sum(): lax.ppermute(flat, axis, [(j, j ^ step) for j in range(count)])  13.3 us
    all_gather x1, blocking collectives, per_device(): lax.all_gather(jnp.stack([images, out_grad]), 'space', axis=2, tiled=True)  13.2 us
    ppermute x3, waiting for transfers between devices, per_device(): upstream = lax.ppermute(carried, 'section', [(active + 1, active)])  9.78 us
  transfers between devices with their start and end apart: 17, of which 12 were waited for; matrix products, arithmetic and copies ran while one was open for 7% of the time, Pallas kernels for 0%

profile of v8, /device:TPU:1, one launch (start us, length us, event | category | flops | bytes accessed | tf_op | source)
XLA Modules:
  0.0 200.7 jit_solution(10747213259299467984)
XLA Ops:
  1.6 13.2 %all_gather.3 = bf16[2,2,4,64,256]{4,3,2,1,0:T(8,128)(2,1)S(1)} all-gather(bf16[2,2,1,64,256]{4,3,2,1,0:T(8,128)(2,1)S(1)} %pad_maximum_fusion), channel_id=1, replica_groups=mesh['dy'=8,'dx'=4,'section'=4,'space'=4] {'space'}, dimensions={2}, use_global_device_ids=true | all-gather | bytes 655360 | tf_op jit(solution)/shard_map/all_gather | solution.py:165
  19.2 1.5 fusion
  20.7 2.0 collective-permute-start
  22.7 5.3 %collective-permute-start.3 = (bf16[2,4,64,256]{3,2,1,0:T(8,128)(2,1)}, bf16[2,4,64,256]{3,2,1,0:T(8,128)(2,1)}, u32[]{:S(2)}, u32[]{:S(2)}) collective-permute-start(bf16[2,4,64,256]{3,2,1,0:T(8,128)(2,1)} %fusion), channel_id=1, source_target_pairs={{0,12},{1,13},{2,14},{3,15},{16,28},{17,29},{18,30},{19,31},{32,44... | collective-permute-start | bytes 786440 | tf_op jit(solution)/shard_map/ppermute | solution.py:191
  34.9 1.5 fusion.2
  36.4 1.3 collective-permute-start.2
  38.5 1.6 copy.9
  48.4 2.7 %fusion.60 = (f32[2,256]{1,0:T(2,128)S(1)}, f32[256]{0:T(256)S(1)}, f32[2,256]{1,0:T(2,128)S(1)}, f32[2,256]{1,0:T(2,128)S(1)}, f32[2,256]{1,0:T(2,128)S(1)}, /*index=5*/f32[2,4,64,256]{3,2,1,0:T(8,128)S(1)}) fusion(bf16[2,4,64,256]{3,2,1,0:T(8,128)(2,1)S(1)} %get-tuple-element.36, f32[2,256]{1,0:T(2,128)S(1)} %rsqrt.26, ...), kind=kOutput, calls=%fused_computation.138 | convolution fusion | flops 607254272 | bytes 4343808 | tf_op jit(solution)/shard_map/dot_general | solution.py:74
  55.4 1.5 collective-permute-start.7
  59.2 1.3 collective-permute-start.6
  60.6 18.5 %collective-permute-done.7 = bf16[2,4,64,256]{3,2,1,0:T(8,128)(2,1)S(1)} collective-permute-done((bf16[2,4,64,256]{3,2,1,0:T(8,128)(2,1)S(1)}, bf16[2,4,64,256]{3,2,1,0:T(8,128)(2,1)S(1)}, u32[]{:S(2)}, u32[]{:S(2)}) %collective-permute-start.7) | collective-permute-done | bytes 262176 | tf_op jit(solution)/shard_map/ppermute | solution.py:211
  79.1 9.8 %collective-permute-done.6 = bf16[2,4,64,256]{3,2,1,0:T(8,128)(2,1)} collective-permute-done((bf16[2,4,64,256]{3,2,1,0:T(8,128)(2,1)S(1)}, bf16[2,4,64,256]{3,2,1,0:T(8,128)(2,1)}, u32[]{:S(2)}, u32[]{:S(2)}) %collective-permute-start.6) | collective-permute-done | bytes 262176 | tf_op jit(solution)/shard_map/ppermute | solution.py:202
  100.2 1.8 fusion.54
  102.2 3.1 %collective-permute-start.8 = (f32[368,256]{1,0:T(8,128)S(1)}, f32[368,256]{1,0:T(8,128)S(1)}, u32[]{:S(2)}, u32[]{:S(2)}) collective-permute-start(f32[368,256]{1,0:T(8,128)S(1)} %constant_dynamic-slice_fusion.1), channel_id=1, source_target_pairs={{0,16},{16,0},{32,48},{48,32},{1,17},{17,1},{33,49},{49,33},{2,18}... | collective-permute-start | bytes 1130504 | tf_op jit(solution)/shard_map/ppermute | solution.py:243
  105.4 5.2 %collective-permute-done.8 = f32[368,256]{1,0:T(8,128)S(1)} collective-permute-done((f32[368,256]{1,0:T(8,128)S(1)}, f32[368,256]{1,0:T(8,128)S(1)}, u32[]{:S(2)}, u32[]{:S(2)}) %collective-permute-start.8) | collective-permute-done | bytes 376864 | tf_op jit(solution)/shard_map/ppermute | solution.py:243
  110.7 4.7 %collective-permute-start.9 = (f32[184,256]{1,0:T(8,128)S(1)}, f32[184,256]{1,0:T(8,128)S(1)}, u32[]{:S(2)}, u32[]{:S(2)}) collective-permute-start(f32[184,256]{1,0:T(8,128)S(1)} %constant_dynamic-slice_fusion), channel_id=1, source_target_pairs={{0,32},{16,48},{32,0},{48,16},{1,33},{17,49},{33,1},{49,17},{2,34}... | collective-permute-start | bytes 565256 | tf_op jit(solution)/shard_map/ppermute | solution.py:243
  115.3 3.9 %collective-permute-done.9 = f32[184,256]{1,0:T(8,128)S(1)} collective-permute-done((f32[184,256]{1,0:T(8,128)S(1)}, f32[184,256]{1,0:T(8,128)S(1)}, u32[]{:S(2)}, u32[]{:S(2)}) %collective-permute-start.9) | collective-permute-done | bytes 188448 | tf_op jit(solution)/shard_map/ppermute | solution.py:243
  119.3 3.2 %collective-permute-start.10 = (f32[184,256]{1,0:T(8,128)S(1)}, f32[184,256]{1,0:T(8,128)S(1)}, u32[]{:S(2)}, u32[]{:S(2)}) collective-permute-start(f32[184,256]{1,0:T(8,128)S(1)} %dynamic-slice_add_fusion.1), channel_id=1, source_target_pairs={{0,64},{64,0},{128,192},{192,128},{256,320},{320,256},{384,448},{4... | collective-permute-start | bytes 565256 | tf_op jit(solution)/shard_map/ppermute | solution.py:252
  122.5 3.1 %collective-permute-done.10 = f32[184,256]{1,0:T(8,128)S(1)} collective-permute-done((f32[184,256]{1,0:T(8,128)S(1)}, f32[184,256]{1,0:T(8,128)S(1)}, u32[]{:S(2)}, u32[]{:S(2)}) %collective-permute-start.10) | collective-permute-done | bytes 188448 | tf_op jit(solution)/shard_map/ppermute | solution.py:252
  125.6 4.2 %collective-permute-start.11 = (f32[184,256]{1,0:T(8,128)S(1)}, f32[184,256]{1,0:T(8,128)S(1)}, u32[]{:S(2)}, u32[]{:S(2)}) collective-permute-start(f32[184,256]{1,0:T(8,128)S(1)} %add.292), channel_id=1, source_target_pairs={{0,128},{64,192},{128,0},{192,64},{256,384},{320,448},{384,256},{4... | collective-permute-start | bytes 565256 | tf_op jit(solution)/shard_map/ppermute | solution.py:252
  129.8 4.1 %collective-permute-done.11 = f32[184,256]{1,0:T(8,128)S(1)} collective-permute-done((f32[184,256]{1,0:T(8,128)S(1)}, f32[184,256]{1,0:T(8,128)S(1)}, u32[]{:S(2)}, u32[]{:S(2)}) %collective-permute-start.11) | collective-permute-done | bytes 188448 | tf_op jit(solution)/shard_map/ppermute | solution.py:252
  134.0 8.4 %collective-permute-start.12 = (f32[184,256]{1,0:T(8,128)S(1)}, f32[184,256]{1,0:T(8,128)S(1)}, u32[]{:S(2)}, u32[]{:S(2)}) collective-permute-start(f32[184,256]{1,0:T(8,128)S(1)} %add.293), channel_id=1, source_target_pairs={{0,256},{64,320},{128,384},{192,448},{256,0},{320,64},{384,128},{4... | collective-permute-start | bytes 565256 | tf_op jit(solution)/shard_map/ppermute | solution.py:252
  142.3 6.1 %collective-permute-done.12 = f32[184,256]{1,0:T(8,128)S(1)} collective-permute-done((f32[184,256]{1,0:T(8,128)S(1)}, f32[184,256]{1,0:T(8,128)S(1)}, u32[]{:S(2)}, u32[]{:S(2)}) %collective-permute-start.12) | collective-permute-done | bytes 188448 | tf_op jit(solution)/shard_map/ppermute | solution.py:252
  148.4 3.2 %collective-permute-start.13 = (bf16[184,256]{1,0:T(8,128)(2,1)S(1)}, bf16[184,256]{1,0:T(8,128)(2,1)S(1)}, u32[]{:S(2)}, u32[]{:S(2)}) collective-permute-start(bf16[184,256]{1,0:T(8,128)(2,1)S(1)} %add_convert_fusion.2), channel_id=1, source_target_pairs={{0,32},{16,48},{32,0},{48,16},{1,33},{17,49},{33,1},{49,17},{2,34}... | collective-permute-start | bytes 282632 | tf_op jit(solution)/shard_map/ppermute | solution.py:262
  151.6 3.6 %collective-permute-done.13 = bf16[184,256]{1,0:T(8,128)(2,1)S(1)} collective-permute-done((bf16[184,256]{1,0:T(8,128)(2,1)S(1)}, bf16[184,256]{1,0:T(8,128)(2,1)S(1)}, u32[]{:S(2)}, u32[]{:S(2)}) %collective-permute-start.13) | collective-permute-done | bytes 94240 | tf_op jit(solution)/shard_map/ppermute | solution.py:262
  155.3 1.9 collective-permute-start.14
  157.2 4.4 %collective-permute-done.14 = bf16[368,256]{1,0:T(8,128)(2,1)S(1)} collective-permute-done((bf16[368,256]{1,0:T(8,128)(2,1)S(1)}, bf16[368,256]{1,0:T(8,128)(2,1)S(1)}, u32[]{:S(2)}, u32[]{:S(2)}) %collective-permute-start.14) | collective-permute-done | bytes 188448 | tf_op jit(solution)/shard_map/ppermute | solution.py:262
  161.8 10.0 %collective-permute-start.15 = (bf16[736,256]{1,0:T(8,128)(2,1)S(1)}, bf16[736,256]{1,0:T(8,128)(2,1)S(1)}, u32[]{:S(2)}, u32[]{:S(2)}) collective-permute-start(bf16[736,256]{1,0:T(8,128)(2,1)S(1)} %maximum_select_fusion.2), channel_id=1, source_target_pairs={{0,2},{1,3},{2,0},{3,1},{4,6},{5,7},{6,4},{7,5},{8,10},{9,11},{10,... | collective-permute-start | bytes 1130504 | tf_op jit(solution)/shard_map/ppermute | solution.py:262
  171.8 5.1 %collective-permute-done.15 = bf16[736,256]{1,0:T(8,128)(2,1)S(1)} collective-permute-done((bf16[736,256]{1,0:T(8,128)(2,1)S(1)}, bf16[736,256]{1,0:T(8,128)(2,1)S(1)}, u32[]{:S(2)}, u32[]{:S(2)}) %collective-permute-start.15) | collective-permute-done | bytes 376864 | tf_op jit(solution)/shard_map/ppermute | solution.py:262
  177.2 17.9 %collective-permute-start.16 = (bf16[1472,256]{1,0:T(8,128)(2,1)S(1)}, bf16[1472,256]{1,0:T(8,128)(2,1)S(1)}, u32[]{:S(2)}, u32[]{:S(2)}) collective-permute-start(bf16[1472,256]{1,0:T(8,128)(2,1)S(1)} %maximum_select_fusion.1), channel_id=1, source_target_pairs={{0,1},{1,0},{2,3},{3,2},{4,5},{5,4},{6,7},{7,6},{8,9},{9,8},{10,11... | collective-permute-start | bytes 2261000 | tf_op jit(solution)/shard_map/ppermute | solution.py:262
  195.1 1.8 collective-permute-done.16
  197.5 1.6 slice.308
  (179 shorter events, 41.5 us)
Async XLA Ops:
  0.6 15.1 %copy-start = (bf16[1,256,512]{2,1,0:T(8,128)(2,1)S(1)}, bf16[1,256,512]{2,1,0:T(8,128)(2,1)}, u32[]{:S(2)}) copy-start(bf16[1,256,512]{2,1,0:T(8,128)(2,1)} %param.11) | copy-start | bytes 786436
  0.6 17.5 %copy-start.4 = (f32[1,256]{1,0:T(1,128)S(1)}, f32[1,256]{1,0:T(1,128)}, u32[]{:S(2)}) copy-start(f32[1,256]{1,0:T(1,128)} %param.10) | copy-start | bytes 3076
  0.7 32.5 %copy-start.7 = (s32[256]{0:T(256)}, s32[256]{0:T(256)S(1)}, u32[]{:S(2)}) copy-start(s32[256]{0:T(256)S(1)} %and_select_fusion) | copy-start | bytes 3076
  15.7 2.9 %copy-start.5 = (f32[2,128]{1,0:T(2,128)}, f32[2,128]{1,0:T(2,128)S(1)}, u32[]{:S(2)}) copy-start(f32[2,128]{1,0:T(2,128)S(1)} %get-tuple-element.49) | copy-start | bytes 3076
  16.2 2.4 %copy-start.9 = (f32[2,256]{1,0:T(2,128)}, f32[2,256]{1,0:T(2,128)S(1)}, u32[]{:S(2)}) copy-start(f32[2,256]{1,0:T(2,128)S(1)} %fusion.27) | copy-start | bytes 6148
  20.7 7.9 %collective-permute-start = (bf16[2,4,64,256]{3,2,1,0:T(8,128)(2,1)}, bf16[2,4,64,256]{3,2,1,0:T(8,128)(2,1)S(1)}, u32[]{:S(2)}, u32[]{:S(2)}) collective-permute-start(bf16[2,4,64,256]{3,2,1,0:T(8,128)(2,1)} %fusion), channel_id=1, source_target_pairs={{0,4},{1,5},{2,6},{3,7},{16,20},{17,21},{18,22},{19,23},{32,36},{3... | collective-permute-start | bytes 786440 | tf_op jit(solution)/shard_map/ppermute | solution.py:186
  22.7 20.0 %collective-permute-start.3 = (bf16[2,4,64,256]{3,2,1,0:T(8,128)(2,1)}, bf16[2,4,64,256]{3,2,1,0:T(8,128)(2,1)}, u32[]{:S(2)}, u32[]{:S(2)}) collective-permute-start(bf16[2,4,64,256]{3,2,1,0:T(8,128)(2,1)} %fusion), channel_id=1, source_target_pairs={{0,12},{1,13},{2,14},{3,15},{16,28},{17,29},{18,30},{19,31},{32,44... | collective-permute-start | bytes 786440 | tf_op jit(solution)/shard_map/ppermute | solution.py:191
  28.9 1.7 copy-start.11
  31.4 1.5 collective-permute-start.1
  36.4 6.3 %collective-permute-start.2 = (bf16[2,4,64,256]{3,2,1,0:T(8,128)(2,1)}, bf16[2,4,64,256]{3,2,1,0:T(8,128)(2,1)}, u32[]{:S(2)}, u32[]{:S(2)}) collective-permute-start(bf16[2,4,64,256]{3,2,1,0:T(8,128)(2,1)} %fusion.2), channel_id=1, source_target_pairs={{8,12},{9,13},{10,14},{11,15},{24,28},{25,29},{26,30},{27,31},{40,... | collective-permute-start | bytes 786440 | tf_op jit(solution)/shard_map/ppermute | solution.py:186
  42.7 5.1 %copy-start.8 = (s32[256]{0:T(256)S(1)}, s32[256]{0:T(256)}, u32[]{:S(2)}) copy-start(s32[256]{0:T(256)} %copy-done.7) | copy-start | bytes 3076
  42.7 5.3 %copy-start.10 = (f32[2,256]{1,0:T(2,128)S(1)}, f32[2,256]{1,0:T(2,128)}, u32[]{:S(2)}) copy-start(f32[2,256]{1,0:T(2,128)} %copy-done.9) | copy-start | bytes 6148
  42.7 5.4 %copy-start.12 = (f32[2,256]{1,0:T(2,128)S(1)}, f32[2,256]{1,0:T(2,128)}, u32[]{:S(2)}) copy-start(f32[2,256]{1,0:T(2,128)} %copy-done.11) | copy-start | bytes 6148
  42.7 5.4 %copy-start.14 = (f32[2,256]{1,0:T(2,128)S(1)}, f32[2,256]{1,0:T(2,128)}, u32[]{:S(2)}) copy-start(f32[2,256]{1,0:T(2,128)} %copy-done.13) | copy-start | bytes 6148
  42.7 5.4 %copy-start.15 = (f32[2,256]{1,0:T(2,128)S(1)}, f32[2,256]{1,0:T(2,128)}, u32[]{:S(2)}) copy-start(f32[2,256]{1,0:T(2,128)} %get-tuple-element.50) | copy-start | bytes 6148
  42.7 5.4 %copy-start.16 = (f32[2,256]{1,0:T(2,128)S(1)}, f32[2,256]{1,0:T(2,128)}, u32[]{:S(2)}) copy-start(f32[2,256]{1,0:T(2,128)} %get-tuple-element.51) | copy-start | bytes 6148
  42.7 5.4 %copy-start.17 = (f32[2,256]{1,0:T(2,128)S(1)}, f32[2,256]{1,0:T(2,128)}, u32[]{:S(2)}) copy-start(f32[2,256]{1,0:T(2,128)} %get-tuple-element.52) | copy-start | bytes 6148
  42.7 5.7 %copy-start.2 = (bf16[3,3,256,256]{2,3,1,0:T(8,128)(2,1)S(1)}, bf16[3,3,256,256]{2,3,1,0:T(8,128)(2,1)}, u32[]{:S(2)}) copy-start(bf16[3,3,256,256]{2,3,1,0:T(8,128)(2,1)} %rev.3) | copy-start | bytes 3538948
  51.8 0.7 collective-permute-start.4
  54.8 2.2 %collective-permute-start.5 = (bf16[2,4,64,256]{3,2,1,0:T(8,128)(2,1)S(1)}, bf16[2,4,64,256]{3,2,1,0:T(8,128)(2,1)S(1)}, u32[]{:S(2)}, u32[]{:S(2)}) collective-permute-start(bf16[2,4,64,256]{3,2,1,0:T(8,128)(2,1)S(1)} %fusion.93), channel_id=1, source_target_pairs={{8,4},{9,5},{10,6},{11,7},{24,20},{25,21},{26,22},{27,23},{40,36},... | collective-permute-start | bytes 786440 | tf_op jit(solution)/shard_map/ppermute | solution.py:202
  55.4 23.6 %collective-permute-start.7 = (bf16[2,4,64,256]{3,2,1,0:T(8,128)(2,1)S(1)}, bf16[2,4,64,256]{3,2,1,0:T(8,128)(2,1)S(1)}, u32[]{:S(2)}, u32[]{:S(2)}) collective-permute-start(bf16[2,4,64,256]{3,2,1,0:T(8,128)(2,1)S(1)} %fusion.90), channel_id=1, source_target_pairs={{12,0},{13,1},{14,2},{15,3},{28,16},{29,17},{30,18},{31,19},{44,32... | collective-permute-start | bytes 786440 | tf_op jit(solution)/shard_map/ppermute | solution.py:211
  59.2 29.7 %collective-permute-start.6 = (bf16[2,4,64,256]{3,2,1,0:T(8,128)(2,1)S(1)}, bf16[2,4,64,256]{3,2,1,0:T(8,128)(2,1)}, u32[]{:S(2)}, u32[]{:S(2)}) collective-permute-start(bf16[2,4,64,256]{3,2,1,0:T(8,128)(2,1)S(1)} %fusion.96), channel_id=1, source_target_pairs={{4,0},{5,1},{6,2},{7,3},{20,16},{21,17},{22,18},{23,19},{36,32},{3... | collective-permute-start | bytes 786440 | tf_op jit(solution)/shard_map/ppermute | solution.py:202
  93.0 6.8 %copy-start.6 = (f32[2,128]{1,0:T(2,128)S(1)}, f32[2,128]{1,0:T(2,128)}, u32[]{:S(2)}) copy-start(f32[2,128]{1,0:T(2,128)} %copy-done.5) | copy-start | bytes 3076
  102.2 8.3 %collective-permute-start.8 = (f32[368,256]{1,0:T(8,128)S(1)}, f32[368,256]{1,0:T(8,128)S(1)}, u32[]{:S(2)}, u32[]{:S(2)}) collective-permute-start(f32[368,256]{1,0:T(8,128)S(1)} %constant_dynamic-slice_fusion.1), channel_id=1, source_target_pairs={{0,16},{16,0},{32,48},{48,32},{1,17},{17,1},{33,49},{49,33},{2,18}... | collective-permute-start | bytes 1130504 | tf_op jit(solution)/shard_map/ppermute | solution.py:243
  110.7 8.6 %collective-permute-start.9 = (f32[184,256]{1,0:T(8,128)S(1)}, f32[184,256]{1,0:T(8,128)S(1)}, u32[]{:S(2)}, u32[]{:S(2)}) collective-permute-start(f32[184,256]{1,0:T(8,128)S(1)} %constant_dynamic-slice_fusion), channel_id=1, source_target_pairs={{0,32},{16,48},{32,0},{48,16},{1,33},{17,49},{33,1},{49,17},{2,34}... | collective-permute-start | bytes 565256 | tf_op jit(solution)/shard_map/ppermute | solution.py:243
  119.3 6.3 %collective-permute-start.10 = (f32[184,256]{1,0:T(8,128)S(1)}, f32[184,256]{1,0:T(8,128)S(1)}, u32[]{:S(2)}, u32[]{:S(2)}) collective-permute-start(f32[184,256]{1,0:T(8,128)S(1)} %dynamic-slice_add_fusion.1), channel_id=1, source_target_pairs={{0,64},{64,0},{128,192},{192,128},{256,320},{320,256},{384,448},{4... | collective-permute-start | bytes 565256 | tf_op jit(solution)/shard_map/ppermute | solution.py:252
  125.6 8.3 %collective-permute-start.11 = (f32[184,256]{1,0:T(8,128)S(1)}, f32[184,256]{1,0:T(8,128)S(1)}, u32[]{:S(2)}, u32[]{:S(2)}) collective-permute-start(f32[184,256]{1,0:T(8,128)S(1)} %add.292), channel_id=1, source_target_pairs={{0,128},{64,192},{128,0},{192,64},{256,384},{320,448},{384,256},{4... | collective-permute-start | bytes 565256 | tf_op jit(solution)/shard_map/ppermute | solution.py:252
  134.0 14.4 %collective-permute-start.12 = (f32[184,256]{1,0:T(8,128)S(1)}, f32[184,256]{1,0:T(8,128)S(1)}, u32[]{:S(2)}, u32[]{:S(2)}) collective-permute-start(f32[184,256]{1,0:T(8,128)S(1)} %add.293), channel_id=1, source_target_pairs={{0,256},{64,320},{128,384},{192,448},{256,0},{320,64},{384,128},{4... | collective-permute-start | bytes 565256 | tf_op jit(solution)/shard_map/ppermute | solution.py:252
  148.4 6.8 %collective-permute-start.13 = (bf16[184,256]{1,0:T(8,128)(2,1)S(1)}, bf16[184,256]{1,0:T(8,128)(2,1)S(1)}, u32[]{:S(2)}, u32[]{:S(2)}) collective-permute-start(bf16[184,256]{1,0:T(8,128)(2,1)S(1)} %add_convert_fusion.2), channel_id=1, source_target_pairs={{0,32},{16,48},{32,0},{48,16},{1,33},{17,49},{33,1},{49,17},{2,34}... | collective-permute-start | bytes 282632 | tf_op jit(solution)/shard_map/ppermute | solution.py:262
  155.3 6.3 %collective-permute-start.14 = (bf16[368,256]{1,0:T(8,128)(2,1)S(1)}, bf16[368,256]{1,0:T(8,128)(2,1)S(1)}, u32[]{:S(2)}, u32[]{:S(2)}) collective-permute-start(bf16[368,256]{1,0:T(8,128)(2,1)S(1)} %maximum_select_fusion.3), channel_id=1, source_target_pairs={{0,16},{16,0},{32,48},{48,32},{1,17},{17,1},{33,49},{49,33},{2,18}... | collective-permute-start | bytes 565256 | tf_op jit(solution)/shard_map/ppermute | solution.py:262
  161.8 15.1 %collective-permute-start.15 = (bf16[736,256]{1,0:T(8,128)(2,1)S(1)}, bf16[736,256]{1,0:T(8,128)(2,1)S(1)}, u32[]{:S(2)}, u32[]{:S(2)}) collective-permute-start(bf16[736,256]{1,0:T(8,128)(2,1)S(1)} %maximum_select_fusion.2), channel_id=1, source_target_pairs={{0,2},{1,3},{2,0},{3,1},{4,6},{5,7},{6,4},{7,5},{8,10},{9,11},{10,... | collective-permute-start | bytes 1130504 | tf_op jit(solution)/shard_map/ppermute | solution.py:262
  177.2 19.7 %collective-permute-start.16 = (bf16[1472,256]{1,0:T(8,128)(2,1)S(1)}, bf16[1472,256]{1,0:T(8,128)(2,1)S(1)}, u32[]{:S(2)}, u32[]{:S(2)}) collective-permute-start(bf16[1472,256]{1,0:T(8,128)(2,1)S(1)} %maximum_select_fusion.1), channel_id=1, source_target_pairs={{0,1},{1,0},{2,3},{3,2},{4,5},{5,4},{6,7},{7,6},{8,9},{9,8},{10,11... | collective-permute-start | bytes 2261000 | tf_op jit(solution)/shard_map/ppermute | solution.py:262
  (3 other events, 3.4 us)

commit v9 on v7

--- a/solution.py
+++ b/solution.py
@@ -253,13 +253,15 @@
     return flat
 
 
-def butterfly_gather(flat, axis, steps):
+def butterfly_gather(flat, axis, steps, dim=0):
     count = lax.axis_size(axis)
     index = lax.axis_index(axis)
     for step in steps:
         bit = (index // step) % 2
         got = lax.ppermute(flat, axis, [(j, j ^ step) for j in range(count)])
-        flat = jnp.where(bit == 1, jnp.concatenate([got, flat]), jnp.concatenate([flat, got]))
+        flat = jnp.where(
+            bit == 1, jnp.concatenate([got, flat], axis=dim), jnp.concatenate([flat, got], axis=dim)
+        )
     return flat
 
 
@@ -286,10 +288,11 @@
     flat = jnp.concatenate(parts, axis=0)
     flat = butterfly_scatter(flat, "dx")
     flat = butterfly_sum(flat, "dy")
-    flat = butterfly_gather(flat.astype(jnp.bfloat16), "dx", descending(lax.axis_size("dx")))
     space_count = lax.axis_size("space")
-    flat = butterfly_gather(flat, "space", descending(space_count))
-    flat = flat.reshape(space_count, padded_rows, channels).astype(jnp.float32)
+    flat = butterfly_gather(flat.astype(jnp.bfloat16), "space", descending(space_count))
+    flat = flat.reshape(space_count, -1, channels)
+    flat = butterfly_gather(flat, "dx", descending(lax.axis_size("dx")), dim=1)
+    flat = flat.astype(jnp.float32)
     weight_rows = weight_grad.shape[0]
     emb_rows = emb_grad.size // channels
     conv = flat[:, :weight_rows].reshape(1, 3, 3, channels, channels)

time: 199 us -> 213 us (1.070)
  waiting for transfers between devices: 63.2 us -> 74.8 us
    ppermute x4, waiting for transfers between devices: 16.1 us -> 27.7 us  [butterfly_gather(): got = lax.ppermute(flat, axis, [(j, j ^ step) for j in range(count)])]
where the time goes in v9:
time: 213 us; the launch traced here: 212 us
  waiting for transfers between devices  74.8 us (35%)
  starting transfers between devices  70.2 us (33%)
  blocking collectives  22.3 us (10%)
  matrix products  20.2 us (9%)
  local copies, waits for them, and re-layouts  13.6 us (6%)
  other arithmetic  8.41 us (4%)
    ppermute x4, starting transfers between devices, butterfly_gather(): got = lax.ppermute(flat, axis, [(j, j ^ step) for j in range(count)])  33.9 us
    ppermute x4, waiting for transfers between devices, butterfly_gather(): got = lax.ppermute(flat, axis, [(j, j ^ step) for j in range(count)])  27.7 us
    ppermute x3, starting transfers between devices, butterfly_sum(): lax.ppermute(flat, axis, [(j, j ^ step) for j in range(count)])  15.8 us
    ppermute x1, waiting for transfers between devices, per_device(): skip_grad = lax.ppermute(d_input, 'section', [(last, 0)])  14.4 us
    ppermute x3, waiting for transfers between devices, butterfly_sum(): lax.ppermute(flat, axis, [(j, j ^ step) for j in range(count)])  13.2 us
    all_gather x1, blocking collectives, per_device(): images = lax.all_gather(images, 'space', axis=1, tiled=True)  12.8 us
    dot_general x7, matrix products, convolve(): jnp.dot(flat, matrix, preferred_element_type=jnp.float32)  11.6 us
    ppermute x3, waiting for transfers between devices, per_device(): upstream = lax.ppermute(carried, 'section', [(active + 1, active)])  9.95 us
  transfers between devices with their start and end apart: 17, of which 11 were waited for; matrix products, arithmetic and copies ran while one was open for 7% of the time, Pallas kernels for 0%

profile of v9, /device:TPU:1, one launch (start us, length us, event | category | flops | bytes accessed | tf_op | source)
XLA Modules:
  0.0 211.5 jit_solution(10379251247038305617)
XLA Ops:
  0.7 12.8 %all_gather.6 = bf16[2,4,64,256]{3,2,1,0:T(8,128)(2,1)S(1)} all-gather(bf16[2,1,64,256]{3,2,1,0:T(8,128)(2,1)} %param.6), channel_id=1, replica_groups=mesh['dy'=8,'dx'=4,'section'=4,'space'=4] {'space'}, dimensions={1}, use_global_device_ids=true | all-gather | bytes 327680 | tf_op jit(solution)/shard_map/all_gather | solution.py:165
  17.9 1.5 fusion.1
  19.4 5.3 %collective-permute-start.3 = (bf16[2,4,64,256]{3,2,1,0:T(8,128)(2,1)}, bf16[2,4,64,256]{3,2,1,0:T(8,128)(2,1)S(1)}, u32[]{:S(2)}, u32[]{:S(2)}) collective-permute-start(bf16[2,4,64,256]{3,2,1,0:T(8,128)(2,1)} %fusion.1), channel_id=1, source_target_pairs={{0,12},{1,13},{2,14},{3,15},{16,28},{17,29},{18,30},{19,31},{32,44... | collective-permute-start | bytes 786440 | tf_op jit(solution)/shard_map/ppermute | solution.py:190
  26.0 9.4 %all_gather.7 = bf16[2,4,64,256]{3,2,1,0:T(8,128)(2,1)S(1)} all-gather(bf16[2,1,64,256]{3,2,1,0:T(8,128)(2,1)S(1)} %copy-done.6), channel_id=1, replica_groups=mesh['dy'=8,'dx'=4,'section'=4,'space'=4] {'space'}, dimensions={1}, use_global_device_ids=true | all-gather | bytes 327680 | tf_op jit(solution)/shard_map/all_gather | solution.py:166
  41.4 1.5 fusion.3
  44.3 1.4 copy-done.7
  45.7 1.6 copy.9
  51.9 1.7 divide_multiply_fusion
  53.7 3.3 %fusion.61 = (f32[2,256]{1,0:T(2,128)}, f32[256]{0:T(256)}, f32[2,256]{1,0:T(2,128)S(1)}, f32[2,256]{1,0:T(2,128)S(1)}, f32[2,256]{1,0:T(2,128)}, /*index=5*/f32[2,4,64,256]{3,2,1,0:T(8,128)S(1)}) fusion(bf16[2,4,64,256]{3,2,1,0:T(8,128)(2,1)S(1)} %select_select_fusion.1, f32[2,256]{1,0:T(2,128)S(1)} %rsqrt.26, f32[2,256]{1,0:T(2,128)S(1)} %get-tuple-element.33, ...), kind=kOutput, calls=%fused_computation.139 | convolution fusion | flops 607254272 | bytes 4343808 | tf_op jit(solution)/shard_map/dot_general | solution.py:74
  59.5 1.7 fusion.60
  62.6 1.5 collective-permute-start.7
  64.5 1.7 fusion.59
  68.9 14.4 %collective-permute-done.7 = bf16[2,4,64,256]{3,2,1,0:T(8,128)(2,1)} collective-permute-done((bf16[2,4,64,256]{3,2,1,0:T(8,128)(2,1)}, bf16[2,4,64,256]{3,2,1,0:T(8,128)(2,1)}, u32[]{:S(2)}, u32[]{:S(2)}) %collective-permute-start.7) | collective-permute-done | bytes 262176 | tf_op jit(solution)/shard_map/ppermute | solution.py:210
  83.4 9.9 %collective-permute-done.6 = bf16[2,4,64,256]{3,2,1,0:T(8,128)(2,1)} collective-permute-done((bf16[2,4,64,256]{3,2,1,0:T(8,128)(2,1)S(1)}, bf16[2,4,64,256]{3,2,1,0:T(8,128)(2,1)}, u32[]{:S(2)}, u32[]{:S(2)}) %collective-permute-start.6) | collective-permute-done | bytes 262176 | tf_op jit(solution)/shard_map/ppermute | solution.py:201
  99.3 3.1 %collective-permute-start.8 = (f32[368,256]{1,0:T(8,128)S(1)}, f32[368,256]{1,0:T(8,128)S(1)}, u32[]{:S(2)}, u32[]{:S(2)}) collective-permute-start(f32[368,256]{1,0:T(8,128)S(1)} %constant_dynamic-slice_fusion.1), channel_id=1, source_target_pairs={{0,16},{16,0},{32,48},{48,32},{1,17},{17,1},{33,49},{49,33},{2,18}... | collective-permute-start | bytes 1130504 | tf_op jit(solution)/shard_map/ppermute | solution.py:242
  102.5 5.2 %collective-permute-done.8 = f32[368,256]{1,0:T(8,128)S(1)} collective-permute-done((f32[368,256]{1,0:T(8,128)S(1)}, f32[368,256]{1,0:T(8,128)S(1)}, u32[]{:S(2)}, u32[]{:S(2)}) %collective-permute-start.8) | collective-permute-done | bytes 376864 | tf_op jit(solution)/shard_map/ppermute | solution.py:242
  107.8 4.7 %collective-permute-start.9 = (f32[184,256]{1,0:T(8,128)S(1)}, f32[184,256]{1,0:T(8,128)S(1)}, u32[]{:S(2)}, u32[]{:S(2)}) collective-permute-start(f32[184,256]{1,0:T(8,128)S(1)} %constant_dynamic-slice_fusion), channel_id=1, source_target_pairs={{0,32},{16,48},{32,0},{48,16},{1,33},{17,49},{33,1},{49,17},{2,34}... | collective-permute-start | bytes 565256 | tf_op jit(solution)/shard_map/ppermute | solution.py:242
  112.4 4.3 %collective-permute-done.9 = f32[184,256]{1,0:T(8,128)S(1)} collective-permute-done((f32[184,256]{1,0:T(8,128)S(1)}, f32[184,256]{1,0:T(8,128)S(1)}, u32[]{:S(2)}, u32[]{:S(2)}) %collective-permute-start.9) | collective-permute-done | bytes 188448 | tf_op jit(solution)/shard_map/ppermute | solution.py:242
  116.7 3.2 %collective-permute-start.10 = (f32[184,256]{1,0:T(8,128)S(1)}, f32[184,256]{1,0:T(8,128)S(1)}, u32[]{:S(2)}, u32[]{:S(2)}) collective-permute-start(f32[184,256]{1,0:T(8,128)S(1)} %dynamic-slice_add_fusion.1), channel_id=1, source_target_pairs={{0,64},{64,0},{128,192},{192,128},{256,320},{320,256},{384,448},{4... | collective-permute-start | bytes 565256 | tf_op jit(solution)/shard_map/ppermute | solution.py:251
  120.0 3.1 %collective-permute-done.10 = f32[184,256]{1,0:T(8,128)S(1)} collective-permute-done((f32[184,256]{1,0:T(8,128)S(1)}, f32[184,256]{1,0:T(8,128)S(1)}, u32[]{:S(2)}, u32[]{:S(2)}) %collective-permute-start.10) | collective-permute-done | bytes 188448 | tf_op jit(solution)/shard_map/ppermute | solution.py:251
  123.1 4.2 %collective-permute-start.11 = (f32[184,256]{1,0:T(8,128)S(1)}, f32[184,256]{1,0:T(8,128)S(1)}, u32[]{:S(2)}, u32[]{:S(2)}) collective-permute-start(f32[184,256]{1,0:T(8,128)S(1)} %add.292), channel_id=1, source_target_pairs={{0,128},{64,192},{128,0},{192,64},{256,384},{320,448},{384,256},{4... | collective-permute-start | bytes 565256 | tf_op jit(solution)/shard_map/ppermute | solution.py:251
  127.3 4.1 %collective-permute-done.11 = f32[184,256]{1,0:T(8,128)S(1)} collective-permute-done((f32[184,256]{1,0:T(8,128)S(1)}, f32[184,256]{1,0:T(8,128)S(1)}, u32[]{:S(2)}, u32[]{:S(2)}) %collective-permute-start.11) | collective-permute-done | bytes 188448 | tf_op jit(solution)/shard_map/ppermute | solution.py:251
  131.4 8.4 %collective-permute-start.12 = (f32[184,256]{1,0:T(8,128)S(1)}, f32[184,256]{1,0:T(8,128)S(1)}, u32[]{:S(2)}, u32[]{:S(2)}) collective-permute-start(f32[184,256]{1,0:T(8,128)S(1)} %add.293), channel_id=1, source_target_pairs={{0,256},{64,320},{128,384},{192,448},{256,0},{320,64},{384,128},{4... | collective-permute-start | bytes 565256 | tf_op jit(solution)/shard_map/ppermute | solution.py:251
  139.8 6.0 %collective-permute-done.12 = f32[184,256]{1,0:T(8,128)S(1)} collective-permute-done((f32[184,256]{1,0:T(8,128)S(1)}, f32[184,256]{1,0:T(8,128)S(1)}, u32[]{:S(2)}, u32[]{:S(2)}) %collective-permute-start.12) | collective-permute-done | bytes 188448 | tf_op jit(solution)/shard_map/ppermute | solution.py:251
  145.9 10.1 %collective-permute-start.13 = (bf16[184,256]{1,0:T(8,128)(2,1)S(1)}, bf16[184,256]{1,0:T(8,128)(2,1)S(1)}, u32[]{:S(2)}, u32[]{:S(2)}) collective-permute-start(bf16[184,256]{1,0:T(8,128)(2,1)S(1)} %add_convert_fusion.2), channel_id=1, source_target_pairs={{0,2},{1,3},{2,0},{3,1},{4,6},{5,7},{6,4},{7,5},{8,10},{9,11},{10,... | collective-permute-start | bytes 282632 | tf_op jit(solution)/shard_map/ppermute | solution.py:261
  156.0 2.2 %collective-permute-done.13 = bf16[184,256]{1,0:T(8,128)(2,1)S(1)} collective-permute-done((bf16[184,256]{1,0:T(8,128)(2,1)S(1)}, bf16[184,256]{1,0:T(8,128)(2,1)S(1)}, u32[]{:S(2)}, u32[]{:S(2)}) %collective-permute-start.13) | collective-permute-done | bytes 94240 | tf_op jit(solution)/shard_map/ppermute | solution.py:261
  158.3 15.9 %collective-permute-start.14 = (bf16[368,256]{1,0:T(8,128)(2,1)S(1)}, bf16[368,256]{1,0:T(8,128)(2,1)S(1)}, u32[]{:S(2)}, u32[]{:S(2)}) collective-permute-start(bf16[368,256]{1,0:T(8,128)(2,1)S(1)} %maximum_select_fusion.3), channel_id=1, source_target_pairs={{0,1},{1,0},{2,3},{3,2},{4,5},{5,4},{6,7},{7,6},{8,9},{9,8},{10,11... | collective-permute-start | bytes 565256 | tf_op jit(solution)/shard_map/ppermute | solution.py:261
  175.4 4.7 %collective-permute-start.15 = (bf16[4,184,256]{2,1,0:T(8,128)(2,1)S(1)}, bf16[4,184,256]{2,1,0:T(8,128)(2,1)S(1)}, u32[]{:S(2)}, u32[]{:S(2)}) collective-permute-start(bf16[4,184,256]{2,1,0:T(8,128)(2,1)S(1)} %bitcast.49), channel_id=1, source_target_pairs={{0,32},{16,48},{32,0},{48,16},{1,33},{17,49},{33,1},{49,17},{2,34}... | collective-permute-start | bytes 1130504 | tf_op jit(solution)/shard_map/ppermute | solution.py:261
  180.1 8.7 %collective-permute-done.15 = bf16[4,184,256]{2,1,0:T(8,128)(2,1)S(1)} collective-permute-done((bf16[4,184,256]{2,1,0:T(8,128)(2,1)S(1)}, bf16[4,184,256]{2,1,0:T(8,128)(2,1)S(1)}, u32[]{:S(2)}, u32[]{:S(2)}) %collective-permute-start.15) | collective-permute-done | bytes 376864 | tf_op jit(solution)/shard_map/ppermute | solution.py:261
  189.1 3.2 %collective-permute-start.16 = (bf16[4,368,256]{2,1,0:T(8,128)(2,1)S(1)}, bf16[4,368,256]{2,1,0:T(8,128)(2,1)S(1)}, u32[]{:S(2)}, u32[]{:S(2)}) collective-permute-start(bf16[4,368,256]{2,1,0:T(8,128)(2,1)S(1)} %maximum_select_fusion.1), channel_id=1, source_target_pairs={{0,16},{16,0},{32,48},{48,32},{1,17},{17,1},{33,49},{49,33},{2,18}... | collective-permute-start | bytes 2261000 | tf_op jit(solution)/shard_map/ppermute | solution.py:261
  192.3 15.8 %collective-permute-done.16 = bf16[4,368,256]{2,1,0:T(8,128)(2,1)S(1)} collective-permute-done((bf16[4,368,256]{2,1,0:T(8,128)(2,1)S(1)}, bf16[4,368,256]{2,1,0:T(8,128)(2,1)S(1)}, u32[]{:S(2)}, u32[]{:S(2)}) %collective-permute-start.16) | collective-permute-done | bytes 753696 | tf_op jit(solution)/shard_map/ppermute | solution.py:261
  208.4 1.6 slice.298
  (204 shorter events, 33.4 us)
Async XLA Ops:
  0.6 13.7 %copy-start = (bf16[1,256,512]{2,1,0:T(8,128)(2,1)S(1)}, bf16[1,256,512]{2,1,0:T(8,128)(2,1)}, u32[]{:S(2)}) copy-start(bf16[1,256,512]{2,1,0:T(8,128)(2,1)} %param.11) | copy-start | bytes 786436
  0.6 16.2 %copy-start.5 = (f32[1,256]{1,0:T(1,128)S(1)}, f32[1,256]{1,0:T(1,128)}, u32[]{:S(2)}) copy-start(f32[1,256]{1,0:T(1,128)} %param.10) | copy-start | bytes 3076
  0.7 38.9 %copy-start.22 = (s32[256]{0:T(256)}, s32[256]{0:T(256)S(1)}, u32[]{:S(2)}) copy-start(s32[256]{0:T(256)S(1)} %and_select_fusion) | copy-start | bytes 3076
  14.3 1.4 copy-start.9
  14.3 1.4 copy-start.11
  16.7 1.3 copy-start.1
  17.3 8.7 %copy-start.6 = (bf16[2,1,64,256]{3,2,1,0:T(8,128)(2,1)S(1)}, bf16[2,1,64,256]{3,2,1,0:T(8,128)(2,1)}, u32[]{:S(2)}) copy-start(bf16[2,1,64,256]{3,2,1,0:T(8,128)(2,1)} %param.8) | copy-start | bytes 196612
  19.4 30.4 %collective-permute-start.3 = (bf16[2,4,64,256]{3,2,1,0:T(8,128)(2,1)}, bf16[2,4,64,256]{3,2,1,0:T(8,128)(2,1)S(1)}, u32[]{:S(2)}, u32[]{:S(2)}) collective-permute-start(bf16[2,4,64,256]{3,2,1,0:T(8,128)(2,1)} %fusion.1), channel_id=1, source_target_pairs={{0,12},{1,13},{2,14},{3,15},{16,28},{17,29},{18,30},{19,31},{32,44... | collective-permute-start | bytes 786440 | tf_op jit(solution)/shard_map/ppermute | solution.py:190
  24.7 10.9 %collective-permute-start = (bf16[2,4,64,256]{3,2,1,0:T(8,128)(2,1)}, bf16[2,4,64,256]{3,2,1,0:T(8,128)(2,1)S(1)}, u32[]{:S(2)}, u32[]{:S(2)}) collective-permute-start(bf16[2,4,64,256]{3,2,1,0:T(8,128)(2,1)} %fusion.1), channel_id=1, source_target_pairs={{0,4},{1,5},{2,6},{3,7},{16,20},{17,21},{18,22},{19,23},{32,36},{3... | collective-permute-start | bytes 786440 | tf_op jit(solution)/shard_map/ppermute | solution.py:185
  35.9 1.7 copy-start.25
  38.4 0.9 collective-permute-start.1
  42.9 7.0 %collective-permute-start.2 = (bf16[2,4,64,256]{3,2,1,0:T(8,128)(2,1)}, bf16[2,4,64,256]{3,2,1,0:T(8,128)(2,1)}, u32[]{:S(2)}, u32[]{:S(2)}) collective-permute-start(bf16[2,4,64,256]{3,2,1,0:T(8,128)(2,1)} %fusion.3), channel_id=1, source_target_pairs={{8,12},{9,13},{10,14},{11,15},{24,28},{25,29},{26,30},{27,31},{40,... | collective-permute-start | bytes 786440 | tf_op jit(solution)/shard_map/ppermute | solution.py:185
  44.3 1.4 copy-start.7
  48.3 5.3 %copy-start.2 = (bf16[3,3,256,256]{2,3,1,0:T(8,128)(2,1)S(1)}, bf16[3,3,256,256]{2,3,1,0:T(8,128)(2,1)}, u32[]{:S(2)}) copy-start(bf16[3,3,256,256]{2,3,1,0:T(8,128)(2,1)} %rev.3) | copy-start | bytes 3538948
  50.9 2.7 %copy-start.3 = (bf16[2,4,64,256]{3,2,1,0:T(8,128)(2,1)}, bf16[2,4,64,256]{3,2,1,0:T(8,128)(2,1)S(1)}, u32[]{:S(2)}) copy-start(bf16[2,4,64,256]{3,2,1,0:T(8,128)(2,1)S(1)} %get-tuple-element.34) | copy-start | bytes 786436
  53.6 12.8 %copy-start.27 = (f32[2,256]{1,0:T(2,128)}, f32[2,256]{1,0:T(2,128)S(1)}, u32[]{:S(2)}) copy-start(f32[2,256]{1,0:T(2,128)S(1)} %get-tuple-element.33) | copy-start | bytes 6148
  53.6 3.3 %copy-start.23 = (s32[256]{0:T(256)S(1)}, s32[256]{0:T(256)}, u32[]{:S(2)}) copy-start(s32[256]{0:T(256)} %copy-done.22) | copy-start | bytes 3076
  58.4 0.7 collective-permute-start.4
  61.9 2.2 %collective-permute-start.5 = (bf16[2,4,64,256]{3,2,1,0:T(8,128)(2,1)S(1)}, bf16[2,4,64,256]{3,2,1,0:T(8,128)(2,1)S(1)}, u32[]{:S(2)}, u32[]{:S(2)}) collective-permute-start(bf16[2,4,64,256]{3,2,1,0:T(8,128)(2,1)S(1)} %fusion.94), channel_id=1, source_target_pairs={{8,4},{9,5},{10,6},{11,7},{24,20},{25,21},{26,22},{27,23},{40,36},... | collective-permute-start | bytes 786440 | tf_op jit(solution)/shard_map/ppermute | solution.py:201
  62.6 20.8 %collective-permute-start.7 = (bf16[2,4,64,256]{3,2,1,0:T(8,128)(2,1)}, bf16[2,4,64,256]{3,2,1,0:T(8,128)(2,1)}, u32[]{:S(2)}, u32[]{:S(2)}) collective-permute-start(bf16[2,4,64,256]{3,2,1,0:T(8,128)(2,1)} %fusion.91), channel_id=1, source_target_pairs={{12,0},{13,1},{14,2},{15,3},{28,16},{29,17},{30,18},{31,19},{44,32... | collective-permute-start | bytes 786440 | tf_op jit(solution)/shard_map/ppermute | solution.py:210
  66.9 26.4 %collective-permute-start.6 = (bf16[2,4,64,256]{3,2,1,0:T(8,128)(2,1)S(1)}, bf16[2,4,64,256]{3,2,1,0:T(8,128)(2,1)}, u32[]{:S(2)}, u32[]{:S(2)}) collective-permute-start(bf16[2,4,64,256]{3,2,1,0:T(8,128)(2,1)S(1)} %fusion.97), channel_id=1, source_target_pairs={{4,0},{5,1},{6,2},{7,3},{20,16},{21,17},{22,18},{23,19},{36,32},{3... | collective-permute-start | bytes 786440 | tf_op jit(solution)/shard_map/ppermute | solution.py:201
  95.6 1.3 copy-start.10
  95.6 1.3 copy-start.12
  99.3 8.3 %collective-permute-start.8 = (f32[368,256]{1,0:T(8,128)S(1)}, f32[368,256]{1,0:T(8,128)S(1)}, u32[]{:S(2)}, u32[]{:S(2)}) collective-permute-start(f32[368,256]{1,0:T(8,128)S(1)} %constant_dynamic-slice_fusion.1), channel_id=1, source_target_pairs={{0,16},{16,0},{32,48},{48,32},{1,17},{17,1},{33,49},{49,33},{2,18}... | collective-permute-start | bytes 1130504 | tf_op jit(solution)/shard_map/ppermute | solution.py:242
  107.8 9.0 %collective-permute-start.9 = (f32[184,256]{1,0:T(8,128)S(1)}, f32[184,256]{1,0:T(8,128)S(1)}, u32[]{:S(2)}, u32[]{:S(2)}) collective-permute-start(f32[184,256]{1,0:T(8,128)S(1)} %constant_dynamic-slice_fusion), channel_id=1, source_target_pairs={{0,32},{16,48},{32,0},{48,16},{1,33},{17,49},{33,1},{49,17},{2,34}... | collective-permute-start | bytes 565256 | tf_op jit(solution)/shard_map/ppermute | solution.py:242
  116.7 6.3 %collective-permute-start.10 = (f32[184,256]{1,0:T(8,128)S(1)}, f32[184,256]{1,0:T(8,128)S(1)}, u32[]{:S(2)}, u32[]{:S(2)}) collective-permute-start(f32[184,256]{1,0:T(8,128)S(1)} %dynamic-slice_add_fusion.1), channel_id=1, source_target_pairs={{0,64},{64,0},{128,192},{192,128},{256,320},{320,256},{384,448},{4... | collective-permute-start | bytes 565256 | tf_op jit(solution)/shard_map/ppermute | solution.py:251
  123.1 8.3 %collective-permute-start.11 = (f32[184,256]{1,0:T(8,128)S(1)}, f32[184,256]{1,0:T(8,128)S(1)}, u32[]{:S(2)}, u32[]{:S(2)}) collective-permute-start(f32[184,256]{1,0:T(8,128)S(1)} %add.292), channel_id=1, source_target_pairs={{0,128},{64,192},{128,0},{192,64},{256,384},{320,448},{384,256},{4... | collective-permute-start | bytes 565256 | tf_op jit(solution)/shard_map/ppermute | solution.py:251
  131.4 14.4 %collective-permute-start.12 = (f32[184,256]{1,0:T(8,128)S(1)}, f32[184,256]{1,0:T(8,128)S(1)}, u32[]{:S(2)}, u32[]{:S(2)}) collective-permute-start(f32[184,256]{1,0:T(8,128)S(1)} %add.293), channel_id=1, source_target_pairs={{0,256},{64,320},{128,384},{192,448},{256,0},{320,64},{384,128},{4... | collective-permute-start | bytes 565256 | tf_op jit(solution)/shard_map/ppermute | solution.py:251
  145.9 12.4 %collective-permute-start.13 = (bf16[184,256]{1,0:T(8,128)(2,1)S(1)}, bf16[184,256]{1,0:T(8,128)(2,1)S(1)}, u32[]{:S(2)}, u32[]{:S(2)}) collective-permute-start(bf16[184,256]{1,0:T(8,128)(2,1)S(1)} %add_convert_fusion.2), channel_id=1, source_target_pairs={{0,2},{1,3},{2,0},{3,1},{4,6},{5,7},{6,4},{7,5},{8,10},{9,11},{10,... | collective-permute-start | bytes 282632 | tf_op jit(solution)/shard_map/ppermute | solution.py:261
  158.3 16.9 %collective-permute-start.14 = (bf16[368,256]{1,0:T(8,128)(2,1)S(1)}, bf16[368,256]{1,0:T(8,128)(2,1)S(1)}, u32[]{:S(2)}, u32[]{:S(2)}) collective-permute-start(bf16[368,256]{1,0:T(8,128)(2,1)S(1)} %maximum_select_fusion.3), channel_id=1, source_target_pairs={{0,1},{1,0},{2,3},{3,2},{4,5},{5,4},{6,7},{7,6},{8,9},{9,8},{10,11... | collective-permute-start | bytes 565256 | tf_op jit(solution)/shard_map/ppermute | solution.py:261
  175.4 13.4 %collective-permute-start.15 = (bf16[4,184,256]{2,1,0:T(8,128)(2,1)S(1)}, bf16[4,184,256]{2,1,0:T(8,128)(2,1)S(1)}, u32[]{:S(2)}, u32[]{:S(2)}) collective-permute-start(bf16[4,184,256]{2,1,0:T(8,128)(2,1)S(1)} %bitcast.49), channel_id=1, source_target_pairs={{0,32},{16,48},{32,0},{48,16},{1,33},{17,49},{33,1},{49,17},{2,34}... | collective-permute-start | bytes 1130504 | tf_op jit(solution)/shard_map/ppermute | solution.py:261
  189.1 19.0 %collective-permute-start.16 = (bf16[4,368,256]{2,1,0:T(8,128)(2,1)S(1)}, bf16[4,368,256]{2,1,0:T(8,128)(2,1)S(1)}, u32[]{:S(2)}, u32[]{:S(2)}) collective-permute-start(bf16[4,368,256]{2,1,0:T(8,128)(2,1)S(1)} %maximum_select_fusion.1), channel_id=1, source_target_pairs={{0,16},{16,0},{32,48},{48,32},{1,17},{17,1},{33,49},{49,33},{2,18}... | collective-permute-start | bytes 2261000 | tf_op jit(solution)/shard_map/ppermute | solution.py:261
  (16 other events, 17.4 us)

commit v10 on v7

--- a/solution.py
+++ b/solution.py
@@ -123,6 +123,17 @@
     return normed * (1.0 + scales[:, None, None, :]) + shifts[:, None, None, :]
 
 
+def conv_same(tensor, kernel):
+    return lax.conv_general_dilated(
+        tensor,
+        kernel,
+        (1, 1),
+        ((1, 1), (1, 1)),
+        dimension_numbers=("NHWC", "HWIO", "NHWC"),
+        preferred_element_type=jnp.float32,
+    )
+
+
 def block_forward(inputs, flat_weight, gains, scales, shifts, cell_count):
     tensor = inputs.astype(jnp.float32)
     blocks = group_blocks(tensor.shape[3])
@@ -131,7 +142,7 @@
     pre_act = normalize_spread(tensor, first_c, square_c, gains, scales, shifts, cell_count)
     activation = jax.nn.silu(pre_act).astype(jnp.bfloat16)
     padded = pad_both(activation)
-    output = (tensor + convolve(padded, flat_weight)).astype(jnp.bfloat16)
+    output = (tensor + conv_same(activation, flat_weight)).astype(jnp.bfloat16)
     return output, (first_c, square_c, padded)
 
 
@@ -140,7 +151,7 @@
     tensor = inputs.astype(jnp.float32)
     blocks = group_blocks(tensor.shape[3])
     pre_act = normalize_spread(tensor, first_c, square_c, gains, scales, shifts, cell_count)
-    d_act = convolve(pad_both(upstream), flipped)
+    d_act = conv_same(upstream, flipped)
     d_pre = d_act * silu_slope(pre_act)
 
     def mapping(tensor_v, first_v, square_v, gains_v, scales_v, shifts_v):
@@ -169,8 +180,8 @@
     channels = images.shape[3]
     cell_count = row_count * col_count * (channels // G)
     weight = conv_weight[0]
-    flat_weight = weight.reshape(9 * channels, channels)
-    flipped = flip_weight(weight)
+    flat_weight = weight
+    flipped = jnp.transpose(weight[::-1, ::-1], (0, 1, 3, 2))
     gains = gn_gain[0]
     features = sinusoid(steps, FREQ)
     embedded = jnp.dot(features, emb_weight[0].astype(jnp.float32), precision=lax.Precision.HIGHEST)

time: 199 us -> 194 us (0.975)
  matrix products: 20.2 us -> 12.9 us
  other arithmetic: 8.74 us -> 15.6 us
  waiting for transfers between devices: 63.2 us -> 59 us
  starting transfers between devices: 68.7 us -> 66.5 us
    ppermute x1, waiting for transfers between devices: 14.4 us -> 2.42 us  [per_device(): skip_grad = lax.ppermute(d_input, 'section', [(last, 0)])]
    dot_general x7 -> x0, matrix products: 11.6 us -> none  [convolve(): jnp.dot(flat, matrix, preferred_element_type=jnp.float32)]
    ppermute x3, waiting for transfers between devices: 9.95 us -> 19.1 us  [per_device(): upstream = lax.ppermute(carried, 'section', [(active + 1, active)])]
    conv_general_dilated x0 -> x7, matrix products: none -> 6.09 us  [conv_same(): lax.conv_general_dilated(tensor, kernel, (1, 1), ((1, 1), (1, 1)), dimens...]
    unnamed x124 -> x23, local copies, waits for them, and re-layouts: 7.55 us -> 3.23 us
    dot_general x14, matrix products: 7.37 us -> 3.47 us  [over_groups(): return jnp.dot(values, blocks, precision=lax.Precision.HIGHEST)]
    reduce_sum x0 -> x4, other arithmetic: none -> 3.78 us  [normalize_spread(): return normed * (1.0 + scales[:, None, None, :]) + shifts[:, None, None, :]]
    conv_general_dilated x0 -> x14, local copies, waits for them, and re-layouts: none -> 2.97 us  [conv_same(): lax.conv_general_dilated(tensor, kernel, (1, 1), ((1, 1), (1, 1)), dimens...]
  transfers between devices with their start and end apart: 17 -> 17, of which waited for: 11 -> 11; matrix products, arithmetic and copies ran while one was open for 7% -> 11% of each run, Pallas kernels for 0% -> 0%
where the time goes in v10:
time: 194 us; the launch traced here: 192 us
  starting transfers between devices  66.5 us (34%)
  waiting for transfers between devices  59 us (30%)
  blocking collectives  23.3 us (12%)
  other arithmetic  15.6 us (8%)
  local copies, waits for them, and re-layouts  12.9 us (7%)
  matrix products  12.9 us (7%)
    ppermute x4, starting transfers between devices, butterfly_gather(): got = lax.ppermute(flat, axis, [(j, j ^ step) for j in range(count)])  31.4 us
    ppermute x3, waiting for transfers between devices, per_device(): upstream = lax.ppermute(carried, 'section', [(active + 1, active)])  19.1 us
    ppermute x3, starting transfers between devices, butterfly_sum(): lax.ppermute(flat, axis, [(j, j ^ step) for j in range(count)])  15.8 us
    ppermute x4, waiting for transfers between devices, butterfly_gather(): got = lax.ppermute(flat, axis, [(j, j ^ step) for j in range(count)])  15.1 us
    ppermute x3, waiting for transfers between devices, butterfly_sum(): lax.ppermute(flat, axis, [(j, j ^ step) for j in range(count)])  13.3 us
    all_gather x1, blocking collectives, per_device(): images = lax.all_gather(images, 'space', axis=1, tiled=True)  12.8 us
    all_gather x1, blocking collectives, per_device(): out_grad = lax.all_gather(out_grad, 'space', axis=1, tiled=True)  10.5 us
    ppermute x2, waiting for transfers between devices, butterfly_scatter(): lax.ppermute(sent, axis, [(j, j ^ step) for j in range(count)])  9.09 us
  transfers between devices with their start and end apart: 17, of which 11 were waited for; matrix products, arithmetic and copies ran while one was open for 11% of the time, Pallas kernels for 0%

profile of v10, /device:TPU:1, one launch (start us, length us, event | category | flops | bytes accessed | tf_op | source)
XLA Modules:
  0.0 192.0 jit_solution(11822268414732829626)
XLA Ops:
  0.7 12.8 %all_gather.6 = bf16[2,4,64,256]{3,2,0,1:T(8,128)(2,1)S(1)} all-gather(bf16[2,1,64,256]{3,2,0,1:T(8,128)(2,1)} %bitcast.164), channel_id=1, replica_groups=mesh['dy'=8,'dx'=4,'section'=4,'space'=4] {'space'}, dimensions={1}, use_global_device_ids=true | all-gather | bytes 327680 | tf_op jit(solution)/shard_map/all_gather | solution.py:176
  14.6 1.2 fusion.130
  16.3 1.2 fusion.221
  19.9 1.3 collective-permute-start
  21.2 4.7 %collective-permute-start.3 = (bf16[2,4,64,256]{3,1,2,0:T(4,128)(2,1)S(1)}, bf16[2,4,64,256]{3,1,2,0:T(4,128)(2,1)S(1)}, u32[]{:S(2)}, u32[]{:S(2)}) collective-permute-start(bf16[2,4,64,256]{3,1,2,0:T(4,128)(2,1)S(1)} %fusion.79), channel_id=1, source_target_pairs={{0,12},{1,13},{2,14},{3,15},{16,28},{17,29},{18,30},{19,31},{32,44... | collective-permute-start | bytes 786440 | tf_op jit(solution)/shard_map/ppermute | solution.py:201
  25.9 10.5 %all_gather.7 = bf16[2,4,64,256]{3,2,0,1:T(8,128)(2,1)S(1)} all-gather(bf16[2,1,64,256]{3,2,0,1:T(8,128)(2,1)S(1)} %bitcast.165), channel_id=1, replica_groups=mesh['dy'=8,'dx'=4,'section'=4,'space'=4] {'space'}, dimensions={1}, use_global_device_ids=true | all-gather | bytes 327680 | tf_op jit(solution)/shard_map/all_gather | solution.py:177
  49.4 1.8 multiply_reduce_fusion
  52.8 1.3 collective-permute-start.7
  64.5 1.3 collective-permute-start.6
  66.2 1.6 copy.82
  67.8 2.4 %collective-permute-done.7 = bf16[2,4,64,256]{3,1,2,0:T(4,128)(2,1)S(1)} collective-permute-done((bf16[2,4,64,256]{3,1,2,0:T(4,128)(2,1)S(1)}, bf16[2,4,64,256]{3,1,2,0:T(4,128)(2,1)S(1)}, u32[]{:S(2)}, u32[]{:S(2)}) %collective-permute-start.7) | collective-permute-done | bytes 262176 | tf_op jit(solution)/shard_map/ppermute | solution.py:221
  70.2 19.1 %collective-permute-done.6 = bf16[2,4,64,256]{3,1,2,0:T(4,128)(2,1)S(1)} collective-permute-done((bf16[2,4,64,256]{3,1,2,0:T(4,128)(2,1)S(1)}, bf16[2,4,64,256]{3,1,2,0:T(4,128)(2,1)S(1)}, u32[]{:S(2)}, u32[]{:S(2)}) %collective-permute-start.6) | collective-permute-done | bytes 262176 | tf_op jit(solution)/shard_map/ppermute | solution.py:212
  93.1 1.8 fusion.55
  95.1 3.1 %collective-permute-start.8 = (f32[368,256]{1,0:T(8,128)S(1)}, f32[368,256]{1,0:T(8,128)S(1)}, u32[]{:S(2)}, u32[]{:S(2)}) collective-permute-start(f32[368,256]{1,0:T(8,128)S(1)} %constant_dynamic-slice_fusion.1), channel_id=1, source_target_pairs={{0,16},{16,0},{32,48},{48,32},{1,17},{17,1},{33,49},{49,33},{2,18}... | collective-permute-start | bytes 1130504 | tf_op jit(solution)/shard_map/ppermute | solution.py:253
  98.2 5.2 %collective-permute-done.8 = f32[368,256]{1,0:T(8,128)S(1)} collective-permute-done((f32[368,256]{1,0:T(8,128)S(1)}, f32[368,256]{1,0:T(8,128)S(1)}, u32[]{:S(2)}, u32[]{:S(2)}) %collective-permute-start.8) | collective-permute-done | bytes 376864 | tf_op jit(solution)/shard_map/ppermute | solution.py:253
  103.5 4.7 %collective-permute-start.9 = (f32[184,256]{1,0:T(8,128)S(1)}, f32[184,256]{1,0:T(8,128)S(1)}, u32[]{:S(2)}, u32[]{:S(2)}) collective-permute-start(f32[184,256]{1,0:T(8,128)S(1)} %constant_dynamic-slice_fusion), channel_id=1, source_target_pairs={{0,32},{16,48},{32,0},{48,16},{1,33},{17,49},{33,1},{49,17},{2,34}... | collective-permute-start | bytes 565256 | tf_op jit(solution)/shard_map/ppermute | solution.py:253
  108.2 3.9 %collective-permute-done.9 = f32[184,256]{1,0:T(8,128)S(1)} collective-permute-done((f32[184,256]{1,0:T(8,128)S(1)}, f32[184,256]{1,0:T(8,128)S(1)}, u32[]{:S(2)}, u32[]{:S(2)}) %collective-permute-start.9) | collective-permute-done | bytes 188448 | tf_op jit(solution)/shard_map/ppermute | solution.py:253
  112.1 3.2 %collective-permute-start.10 = (f32[184,256]{1,0:T(8,128)S(1)}, f32[184,256]{1,0:T(8,128)S(1)}, u32[]{:S(2)}, u32[]{:S(2)}) collective-permute-start(f32[184,256]{1,0:T(8,128)S(1)} %dynamic-slice_add_fusion.1), channel_id=1, source_target_pairs={{0,64},{64,0},{128,192},{192,128},{256,320},{320,256},{384,448},{4... | collective-permute-start | bytes 565256 | tf_op jit(solution)/shard_map/ppermute | solution.py:262
  115.3 3.1 %collective-permute-done.10 = f32[184,256]{1,0:T(8,128)S(1)} collective-permute-done((f32[184,256]{1,0:T(8,128)S(1)}, f32[184,256]{1,0:T(8,128)S(1)}, u32[]{:S(2)}, u32[]{:S(2)}) %collective-permute-start.10) | collective-permute-done | bytes 188448 | tf_op jit(solution)/shard_map/ppermute | solution.py:262
  118.4 4.2 %collective-permute-start.11 = (f32[184,256]{1,0:T(8,128)S(1)}, f32[184,256]{1,0:T(8,128)S(1)}, u32[]{:S(2)}, u32[]{:S(2)}) collective-permute-start(f32[184,256]{1,0:T(8,128)S(1)} %add.284), channel_id=1, source_target_pairs={{0,128},{64,192},{128,0},{192,64},{256,384},{320,448},{384,256},{4... | collective-permute-start | bytes 565256 | tf_op jit(solution)/shard_map/ppermute | solution.py:262
  122.7 4.1 %collective-permute-done.11 = f32[184,256]{1,0:T(8,128)S(1)} collective-permute-done((f32[184,256]{1,0:T(8,128)S(1)}, f32[184,256]{1,0:T(8,128)S(1)}, u32[]{:S(2)}, u32[]{:S(2)}) %collective-permute-start.11) | collective-permute-done | bytes 188448 | tf_op jit(solution)/shard_map/ppermute | solution.py:262
  126.8 8.3 %collective-permute-start.12 = (f32[184,256]{1,0:T(8,128)S(1)}, f32[184,256]{1,0:T(8,128)S(1)}, u32[]{:S(2)}, u32[]{:S(2)}) collective-permute-start(f32[184,256]{1,0:T(8,128)S(1)} %add.285), channel_id=1, source_target_pairs={{0,256},{64,320},{128,384},{192,448},{256,0},{320,64},{384,128},{4... | collective-permute-start | bytes 565256 | tf_op jit(solution)/shard_map/ppermute | solution.py:262
  135.1 6.1 %collective-permute-done.12 = f32[184,256]{1,0:T(8,128)S(1)} collective-permute-done((f32[184,256]{1,0:T(8,128)S(1)}, f32[184,256]{1,0:T(8,128)S(1)}, u32[]{:S(2)}, u32[]{:S(2)}) %collective-permute-start.12) | collective-permute-done | bytes 188448 | tf_op jit(solution)/shard_map/ppermute | solution.py:262
  141.3 3.2 %collective-permute-start.13 = (bf16[184,256]{1,0:T(8,128)(2,1)S(1)}, bf16[184,256]{1,0:T(8,128)(2,1)S(1)}, u32[]{:S(2)}, u32[]{:S(2)}) collective-permute-start(bf16[184,256]{1,0:T(8,128)(2,1)S(1)} %add_convert_fusion.2), channel_id=1, source_target_pairs={{0,32},{16,48},{32,0},{48,16},{1,33},{17,49},{33,1},{49,17},{2,34}... | collective-permute-start | bytes 282632 | tf_op jit(solution)/shard_map/ppermute | solution.py:272
  144.5 3.6 %collective-permute-done.13 = bf16[184,256]{1,0:T(8,128)(2,1)S(1)} collective-permute-done((bf16[184,256]{1,0:T(8,128)(2,1)S(1)}, bf16[184,256]{1,0:T(8,128)(2,1)S(1)}, u32[]{:S(2)}, u32[]{:S(2)}) %collective-permute-start.13) | collective-permute-done | bytes 94240 | tf_op jit(solution)/shard_map/ppermute | solution.py:272
  148.2 1.9 %collective-permute-start.14 = (bf16[368,256]{1,0:T(8,128)(2,1)S(1)}, bf16[368,256]{1,0:T(8,128)(2,1)S(1)}, u32[]{:S(2)}, u32[]{:S(2)}) collective-permute-start(bf16[368,256]{1,0:T(8,128)(2,1)S(1)} %maximum_select_fusion.3), channel_id=1, source_target_pairs={{0,16},{16,0},{32,48},{48,32},{1,17},{17,1},{33,49},{49,33},{2,18}... | collective-permute-start | bytes 565256 | tf_op jit(solution)/shard_map/ppermute | solution.py:272
  150.1 4.4 %collective-permute-done.14 = bf16[368,256]{1,0:T(8,128)(2,1)S(1)} collective-permute-done((bf16[368,256]{1,0:T(8,128)(2,1)S(1)}, bf16[368,256]{1,0:T(8,128)(2,1)S(1)}, u32[]{:S(2)}, u32[]{:S(2)}) %collective-permute-start.14) | collective-permute-done | bytes 188448 | tf_op jit(solution)/shard_map/ppermute | solution.py:272
  154.6 9.1 %collective-permute-start.15 = (bf16[736,256]{1,0:T(8,128)(2,1)S(1)}, bf16[736,256]{1,0:T(8,128)(2,1)S(1)}, u32[]{:S(2)}, u32[]{:S(2)}) collective-permute-start(bf16[736,256]{1,0:T(8,128)(2,1)S(1)} %maximum_select_fusion.2), channel_id=1, source_target_pairs={{0,2},{1,3},{2,0},{3,1},{4,6},{5,7},{6,4},{7,5},{8,10},{9,11},{10,... | collective-permute-start | bytes 1130504 | tf_op jit(solution)/shard_map/ppermute | solution.py:272
  163.7 5.3 %collective-permute-done.15 = bf16[736,256]{1,0:T(8,128)(2,1)S(1)} collective-permute-done((bf16[736,256]{1,0:T(8,128)(2,1)S(1)}, bf16[736,256]{1,0:T(8,128)(2,1)S(1)}, u32[]{:S(2)}, u32[]{:S(2)}) %collective-permute-start.15) | collective-permute-done | bytes 376864 | tf_op jit(solution)/shard_map/ppermute | solution.py:272
  169.2 17.2 %collective-permute-start.16 = (bf16[1472,256]{1,0:T(8,128)(2,1)S(1)}, bf16[1472,256]{1,0:T(8,128)(2,1)S(1)}, u32[]{:S(2)}, u32[]{:S(2)}) collective-permute-start(bf16[1472,256]{1,0:T(8,128)(2,1)S(1)} %maximum_select_fusion.1), channel_id=1, source_target_pairs={{0,1},{1,0},{2,3},{3,2},{4,5},{5,4},{6,7},{7,6},{8,9},{9,8},{10,11... | collective-permute-start | bytes 2261000 | tf_op jit(solution)/shard_map/ppermute | solution.py:272
  186.4 1.8 collective-permute-done.16
  188.9 1.6 slice.95
  (133 shorter events, 35.4 us)
Async XLA Ops:
  0.6 17.7 %copy-start = (bf16[1,3,3,256,256]{4,3,2,1,0:T(8,128)(2,1)S(1)}, bf16[1,3,3,256,256]{4,3,2,1,0:T(8,128)(2,1)}, u32[]{:S(2)}) copy-start(bf16[1,3,3,256,256]{4,3,2,1,0:T(8,128)(2,1)} %param.9) | copy-start | bytes 3538948
  0.6 17.7 %copy-start.3 = (pred[16,9]{0,1:T(8,128)(4,1)S(1)}, pred[16,9]{0,1:T(8,128)(4,1)}, u32[]{:S(2)}) copy-start(pred[16,9]{0,1:T(8,128)(4,1)} %constant.213) | copy-start | bytes 436
  18.3 7.5 %copy-start.2 = (bf16[2,1,64,256]{3,2,1,0:T(8,128)(2,1)S(1)}, bf16[2,1,64,256]{3,2,1,0:T(8,128)(2,1)}, u32[]{:S(2)}) copy-start(bf16[2,1,64,256]{3,2,1,0:T(8,128)(2,1)} %param.8) | copy-start | bytes 196612
  19.9 19.3 %collective-permute-start = (bf16[2,4,64,256]{3,1,2,0:T(4,128)(2,1)S(1)}, bf16[2,4,64,256]{3,1,2,0:T(4,128)(2,1)S(1)}, u32[]{:S(2)}, u32[]{:S(2)}) collective-permute-start(bf16[2,4,64,256]{3,1,2,0:T(4,128)(2,1)S(1)} %fusion.79), channel_id=1, source_target_pairs={{0,4},{1,5},{2,6},{3,7},{16,20},{17,21},{18,22},{19,23},{32,36},{3... | collective-permute-start | bytes 786440 | tf_op jit(solution)/shard_map/ppermute | solution.py:196
  21.2 27.4 %collective-permute-start.3 = (bf16[2,4,64,256]{3,1,2,0:T(4,128)(2,1)S(1)}, bf16[2,4,64,256]{3,1,2,0:T(4,128)(2,1)S(1)}, u32[]{:S(2)}, u32[]{:S(2)}) collective-permute-start(bf16[2,4,64,256]{3,1,2,0:T(4,128)(2,1)S(1)} %fusion.79), channel_id=1, source_target_pairs={{0,12},{1,13},{2,14},{3,15},{16,28},{17,29},{18,30},{19,31},{32,44... | collective-permute-start | bytes 786440 | tf_op jit(solution)/shard_map/ppermute | solution.py:201
  36.9 1.8 copy-start.1
  42.6 1.3 collective-permute-start.1
  47.4 1.1 collective-permute-start.2
  52.1 3.4 %collective-permute-start.4 = (bf16[2,4,64,256]{3,1,2,0:T(4,128)(2,1)S(1)}, bf16[2,4,64,256]{3,1,2,0:T(4,128)(2,1)S(1)}, u32[]{:S(2)}, u32[]{:S(2)}) collective-permute-start(bf16[2,4,64,256]{3,1,2,0:T(4,128)(2,1)S(1)} %fusion.94), channel_id=1, source_target_pairs={{12,8},{13,9},{14,10},{15,11},{28,24},{29,25},{30,26},{31,27},{44,... | collective-permute-start | bytes 786440 | tf_op jit(solution)/shard_map/ppermute | solution.py:212
  52.8 17.4 %collective-permute-start.7 = (bf16[2,4,64,256]{3,1,2,0:T(4,128)(2,1)S(1)}, bf16[2,4,64,256]{3,1,2,0:T(4,128)(2,1)S(1)}, u32[]{:S(2)}, u32[]{:S(2)}) collective-permute-start(bf16[2,4,64,256]{3,1,2,0:T(4,128)(2,1)S(1)} %fusion.94), channel_id=1, source_target_pairs={{12,0},{13,1},{14,2},{15,3},{28,16},{29,17},{30,18},{31,19},{44,32... | collective-permute-start | bytes 786440 | tf_op jit(solution)/shard_map/ppermute | solution.py:221
  59.4 1.3 collective-permute-start.5
  64.5 24.9 %collective-permute-start.6 = (bf16[2,4,64,256]{3,1,2,0:T(4,128)(2,1)S(1)}, bf16[2,4,64,256]{3,1,2,0:T(4,128)(2,1)S(1)}, u32[]{:S(2)}, u32[]{:S(2)}) collective-permute-start(bf16[2,4,64,256]{3,1,2,0:T(4,128)(2,1)S(1)} %fusion.100), channel_id=1, source_target_pairs={{4,0},{5,1},{6,2},{7,3},{20,16},{21,17},{22,18},{23,19},{36,32},{3... | collective-permute-start | bytes 786440 | tf_op jit(solution)/shard_map/ppermute | solution.py:212
  95.1 8.3 %collective-permute-start.8 = (f32[368,256]{1,0:T(8,128)S(1)}, f32[368,256]{1,0:T(8,128)S(1)}, u32[]{:S(2)}, u32[]{:S(2)}) collective-permute-start(f32[368,256]{1,0:T(8,128)S(1)} %constant_dynamic-slice_fusion.1), channel_id=1, source_target_pairs={{0,16},{16,0},{32,48},{48,32},{1,17},{17,1},{33,49},{49,33},{2,18}... | collective-permute-start | bytes 1130504 | tf_op jit(solution)/shard_map/ppermute | solution.py:253
  103.5 8.5 %collective-permute-start.9 = (f32[184,256]{1,0:T(8,128)S(1)}, f32[184,256]{1,0:T(8,128)S(1)}, u32[]{:S(2)}, u32[]{:S(2)}) collective-permute-start(f32[184,256]{1,0:T(8,128)S(1)} %constant_dynamic-slice_fusion), channel_id=1, source_target_pairs={{0,32},{16,48},{32,0},{48,16},{1,33},{17,49},{33,1},{49,17},{2,34}... | collective-permute-start | bytes 565256 | tf_op jit(solution)/shard_map/ppermute | solution.py:253
  112.1 6.3 %collective-permute-start.10 = (f32[184,256]{1,0:T(8,128)S(1)}, f32[184,256]{1,0:T(8,128)S(1)}, u32[]{:S(2)}, u32[]{:S(2)}) collective-permute-start(f32[184,256]{1,0:T(8,128)S(1)} %dynamic-slice_add_fusion.1), channel_id=1, source_target_pairs={{0,64},{64,0},{128,192},{192,128},{256,320},{320,256},{384,448},{4... | collective-permute-start | bytes 565256 | tf_op jit(solution)/shard_map/ppermute | solution.py:262
  118.4 8.3 %collective-permute-start.11 = (f32[184,256]{1,0:T(8,128)S(1)}, f32[184,256]{1,0:T(8,128)S(1)}, u32[]{:S(2)}, u32[]{:S(2)}) collective-permute-start(f32[184,256]{1,0:T(8,128)S(1)} %add.284), channel_id=1, source_target_pairs={{0,128},{64,192},{128,0},{192,64},{256,384},{320,448},{384,256},{4... | collective-permute-start | bytes 565256 | tf_op jit(solution)/shard_map/ppermute | solution.py:262
  126.8 14.5 %collective-permute-start.12 = (f32[184,256]{1,0:T(8,128)S(1)}, f32[184,256]{1,0:T(8,128)S(1)}, u32[]{:S(2)}, u32[]{:S(2)}) collective-permute-start(f32[184,256]{1,0:T(8,128)S(1)} %add.285), channel_id=1, source_target_pairs={{0,256},{64,320},{128,384},{192,448},{256,0},{320,64},{384,128},{4... | collective-permute-start | bytes 565256 | tf_op jit(solution)/shard_map/ppermute | solution.py:262
  141.3 6.8 %collective-permute-start.13 = (bf16[184,256]{1,0:T(8,128)(2,1)S(1)}, bf16[184,256]{1,0:T(8,128)(2,1)S(1)}, u32[]{:S(2)}, u32[]{:S(2)}) collective-permute-start(bf16[184,256]{1,0:T(8,128)(2,1)S(1)} %add_convert_fusion.2), channel_id=1, source_target_pairs={{0,32},{16,48},{32,0},{48,16},{1,33},{17,49},{33,1},{49,17},{2,34}... | collective-permute-start | bytes 282632 | tf_op jit(solution)/shard_map/ppermute | solution.py:272
  148.2 6.3 %collective-permute-start.14 = (bf16[368,256]{1,0:T(8,128)(2,1)S(1)}, bf16[368,256]{1,0:T(8,128)(2,1)S(1)}, u32[]{:S(2)}, u32[]{:S(2)}) collective-permute-start(bf16[368,256]{1,0:T(8,128)(2,1)S(1)} %maximum_select_fusion.3), channel_id=1, source_target_pairs={{0,16},{16,0},{32,48},{48,32},{1,17},{17,1},{33,49},{49,33},{2,18}... | collective-permute-start | bytes 565256 | tf_op jit(solution)/shard_map/ppermute | solution.py:272
  154.6 14.3 %collective-permute-start.15 = (bf16[736,256]{1,0:T(8,128)(2,1)S(1)}, bf16[736,256]{1,0:T(8,128)(2,1)S(1)}, u32[]{:S(2)}, u32[]{:S(2)}) collective-permute-start(bf16[736,256]{1,0:T(8,128)(2,1)S(1)} %maximum_select_fusion.2), channel_id=1, source_target_pairs={{0,2},{1,3},{2,0},{3,1},{4,6},{5,7},{6,4},{7,5},{8,10},{9,11},{10,... | collective-permute-start | bytes 1130504 | tf_op jit(solution)/shard_map/ppermute | solution.py:272
  169.2 19.0 %collective-permute-start.16 = (bf16[1472,256]{1,0:T(8,128)(2,1)S(1)}, bf16[1472,256]{1,0:T(8,128)(2,1)S(1)}, u32[]{:S(2)}, u32[]{:S(2)}) collective-permute-start(bf16[1472,256]{1,0:T(8,128)(2,1)S(1)} %maximum_select_fusion.1), channel_id=1, source_target_pairs={{0,1},{1,0},{2,3},{3,2},{4,5},{5,4},{6,7},{7,6},{8,9},{9,8},{10,11... | collective-permute-start | bytes 2261000 | tf_op jit(solution)/shard_map/ppermute | solution.py:272

commit v11 on v10

--- a/solution.py
+++ b/solution.py
@@ -270,7 +270,10 @@
     for step in steps:
         bit = (index // step) % 2
         got = lax.ppermute(flat, axis, [(j, j ^ step) for j in range(count)])
-        flat = jnp.where(bit == 1, jnp.concatenate([got, flat]), jnp.concatenate([flat, got]))
+        length = flat.shape[0]
+        joined = jnp.zeros((2 * length, *flat.shape[1:]), flat.dtype)
+        joined = lax.dynamic_update_slice_in_dim(joined, flat, bit * length, 0)
+        flat = lax.dynamic_update_slice_in_dim(joined, got, (1 - bit) * length, 0)
     return flat
 
 

time: 194 us -> 193 us (level)
  no operation moved by 1% of the time
where the time goes in v11:
time: 193 us; the launch traced here: 191 us
  starting transfers between devices  66.5 us (34%)
  waiting for transfers between devices  58.7 us (30%)
  blocking collectives  23.3 us (12%)
  other arithmetic  14.8 us (8%)
  local copies, waits for them, and re-layouts  13.3 us (7%)
  matrix products  12.9 us (7%)
    ppermute x4, starting transfers between devices, butterfly_gather(): got = lax.ppermute(flat, axis, [(j, j ^ step) for j in range(count)])  31.4 us
    ppermute x3, waiting for transfers between devices, per_device(): upstream = lax.ppermute(carried, 'section', [(active + 1, active)])  19.1 us
    ppermute x3, starting transfers between devices, butterfly_sum(): lax.ppermute(flat, axis, [(j, j ^ step) for j in range(count)])  15.8 us
    ppermute x4, waiting for transfers between devices, butterfly_gather(): got = lax.ppermute(flat, axis, [(j, j ^ step) for j in range(count)])  14.7 us
    ppermute x3, waiting for transfers between devices, butterfly_sum(): lax.ppermute(flat, axis, [(j, j ^ step) for j in range(count)])  13.3 us
    all_gather x1, blocking collectives, per_device(): images = lax.all_gather(images, 'space', axis=1, tiled=True)  12.8 us
    all_gather x1, blocking collectives, per_device(): out_grad = lax.all_gather(out_grad, 'space', axis=1, tiled=True)  10.5 us
    ppermute x2, waiting for transfers between devices, butterfly_scatter(): lax.ppermute(sent, axis, [(j, j ^ step) for j in range(count)])  9.09 us
  transfers between devices with their start and end apart: 17, of which 11 were waited for; matrix products, arithmetic and copies ran while one was open for 11% of the time, Pallas kernels for 0%

profile of v11, /device:TPU:1, one launch (start us, length us, event | category | flops | bytes accessed | tf_op | source)
XLA Modules:
  0.0 191.3 jit_solution(9243266597374263618)
XLA Ops:
  0.7 12.8 %all_gather.6 = bf16[2,4,64,256]{3,2,0,1:T(8,128)(2,1)S(1)} all-gather(bf16[2,1,64,256]{3,2,0,1:T(8,128)(2,1)} %bitcast.164), channel_id=1, replica_groups=mesh['dy'=8,'dx'=4,'section'=4,'space'=4] {'space'}, dimensions={1}, use_global_device_ids=true | all-gather | bytes 327680 | tf_op jit(solution)/shard_map/all_gather | solution.py:176
  14.6 1.2 fusion.130
  16.3 1.2 fusion.221
  19.9 1.3 collective-permute-start
  21.2 4.7 %collective-permute-start.3 = (bf16[2,4,64,256]{3,1,2,0:T(4,128)(2,1)S(1)}, bf16[2,4,64,256]{3,1,2,0:T(4,128)(2,1)S(1)}, u32[]{:S(2)}, u32[]{:S(2)}) collective-permute-start(bf16[2,4,64,256]{3,1,2,0:T(4,128)(2,1)S(1)} %fusion.79), channel_id=1, source_target_pairs={{0,12},{1,13},{2,14},{3,15},{16,28},{17,29},{18,30},{19,31},{32,44... | collective-permute-start | bytes 786440 | tf_op jit(solution)/shard_map/ppermute | solution.py:201
  25.9 10.5 %all_gather.7 = bf16[2,4,64,256]{3,2,0,1:T(8,128)(2,1)S(1)} all-gather(bf16[2,1,64,256]{3,2,0,1:T(8,128)(2,1)S(1)} %bitcast.165), channel_id=1, replica_groups=mesh['dy'=8,'dx'=4,'section'=4,'space'=4] {'space'}, dimensions={1}, use_global_device_ids=true | all-gather | bytes 327680 | tf_op jit(solution)/shard_map/all_gather | solution.py:177
  49.4 1.8 multiply_reduce_fusion
  52.8 1.3 collective-permute-start.7
  64.5 1.3 collective-permute-start.6
  66.2 1.6 copy.82
  67.8 2.4 %collective-permute-done.7 = bf16[2,4,64,256]{3,1,2,0:T(4,128)(2,1)S(1)} collective-permute-done((bf16[2,4,64,256]{3,1,2,0:T(4,128)(2,1)S(1)}, bf16[2,4,64,256]{3,1,2,0:T(4,128)(2,1)S(1)}, u32[]{:S(2)}, u32[]{:S(2)}) %collective-permute-start.7) | collective-permute-done | bytes 262176 | tf_op jit(solution)/shard_map/ppermute | solution.py:221
  70.2 19.1 %collective-permute-done.6 = bf16[2,4,64,256]{3,1,2,0:T(4,128)(2,1)S(1)} collective-permute-done((bf16[2,4,64,256]{3,1,2,0:T(4,128)(2,1)S(1)}, bf16[2,4,64,256]{3,1,2,0:T(4,128)(2,1)S(1)}, u32[]{:S(2)}, u32[]{:S(2)}) %collective-permute-start.6) | collective-permute-done | bytes 262176 | tf_op jit(solution)/shard_map/ppermute | solution.py:212
  93.1 1.8 fusion.55
  95.1 3.1 %collective-permute-start.8 = (f32[368,256]{1,0:T(8,128)S(1)}, f32[368,256]{1,0:T(8,128)S(1)}, u32[]{:S(2)}, u32[]{:S(2)}) collective-permute-start(f32[368,256]{1,0:T(8,128)S(1)} %constant_dynamic-slice_fusion.2), channel_id=1, source_target_pairs={{0,16},{16,0},{32,48},{48,32},{1,17},{17,1},{33,49},{49,33},{2,18}... | collective-permute-start | bytes 1130504 | tf_op jit(solution)/shard_map/ppermute | solution.py:253
  98.2 5.2 %collective-permute-done.8 = f32[368,256]{1,0:T(8,128)S(1)} collective-permute-done((f32[368,256]{1,0:T(8,128)S(1)}, f32[368,256]{1,0:T(8,128)S(1)}, u32[]{:S(2)}, u32[]{:S(2)}) %collective-permute-start.8) | collective-permute-done | bytes 376864 | tf_op jit(solution)/shard_map/ppermute | solution.py:253
  103.5 4.7 %collective-permute-start.9 = (f32[184,256]{1,0:T(8,128)S(1)}, f32[184,256]{1,0:T(8,128)S(1)}, u32[]{:S(2)}, u32[]{:S(2)}) collective-permute-start(f32[184,256]{1,0:T(8,128)S(1)} %constant_dynamic-slice_fusion.1), channel_id=1, source_target_pairs={{0,32},{16,48},{32,0},{48,16},{1,33},{17,49},{33,1},{49,17},{2,34}... | collective-permute-start | bytes 565256 | tf_op jit(solution)/shard_map/ppermute | solution.py:253
  108.2 3.9 %collective-permute-done.9 = f32[184,256]{1,0:T(8,128)S(1)} collective-permute-done((f32[184,256]{1,0:T(8,128)S(1)}, f32[184,256]{1,0:T(8,128)S(1)}, u32[]{:S(2)}, u32[]{:S(2)}) %collective-permute-start.9) | collective-permute-done | bytes 188448 | tf_op jit(solution)/shard_map/ppermute | solution.py:253
  112.1 3.2 %collective-permute-start.10 = (f32[184,256]{1,0:T(8,128)S(1)}, f32[184,256]{1,0:T(8,128)S(1)}, u32[]{:S(2)}, u32[]{:S(2)}) collective-permute-start(f32[184,256]{1,0:T(8,128)S(1)} %dynamic-slice_add_fusion.1), channel_id=1, source_target_pairs={{0,64},{64,0},{128,192},{192,128},{256,320},{320,256},{384,448},{4... | collective-permute-start | bytes 565256 | tf_op jit(solution)/shard_map/ppermute | solution.py:262
  115.3 3.1 %collective-permute-done.10 = f32[184,256]{1,0:T(8,128)S(1)} collective-permute-done((f32[184,256]{1,0:T(8,128)S(1)}, f32[184,256]{1,0:T(8,128)S(1)}, u32[]{:S(2)}, u32[]{:S(2)}) %collective-permute-start.10) | collective-permute-done | bytes 188448 | tf_op jit(solution)/shard_map/ppermute | solution.py:262
  118.4 4.2 %collective-permute-start.11 = (f32[184,256]{1,0:T(8,128)S(1)}, f32[184,256]{1,0:T(8,128)S(1)}, u32[]{:S(2)}, u32[]{:S(2)}) collective-permute-start(f32[184,256]{1,0:T(8,128)S(1)} %add.299), channel_id=1, source_target_pairs={{0,128},{64,192},{128,0},{192,64},{256,384},{320,448},{384,256},{4... | collective-permute-start | bytes 565256 | tf_op jit(solution)/shard_map/ppermute | solution.py:262
  122.7 4.1 %collective-permute-done.11 = f32[184,256]{1,0:T(8,128)S(1)} collective-permute-done((f32[184,256]{1,0:T(8,128)S(1)}, f32[184,256]{1,0:T(8,128)S(1)}, u32[]{:S(2)}, u32[]{:S(2)}) %collective-permute-start.11) | collective-permute-done | bytes 188448 | tf_op jit(solution)/shard_map/ppermute | solution.py:262
  126.8 8.3 %collective-permute-start.12 = (f32[184,256]{1,0:T(8,128)S(1)}, f32[184,256]{1,0:T(8,128)S(1)}, u32[]{:S(2)}, u32[]{:S(2)}) collective-permute-start(f32[184,256]{1,0:T(8,128)S(1)} %add.300), channel_id=1, source_target_pairs={{0,256},{64,320},{128,384},{192,448},{256,0},{320,64},{384,128},{4... | collective-permute-start | bytes 565256 | tf_op jit(solution)/shard_map/ppermute | solution.py:262
  135.1 6.1 %collective-permute-done.12 = f32[184,256]{1,0:T(8,128)S(1)} collective-permute-done((f32[184,256]{1,0:T(8,128)S(1)}, f32[184,256]{1,0:T(8,128)S(1)}, u32[]{:S(2)}, u32[]{:S(2)}) %collective-permute-start.12) | collective-permute-done | bytes 188448 | tf_op jit(solution)/shard_map/ppermute | solution.py:262
  141.3 3.2 %collective-permute-start.13 = (bf16[184,256]{1,0:T(8,128)(2,1)S(1)}, bf16[184,256]{1,0:T(8,128)(2,1)S(1)}, u32[]{:S(2)}, u32[]{:S(2)}) collective-permute-start(bf16[184,256]{1,0:T(8,128)(2,1)S(1)} %get-tuple-element.30), channel_id=1, source_target_pairs={{0,32},{16,48},{32,0},{48,16},{1,33},{17,49},{33,1},{49,17},{2,34}... | collective-permute-start | bytes 282632 | tf_op jit(solution)/shard_map/ppermute | solution.py:272
  144.5 3.6 %collective-permute-done.13 = bf16[184,256]{1,0:T(8,128)(2,1)S(1)} collective-permute-done((bf16[184,256]{1,0:T(8,128)(2,1)S(1)}, bf16[184,256]{1,0:T(8,128)(2,1)S(1)}, u32[]{:S(2)}, u32[]{:S(2)}) %collective-permute-start.13) | collective-permute-done | bytes 94240 | tf_op jit(solution)/shard_map/ppermute | solution.py:272
  148.1 1.9 %collective-permute-start.14 = (bf16[368,256]{1,0:T(8,128)(2,1)S(1)}, bf16[368,256]{1,0:T(8,128)(2,1)S(1)}, u32[]{:S(2)}, u32[]{:S(2)}) collective-permute-start(bf16[368,256]{1,0:T(8,128)(2,1)S(1)} %constant_dynamic-update-slice_fusion.6), channel_id=1, source_target_pairs={{0,16},{16,0},{32,48},{48,32},{1,17},{17,1},{33,49},{49,33},{2,18}... | collective-permute-start | bytes 565256 | tf_op jit(solution)/shard_map/ppermute | solution.py:272
  150.1 4.3 %collective-permute-done.14 = bf16[368,256]{1,0:T(8,128)(2,1)S(1)} collective-permute-done((bf16[368,256]{1,0:T(8,128)(2,1)S(1)}, bf16[368,256]{1,0:T(8,128)(2,1)S(1)}, u32[]{:S(2)}, u32[]{:S(2)}) %collective-permute-start.14) | collective-permute-done | bytes 188448 | tf_op jit(solution)/shard_map/ppermute | solution.py:272
  154.5 9.1 %collective-permute-start.15 = (bf16[736,256]{1,0:T(8,128)(2,1)S(1)}, bf16[736,256]{1,0:T(8,128)(2,1)S(1)}, u32[]{:S(2)}, u32[]{:S(2)}) collective-permute-start(bf16[736,256]{1,0:T(8,128)(2,1)S(1)} %constant_dynamic-update-slice_fusion.4), channel_id=1, source_target_pairs={{0,2},{1,3},{2,0},{3,1},{4,6},{5,7},{6,4},{7,5},{8,10},{9,11},{10,... | collective-permute-start | bytes 1130504 | tf_op jit(solution)/shard_map/ppermute | solution.py:272
  163.7 5.1 %collective-permute-done.15 = bf16[736,256]{1,0:T(8,128)(2,1)S(1)} collective-permute-done((bf16[736,256]{1,0:T(8,128)(2,1)S(1)}, bf16[736,256]{1,0:T(8,128)(2,1)S(1)}, u32[]{:S(2)}, u32[]{:S(2)}) %collective-permute-start.15) | collective-permute-done | bytes 376864 | tf_op jit(solution)/shard_map/ppermute | solution.py:272
  168.8 17.2 %collective-permute-start.16 = (bf16[1472,256]{1,0:T(8,128)(2,1)S(1)}, bf16[1472,256]{1,0:T(8,128)(2,1)S(1)}, u32[]{:S(2)}, u32[]{:S(2)}) collective-permute-start(bf16[1472,256]{1,0:T(8,128)(2,1)S(1)} %constant_dynamic-update-slice_fusion.2), channel_id=1, source_target_pairs={{0,1},{1,0},{2,3},{3,2},{4,5},{5,4},{6,7},{7,6},{8,9},{9,8},{10,11... | collective-permute-start | bytes 2261000 | tf_op jit(solution)/shard_map/ppermute | solution.py:272
  186.2 1.7 collective-permute-done.16
  188.2 1.6 slice.95
  (140 shorter events, 35.0 us)
Async XLA Ops:
  0.6 17.7 %copy-start = (bf16[1,3,3,256,256]{4,3,2,1,0:T(8,128)(2,1)S(1)}, bf16[1,3,3,256,256]{4,3,2,1,0:T(8,128)(2,1)}, u32[]{:S(2)}) copy-start(bf16[1,3,3,256,256]{4,3,2,1,0:T(8,128)(2,1)} %param.9) | copy-start | bytes 3538948
  0.6 17.7 %copy-start.3 = (pred[16,9]{0,1:T(8,128)(4,1)S(1)}, pred[16,9]{0,1:T(8,128)(4,1)}, u32[]{:S(2)}) copy-start(pred[16,9]{0,1:T(8,128)(4,1)} %constant.221) | copy-start | bytes 436
  18.3 7.5 %copy-start.2 = (bf16[2,1,64,256]{3,2,1,0:T(8,128)(2,1)S(1)}, bf16[2,1,64,256]{3,2,1,0:T(8,128)(2,1)}, u32[]{:S(2)}) copy-start(bf16[2,1,64,256]{3,2,1,0:T(8,128)(2,1)} %param.8) | copy-start | bytes 196612
  19.9 19.3 %collective-permute-start = (bf16[2,4,64,256]{3,1,2,0:T(4,128)(2,1)S(1)}, bf16[2,4,64,256]{3,1,2,0:T(4,128)(2,1)S(1)}, u32[]{:S(2)}, u32[]{:S(2)}) collective-permute-start(bf16[2,4,64,256]{3,1,2,0:T(4,128)(2,1)S(1)} %fusion.79), channel_id=1, source_target_pairs={{0,4},{1,5},{2,6},{3,7},{16,20},{17,21},{18,22},{19,23},{32,36},{3... | collective-permute-start | bytes 786440 | tf_op jit(solution)/shard_map/ppermute | solution.py:196
  21.2 27.4 %collective-permute-start.3 = (bf16[2,4,64,256]{3,1,2,0:T(4,128)(2,1)S(1)}, bf16[2,4,64,256]{3,1,2,0:T(4,128)(2,1)S(1)}, u32[]{:S(2)}, u32[]{:S(2)}) collective-permute-start(bf16[2,4,64,256]{3,1,2,0:T(4,128)(2,1)S(1)} %fusion.79), channel_id=1, source_target_pairs={{0,12},{1,13},{2,14},{3,15},{16,28},{17,29},{18,30},{19,31},{32,44... | collective-permute-start | bytes 786440 | tf_op jit(solution)/shard_map/ppermute | solution.py:201
  36.9 1.8 copy-start.1
  42.6 1.3 collective-permute-start.1
  47.4 1.1 collective-permute-start.2
  52.1 3.4 %collective-permute-start.4 = (bf16[2,4,64,256]{3,1,2,0:T(4,128)(2,1)S(1)}, bf16[2,4,64,256]{3,1,2,0:T(4,128)(2,1)S(1)}, u32[]{:S(2)}, u32[]{:S(2)}) collective-permute-start(bf16[2,4,64,256]{3,1,2,0:T(4,128)(2,1)S(1)} %fusion.94), channel_id=1, source_target_pairs={{12,8},{13,9},{14,10},{15,11},{28,24},{29,25},{30,26},{31,27},{44,... | collective-permute-start | bytes 786440 | tf_op jit(solution)/shard_map/ppermute | solution.py:212
  52.8 17.4 %collective-permute-start.7 = (bf16[2,4,64,256]{3,1,2,0:T(4,128)(2,1)S(1)}, bf16[2,4,64,256]{3,1,2,0:T(4,128)(2,1)S(1)}, u32[]{:S(2)}, u32[]{:S(2)}) collective-permute-start(bf16[2,4,64,256]{3,1,2,0:T(4,128)(2,1)S(1)} %fusion.94), channel_id=1, source_target_pairs={{12,0},{13,1},{14,2},{15,3},{28,16},{29,17},{30,18},{31,19},{44,32... | collective-permute-start | bytes 786440 | tf_op jit(solution)/shard_map/ppermute | solution.py:221
  59.4 1.3 collective-permute-start.5
  64.5 24.9 %collective-permute-start.6 = (bf16[2,4,64,256]{3,1,2,0:T(4,128)(2,1)S(1)}, bf16[2,4,64,256]{3,1,2,0:T(4,128)(2,1)S(1)}, u32[]{:S(2)}, u32[]{:S(2)}) collective-permute-start(bf16[2,4,64,256]{3,1,2,0:T(4,128)(2,1)S(1)} %fusion.100), channel_id=1, source_target_pairs={{4,0},{5,1},{6,2},{7,3},{20,16},{21,17},{22,18},{23,19},{36,32},{3... | collective-permute-start | bytes 786440 | tf_op jit(solution)/shard_map/ppermute | solution.py:212
  95.1 8.3 %collective-permute-start.8 = (f32[368,256]{1,0:T(8,128)S(1)}, f32[368,256]{1,0:T(8,128)S(1)}, u32[]{:S(2)}, u32[]{:S(2)}) collective-permute-start(f32[368,256]{1,0:T(8,128)S(1)} %constant_dynamic-slice_fusion.2), channel_id=1, source_target_pairs={{0,16},{16,0},{32,48},{48,32},{1,17},{17,1},{33,49},{49,33},{2,18}... | collective-permute-start | bytes 1130504 | tf_op jit(solution)/shard_map/ppermute | solution.py:253
  103.5 8.5 %collective-permute-start.9 = (f32[184,256]{1,0:T(8,128)S(1)}, f32[184,256]{1,0:T(8,128)S(1)}, u32[]{:S(2)}, u32[]{:S(2)}) collective-permute-start(f32[184,256]{1,0:T(8,128)S(1)} %constant_dynamic-slice_fusion.1), channel_id=1, source_target_pairs={{0,32},{16,48},{32,0},{48,16},{1,33},{17,49},{33,1},{49,17},{2,34}... | collective-permute-start | bytes 565256 | tf_op jit(solution)/shard_map/ppermute | solution.py:253
  112.1 6.3 %collective-permute-start.10 = (f32[184,256]{1,0:T(8,128)S(1)}, f32[184,256]{1,0:T(8,128)S(1)}, u32[]{:S(2)}, u32[]{:S(2)}) collective-permute-start(f32[184,256]{1,0:T(8,128)S(1)} %dynamic-slice_add_fusion.1), channel_id=1, source_target_pairs={{0,64},{64,0},{128,192},{192,128},{256,320},{320,256},{384,448},{4... | collective-permute-start | bytes 565256 | tf_op jit(solution)/shard_map/ppermute | solution.py:262
  118.4 8.3 %collective-permute-start.11 = (f32[184,256]{1,0:T(8,128)S(1)}, f32[184,256]{1,0:T(8,128)S(1)}, u32[]{:S(2)}, u32[]{:S(2)}) collective-permute-start(f32[184,256]{1,0:T(8,128)S(1)} %add.299), channel_id=1, source_target_pairs={{0,128},{64,192},{128,0},{192,64},{256,384},{320,448},{384,256},{4... | collective-permute-start | bytes 565256 | tf_op jit(solution)/shard_map/ppermute | solution.py:262
  126.8 14.5 %collective-permute-start.12 = (f32[184,256]{1,0:T(8,128)S(1)}, f32[184,256]{1,0:T(8,128)S(1)}, u32[]{:S(2)}, u32[]{:S(2)}) collective-permute-start(f32[184,256]{1,0:T(8,128)S(1)} %add.300), channel_id=1, source_target_pairs={{0,256},{64,320},{128,384},{192,448},{256,0},{320,64},{384,128},{4... | collective-permute-start | bytes 565256 | tf_op jit(solution)/shard_map/ppermute | solution.py:262
  141.3 6.8 %collective-permute-start.13 = (bf16[184,256]{1,0:T(8,128)(2,1)S(1)}, bf16[184,256]{1,0:T(8,128)(2,1)S(1)}, u32[]{:S(2)}, u32[]{:S(2)}) collective-permute-start(bf16[184,256]{1,0:T(8,128)(2,1)S(1)} %get-tuple-element.30), channel_id=1, source_target_pairs={{0,32},{16,48},{32,0},{48,16},{1,33},{17,49},{33,1},{49,17},{2,34}... | collective-permute-start | bytes 282632 | tf_op jit(solution)/shard_map/ppermute | solution.py:272
  148.1 6.3 %collective-permute-start.14 = (bf16[368,256]{1,0:T(8,128)(2,1)S(1)}, bf16[368,256]{1,0:T(8,128)(2,1)S(1)}, u32[]{:S(2)}, u32[]{:S(2)}) collective-permute-start(bf16[368,256]{1,0:T(8,128)(2,1)S(1)} %constant_dynamic-update-slice_fusion.6), channel_id=1, source_target_pairs={{0,16},{16,0},{32,48},{48,32},{1,17},{17,1},{33,49},{49,33},{2,18}... | collective-permute-start | bytes 565256 | tf_op jit(solution)/shard_map/ppermute | solution.py:272
  154.5 14.3 %collective-permute-start.15 = (bf16[736,256]{1,0:T(8,128)(2,1)S(1)}, bf16[736,256]{1,0:T(8,128)(2,1)S(1)}, u32[]{:S(2)}, u32[]{:S(2)}) collective-permute-start(bf16[736,256]{1,0:T(8,128)(2,1)S(1)} %constant_dynamic-update-slice_fusion.4), channel_id=1, source_target_pairs={{0,2},{1,3},{2,0},{3,1},{4,6},{5,7},{6,4},{7,5},{8,10},{9,11},{10,... | collective-permute-start | bytes 1130504 | tf_op jit(solution)/shard_map/ppermute | solution.py:272
  168.8 19.0 %collective-permute-start.16 = (bf16[1472,256]{1,0:T(8,128)(2,1)S(1)}, bf16[1472,256]{1,0:T(8,128)(2,1)S(1)}, u32[]{:S(2)}, u32[]{:S(2)}) collective-permute-start(bf16[1472,256]{1,0:T(8,128)(2,1)S(1)} %constant_dynamic-update-slice_fusion.2), channel_id=1, source_target_pairs={{0,1},{1,0},{2,3},{3,2},{4,5},{5,4},{6,7},{7,6},{8,9},{9,8},{10,11... | collective-permute-start | bytes 2261000 | tf_op jit(solution)/shard_map/ppermute | solution.py:272

commit v12 on v11

--- a/solution.py
+++ b/solution.py
@@ -143,16 +143,15 @@
     activation = jax.nn.silu(pre_act).astype(jnp.bfloat16)
     padded = pad_both(activation)
     output = (tensor + conv_same(activation, flat_weight)).astype(jnp.bfloat16)
-    return output, (first_c, square_c, padded)
+    return output, (first_c, square_c, padded, silu_slope(pre_act))
 
 
 def block_backward(upstream, inputs, saved, flipped, gains, scales, shifts, cell_count):
-    first_c, square_c, _ = saved
+    first_c, square_c, _, slope = saved
     tensor = inputs.astype(jnp.float32)
     blocks = group_blocks(tensor.shape[3])
-    pre_act = normalize_spread(tensor, first_c, square_c, gains, scales, shifts, cell_count)
     d_act = conv_same(upstream, flipped)
-    d_pre = d_act * silu_slope(pre_act)
+    d_pre = d_act * slope
 
     def mapping(tensor_v, first_v, square_v, gains_v, scales_v, shifts_v):
         return normalize_spread(tensor_v, first_v, square_v, gains_v, scales_v, shifts_v, cell_count)

time: 193 us -> 196 us (1.016)
  blocking collectives: 23.3 us -> 29.6 us
  other arithmetic: 14.8 us -> 17.8 us
  waiting for transfers between devices: 58.7 us -> 55.7 us
  starting transfers between devices: 66.5 us -> 64.1 us
    ppermute x3, waiting for transfers between devices: 19.1 us -> 6.33 us  [per_device(): upstream = lax.ppermute(carried, 'section', [(active + 1, active)])]
    all_gather x1, blocking collectives: 10.5 us -> 16.7 us  [per_device(): out_grad = lax.all_gather(out_grad, 'space', axis=1, tiled=True)]
    ppermute x3, waiting for transfers between devices: 0.01 us -> 5.9 us  [per_device(): inputs = lax.ppermute(carried, 'section', [(moment - 1, moment)])]
    ppermute x1, starting transfers between devices: 4.67 us -> 1.31 us  [per_device(): skip = lax.ppermute(output, 'section', [(0, last)])]
  transfers between devices with their start and end apart: 17 -> 17, of which waited for: 11 -> 12; matrix products, arithmetic and copies ran while one was open for 11% -> 6% of each run, Pallas kernels for 0% -> 0%
where the time goes in v12:
time: 196 us; the launch traced here: 195 us
  starting transfers between devices  64.1 us (33%)
  waiting for transfers between devices  55.7 us (28%)
  blocking collectives  29.6 us (15%)
  other arithmetic  17.8 us (9%)
  local copies, waits for them, and re-layouts  13.3 us (7%)
  matrix products  12.9 us (7%)
    ppermute x4, starting transfers between devices, butterfly_gather(): got = lax.ppermute(flat, axis, [(j, j ^ step) for j in range(count)])  32.2 us
    all_gather x1, blocking collectives, per_device(): out_grad = lax.all_gather(out_grad, 'space', axis=1, tiled=True)  16.7 us
    ppermute x4, waiting for transfers between devices, butterfly_gather(): got = lax.ppermute(flat, axis, [(j, j ^ step) for j in range(count)])  16 us
    ppermute x3, starting transfers between devices, butterfly_sum(): lax.ppermute(flat, axis, [(j, j ^ step) for j in range(count)])  15.8 us
    ppermute x3, waiting for transfers between devices, butterfly_sum(): lax.ppermute(flat, axis, [(j, j ^ step) for j in range(count)])  13.2 us
    all_gather x1, blocking collectives, per_device(): images = lax.all_gather(images, 'space', axis=1, tiled=True)  12.8 us
    ppermute x2, waiting for transfers between devices, butterfly_scatter(): lax.ppermute(sent, axis, [(j, j ^ step) for j in range(count)])  9.8 us
    ppermute x2, starting transfers between devices, butterfly_scatter(): lax.ppermute(sent, axis, [(j, j ^ step) for j in range(count)])  7.83 us
  transfers between devices with their start and end apart: 17, of which 12 were waited for; matrix products, arithmetic and copies ran while one was open for 6% of the time, Pallas kernels for 0%

profile of v12, /device:TPU:1, one launch (start us, length us, event | category | flops | bytes accessed | tf_op | source)
XLA Modules:
  0.0 195.2 jit_solution(13829696705477760555)
XLA Ops:
  0.7 12.8 %all_gather.6 = bf16[2,4,64,256]{3,2,0,1:T(8,128)(2,1)S(1)} all-gather(bf16[2,1,64,256]{3,2,0,1:T(8,128)(2,1)} %bitcast.164), channel_id=1, replica_groups=mesh['dy'=8,'dx'=4,'section'=4,'space'=4] {'space'}, dimensions={1}, use_global_device_ids=true | all-gather | bytes 327680 | tf_op jit(solution)/shard_map/all_gather | solution.py:175
  16.3 1.2 fusion.217
  20.6 1.3 collective-permute-start
  21.9 5.9 %collective-permute-done = bf16[2,4,64,256]{3,1,2,0:T(4,128)(2,1)S(1)} collective-permute-done((bf16[2,4,64,256]{3,1,2,0:T(4,128)(2,1)}, bf16[2,4,64,256]{3,1,2,0:T(4,128)(2,1)S(1)}, u32[]{:S(2)}, u32[]{:S(2)}) %collective-permute-start) | collective-permute-done | bytes 262176 | tf_op jit(solution)/shard_map/ppermute | solution.py:195
  31.9 1.3 collective-permute-start.3
  33.3 16.7 %all_gather.7 = bf16[2,4,64,256]{3,2,0,1:T(8,128)(2,1)S(1)} all-gather(bf16[2,1,64,256]{3,2,0,1:T(8,128)(2,1)S(1)} %bitcast.165), channel_id=1, replica_groups=mesh['dy'=8,'dx'=4,'section'=4,'space'=4] {'space'}, dimensions={1}, use_global_device_ids=true | all-gather | bytes 327680 | tf_op jit(solution)/shard_map/all_gather | solution.py:176
  58.2 3.0 %multiply_reduce_fusion = (f32[2,256]{1,0:T(2,128)S(1)}, f32[256]{0:T(256)S(1)}, f32[2,256]{1,0:T(2,128)S(1)}, f32[2,256]{1,0:T(2,128)S(1)}, f32[2,256]{1,0:T(2,...) fusion(f32[2,256]{1,0:T(2,128)S(1)} %get-tuple-element.35, ...), kind=kLoop, calls=%fused_computation.135 | loop fusion | flops 9697024 | bytes 2918403 | tf_op jit(solution)/shard_map/transpose(jvp())/reduce_sum | solution.py:123
  68.2 1.3 collective-permute-start.7
  73.4 1.5 collective-permute-start.6
  75.3 4.4 %collective-permute-done.7 = bf16[2,4,64,256]{3,1,2,0:T(4,128)(2,1)S(1)} collective-permute-done((bf16[2,4,64,256]{3,1,2,0:T(4,128)(2,1)S(1)}, bf16[2,4,64,256]{3,1,2,0:T(4,128)(2,1)S(1)}, u32[]{:S(2)}, u32[]{:S(2)}) %collective-permute-start.7) | collective-permute-done | bytes 262176 | tf_op jit(solution)/shard_map/ppermute | solution.py:220
  79.7 6.3 %collective-permute-done.6 = bf16[2,4,64,256]{3,1,2,0:T(4,128)(2,1)S(1)} collective-permute-done((bf16[2,4,64,256]{3,1,2,0:T(4,128)(2,1)S(1)}, bf16[2,4,64,256]{3,1,2,0:T(4,128)(2,1)S(1)}, u32[]{:S(2)}, u32[]{:S(2)}) %collective-permute-start.6) | collective-permute-done | bytes 262176 | tf_op jit(solution)/shard_map/ppermute | solution.py:211
  91.4 1.6 copy.82
  94.0 1.8 fusion.55
  96.0 3.1 %collective-permute-start.8 = (f32[368,256]{1,0:T(8,128)S(1)}, f32[368,256]{1,0:T(8,128)S(1)}, u32[]{:S(2)}, u32[]{:S(2)}) collective-permute-start(f32[368,256]{1,0:T(8,128)S(1)} %constant_dynamic-slice_fusion.2), channel_id=1, source_target_pairs={{0,16},{16,0},{32,48},{48,32},{1,17},{17,1},{33,49},{49,33},{2,18}... | collective-permute-start | bytes 1130504 | tf_op jit(solution)/shard_map/ppermute | solution.py:252
  99.2 5.2 %collective-permute-done.8 = f32[368,256]{1,0:T(8,128)S(1)} collective-permute-done((f32[368,256]{1,0:T(8,128)S(1)}, f32[368,256]{1,0:T(8,128)S(1)}, u32[]{:S(2)}, u32[]{:S(2)}) %collective-permute-start.8) | collective-permute-done | bytes 376864 | tf_op jit(solution)/shard_map/ppermute | solution.py:252
  104.5 4.7 %collective-permute-start.9 = (f32[184,256]{1,0:T(8,128)S(1)}, f32[184,256]{1,0:T(8,128)S(1)}, u32[]{:S(2)}, u32[]{:S(2)}) collective-permute-start(f32[184,256]{1,0:T(8,128)S(1)} %constant_dynamic-slice_fusion.1), channel_id=1, source_target_pairs={{0,32},{16,48},{32,0},{48,16},{1,33},{17,49},{33,1},{49,17},{2,34}... | collective-permute-start | bytes 565256 | tf_op jit(solution)/shard_map/ppermute | solution.py:252
  109.2 4.6 %collective-permute-done.9 = f32[184,256]{1,0:T(8,128)S(1)} collective-permute-done((f32[184,256]{1,0:T(8,128)S(1)}, f32[184,256]{1,0:T(8,128)S(1)}, u32[]{:S(2)}, u32[]{:S(2)}) %collective-permute-start.9) | collective-permute-done | bytes 188448 | tf_op jit(solution)/shard_map/ppermute | solution.py:252
  113.8 3.2 %collective-permute-start.10 = (f32[184,256]{1,0:T(8,128)S(1)}, f32[184,256]{1,0:T(8,128)S(1)}, u32[]{:S(2)}, u32[]{:S(2)}) collective-permute-start(f32[184,256]{1,0:T(8,128)S(1)} %dynamic-slice_add_fusion.1), channel_id=1, source_target_pairs={{0,64},{64,0},{128,192},{192,128},{256,320},{320,256},{384,448},{4... | collective-permute-start | bytes 565256 | tf_op jit(solution)/shard_map/ppermute | solution.py:261
  117.1 3.1 %collective-permute-done.10 = f32[184,256]{1,0:T(8,128)S(1)} collective-permute-done((f32[184,256]{1,0:T(8,128)S(1)}, f32[184,256]{1,0:T(8,128)S(1)}, u32[]{:S(2)}, u32[]{:S(2)}) %collective-permute-start.10) | collective-permute-done | bytes 188448 | tf_op jit(solution)/shard_map/ppermute | solution.py:261
  120.2 4.2 %collective-permute-start.11 = (f32[184,256]{1,0:T(8,128)S(1)}, f32[184,256]{1,0:T(8,128)S(1)}, u32[]{:S(2)}, u32[]{:S(2)}) collective-permute-start(f32[184,256]{1,0:T(8,128)S(1)} %add.278), channel_id=1, source_target_pairs={{0,128},{64,192},{128,0},{192,64},{256,384},{320,448},{384,256},{4... | collective-permute-start | bytes 565256 | tf_op jit(solution)/shard_map/ppermute | solution.py:261
  124.4 4.1 %collective-permute-done.11 = f32[184,256]{1,0:T(8,128)S(1)} collective-permute-done((f32[184,256]{1,0:T(8,128)S(1)}, f32[184,256]{1,0:T(8,128)S(1)}, u32[]{:S(2)}, u32[]{:S(2)}) %collective-permute-start.11) | collective-permute-done | bytes 188448 | tf_op jit(solution)/shard_map/ppermute | solution.py:261
  128.5 8.4 %collective-permute-start.12 = (f32[184,256]{1,0:T(8,128)S(1)}, f32[184,256]{1,0:T(8,128)S(1)}, u32[]{:S(2)}, u32[]{:S(2)}) collective-permute-start(f32[184,256]{1,0:T(8,128)S(1)} %add.279), channel_id=1, source_target_pairs={{0,256},{64,320},{128,384},{192,448},{256,0},{320,64},{384,128},{4... | collective-permute-start | bytes 565256 | tf_op jit(solution)/shard_map/ppermute | solution.py:261
  136.9 6.1 %collective-permute-done.12 = f32[184,256]{1,0:T(8,128)S(1)} collective-permute-done((f32[184,256]{1,0:T(8,128)S(1)}, f32[184,256]{1,0:T(8,128)S(1)}, u32[]{:S(2)}, u32[]{:S(2)}) %collective-permute-start.12) | collective-permute-done | bytes 188448 | tf_op jit(solution)/shard_map/ppermute | solution.py:261
  143.1 1.9 collective-permute-start.13
  145.0 4.9 %collective-permute-done.13 = bf16[184,256]{1,0:T(8,128)(2,1)S(1)} collective-permute-done((bf16[184,256]{1,0:T(8,128)(2,1)S(1)}, bf16[184,256]{1,0:T(8,128)(2,1)S(1)}, u32[]{:S(2)}, u32[]{:S(2)}) %collective-permute-start.13) | collective-permute-done | bytes 94240 | tf_op jit(solution)/shard_map/ppermute | solution.py:271
  149.9 1.9 collective-permute-start.14
  151.9 4.3 %collective-permute-done.14 = bf16[368,256]{1,0:T(8,128)(2,1)S(1)} collective-permute-done((bf16[368,256]{1,0:T(8,128)(2,1)S(1)}, bf16[368,256]{1,0:T(8,128)(2,1)S(1)}, u32[]{:S(2)}, u32[]{:S(2)}) %collective-permute-start.14) | collective-permute-done | bytes 188448 | tf_op jit(solution)/shard_map/ppermute | solution.py:271
  156.2 9.9 %collective-permute-start.15 = (bf16[736,256]{1,0:T(8,128)(2,1)S(1)}, bf16[736,256]{1,0:T(8,128)(2,1)S(1)}, u32[]{:S(2)}, u32[]{:S(2)}) collective-permute-start(bf16[736,256]{1,0:T(8,128)(2,1)S(1)} %constant_dynamic-update-slice_fusion.4), channel_id=1, source_target_pairs={{0,2},{1,3},{2,0},{3,1},{4,6},{5,7},{6,4},{7,5},{8,10},{9,11},{10,... | collective-permute-start | bytes 1130504 | tf_op jit(solution)/shard_map/ppermute | solution.py:271
  166.2 5.1 %collective-permute-done.15 = bf16[736,256]{1,0:T(8,128)(2,1)S(1)} collective-permute-done((bf16[736,256]{1,0:T(8,128)(2,1)S(1)}, bf16[736,256]{1,0:T(8,128)(2,1)S(1)}, u32[]{:S(2)}, u32[]{:S(2)}) %collective-permute-start.15) | collective-permute-done | bytes 376864 | tf_op jit(solution)/shard_map/ppermute | solution.py:271
  171.4 18.5 %collective-permute-start.16 = (bf16[1472,256]{1,0:T(8,128)(2,1)S(1)}, bf16[1472,256]{1,0:T(8,128)(2,1)S(1)}, u32[]{:S(2)}, u32[]{:S(2)}) collective-permute-start(bf16[1472,256]{1,0:T(8,128)(2,1)S(1)} %constant_dynamic-update-slice_fusion.2), channel_id=1, source_target_pairs={{0,1},{1,0},{2,3},{3,2},{4,5},{5,4},{6,7},{7,6},{8,9},{9,8},{10,11... | collective-permute-start | bytes 2261000 | tf_op jit(solution)/shard_map/ppermute | solution.py:271
  190.1 1.7 collective-permute-done.16
  192.0 1.6 slice.95
  (140 shorter events, 37.7 us)
Async XLA Ops:
  0.6 17.7 %copy-start = (bf16[1,3,3,256,256]{4,3,2,1,0:T(8,128)(2,1)S(1)}, bf16[1,3,3,256,256]{4,3,2,1,0:T(8,128)(2,1)}, u32[]{:S(2)}) copy-start(bf16[1,3,3,256,256]{4,3,2,1,0:T(8,128)(2,1)} %param.9) | copy-start | bytes 3538948
  0.6 17.7 %copy-start.3 = (pred[16,9]{0,1:T(8,128)(4,1)S(1)}, pred[16,9]{0,1:T(8,128)(4,1)}, u32[]{:S(2)}) copy-start(pred[16,9]{0,1:T(8,128)(4,1)} %constant.221) | copy-start | bytes 436
  18.3 10.2 %copy-start.1 = (f32[1,256]{1,0:T(1,128)S(1)}, f32[1,256]{1,0:T(1,128)}, u32[]{:S(2)}) copy-start(f32[1,256]{1,0:T(1,128)} %param.10) | copy-start | bytes 3076
  20.6 7.2 %collective-permute-start = (bf16[2,4,64,256]{3,1,2,0:T(4,128)(2,1)}, bf16[2,4,64,256]{3,1,2,0:T(4,128)(2,1)S(1)}, u32[]{:S(2)}, u32[]{:S(2)}) collective-permute-start(bf16[2,4,64,256]{3,1,2,0:T(4,128)(2,1)} %fusion.79), channel_id=1, source_target_pairs={{0,4},{1,5},{2,6},{3,7},{16,20},{17,21},{18,22},{19,23},{32,36},{3... | collective-permute-start | bytes 786440 | tf_op jit(solution)/shard_map/ppermute | solution.py:195
  29.8 3.4 %copy-start.2 = (bf16[2,1,64,256]{3,2,1,0:T(8,128)(2,1)S(1)}, bf16[2,1,64,256]{3,2,1,0:T(8,128)(2,1)}, u32[]{:S(2)}) copy-start(bf16[2,1,64,256]{3,2,1,0:T(8,128)(2,1)} %param.8) | copy-start | bytes 196612
  31.2 19.6 %collective-permute-start.1 = (bf16[2,4,64,256]{3,1,2,0:T(4,128)(2,1)S(1)}, bf16[2,4,64,256]{3,1,2,0:T(4,128)(2,1)S(1)}, u32[]{:S(2)}, u32[]{:S(2)}) collective-permute-start(bf16[2,4,64,256]{3,1,2,0:T(4,128)(2,1)S(1)} %fusion.85), channel_id=1, source_target_pairs={{4,8},{5,9},{6,10},{7,11},{20,24},{21,25},{22,26},{23,27},{36,40},... | collective-permute-start | bytes 786440 | tf_op jit(solution)/shard_map/ppermute | solution.py:195
  31.9 25.4 %collective-permute-start.3 = (bf16[2,4,64,256]{3,1,2,0:T(4,128)(2,1)}, bf16[2,4,64,256]{3,1,2,0:T(4,128)(2,1)S(1)}, u32[]{:S(2)}, u32[]{:S(2)}) collective-permute-start(bf16[2,4,64,256]{3,1,2,0:T(4,128)(2,1)} %fusion.79), channel_id=1, source_target_pairs={{0,12},{1,13},{2,14},{3,15},{16,28},{17,29},{18,30},{19,31},{32,44... | collective-permute-start | bytes 786440 | tf_op jit(solution)/shard_map/ppermute | solution.py:200
  55.0 2.3 %collective-permute-start.2 = (bf16[2,4,64,256]{3,1,2,0:T(4,128)(2,1)}, bf16[2,4,64,256]{3,1,2,0:T(4,128)(2,1)S(1)}, u32[]{:S(2)}, u32[]{:S(2)}) collective-permute-start(bf16[2,4,64,256]{3,1,2,0:T(4,128)(2,1)} %fusion.91), channel_id=1, source_target_pairs={{8,12},{9,13},{10,14},{11,15},{24,28},{25,29},{26,30},{27,31},{40,... | collective-permute-start | bytes 786440 | tf_op jit(solution)/shard_map/ppermute | solution.py:195
  62.1 1.2 collective-permute-start.4
  67.1 2.4 %collective-permute-start.5 = (bf16[2,4,64,256]{3,1,2,0:T(4,128)(2,1)S(1)}, bf16[2,4,64,256]{3,1,2,0:T(4,128)(2,1)S(1)}, u32[]{:S(2)}, u32[]{:S(2)}) collective-permute-start(bf16[2,4,64,256]{3,1,2,0:T(4,128)(2,1)S(1)} %fusion.97), channel_id=1, source_target_pairs={{8,4},{9,5},{10,6},{11,7},{24,20},{25,21},{26,22},{27,23},{40,36},... | collective-permute-start | bytes 786440 | tf_op jit(solution)/shard_map/ppermute | solution.py:211
  68.2 11.4 %collective-permute-start.7 = (bf16[2,4,64,256]{3,1,2,0:T(4,128)(2,1)S(1)}, bf16[2,4,64,256]{3,1,2,0:T(4,128)(2,1)S(1)}, u32[]{:S(2)}, u32[]{:S(2)}) collective-permute-start(bf16[2,4,64,256]{3,1,2,0:T(4,128)(2,1)S(1)} %fusion.94), channel_id=1, source_target_pairs={{12,0},{13,1},{14,2},{15,3},{28,16},{29,17},{30,18},{31,19},{44,32... | collective-permute-start | bytes 786440 | tf_op jit(solution)/shard_map/ppermute | solution.py:220
  73.4 12.6 %collective-permute-start.6 = (bf16[2,4,64,256]{3,1,2,0:T(4,128)(2,1)S(1)}, bf16[2,4,64,256]{3,1,2,0:T(4,128)(2,1)S(1)}, u32[]{:S(2)}, u32[]{:S(2)}) collective-permute-start(bf16[2,4,64,256]{3,1,2,0:T(4,128)(2,1)S(1)} %fusion.100), channel_id=1, source_target_pairs={{4,0},{5,1},{6,2},{7,3},{20,16},{21,17},{22,18},{23,19},{36,32},{3... | collective-permute-start | bytes 786440 | tf_op jit(solution)/shard_map/ppermute | solution.py:211
  96.0 8.3 %collective-permute-start.8 = (f32[368,256]{1,0:T(8,128)S(1)}, f32[368,256]{1,0:T(8,128)S(1)}, u32[]{:S(2)}, u32[]{:S(2)}) collective-permute-start(f32[368,256]{1,0:T(8,128)S(1)} %constant_dynamic-slice_fusion.2), channel_id=1, source_target_pairs={{0,16},{16,0},{32,48},{48,32},{1,17},{17,1},{33,49},{49,33},{2,18}... | collective-permute-start | bytes 1130504 | tf_op jit(solution)/shard_map/ppermute | solution.py:252
  104.5 9.4 %collective-permute-start.9 = (f32[184,256]{1,0:T(8,128)S(1)}, f32[184,256]{1,0:T(8,128)S(1)}, u32[]{:S(2)}, u32[]{:S(2)}) collective-permute-start(f32[184,256]{1,0:T(8,128)S(1)} %constant_dynamic-slice_fusion.1), channel_id=1, source_target_pairs={{0,32},{16,48},{32,0},{48,16},{1,33},{17,49},{33,1},{49,17},{2,34}... | collective-permute-start | bytes 565256 | tf_op jit(solution)/shard_map/ppermute | solution.py:252
  113.8 6.3 %collective-permute-start.10 = (f32[184,256]{1,0:T(8,128)S(1)}, f32[184,256]{1,0:T(8,128)S(1)}, u32[]{:S(2)}, u32[]{:S(2)}) collective-permute-start(f32[184,256]{1,0:T(8,128)S(1)} %dynamic-slice_add_fusion.1), channel_id=1, source_target_pairs={{0,64},{64,0},{128,192},{192,128},{256,320},{320,256},{384,448},{4... | collective-permute-start | bytes 565256 | tf_op jit(solution)/shard_map/ppermute | solution.py:261
  120.2 8.3 %collective-permute-start.11 = (f32[184,256]{1,0:T(8,128)S(1)}, f32[184,256]{1,0:T(8,128)S(1)}, u32[]{:S(2)}, u32[]{:S(2)}) collective-permute-start(f32[184,256]{1,0:T(8,128)S(1)} %add.278), channel_id=1, source_target_pairs={{0,128},{64,192},{128,0},{192,64},{256,384},{320,448},{384,256},{4... | collective-permute-start | bytes 565256 | tf_op jit(solution)/shard_map/ppermute | solution.py:261
  128.5 14.5 %collective-permute-start.12 = (f32[184,256]{1,0:T(8,128)S(1)}, f32[184,256]{1,0:T(8,128)S(1)}, u32[]{:S(2)}, u32[]{:S(2)}) collective-permute-start(f32[184,256]{1,0:T(8,128)S(1)} %add.279), channel_id=1, source_target_pairs={{0,256},{64,320},{128,384},{192,448},{256,0},{320,64},{384,128},{4... | collective-permute-start | bytes 565256 | tf_op jit(solution)/shard_map/ppermute | solution.py:261
  143.1 6.8 %collective-permute-start.13 = (bf16[184,256]{1,0:T(8,128)(2,1)S(1)}, bf16[184,256]{1,0:T(8,128)(2,1)S(1)}, u32[]{:S(2)}, u32[]{:S(2)}) collective-permute-start(bf16[184,256]{1,0:T(8,128)(2,1)S(1)} %get-tuple-element.30), channel_id=1, source_target_pairs={{0,32},{16,48},{32,0},{48,16},{1,33},{17,49},{33,1},{49,17},{2,34}... | collective-permute-start | bytes 282632 | tf_op jit(solution)/shard_map/ppermute | solution.py:271
  149.9 6.3 %collective-permute-start.14 = (bf16[368,256]{1,0:T(8,128)(2,1)S(1)}, bf16[368,256]{1,0:T(8,128)(2,1)S(1)}, u32[]{:S(2)}, u32[]{:S(2)}) collective-permute-start(bf16[368,256]{1,0:T(8,128)(2,1)S(1)} %constant_dynamic-update-slice_fusion.6), channel_id=1, source_target_pairs={{0,16},{16,0},{32,48},{48,32},{1,17},{17,1},{33,49},{49,33},{2,18}... | collective-permute-start | bytes 565256 | tf_op jit(solution)/shard_map/ppermute | solution.py:271
  156.2 15.1 %collective-permute-start.15 = (bf16[736,256]{1,0:T(8,128)(2,1)S(1)}, bf16[736,256]{1,0:T(8,128)(2,1)S(1)}, u32[]{:S(2)}, u32[]{:S(2)}) collective-permute-start(bf16[736,256]{1,0:T(8,128)(2,1)S(1)} %constant_dynamic-update-slice_fusion.4), channel_id=1, source_target_pairs={{0,2},{1,3},{2,0},{3,1},{4,6},{5,7},{6,4},{7,5},{8,10},{9,11},{10,... | collective-permute-start | bytes 1130504 | tf_op jit(solution)/shard_map/ppermute | solution.py:271
  171.4 20.3 %collective-permute-start.16 = (bf16[1472,256]{1,0:T(8,128)(2,1)S(1)}, bf16[1472,256]{1,0:T(8,128)(2,1)S(1)}, u32[]{:S(2)}, u32[]{:S(2)}) collective-permute-start(bf16[1472,256]{1,0:T(8,128)(2,1)S(1)} %constant_dynamic-update-slice_fusion.2), channel_id=1, source_target_pairs={{0,1},{1,0},{2,3},{3,2},{4,5},{5,4},{6,7},{7,6},{8,9},{9,8},{10,11... | collective-permute-start | bytes 2261000 | tf_op jit(solution)/shard_map/ppermute | solution.py:271

commit v13 on v11

--- a/solution.py
+++ b/solution.py
@@ -271,8 +271,7 @@
         bit = (index // step) % 2
         got = lax.ppermute(flat, axis, [(j, j ^ step) for j in range(count)])
         length = flat.shape[0]
-        joined = jnp.zeros((2 * length, *flat.shape[1:]), flat.dtype)
-        joined = lax.dynamic_update_slice_in_dim(joined, flat, bit * length, 0)
+        joined = jnp.concatenate([flat, flat])
         flat = lax.dynamic_update_slice_in_dim(joined, got, (1 - bit) * length, 0)
     return flat
 

time: 193 us -> 193 us (level)
  no operation moved by 1% of the time
where the time goes in v13:
time: 193 us; the launch traced here: 191 us
  starting transfers between devices  66.5 us (34%)
  waiting for transfers between devices  58.7 us (30%)
  blocking collectives  23.3 us (12%)
  other arithmetic  15 us (8%)
  local copies, waits for them, and re-layouts  13 us (7%)
  matrix products  12.9 us (7%)
    ppermute x4, starting transfers between devices, butterfly_gather(): got = lax.ppermute(flat, axis, [(j, j ^ step) for j in range(count)])  31.4 us
    ppermute x3, waiting for transfers between devices, per_device(): upstream = lax.ppermute(carried, 'section', [(active + 1, active)])  19.1 us
    ppermute x3, starting transfers between devices, butterfly_sum(): lax.ppermute(flat, axis, [(j, j ^ step) for j in range(count)])  15.8 us
    ppermute x4, waiting for transfers between devices, butterfly_gather(): got = lax.ppermute(flat, axis, [(j, j ^ step) for j in range(count)])  14.8 us
    ppermute x3, waiting for transfers between devices, butterfly_sum(): lax.ppermute(flat, axis, [(j, j ^ step) for j in range(count)])  13.3 us
    all_gather x1, blocking collectives, per_device(): images = lax.all_gather(images, 'space', axis=1, tiled=True)  12.8 us
    all_gather x1, blocking collectives, per_device(): out_grad = lax.all_gather(out_grad, 'space', axis=1, tiled=True)  10.5 us
    ppermute x2, waiting for transfers between devices, butterfly_scatter(): lax.ppermute(sent, axis, [(j, j ^ step) for j in range(count)])  9.09 us
  transfers between devices with their start and end apart: 17, of which 11 were waited for; matrix products, arithmetic and copies ran while one was open for 11% of the time, Pallas kernels for 0%

profile of v13, /device:TPU:1, one launch (start us, length us, event | category | flops | bytes accessed | tf_op | source)
XLA Modules:
  0.0 191.3 jit_solution(9327620106959557601)
XLA Ops:
  0.7 12.8 %all_gather.6 = bf16[2,4,64,256]{3,2,0,1:T(8,128)(2,1)S(1)} all-gather(bf16[2,1,64,256]{3,2,0,1:T(8,128)(2,1)} %bitcast.164), channel_id=1, replica_groups=mesh['dy'=8,'dx'=4,'section'=4,'space'=4] {'space'}, dimensions={1}, use_global_device_ids=true | all-gather | bytes 327680 | tf_op jit(solution)/shard_map/all_gather | solution.py:176
  14.6 1.2 fusion.130
  16.3 1.2 fusion.221
  19.9 1.3 collective-permute-start
  21.2 4.7 %collective-permute-start.3 = (bf16[2,4,64,256]{3,1,2,0:T(4,128)(2,1)S(1)}, bf16[2,4,64,256]{3,1,2,0:T(4,128)(2,1)S(1)}, u32[]{:S(2)}, u32[]{:S(2)}) collective-permute-start(bf16[2,4,64,256]{3,1,2,0:T(4,128)(2,1)S(1)} %fusion.79), channel_id=1, source_target_pairs={{0,12},{1,13},{2,14},{3,15},{16,28},{17,29},{18,30},{19,31},{32,44... | collective-permute-start | bytes 786440 | tf_op jit(solution)/shard_map/ppermute | solution.py:201
  25.9 10.5 %all_gather.7 = bf16[2,4,64,256]{3,2,0,1:T(8,128)(2,1)S(1)} all-gather(bf16[2,1,64,256]{3,2,0,1:T(8,128)(2,1)S(1)} %bitcast.165), channel_id=1, replica_groups=mesh['dy'=8,'dx'=4,'section'=4,'space'=4] {'space'}, dimensions={1}, use_global_device_ids=true | all-gather | bytes 327680 | tf_op jit(solution)/shard_map/all_gather | solution.py:177
  49.4 1.8 multiply_reduce_fusion
  52.8 1.3 collective-permute-start.7
  64.5 1.3 collective-permute-start.6
  66.2 1.6 copy.82
  67.8 2.4 %collective-permute-done.7 = bf16[2,4,64,256]{3,1,2,0:T(4,128)(2,1)S(1)} collective-permute-done((bf16[2,4,64,256]{3,1,2,0:T(4,128)(2,1)S(1)}, bf16[2,4,64,256]{3,1,2,0:T(4,128)(2,1)S(1)}, u32[]{:S(2)}, u32[]{:S(2)}) %collective-permute-start.7) | collective-permute-done | bytes 262176 | tf_op jit(solution)/shard_map/ppermute | solution.py:221
  70.2 19.1 %collective-permute-done.6 = bf16[2,4,64,256]{3,1,2,0:T(4,128)(2,1)S(1)} collective-permute-done((bf16[2,4,64,256]{3,1,2,0:T(4,128)(2,1)S(1)}, bf16[2,4,64,256]{3,1,2,0:T(4,128)(2,1)S(1)}, u32[]{:S(2)}, u32[]{:S(2)}) %collective-permute-start.6) | collective-permute-done | bytes 262176 | tf_op jit(solution)/shard_map/ppermute | solution.py:212
  93.1 1.8 fusion.55
  95.1 3.1 %collective-permute-start.8 = (f32[368,256]{1,0:T(8,128)S(1)}, f32[368,256]{1,0:T(8,128)S(1)}, u32[]{:S(2)}, u32[]{:S(2)}) collective-permute-start(f32[368,256]{1,0:T(8,128)S(1)} %constant_dynamic-slice_fusion.2), channel_id=1, source_target_pairs={{0,16},{16,0},{32,48},{48,32},{1,17},{17,1},{33,49},{49,33},{2,18}... | collective-permute-start | bytes 1130504 | tf_op jit(solution)/shard_map/ppermute | solution.py:253
  98.2 5.2 %collective-permute-done.8 = f32[368,256]{1,0:T(8,128)S(1)} collective-permute-done((f32[368,256]{1,0:T(8,128)S(1)}, f32[368,256]{1,0:T(8,128)S(1)}, u32[]{:S(2)}, u32[]{:S(2)}) %collective-permute-start.8) | collective-permute-done | bytes 376864 | tf_op jit(solution)/shard_map/ppermute | solution.py:253
  103.5 4.7 %collective-permute-start.9 = (f32[184,256]{1,0:T(8,128)S(1)}, f32[184,256]{1,0:T(8,128)S(1)}, u32[]{:S(2)}, u32[]{:S(2)}) collective-permute-start(f32[184,256]{1,0:T(8,128)S(1)} %constant_dynamic-slice_fusion.1), channel_id=1, source_target_pairs={{0,32},{16,48},{32,0},{48,16},{1,33},{17,49},{33,1},{49,17},{2,34}... | collective-permute-start | bytes 565256 | tf_op jit(solution)/shard_map/ppermute | solution.py:253
  108.2 3.9 %collective-permute-done.9 = f32[184,256]{1,0:T(8,128)S(1)} collective-permute-done((f32[184,256]{1,0:T(8,128)S(1)}, f32[184,256]{1,0:T(8,128)S(1)}, u32[]{:S(2)}, u32[]{:S(2)}) %collective-permute-start.9) | collective-permute-done | bytes 188448 | tf_op jit(solution)/shard_map/ppermute | solution.py:253
  112.1 3.2 %collective-permute-start.10 = (f32[184,256]{1,0:T(8,128)S(1)}, f32[184,256]{1,0:T(8,128)S(1)}, u32[]{:S(2)}, u32[]{:S(2)}) collective-permute-start(f32[184,256]{1,0:T(8,128)S(1)} %dynamic-slice_add_fusion.1), channel_id=1, source_target_pairs={{0,64},{64,0},{128,192},{192,128},{256,320},{320,256},{384,448},{4... | collective-permute-start | bytes 565256 | tf_op jit(solution)/shard_map/ppermute | solution.py:262
  115.3 3.1 %collective-permute-done.10 = f32[184,256]{1,0:T(8,128)S(1)} collective-permute-done((f32[184,256]{1,0:T(8,128)S(1)}, f32[184,256]{1,0:T(8,128)S(1)}, u32[]{:S(2)}, u32[]{:S(2)}) %collective-permute-start.10) | collective-permute-done | bytes 188448 | tf_op jit(solution)/shard_map/ppermute | solution.py:262
  118.4 4.2 %collective-permute-start.11 = (f32[184,256]{1,0:T(8,128)S(1)}, f32[184,256]{1,0:T(8,128)S(1)}, u32[]{:S(2)}, u32[]{:S(2)}) collective-permute-start(f32[184,256]{1,0:T(8,128)S(1)} %add.291), channel_id=1, source_target_pairs={{0,128},{64,192},{128,0},{192,64},{256,384},{320,448},{384,256},{4... | collective-permute-start | bytes 565256 | tf_op jit(solution)/shard_map/ppermute | solution.py:262
  122.7 4.1 %collective-permute-done.11 = f32[184,256]{1,0:T(8,128)S(1)} collective-permute-done((f32[184,256]{1,0:T(8,128)S(1)}, f32[184,256]{1,0:T(8,128)S(1)}, u32[]{:S(2)}, u32[]{:S(2)}) %collective-permute-start.11) | collective-permute-done | bytes 188448 | tf_op jit(solution)/shard_map/ppermute | solution.py:262
  126.8 8.3 %collective-permute-start.12 = (f32[184,256]{1,0:T(8,128)S(1)}, f32[184,256]{1,0:T(8,128)S(1)}, u32[]{:S(2)}, u32[]{:S(2)}) collective-permute-start(f32[184,256]{1,0:T(8,128)S(1)} %add.292), channel_id=1, source_target_pairs={{0,256},{64,320},{128,384},{192,448},{256,0},{320,64},{384,128},{4... | collective-permute-start | bytes 565256 | tf_op jit(solution)/shard_map/ppermute | solution.py:262
  135.1 6.1 %collective-permute-done.12 = f32[184,256]{1,0:T(8,128)S(1)} collective-permute-done((f32[184,256]{1,0:T(8,128)S(1)}, f32[184,256]{1,0:T(8,128)S(1)}, u32[]{:S(2)}, u32[]{:S(2)}) %collective-permute-start.12) | collective-permute-done | bytes 188448 | tf_op jit(solution)/shard_map/ppermute | solution.py:262
  141.3 3.2 %collective-permute-start.13 = (bf16[184,256]{1,0:T(8,128)(2,1)S(1)}, bf16[184,256]{1,0:T(8,128)(2,1)S(1)}, u32[]{:S(2)}, u32[]{:S(2)}) collective-permute-start(bf16[184,256]{1,0:T(8,128)(2,1)S(1)} %add_convert_fusion.2), channel_id=1, source_target_pairs={{0,32},{16,48},{32,0},{48,16},{1,33},{17,49},{33,1},{49,17},{2,34}... | collective-permute-start | bytes 282632 | tf_op jit(solution)/shard_map/ppermute | solution.py:272
  144.5 3.6 %collective-permute-done.13 = bf16[184,256]{1,0:T(8,128)(2,1)S(1)} collective-permute-done((bf16[184,256]{1,0:T(8,128)(2,1)S(1)}, bf16[184,256]{1,0:T(8,128)(2,1)S(1)}, u32[]{:S(2)}, u32[]{:S(2)}) %collective-permute-start.13) | collective-permute-done | bytes 94240 | tf_op jit(solution)/shard_map/ppermute | solution.py:272
  148.1 1.9 %collective-permute-start.14 = (bf16[368,256]{1,0:T(8,128)(2,1)S(1)}, bf16[368,256]{1,0:T(8,128)(2,1)S(1)}, u32[]{:S(2)}, u32[]{:S(2)}) collective-permute-start(bf16[368,256]{1,0:T(8,128)(2,1)S(1)} %constant_dynamic-update-slice_fusion.3), channel_id=1, source_target_pairs={{0,16},{16,0},{32,48},{48,32},{1,17},{17,1},{33,49},{49,33},{2,18}... | collective-permute-start | bytes 565256 | tf_op jit(solution)/shard_map/ppermute | solution.py:272
  150.1 4.4 %collective-permute-done.14 = bf16[368,256]{1,0:T(8,128)(2,1)S(1)} collective-permute-done((bf16[368,256]{1,0:T(8,128)(2,1)S(1)}, bf16[368,256]{1,0:T(8,128)(2,1)S(1)}, u32[]{:S(2)}, u32[]{:S(2)}) %collective-permute-start.14) | collective-permute-done | bytes 188448 | tf_op jit(solution)/shard_map/ppermute | solution.py:272
  154.4 9.1 %collective-permute-start.15 = (bf16[736,256]{1,0:T(8,128)(2,1)S(1)}, bf16[736,256]{1,0:T(8,128)(2,1)S(1)}, u32[]{:S(2)}, u32[]{:S(2)}) collective-permute-start(bf16[736,256]{1,0:T(8,128)(2,1)S(1)} %constant_dynamic-update-slice_fusion.2), channel_id=1, source_target_pairs={{0,2},{1,3},{2,0},{3,1},{4,6},{5,7},{6,4},{7,5},{8,10},{9,11},{10,... | collective-permute-start | bytes 1130504 | tf_op jit(solution)/shard_map/ppermute | solution.py:272
  163.6 5.2 %collective-permute-done.15 = bf16[736,256]{1,0:T(8,128)(2,1)S(1)} collective-permute-done((bf16[736,256]{1,0:T(8,128)(2,1)S(1)}, bf16[736,256]{1,0:T(8,128)(2,1)S(1)}, u32[]{:S(2)}, u32[]{:S(2)}) %collective-permute-start.15) | collective-permute-done | bytes 376864 | tf_op jit(solution)/shard_map/ppermute | solution.py:272
  168.8 17.2 %collective-permute-start.16 = (bf16[1472,256]{1,0:T(8,128)(2,1)S(1)}, bf16[1472,256]{1,0:T(8,128)(2,1)S(1)}, u32[]{:S(2)}, u32[]{:S(2)}) collective-permute-start(bf16[1472,256]{1,0:T(8,128)(2,1)S(1)} %constant_dynamic-update-slice_fusion.1), channel_id=1, source_target_pairs={{0,1},{1,0},{2,3},{3,2},{4,5},{5,4},{6,7},{7,6},{8,9},{9,8},{10,11... | collective-permute-start | bytes 2261000 | tf_op jit(solution)/shard_map/ppermute | solution.py:272
  186.2 1.7 collective-permute-done.16
  188.2 1.6 slice.95
  (137 shorter events, 34.9 us)
Async XLA Ops:
  0.6 17.7 %copy-start = (bf16[1,3,3,256,256]{4,3,2,1,0:T(8,128)(2,1)S(1)}, bf16[1,3,3,256,256]{4,3,2,1,0:T(8,128)(2,1)}, u32[]{:S(2)}) copy-start(bf16[1,3,3,256,256]{4,3,2,1,0:T(8,128)(2,1)} %param.9) | copy-start | bytes 3538948
  0.6 17.7 %copy-start.3 = (pred[16,9]{0,1:T(8,128)(4,1)S(1)}, pred[16,9]{0,1:T(8,128)(4,1)}, u32[]{:S(2)}) copy-start(pred[16,9]{0,1:T(8,128)(4,1)} %constant.217) | copy-start | bytes 436
  18.3 7.5 %copy-start.2 = (bf16[2,1,64,256]{3,2,1,0:T(8,128)(2,1)S(1)}, bf16[2,1,64,256]{3,2,1,0:T(8,128)(2,1)}, u32[]{:S(2)}) copy-start(bf16[2,1,64,256]{3,2,1,0:T(8,128)(2,1)} %param.8) | copy-start | bytes 196612
  19.9 19.3 %collective-permute-start = (bf16[2,4,64,256]{3,1,2,0:T(4,128)(2,1)S(1)}, bf16[2,4,64,256]{3,1,2,0:T(4,128)(2,1)S(1)}, u32[]{:S(2)}, u32[]{:S(2)}) collective-permute-start(bf16[2,4,64,256]{3,1,2,0:T(4,128)(2,1)S(1)} %fusion.79), channel_id=1, source_target_pairs={{0,4},{1,5},{2,6},{3,7},{16,20},{17,21},{18,22},{19,23},{32,36},{3... | collective-permute-start | bytes 786440 | tf_op jit(solution)/shard_map/ppermute | solution.py:196
  21.2 27.4 %collective-permute-start.3 = (bf16[2,4,64,256]{3,1,2,0:T(4,128)(2,1)S(1)}, bf16[2,4,64,256]{3,1,2,0:T(4,128)(2,1)S(1)}, u32[]{:S(2)}, u32[]{:S(2)}) collective-permute-start(bf16[2,4,64,256]{3,1,2,0:T(4,128)(2,1)S(1)} %fusion.79), channel_id=1, source_target_pairs={{0,12},{1,13},{2,14},{3,15},{16,28},{17,29},{18,30},{19,31},{32,44... | collective-permute-start | bytes 786440 | tf_op jit(solution)/shard_map/ppermute | solution.py:201
  36.9 1.8 copy-start.1
  42.6 1.3 collective-permute-start.1
  47.4 1.1 collective-permute-start.2
  52.1 3.4 %collective-permute-start.4 = (bf16[2,4,64,256]{3,1,2,0:T(4,128)(2,1)S(1)}, bf16[2,4,64,256]{3,1,2,0:T(4,128)(2,1)S(1)}, u32[]{:S(2)}, u32[]{:S(2)}) collective-permute-start(bf16[2,4,64,256]{3,1,2,0:T(4,128)(2,1)S(1)} %fusion.94), channel_id=1, source_target_pairs={{12,8},{13,9},{14,10},{15,11},{28,24},{29,25},{30,26},{31,27},{44,... | collective-permute-start | bytes 786440 | tf_op jit(solution)/shard_map/ppermute | solution.py:212
  52.8 17.4 %collective-permute-start.7 = (bf16[2,4,64,256]{3,1,2,0:T(4,128)(2,1)S(1)}, bf16[2,4,64,256]{3,1,2,0:T(4,128)(2,1)S(1)}, u32[]{:S(2)}, u32[]{:S(2)}) collective-permute-start(bf16[2,4,64,256]{3,1,2,0:T(4,128)(2,1)S(1)} %fusion.94), channel_id=1, source_target_pairs={{12,0},{13,1},{14,2},{15,3},{28,16},{29,17},{30,18},{31,19},{44,32... | collective-permute-start | bytes 786440 | tf_op jit(solution)/shard_map/ppermute | solution.py:221
  59.4 1.3 collective-permute-start.5
  64.5 24.9 %collective-permute-start.6 = (bf16[2,4,64,256]{3,1,2,0:T(4,128)(2,1)S(1)}, bf16[2,4,64,256]{3,1,2,0:T(4,128)(2,1)S(1)}, u32[]{:S(2)}, u32[]{:S(2)}) collective-permute-start(bf16[2,4,64,256]{3,1,2,0:T(4,128)(2,1)S(1)} %fusion.100), channel_id=1, source_target_pairs={{4,0},{5,1},{6,2},{7,3},{20,16},{21,17},{22,18},{23,19},{36,32},{3... | collective-permute-start | bytes 786440 | tf_op jit(solution)/shard_map/ppermute | solution.py:212
  95.1 8.3 %collective-permute-start.8 = (f32[368,256]{1,0:T(8,128)S(1)}, f32[368,256]{1,0:T(8,128)S(1)}, u32[]{:S(2)}, u32[]{:S(2)}) collective-permute-start(f32[368,256]{1,0:T(8,128)S(1)} %constant_dynamic-slice_fusion.2), channel_id=1, source_target_pairs={{0,16},{16,0},{32,48},{48,32},{1,17},{17,1},{33,49},{49,33},{2,18}... | collective-permute-start | bytes 1130504 | tf_op jit(solution)/shard_map/ppermute | solution.py:253
  103.5 8.5 %collective-permute-start.9 = (f32[184,256]{1,0:T(8,128)S(1)}, f32[184,256]{1,0:T(8,128)S(1)}, u32[]{:S(2)}, u32[]{:S(2)}) collective-permute-start(f32[184,256]{1,0:T(8,128)S(1)} %constant_dynamic-slice_fusion.1), channel_id=1, source_target_pairs={{0,32},{16,48},{32,0},{48,16},{1,33},{17,49},{33,1},{49,17},{2,34}... | collective-permute-start | bytes 565256 | tf_op jit(solution)/shard_map/ppermute | solution.py:253
  112.1 6.3 %collective-permute-start.10 = (f32[184,256]{1,0:T(8,128)S(1)}, f32[184,256]{1,0:T(8,128)S(1)}, u32[]{:S(2)}, u32[]{:S(2)}) collective-permute-start(f32[184,256]{1,0:T(8,128)S(1)} %dynamic-slice_add_fusion.1), channel_id=1, source_target_pairs={{0,64},{64,0},{128,192},{192,128},{256,320},{320,256},{384,448},{4... | collective-permute-start | bytes 565256 | tf_op jit(solution)/shard_map/ppermute | solution.py:262
  118.4 8.3 %collective-permute-start.11 = (f32[184,256]{1,0:T(8,128)S(1)}, f32[184,256]{1,0:T(8,128)S(1)}, u32[]{:S(2)}, u32[]{:S(2)}) collective-permute-start(f32[184,256]{1,0:T(8,128)S(1)} %add.291), channel_id=1, source_target_pairs={{0,128},{64,192},{128,0},{192,64},{256,384},{320,448},{384,256},{4... | collective-permute-start | bytes 565256 | tf_op jit(solution)/shard_map/ppermute | solution.py:262
  126.8 14.5 %collective-permute-start.12 = (f32[184,256]{1,0:T(8,128)S(1)}, f32[184,256]{1,0:T(8,128)S(1)}, u32[]{:S(2)}, u32[]{:S(2)}) collective-permute-start(f32[184,256]{1,0:T(8,128)S(1)} %add.292), channel_id=1, source_target_pairs={{0,256},{64,320},{128,384},{192,448},{256,0},{320,64},{384,128},{4... | collective-permute-start | bytes 565256 | tf_op jit(solution)/shard_map/ppermute | solution.py:262
  141.3 6.8 %collective-permute-start.13 = (bf16[184,256]{1,0:T(8,128)(2,1)S(1)}, bf16[184,256]{1,0:T(8,128)(2,1)S(1)}, u32[]{:S(2)}, u32[]{:S(2)}) collective-permute-start(bf16[184,256]{1,0:T(8,128)(2,1)S(1)} %add_convert_fusion.2), channel_id=1, source_target_pairs={{0,32},{16,48},{32,0},{48,16},{1,33},{17,49},{33,1},{49,17},{2,34}... | collective-permute-start | bytes 282632 | tf_op jit(solution)/shard_map/ppermute | solution.py:272
  148.1 6.3 %collective-permute-start.14 = (bf16[368,256]{1,0:T(8,128)(2,1)S(1)}, bf16[368,256]{1,0:T(8,128)(2,1)S(1)}, u32[]{:S(2)}, u32[]{:S(2)}) collective-permute-start(bf16[368,256]{1,0:T(8,128)(2,1)S(1)} %constant_dynamic-update-slice_fusion.3), channel_id=1, source_target_pairs={{0,16},{16,0},{32,48},{48,32},{1,17},{17,1},{33,49},{49,33},{2,18}... | collective-permute-start | bytes 565256 | tf_op jit(solution)/shard_map/ppermute | solution.py:272
  154.4 14.3 %collective-permute-start.15 = (bf16[736,256]{1,0:T(8,128)(2,1)S(1)}, bf16[736,256]{1,0:T(8,128)(2,1)S(1)}, u32[]{:S(2)}, u32[]{:S(2)}) collective-permute-start(bf16[736,256]{1,0:T(8,128)(2,1)S(1)} %constant_dynamic-update-slice_fusion.2), channel_id=1, source_target_pairs={{0,2},{1,3},{2,0},{3,1},{4,6},{5,7},{6,4},{7,5},{8,10},{9,11},{10,... | collective-permute-start | bytes 1130504 | tf_op jit(solution)/shard_map/ppermute | solution.py:272
  168.8 19.0 %collective-permute-start.16 = (bf16[1472,256]{1,0:T(8,128)(2,1)S(1)}, bf16[1472,256]{1,0:T(8,128)(2,1)S(1)}, u32[]{:S(2)}, u32[]{:S(2)}) collective-permute-start(bf16[1472,256]{1,0:T(8,128)(2,1)S(1)} %constant_dynamic-update-slice_fusion.1), channel_id=1, source_target_pairs={{0,1},{1,0},{2,3},{3,2},{4,5},{5,4},{6,7},{7,6},{8,9},{9,8},{10,11... | collective-permute-start | bytes 2261000 | tf_op jit(solution)/shard_map/ppermute | solution.py:272
